TPU v7x, 512 devices: a whole 4x8x8 slice. The times are simulated.
512 devices in a mesh: row: 32 (over y, x), col: 16 (over z, core).
Axes of the slice: x: 4, y: 8, z: 8, core: 2. Of those that a mesh axis runs over, the one named last changes fastest.
Arguments:
- stored: float32 [8192, 8192], P('row', 'col'), as said below
Outputs:
- factored: float32 [8192, 8192], P('row', 'col')
Inputs may be any that keep to these rules, and one draw needn't show every extreme that they name: stored is the storage order of a symmetric positive definite matrix.
All inputs are finite; a program needn't handle non-finite values.
Results may differ from a plain program's by a relative error of at most 0.0001.
Values sent between devices are 32-bit elements; how exact they have to be, the bound alone decides.
No kernel may reach another device: no remote copies, remote signals or barrier semaphores. Data moves between devices by JAX's collectives and lax.ppermute only.
A program may use at most 64 MiB of HBM per device.

v0:
```python
import jax
import jax.numpy as jnp
from jax import lax
from jax.sharding import PartitionSpec as P

NB = 64


def spread(array, axis, root):
    mine = lax.axis_index(axis) == root
    return lax.psum(jnp.where(mine, array, jnp.zeros_like(array)), axis)


def factor_panel(matrix, panel_index, row_ids, nrows, ncols):
    local_col = panel_index // ncols
    local_row = panel_index // nrows
    corner = matrix[local_row * NB : (local_row + 1) * NB, local_col * NB : (local_col + 1) * NB]
    corner = spread(corner, "row", panel_index % nrows)
    diag_factor = jnp.linalg.cholesky(corner)
    column_part = matrix[:, local_col * NB : (local_col + 1) * NB]
    solved = jax.scipy.linalg.solve_triangular(diag_factor, column_part.T, lower=True).T
    column_local = jnp.where(row_ids[:, None] > panel_index, solved, 0.0)
    current = column_local[local_row * NB : (local_row + 1) * NB]
    is_diag = row_ids[local_row * NB] == panel_index
    column_local = column_local.at[local_row * NB : (local_row + 1) * NB].set(
        jnp.where(is_diag, diag_factor, current)
    )
    return spread(column_local, "col", panel_index % ncols)


def matching_rows(panel_block, col_pos, nrows, ncols, row_count, col_count):
    gathered = lax.all_gather(panel_block, "row", axis=0, tiled=True)
    ordered = (
        gathered.reshape(nrows, row_count, NB, NB)
        .transpose(1, 0, 2, 3)
        .reshape(nrows * row_count, NB, NB)
    )
    wanted = jnp.arange(col_count, dtype=jnp.int32) * ncols + col_pos
    picked = jnp.take(ordered, wanted, axis=0)
    return picked.reshape(col_count * NB, NB)


def trailing_update(matrix, panel_block, picked, panel_index, row_ids, col_ids):
    product = jnp.dot(
        panel_block, picked.T, precision=lax.Precision.HIGHEST, preferred_element_type=jnp.float32
    )
    keep_cells = (row_ids[:, None] > panel_index) & (col_ids[None, :] > panel_index) & True
    return matrix - jnp.where(keep_cells, product, 0.0)


def set_column(matrix, panel_block, panel_index, col_pos, ncols):
    local_col = panel_index // ncols
    current = matrix[:, local_col * NB : (local_col + 1) * NB]
    return matrix.at[:, local_col * NB : (local_col + 1) * NB].set(
        jnp.where(col_pos == panel_index % ncols, panel_block, current)
    )


def per_device(stored):
    nrows = lax.axis_size("row")
    ncols = lax.axis_size("col")
    row_pos = lax.axis_index("row")
    col_pos = lax.axis_index("col")
    row_count = stored.shape[0] // NB
    col_count = stored.shape[1] // NB
    row_ids = jnp.arange(row_count * NB, dtype=jnp.int32) // NB * nrows + row_pos
    col_ids = jnp.arange(col_count * NB, dtype=jnp.int32) // NB * ncols + col_pos
    matrix = stored
    for panel_index in range(2):
        panel_block = factor_panel(matrix, panel_index, row_ids, nrows, ncols)
        picked = matching_rows(panel_block, col_pos, nrows, ncols, row_count, col_count)
        matrix = trailing_update(matrix, panel_block, picked, panel_index, row_ids, col_ids)
        matrix = set_column(matrix, panel_block, panel_index, col_pos, ncols)
    upper = (col_ids[None, :] >= 2) & (row_ids[:, None] < col_ids[None, :])
    return jnp.where(upper, 0.0, matrix)


def solution(mesh):
    return jax.shard_map(
        per_device,
        mesh=mesh,
        in_specs=(P("row", "col"),),
        out_specs=P("row", "col"),
        check_vma=False,
    )
```

profile of v0, /device:TPU:8, one launch (start us, length us, event | category | flops | bytes accessed | tf_op | source)
XLA Modules:
  0.0 751.8 jit_solution(203462624327193915)
XLA Ops:
  6.6 0.8 slice_select_fusion.3
  7.3 137.1 %psum.28 = f32[64,64]{1,0:T(8,128)S(1)} all-reduce(f32[64,64]{1,0:T(8,128)S(1)} %slice_select_fusion.3), channel_id=1, replica_groups=mesh['row'=32,'col'=16] {'row'}, use_global_device_ids=true, to_apply=%region_0.1 | all-reduce | flops 4096 | bytes 32768 | tf_op jit(solution)/shard_map/psum | solution.py:11
  144.6 5.9 cholesky.44
  150.5 0.6 compare_reduce_fusion.1
  151.2 0.7 select_bitcast_fusion.1
  151.8 4.9 custom-call.6
  157.3 1.2 fusion.3
  159.2 0.7 fusion.8
  159.8 0.7 broadcast_select_fusion.3
  160.6 119.0 %all-reduce.3.cloned.1.call-done = f32[256,64]{1,0:T(8,128)} async-done(((f32[256,64]{1,0:T(8,128)}), f32[256,64]{1,0:T(8,128)}) %all-reduce.3.cloned.1.call-update) | async-done | bytes 65552 | tf_op jit(solution)/shard_map/psum | solution.py:11
  280.3 0.7 compare_reduce_fusion.2
  281.1 89.3 %all-gather.3.cloned.1.call-done = f32[8192,64]{1,0:T(8,128)} async-done(((f32[256,64]{1,0:T(8,128)}), f32[8192,64]{1,0:T(8,128)}) %all-gather.3.cloned.1.call-update) | async-done | bytes 2097168 | tf_op jit(solution)/shard_map/all_gather | solution.py:32
  370.4 4.8 copy.11
  375.2 2.7 gather_fusion
  378.1 0.6 fusion
  378.7 0.7 select_select_fusion.1
  379.4 134.2 %psum.30 = f32[64,64]{1,0:T(8,128)S(1)} all-reduce(f32[64,64]{1,0:T(8,128)S(1)} %slice_select_fusion.1), channel_id=1, replica_groups=mesh['row'=32,'col'=16] {'row'}, use_global_device_ids=true, to_apply=%region_5.9 | all-reduce | flops 4096 | bytes 32768 | tf_op jit(solution)/shard_map/psum | solution.py:11
  513.7 5.9 cholesky.55
  519.6 0.6 compare_reduce_fusion
  520.3 0.7 select_bitcast_fusion
  520.9 4.9 custom-call.7
  526.1 0.7 fusion.7
  526.8 0.7 broadcast_select_fusion.2
  527.5 116.5 %all-reduce.5.cloned.1.call-done = f32[256,64]{1,0:T(8,128)} async-done(((f32[256,64]{1,0:T(8,128)}), f32[256,64]{1,0:T(8,128)}) %all-reduce.5.cloned.1.call-update) | async-done | bytes 65552 | tf_op jit(solution)/shard_map/psum | solution.py:11
  644.1 1.1 scatter.15
  645.2 89.1 %all-gather.5.cloned.1.call-done = f32[8192,64]{1,0:T(8,128)} async-done(((f32[256,64]{1,0:T(8,128)}), f32[8192,64]{1,0:T(8,128)}) %all-gather.5.cloned.1.call-update) | async-done | bytes 2097168 | tf_op jit(solution)/shard_map/all_gather | solution.py:32
  734.2 4.8 copy.15
  739.0 2.7 gather_fusion.1
  741.9 0.6 fusion.1
  742.5 0.7 select_select_fusion
  743.2 1.1 scatter.19
  744.3 0.9 and_select_fusion
  (36 shorter events, 1.7 us)
Async XLA Ops:
  6.5 273.0 %all-reduce.3.cloned.1.call-start = ((), (), s32[]{:S(2)}) async-start(), calls=%async_computation | async-start | bytes 262144 | tf_op jit(solution)/shard_map/psum | solution.py:11
  160.5 209.8 %all-gather.3.cloned.1.call-start = ((), (), s32[]{:S(2)}) async-start(), calls=%async_computation.1 | async-start | bytes 4325376 | tf_op jit(solution)/shard_map/all_gather | solution.py:32
  279.6 364.5 %all-reduce.5.cloned.1.call-start = ((), (), s32[]{:S(2)}) async-start(), calls=%async_computation.2 | async-start | bytes 262144 | tf_op jit(solution)/shard_map/psum | solution.py:11
  370.4 7.7 %copy-start = (f32[256,64]{1,0:T(8,128)S(1)}, f32[256,64]{1,0:T(8,128)}, u32[]{:S(2)}) copy-start(f32[256,64]{1,0:T(8,128)} %all-reduce.3.cloned.1.call-done) | copy-start | bytes 196612
  370.4 7.7 %copy-start.2 = (f32[256,512]{1,0:T(8,128)S(1)}, f32[256,512]{1,0:T(8,128)}, u32[]{:S(2)}) copy-start(f32[256,512]{1,0:T(8,128)} %param.14) | copy-start | bytes 1572868
  527.5 206.7 %all-gather.5.cloned.1.call-start = ((), (), s32[]{:S(2)}) async-start(), calls=%async_computation.3 | async-start | bytes 4325376 | tf_op jit(solution)/shard_map/all_gather | solution.py:32
  734.2 7.6 %copy-start.1 = (f32[256,64]{1,0:T(8,128)S(1)}, f32[256,64]{1,0:T(8,128)}, u32[]{:S(2)}) copy-start(f32[256,64]{1,0:T(8,128)} %all-reduce.5.cloned.1.call-done) | copy-start | bytes 196612
Sparse Core Ops, SparseCore 0:
  160.6 118.8 all-reduce.2
  283.2 87.1 all-gather.2
  527.6 116.3 all-reduce.4
  647.1 87.1 all-gather.4
where the time goes:
time: 752 us
  waiting for transfers between devices  414 us (55%)
  blocking collectives  271 us (36%)
  other arithmetic  30.9 us (4%)
  local copies, waits for them, and re-layouts  18.1 us (2%)
  between operations  14.7 us (2%)
    psum x2, blocking collectives, spread(): return lax.psum(jnp.where(mine, array, jnp.zeros_like(array)), axis)  271 us
    psum x2, waiting for transfers between devices, spread(): return lax.psum(jnp.where(mine, array, jnp.zeros_like(array)), axis)  235 us
    all_gather x2, waiting for transfers between devices, matching_rows(): gathered = lax.all_gather(panel_block, 'row', axis=0, tiled=True)  178 us
  transfers between devices with their start and end apart: 4, of which 4 were waited for; matrix products, arithmetic and copies ran while one was open for 0% of the time, Pallas kernels for 0%

commit v1 on v0

v1 whole, which is shorter than its diff:
```python
import jax
import jax.numpy as jnp
from jax import lax
from jax.sharding import PartitionSpec as P

NB = 64
HIGH = lax.Precision.HIGHEST


def both_axes(x, pairs):
    return lax.ppermute(x, ("row", "col"), pairs)


def gather_corner(stored, swapped, p, q, ncols):
    own = stored[:NB, :NB]
    got = swapped[:NB]
    d00, d01, d10, d11 = 0, 1, ncols, ncols + 1
    from_a = both_axes(own, [(d11, d00), (d00, d10)])
    from_b = both_axes(own, [(d11, d01), (d00, d11)])
    sent = jnp.where(q == 0, from_a, from_b)
    t = jnp.where(q == 0, got, own)
    u = jnp.where(q == 0, own, got)
    a00 = jnp.where(p == 0, u, sent)
    a10 = jnp.where(p == 0, t.T, u)
    a11 = jnp.where(p == 0, sent, t)
    return jnp.concatenate([a00, a10, a11], axis=0)


def spread_corner(corner, p, q, step, ncols):
    lin = lambda r, c: r * ncols + c
    src = [(r, c) for r in range(step) for c in range(step)]
    down = both_axes(corner, [(lin(r, c), lin(r + step, c)) for r, c in src])
    right = both_axes(corner, [(lin(r, c), lin(r, c + step)) for r, c in src])
    diag = both_axes(corner, [(lin(r, c), lin(r + step, c + step)) for r, c in src])
    low_p = (p >= step) & (p < 2 * step)
    low_q = (q >= step) & (q < 2 * step)
    top_p = p < step
    top_q = q < step
    out = jnp.where(low_p & top_q, down, corner)
    out = jnp.where(top_p & low_q, right, out)
    return jnp.where(low_p & low_q, diag, out)


def interleave(a, b, count):
    blocks = jnp.stack([a.reshape(count, NB, NB), b.reshape(count, NB, NB)], axis=1)
    return blocks.reshape(2 * count * NB, NB)


def solve_right(factor, rhs):
    return jax.scipy.linalg.solve_triangular(factor, rhs.T, lower=True).T


def per_device(stored):
    nrows = lax.axis_size("row")
    ncols = lax.axis_size("col")
    assert nrows == 2 * ncols
    half = nrows // 2
    p = lax.axis_index("row")
    q = lax.axis_index("col")
    row_count = stored.shape[0] // NB
    col_count = stored.shape[1] // NB
    assert col_count == 2 * row_count

    mine = stored[:, :NB]
    swapped = lax.ppermute(mine, "col", [(0, 1), (1, 0)])
    panel = jnp.concatenate(
        [jnp.where(q == 0, mine, swapped), jnp.where(q == 0, swapped, mine)], axis=0
    )
    corner = gather_corner(stored, swapped, p, q, ncols)
    step = 2
    while step < ncols:
        got = lax.ppermute(panel, "col", [(c, c + step) for c in range(step)])
        panel = jnp.where((q >= step) & (q < 2 * step), got, panel)
        corner = spread_corner(corner, p, q, step, ncols)
        step *= 2

    lin = lambda r, c: r * ncols + c
    carry = jnp.concatenate([panel, corner], axis=0)
    first_pairs = [(lin(c, r), lin(r, c)) for r in range(half) for c in range(ncols)]
    first_pairs += [(lin(c + half, r - half), lin(r, c)) for r in range(half, nrows) for c in range(ncols)]
    second_pairs = [(lin(c, r - half), lin(r, c)) for r in range(half, nrows) for c in range(ncols)]
    second_pairs += [(lin(c + half, r), lin(r, c)) for r in range(half) for c in range(ncols)]
    first = both_axes(carry, first_pairs)
    second = both_axes(carry, second_pairs)
    low = p < half
    near = jnp.where(low, first, second)
    far = jnp.where(low, second, first)
    rows_len = row_count * NB
    corner = near[2 * rows_len :]
    a00 = corner[:NB]
    a10 = corner[NB : 2 * NB]
    a11 = corner[2 * NB :]
    col0 = interleave(near[:rows_len], far[:rows_len], row_count)
    col1 = interleave(near[rows_len : 2 * rows_len], far[rows_len : 2 * rows_len], row_count)
    rows0 = panel[:rows_len]
    rows1 = panel[rows_len : 2 * rows_len]

    c0 = jnp.linalg.cholesky(a00)
    x = solve_right(c0, jnp.concatenate([a10, rows0, col0], axis=0))
    x1 = x[:NB]
    x_rest = x[NB:]
    c1 = jnp.linalg.cholesky(a11 - jnp.dot(x1, x1.T, precision=HIGH, preferred_element_type=jnp.float32))
    rest1 = jnp.concatenate([rows1, col1], axis=0)
    y = solve_right(c1, rest1 - jnp.dot(x_rest, x1.T, precision=HIGH, preferred_element_type=jnp.float32))
    w_rows = jnp.concatenate([x_rest[:rows_len], y[:rows_len]], axis=1)
    w_cols = jnp.concatenate([x_rest[rows_len:], y[rows_len:]], axis=1)
    update = jnp.dot(w_rows, w_cols.T, precision=HIGH, preferred_element_type=jnp.float32)

    row_ids = jnp.arange(row_count * NB, dtype=jnp.int32) // NB * nrows + p
    col_ids = jnp.arange(col_count * NB, dtype=jnp.int32) // NB * ncols + q
    keep = (col_ids[None, :] >= 2) & (row_ids[:, None] >= col_ids[None, :])
    result = jnp.where(keep, stored - update, 0.0)

    zero_block = jnp.zeros((NB, NB), jnp.float32)
    lead0 = jnp.concatenate([jnp.where(p == 0, c0, x_rest[:NB]), x_rest[NB:rows_len]], axis=0)
    lead1_top = jnp.where(p == 0, zero_block, jnp.where(p == 1, c1, y[:NB]))
    lead1 = jnp.concatenate([lead1_top, y[NB:rows_len]], axis=0)
    lead = jnp.where(q == 0, lead0, lead1)
    head = jnp.where(q < 2, lead, result[:, :NB])
    return jnp.concatenate([head, result[:, NB:]], axis=1)


def solution(mesh):
    return jax.shard_map(
        per_device,
        mesh=mesh,
        in_specs=(P("row", "col"),),
        out_specs=P("row", "col"),
        check_vma=False,
    )
```

time: 752 us -> 167 us (0.22)
  the two profiles are of different devices: /device:TPU:8 before, /device:TPU:320 now
where the time goes in v1:
time: 167 us; the launch traced here: 166 us
  waiting for transfers between devices  112 us (67%)
  other arithmetic  28.5 us (17%)
  starting transfers between devices  15.1 us (9%)
  local copies, waits for them, and re-layouts  7.22 us (4%)
  matrix products  2.18 us (1%)
    ppermute x3, waiting for transfers between devices, per_device(): got = lax.ppermute(panel, 'col', [(c, c + step) for c in range(step)])  64.4 us
    ppermute x13, waiting for transfers between devices, both_axes(): return lax.ppermute(x, ('row', 'col'), pairs)  48.1 us
    ppermute x13, starting transfers between devices, both_axes(): return lax.ppermute(x, ('row', 'col'), pairs)  11.8 us
    another operation x4, other arithmetic, solve_right(): return jax.scipy.linalg.solve_triangular(factor, rhs.T, lower=True).T  11.2 us
    another operation x3, other arithmetic, per_device(): jnp.linalg.cholesky(a11 - jnp.dot(x1, x1.T, precision=HIGH, preferred_ele...  6.6 us
    another operation x3, other arithmetic, per_device(): c0 = jnp.linalg.cholesky(a00)  6.59 us
  transfers between devices with their start and end apart: 17, of which 3 were waited for; matrix products, arithmetic and copies ran while one was open for 1% of the time, Pallas kernels for 0%

profile of v1, /device:TPU:320, one launch (start us, length us, event | category | flops | bytes accessed | tf_op | source)
XLA Modules:
  0.0 166.1 jit_solution(5756395820825669928)
XLA Ops:
  0.0 0.8 slice.97
  2.2 0.9 slice.96
  3.1 0.7 collective-permute-start
  3.9 0.8 broadcast_select_fusion.10
  4.8 0.7 collective-permute-start.8
  5.5 0.7 collective-permute-start.7
  6.1 0.7 collective-permute-start.6
  6.9 0.7 collective-permute-start.1
  8.3 0.7 collective-permute-start.10
  9.0 0.7 collective-permute-start.9
  9.7 0.7 collective-permute-start.2
  11.1 1.3 collective-permute-start.13
  12.4 0.7 collective-permute-start.12
  13.2 1.3 collective-permute-start.3
  14.5 20.9 %collective-permute-done.13 = f32[192,64]{1,0:T(8,128)S(1)} collective-permute-done((f32[192,64]{1,0:T(8,128)S(1)}, f32[192,64]{1,0:T(8,128)S(1)}, u32[]{:S(2)}, u32[]{:S(2)}) %collective-permute-start.13) | collective-permute-done | bytes 49184 | tf_op jit(solution)/shard_map/ppermute | solution.py:11
  35.4 64.4 %collective-permute-done.3 = f32[512,64]{1,0:T(8,128)S(1)} collective-permute-done((f32[512,64]{1,0:T(8,128)S(1)}, f32[512,64]{1,0:T(8,128)S(1)}, u32[]{:S(2)}, u32[]{:S(2)}) %collective-permute-start.3) | collective-permute-done | bytes 131104 | tf_op jit(solution)/shard_map/ppermute | solution.py:72
  99.8 1.9 %collective-permute-start.16 = (f32[704,64]{1,0:T(8,128)S(1)}, f32[704,64]{1,0:T(8,128)S(1)}, u32[]{:S(2)}, u32[]{:S(2)}) collective-permute-start(f32[704,64]{1,0:T(8,128)S(1)} %pad_maximum_fusion.1), channel_id=1, source_target_pairs={{0,256},{16,257},{32,258},{48,259},{64,260},{80,261},{96,262},{112... | collective-permute-start | bytes 540680 | tf_op jit(solution)/shard_map/ppermute | solution.py:11
  101.8 1.9 %collective-permute-start.15 = (f32[704,64]{1,0:T(8,128)S(1)}, f32[704,64]{1,0:T(8,128)S(1)}, u32[]{:S(2)}, u32[]{:S(2)}) collective-permute-start(f32[704,64]{1,0:T(8,128)S(1)} %pad_maximum_fusion.1), channel_id=1, source_target_pairs={{0,0},{16,1},{32,2},{48,3},{64,4},{80,5},{96,6},{112,7},{128,8},{1... | collective-permute-start | bytes 540680 | tf_op jit(solution)/shard_map/ppermute | solution.py:11
  103.9 27.2 %collective-permute-done.16 = f32[704,64]{1,0:T(8,128)S(1)} collective-permute-done((f32[704,64]{1,0:T(8,128)S(1)}, f32[704,64]{1,0:T(8,128)S(1)}, u32[]{:S(2)}, u32[]{:S(2)}) %collective-permute-start.16) | collective-permute-done | bytes 180256 | tf_op jit(solution)/shard_map/ppermute | solution.py:11
  131.4 5.9 %cholesky.44 = f32[64,64]{1,0:T(8,128)S(1)} custom-call(f32[64,64]{1,0:T(8,128)S(1)} %copy.13), custom_call_target="Cholesky" | custom-call | tf_op jit(solution)/shard_map/jit(cholesky)/cholesky | solution.py:98
  137.3 0.7 compare_reduce_fusion.1
  138.0 0.7 fusion.24
  138.7 4.9 %custom-call.10 = f32[1,64,64]{1,2,0:T(8,128)S(1)} custom-call(f32[1,64,64]{2,1,0:T(8,128)S(1)} %fusion.24), custom_call_target="InvertDiagBlocksLowerTriangular" | custom-call | tf_op jit(solution)/shard_map/jit(_solve_triangular)/triangular_solve | solution.py:50
  147.0 5.9 %cholesky.55 = f32[64,64]{1,0:T(8,128)S(1)} custom-call(f32[64,64]{1,0:T(8,128)S(1)} %copy.21), custom_call_target="Cholesky" | custom-call | tf_op jit(solution)/shard_map/jit(cholesky)/cholesky | solution.py:102
  152.9 0.7 compare_reduce_fusion
  153.6 0.7 fusion.25
  154.3 4.9 %custom-call.11 = f32[1,64,64]{1,2,0:T(8,128)S(1)} custom-call(f32[1,64,64]{2,1,0:T(8,128)S(1)} %fusion.25), custom_call_target="InvertDiagBlocksLowerTriangular" | custom-call | tf_op jit(solution)/shard_map/jit(_solve_triangular)/triangular_solve | solution.py:50
  160.3 0.8 slice-done
  162.0 0.7 slice-done.3
  162.8 0.7 fusion
  163.7 1.4 select_select_fusion.5
  165.1 1.0 pad_maximum_fusion
  (83 shorter events, 9.2 us)
Async XLA Ops:
  0.0 4.8 %copy-start.1 = (f32[256,512]{1,0:T(8,128)S(1)}, f32[256,512]{1,0:T(8,128)}, u32[]{:S(2)}) copy-start(f32[256,512]{1,0:T(8,128)} %param.2) | copy-start | bytes 1572868
  0.8 3.0 %collective-permute-start.4 = (f32[64,64]{1,0:T(8,128)S(1)}, f32[64,64]{1,0:T(8,128)S(1)}, u32[]{:S(2)}, u32[]{:S(2)}) collective-permute-start(f32[64,64]{1,0:T(8,128)S(1)} %slice.97), channel_id=1, source_target_pairs={{17,0},{0,16}} | collective-permute-start | bytes 49160 | tf_op jit(solution)/shard_map/ppermute | solution.py:11
  1.5 2.4 %collective-permute-start.5 = (f32[64,64]{1,0:T(8,128)S(1)}, f32[64,64]{1,0:T(8,128)S(1)}, u32[]{:S(2)}, u32[]{:S(2)}) collective-permute-start(f32[64,64]{1,0:T(8,128)S(1)} %slice.97), channel_id=1, source_target_pairs={{17,1},{0,17}} | collective-permute-start | bytes 49160 | tf_op jit(solution)/shard_map/ppermute | solution.py:11
  3.1 0.8 collective-permute-start
  4.8 2.8 %collective-permute-start.8 = (f32[192,64]{1,0:T(8,128)S(1)}, f32[192,64]{1,0:T(8,128)S(1)}, u32[]{:S(2)}, u32[]{:S(2)}) collective-permute-start(f32[192,64]{1,0:T(8,128)S(1)} %pad_maximum_fusion.5), channel_id=1, source_target_pairs={{0,32},{1,33},{16,48},{17,49}} | collective-permute-start | bytes 147464 | tf_op jit(solution)/shard_map/ppermute | solution.py:11
  5.5 2.1 %collective-permute-start.7 = (f32[192,64]{1,0:T(8,128)S(1)}, f32[192,64]{1,0:T(8,128)S(1)}, u32[]{:S(2)}, u32[]{:S(2)}) collective-permute-start(f32[192,64]{1,0:T(8,128)S(1)} %pad_maximum_fusion.5), channel_id=1, source_target_pairs={{0,2},{1,3},{16,18},{17,19}} | collective-permute-start | bytes 147464 | tf_op jit(solution)/shard_map/ppermute | solution.py:11
  6.1 1.4 collective-permute-start.6
  6.9 2.8 %collective-permute-start.1 = (f32[512,64]{1,0:T(8,128)S(1)}, f32[512,64]{1,0:T(8,128)S(1)}, u32[]{:S(2)}, u32[]{:S(2)}) collective-permute-start(f32[512,64]{1,0:T(8,128)S(1)} %pad_maximum_fusion.2), channel_id=1, source_target_pairs={{0,2},{1,3},{16,18},{17,19},{32,34},{33,35},{48,50},{49,51},{64,66... | collective-permute-start | bytes 393224 | tf_op jit(solution)/shard_map/ppermute | solution.py:72
  7.6 2.8 %collective-permute-start.11 = (f32[192,64]{1,0:T(8,128)S(1)}, f32[192,64]{1,0:T(8,128)S(1)}, u32[]{:S(2)}, u32[]{:S(2)}) collective-permute-start(f32[192,64]{1,0:T(8,128)S(1)} %select_select_fusion.2), channel_id=1, source_target_pairs={{0,64},{1,65},{2,66},{3,67},{16,80},{17,81},{18,82},{19,83},{32,96... | collective-permute-start | bytes 147464 | tf_op jit(solution)/shard_map/ppermute | solution.py:11
  8.3 2.1 %collective-permute-start.10 = (f32[192,64]{1,0:T(8,128)S(1)}, f32[192,64]{1,0:T(8,128)S(1)}, u32[]{:S(2)}, u32[]{:S(2)}) collective-permute-start(f32[192,64]{1,0:T(8,128)S(1)} %select_select_fusion.2), channel_id=1, source_target_pairs={{0,4},{1,5},{2,6},{3,7},{16,20},{17,21},{18,22},{19,23},{32,36},{3... | collective-permute-start | bytes 147464 | tf_op jit(solution)/shard_map/ppermute | solution.py:11
  9.0 1.4 collective-permute-start.9
  9.7 3.4 %collective-permute-start.2 = (f32[512,64]{1,0:T(8,128)S(1)}, f32[512,64]{1,0:T(8,128)S(1)}, u32[]{:S(2)}, u32[]{:S(2)}) collective-permute-start(f32[512,64]{1,0:T(8,128)S(1)} %broadcast_select_fusion.2), channel_id=1, source_target_pairs={{0,4},{1,5},{2,6},{3,7},{16,20},{17,21},{18,22},{19,23},{32,36},{3... | collective-permute-start | bytes 393224 | tf_op jit(solution)/shard_map/ppermute | solution.py:72
  10.5 4.0 %collective-permute-start.14 = (f32[192,64]{1,0:T(8,128)S(1)}, f32[192,64]{1,0:T(8,128)S(1)}, u32[]{:S(2)}, u32[]{:S(2)}) collective-permute-start(f32[192,64]{1,0:T(8,128)S(1)} %select_select_fusion.1), channel_id=1, source_target_pairs={{0,128},{1,129},{2,130},{3,131},{4,132},{5,133},{6,134},{7,135},{1... | collective-permute-start | bytes 147464 | tf_op jit(solution)/shard_map/ppermute | solution.py:11
  11.1 24.2 %collective-permute-start.13 = (f32[192,64]{1,0:T(8,128)S(1)}, f32[192,64]{1,0:T(8,128)S(1)}, u32[]{:S(2)}, u32[]{:S(2)}) collective-permute-start(f32[192,64]{1,0:T(8,128)S(1)} %select_select_fusion.1), channel_id=1, source_target_pairs={{0,8},{1,9},{2,10},{3,11},{4,12},{5,13},{6,14},{7,15},{16,24},{17,... | collective-permute-start | bytes 147464 | tf_op jit(solution)/shard_map/ppermute | solution.py:11
  12.4 22.9 %collective-permute-start.12 = (f32[192,64]{1,0:T(8,128)S(1)}, f32[192,64]{1,0:T(8,128)S(1)}, u32[]{:S(2)}, u32[]{:S(2)}) collective-permute-start(f32[192,64]{1,0:T(8,128)S(1)} %select_select_fusion.1), channel_id=1, source_target_pairs={{0,136},{1,137},{2,138},{3,139},{4,140},{5,141},{6,142},{7,143},{1... | collective-permute-start | bytes 147464 | tf_op jit(solution)/shard_map/ppermute | solution.py:11
  13.2 86.6 %collective-permute-start.3 = (f32[512,64]{1,0:T(8,128)S(1)}, f32[512,64]{1,0:T(8,128)S(1)}, u32[]{:S(2)}, u32[]{:S(2)}) collective-permute-start(f32[512,64]{1,0:T(8,128)S(1)} %broadcast_select_fusion.3), channel_id=1, source_target_pairs={{0,8},{1,9},{2,10},{3,11},{4,12},{5,13},{6,14},{7,15},{16,24},{17,... | collective-permute-start | bytes 393224 | tf_op jit(solution)/shard_map/ppermute | solution.py:72
  99.8 31.2 %collective-permute-start.16 = (f32[704,64]{1,0:T(8,128)S(1)}, f32[704,64]{1,0:T(8,128)S(1)}, u32[]{:S(2)}, u32[]{:S(2)}) collective-permute-start(f32[704,64]{1,0:T(8,128)S(1)} %pad_maximum_fusion.1), channel_id=1, source_target_pairs={{0,256},{16,257},{32,258},{48,259},{64,260},{80,261},{96,262},{112... | collective-permute-start | bytes 540680 | tf_op jit(solution)/shard_map/ppermute | solution.py:11
  101.8 29.3 %collective-permute-start.15 = (f32[704,64]{1,0:T(8,128)S(1)}, f32[704,64]{1,0:T(8,128)S(1)}, u32[]{:S(2)}, u32[]{:S(2)}) collective-permute-start(f32[704,64]{1,0:T(8,128)S(1)} %pad_maximum_fusion.1), channel_id=1, source_target_pairs={{0,0},{16,1},{32,2},{48,3},{64,4},{80,5},{96,6},{112,7},{128,8},{1... | collective-permute-start | bytes 540680 | tf_op jit(solution)/shard_map/ppermute | solution.py:11
  144.9 0.7 copy-start
  159.6 0.7 copy-start.2
  160.2 0.8 slice-start
  161.1 0.8 slice-start.1
  161.8 0.9 slice-start.3
  161.9 0.9 slice-start.2

commit v2 on v1

v2 whole, which is shorter than its diff:
```python
import jax
import jax.numpy as jnp
import numpy as np
from jax import lax
from jax.sharding import PartitionSpec as P

NB = 64
HIGH = lax.Precision.HIGHEST


def both_axes(x, pairs):
    return lax.ppermute(x, ("row", "col"), pairs)


def mm(a, b):
    return jnp.dot(a, b, precision=HIGH, preferred_element_type=jnp.float32)


def gather_corner(stored, swapped, p, q, ncols):
    own = stored[:NB, :NB]
    got = swapped[:NB]
    d00, d01, d10, d11 = 0, 1, ncols, ncols + 1
    from_a = both_axes(own, [(d11, d00), (d00, d10)])
    from_b = both_axes(own, [(d11, d01), (d00, d11)])
    sent = jnp.where(q == 0, from_a, from_b)
    t = jnp.where(q == 0, got, own)
    u = jnp.where(q == 0, own, got)
    a00 = jnp.where(p == 0, u, sent)
    a10 = jnp.where(p == 0, t.T, u)
    a11 = jnp.where(p == 0, sent, t)
    return jnp.concatenate([a00, a10, a11], axis=0)


def spread_round(value, holders, offsets, p, q, nrows, ncols):
    pick = np.full((nrows, ncols), -1, np.int32)
    received = []
    grown = set(holders)
    for k, (dr, dc) in enumerate(offsets):
        pairs = []
        for r, c in sorted(holders):
            pairs.append((r * ncols + c, (r + dr) * ncols + c + dc))
            pick[r + dr, c + dc] = k
            grown.add((r + dr, c + dc))
        received.append(both_axes(value, pairs))
    choice = jnp.asarray(pick)[p, q]
    for k, got in enumerate(received):
        value = jnp.where(choice == k, got, value)
    return value, grown


def interleave(a, b, count):
    blocks = jnp.stack([a.reshape(count, NB, NB), b.reshape(count, NB, NB)], axis=1)
    return blocks.reshape(2 * count * NB, NB)


def lower_inverse(factor):
    eye = jnp.eye(NB, dtype=jnp.float32)
    return jax.scipy.linalg.solve_triangular(factor, eye, lower=True)


def per_device(stored):
    nrows = lax.axis_size("row")
    ncols = lax.axis_size("col")
    assert nrows == 2 * ncols and ncols == 16
    half = nrows // 2
    p = lax.axis_index("row")
    q = lax.axis_index("col")
    row_count = stored.shape[0] // NB
    col_count = stored.shape[1] // NB
    assert col_count == 2 * row_count
    rows_len = row_count * NB

    mine = stored[:, :NB]
    swapped = lax.ppermute(mine, "col", [(0, 1), (1, 0)])
    panel = jnp.concatenate(
        [jnp.where(q == 0, mine, swapped), jnp.where(q == 0, swapped, mine)], axis=0
    )
    corner = gather_corner(stored, swapped, p, q, ncols)

    holders_col = [0, 1]
    holders_k = {(0, 0), (0, 1), (1, 0), (1, 1)}
    corner_offsets = [
        [(a * 16 + b * 8, c * 8) for a in (0, 1) for b in (0, 1) for c in (0, 1)][1:],
        [(4, 0), (0, 4), (4, 4)],
        [(2, 0), (0, 2), (2, 2)],
    ]
    for step, offsets in zip((8, 4, 2), corner_offsets):
        got = lax.ppermute(panel, "col", [(c, c + step) for c in holders_col])
        reached = np.zeros((ncols,), bool)
        reached[[c + step for c in holders_col]] = True
        panel = jnp.where(jnp.asarray(reached)[q], got, panel)
        holders_col = holders_col + [c + step for c in holders_col]
        corner, holders_k = spread_round(corner, holders_k, offsets, p, q, nrows, ncols)

    lin = lambda r, c: r * ncols + c
    first_pairs = [(lin(c, r), lin(r, c)) for r in range(half) for c in range(ncols)]
    first_pairs += [(lin(c + half, r - half), lin(r, c)) for r in range(half, nrows) for c in range(ncols)]
    second_pairs = [(lin(c, r - half), lin(r, c)) for r in range(half, nrows) for c in range(ncols)]
    second_pairs += [(lin(c + half, r), lin(r, c)) for r in range(half) for c in range(ncols)]
    first = both_axes(panel, first_pairs)
    second = both_axes(panel, second_pairs)

    a00 = corner[:NB]
    a10 = corner[NB : 2 * NB]
    a11 = corner[2 * NB :]
    rows0 = panel[:rows_len]
    rows1 = panel[rows_len:]
    c0 = jnp.linalg.cholesky(a00)
    inv0_t = lower_inverse(c0).T
    x1 = mm(a10, inv0_t)
    c1 = jnp.linalg.cholesky(a11 - mm(x1, x1.T))
    inv1_t = lower_inverse(c1).T
    x_rows = mm(rows0, inv0_t)
    y_rows = mm(rows1 - mm(x_rows, x1.T), inv1_t)
    cross = -mm(mm(inv0_t, x1.T), inv1_t)
    zero_block = jnp.zeros((NB, NB), jnp.float32)
    h = jnp.concatenate(
        [jnp.concatenate([inv0_t, cross], axis=1), jnp.concatenate([zero_block, inv1_t], axis=1)], axis=0
    )
    w_rows = jnp.concatenate([x_rows, y_rows], axis=1)
    v = mm(w_rows, h.T)

    low = p < half
    near = jnp.where(low, first, second)
    far = jnp.where(low, second, first)
    col0 = interleave(near[:rows_len], far[:rows_len], row_count)
    col1 = interleave(near[rows_len:], far[rows_len:], row_count)
    cols = jnp.concatenate([col0, col1], axis=1)
    update = mm(v, cols.T)

    row_ids = jnp.arange(row_count * NB, dtype=jnp.int32) // NB * nrows + p
    col_ids = jnp.arange(col_count * NB, dtype=jnp.int32) // NB * ncols + q
    keep = (col_ids[None, :] >= 2) & (row_ids[:, None] >= col_ids[None, :])
    result = jnp.where(keep, stored - update, 0.0)

    lead0 = jnp.concatenate([jnp.where(p == 0, c0, x_rows[:NB]), x_rows[NB:]], axis=0)
    lead1_top = jnp.where(p == 0, zero_block, jnp.where(p == 1, c1, y_rows[:NB]))
    lead1 = jnp.concatenate([lead1_top, y_rows[NB:]], axis=0)
    lead = jnp.where(q == 0, lead0, lead1)
    head = jnp.where(q < 2, lead, result[:, :NB])
    return jnp.concatenate([head, result[:, NB:]], axis=1)


def solution(mesh):
    return jax.shard_map(
        per_device,
        mesh=mesh,
        in_specs=(P("row", "col"),),
        out_specs=P("row", "col"),
        check_vma=False,
    )
```

time: 167 us -> 157 us (0.940)
  the two profiles are of different devices: /device:TPU:320 before, /device:TPU:80 now
where the time goes in v2:
time: 157 us; the launch traced here: 156 us
  waiting for transfers between devices  83.2 us (53%)
  other arithmetic  30.2 us (19%)
  starting transfers between devices  17.8 us (11%)
  local copies, waits for them, and re-layouts  12.1 us (8%)
  between operations  9.37 us (6%)
  matrix products  3.25 us (2%)
    ppermute x17, waiting for transfers between devices, both_axes(): return lax.ppermute(x, ('row', 'col'), pairs)  76.4 us
    ppermute x17, starting transfers between devices, both_axes(): return lax.ppermute(x, ('row', 'col'), pairs)  14.4 us
    another operation x4, other arithmetic, lower_inverse(): return jax.scipy.linalg.solve_triangular(factor, eye, lower=True)  11.1 us
    ppermute x3, waiting for transfers between devices, per_device(): got = lax.ppermute(panel, 'col', [(c, c + step) for c in holders_col])  6.8 us
    another operation x3, other arithmetic, per_device(): c1 = jnp.linalg.cholesky(a11 - mm(x1, x1.T))  6.59 us
    another operation x3, other arithmetic, per_device(): c0 = jnp.linalg.cholesky(a00)  6.56 us
    dynamic_slice x3, local copies, waits for them, and re-layouts, spread_round(): choice = jnp.asarray(pick)[p, q]  4 us
  transfers between devices with their start and end apart: 21, of which 3 were waited for; matrix products, arithmetic and copies ran while one was open for 23% of the time, Pallas kernels for 0%

profile of v2, /device:TPU:80, one launch (start us, length us, event | category | flops | bytes accessed | tf_op | source)
XLA Modules:
  0.0 155.8 jit_solution(1608228764807547689)
XLA Ops:
  0.0 0.8 slice.62
  2.2 0.9 slice.63
  3.1 0.7 collective-permute-start
  3.8 0.8 broadcast_select_fusion.10
  4.7 0.7 collective-permute-start.3
  5.4 0.7 collective-permute-start.4
  6.1 1.3 dynamic_slice.20
  8.7 1.4 dynamic_slice.19
  12.8 1.4 dynamic_slice.18
  22.1 0.7 collective-permute-start.6
  23.4 0.7 collective-permute-start.8
  26.3 0.7 collective-permute-start.12
  27.0 0.7 collective-permute-start.16
  28.4 1.3 collective-permute-start.14
  31.1 0.7 collective-permute-start.17
  31.8 36.2 %collective-permute-done.14 = f32[192,64]{1,0:T(8,128)S(1)} collective-permute-done((f32[192,64]{1,0:T(8,128)S(1)}, f32[192,64]{1,0:T(8,128)S(1)}, u32[]{:S(2)}, u32[]{:S(2)}) %collective-permute-start.14) | collective-permute-done | bytes 49184 | tf_op jit(solution)/shard_map/ppermute | solution.py:12
  68.1 5.9 %cholesky.44 = f32[64,64]{1,0:T(8,128)S(1)} custom-call(f32[64,64]{1,0:T(8,128)S(1)} %copy.19), custom_call_target="Cholesky" | custom-call | tf_op jit(solution)/shard_map/jit(cholesky)/cholesky | solution.py:108
  74.0 0.7 compare_reduce_fusion.1
  75.4 4.9 %custom-call.6 = f32[1,64,64]{1,2,0:T(8,128)S(1)} custom-call(f32[1,64,64]{2,1,0:T(8,128)S(1)} %select_bitcast_fusion.1), custom_call_target="InvertDiagBlocksLowerTriangular" | custom-call | tf_op jit(solution)/shard_map/jit(_solve_triangular)/triangular_solve | solution.py:58
  81.2 5.9 %cholesky.55 = f32[64,64]{1,0:T(8,128)S(1)} custom-call(f32[64,64]{1,0:T(8,128)S(1)} %copy.23), custom_call_target="Cholesky" | custom-call | tf_op jit(solution)/shard_map/jit(cholesky)/cholesky | solution.py:111
  87.1 0.7 compare_reduce_fusion
  88.5 4.9 %custom-call.7 = f32[1,64,64]{1,2,0:T(8,128)S(1)} custom-call(f32[1,64,64]{2,1,0:T(8,128)S(1)} %select_bitcast_fusion), custom_call_target="InvertDiagBlocksLowerTriangular" | custom-call | tf_op jit(solution)/shard_map/jit(_solve_triangular)/triangular_solve | solution.py:58
  93.6 0.7 broadcast_select_fusion.3
  94.3 1.3 collective-permute-start.18
  95.8 6.8 %collective-permute-done.18 = f32[512,64]{1,0:T(8,128)S(1)} collective-permute-done((f32[512,64]{1,0:T(8,128)S(1)}, f32[512,64]{1,0:T(8,128)S(1)}, u32[]{:S(2)}, u32[]{:S(2)}) %collective-permute-start.18) | collective-permute-done | bytes 131104 | tf_op jit(solution)/shard_map/ppermute | solution.py:88
  104.2 1.9 %collective-permute-start.19 = (f32[512,64]{1,0:T(8,128)S(1)}, f32[512,64]{1,0:T(8,128)S(1)}, u32[]{:S(2)}, u32[]{:S(2)}) collective-permute-start(f32[512,64]{1,0:T(8,128)S(1)} %broadcast_select_fusion.4), channel_id=1, source_target_pairs={{0,0},{16,1},{32,2},{48,3},{64,4},{80,5},{96,6},{112,7},{128,8},{1... | collective-permute-start | bytes 393224 | tf_op jit(solution)/shard_map/ppermute | solution.py:12
  106.1 1.9 %collective-permute-start.20 = (f32[512,64]{1,0:T(8,128)S(1)}, f32[512,64]{1,0:T(8,128)S(1)}, u32[]{:S(2)}, u32[]{:S(2)}) collective-permute-start(f32[512,64]{1,0:T(8,128)S(1)} %broadcast_select_fusion.4), channel_id=1, source_target_pairs={{0,256},{16,257},{32,258},{48,259},{64,260},{80,261},{96,262},{112... | collective-permute-start | bytes 393224 | tf_op jit(solution)/shard_map/ppermute | solution.py:12
  108.5 0.7 slice-done
  109.2 1.3 select_select_fusion.5
  110.6 0.8 copy-done.2
  112.1 40.2 %collective-permute-done.19 = f32[512,64]{1,0:T(8,128)S(1)} collective-permute-done((f32[512,64]{1,0:T(8,128)S(1)}, f32[512,64]{1,0:T(8,128)S(1)}, u32[]{:S(2)}, u32[]{:S(2)}) %collective-permute-start.19) | collective-permute-done | bytes 131104 | tf_op jit(solution)/shard_map/ppermute | solution.py:12
  154.8 1.0 pad_maximum_fusion
  (96 shorter events, 17.7 us)
Async XLA Ops:
  0.0 4.7 %copy-start = (f32[256,512]{1,0:T(8,128)S(1)}, f32[256,512]{1,0:T(8,128)}, u32[]{:S(2)}) copy-start(f32[256,512]{1,0:T(8,128)} %param.10) | copy-start | bytes 1572868
  0.8 3.0 %collective-permute-start.1 = (f32[64,64]{1,0:T(8,128)S(1)}, f32[64,64]{1,0:T(8,128)S(1)}, u32[]{:S(2)}, u32[]{:S(2)}) collective-permute-start(f32[64,64]{1,0:T(8,128)S(1)} %slice.62), channel_id=1, source_target_pairs={{17,0},{0,16}} | collective-permute-start | bytes 49160 | tf_op jit(solution)/shard_map/ppermute | solution.py:12
  1.5 2.3 %collective-permute-start.2 = (f32[64,64]{1,0:T(8,128)S(1)}, f32[64,64]{1,0:T(8,128)S(1)}, u32[]{:S(2)}, u32[]{:S(2)}) collective-permute-start(f32[64,64]{1,0:T(8,128)S(1)} %slice.62), channel_id=1, source_target_pairs={{17,1},{0,17}} | collective-permute-start | bytes 49160 | tf_op jit(solution)/shard_map/ppermute | solution.py:12
  3.1 0.7 collective-permute-start
  4.7 18.7 %collective-permute-start.3 = (f32[192,64]{1,0:T(8,128)S(1)}, f32[192,64]{1,0:T(8,128)S(1)}, u32[]{:S(2)}, u32[]{:S(2)}) collective-permute-start(f32[192,64]{1,0:T(8,128)S(1)} %pad_maximum_fusion.4), channel_id=1, source_target_pairs={{0,392},{1,393},{16,408},{17,409}} | collective-permute-start | bytes 147464 | tf_op jit(solution)/shard_map/ppermute | solution.py:12
  5.4 18.7 %collective-permute-start.4 = (f32[192,64]{1,0:T(8,128)S(1)}, f32[192,64]{1,0:T(8,128)S(1)}, u32[]{:S(2)}, u32[]{:S(2)}) collective-permute-start(f32[192,64]{1,0:T(8,128)S(1)} %pad_maximum_fusion.4), channel_id=1, source_target_pairs={{0,384},{1,385},{16,400},{17,401}} | collective-permute-start | bytes 147464 | tf_op jit(solution)/shard_map/ppermute | solution.py:12
  16.2 0.7 copy-start.5
  16.9 0.7 copy-start.4
  17.5 0.7 copy-start.3
  21.4 3.4 %collective-permute-start.5 = (f32[192,64]{1,0:T(8,128)S(1)}, f32[192,64]{1,0:T(8,128)S(1)}, u32[]{:S(2)}, u32[]{:S(2)}) collective-permute-start(f32[192,64]{1,0:T(8,128)S(1)} %pad_maximum_fusion.4), channel_id=1, source_target_pairs={{0,264},{1,265},{16,280},{17,281}} | collective-permute-start | bytes 147464 | tf_op jit(solution)/shard_map/ppermute | solution.py:12
  22.1 2.8 %collective-permute-start.6 = (f32[192,64]{1,0:T(8,128)S(1)}, f32[192,64]{1,0:T(8,128)S(1)}, u32[]{:S(2)}, u32[]{:S(2)}) collective-permute-start(f32[192,64]{1,0:T(8,128)S(1)} %pad_maximum_fusion.4), channel_id=1, source_target_pairs={{0,256},{1,257},{16,272},{17,273}} | collective-permute-start | bytes 147464 | tf_op jit(solution)/shard_map/ppermute | solution.py:12
  22.7 2.1 %collective-permute-start.7 = (f32[192,64]{1,0:T(8,128)S(1)}, f32[192,64]{1,0:T(8,128)S(1)}, u32[]{:S(2)}, u32[]{:S(2)}) collective-permute-start(f32[192,64]{1,0:T(8,128)S(1)} %pad_maximum_fusion.4), channel_id=1, source_target_pairs={{0,136},{1,137},{16,152},{17,153}} | collective-permute-start | bytes 147464 | tf_op jit(solution)/shard_map/ppermute | solution.py:12
  23.4 1.4 collective-permute-start.8
  24.1 0.8 collective-permute-start.9
  24.9 2.7 %collective-permute-start.10 = (f32[192,64]{1,0:T(8,128)S(1)}, f32[192,64]{1,0:T(8,128)S(1)}, u32[]{:S(2)}, u32[]{:S(2)}) collective-permute-start(f32[192,64]{1,0:T(8,128)S(1)} %select_select_fusion.2), channel_id=1, source_target_pairs={{0,68},{1,69},{8,76},{9,77},{16,84},{17,85},{24,92},{25,93},{128,1... | collective-permute-start | bytes 147464 | tf_op jit(solution)/shard_map/ppermute | solution.py:12
  25.6 2.1 %collective-permute-start.11 = (f32[192,64]{1,0:T(8,128)S(1)}, f32[192,64]{1,0:T(8,128)S(1)}, u32[]{:S(2)}, u32[]{:S(2)}) collective-permute-start(f32[192,64]{1,0:T(8,128)S(1)} %select_select_fusion.2), channel_id=1, source_target_pairs={{0,4},{1,5},{8,12},{9,13},{16,20},{17,21},{24,28},{25,29},{128,132... | collective-permute-start | bytes 147464 | tf_op jit(solution)/shard_map/ppermute | solution.py:12
  26.3 1.4 collective-permute-start.12
  27.0 3.4 %collective-permute-start.16 = (f32[512,64]{1,0:T(8,128)S(1)}, f32[512,64]{1,0:T(8,128)S(1)}, u32[]{:S(2)}, u32[]{:S(2)}) collective-permute-start(f32[512,64]{1,0:T(8,128)S(1)} %pad_maximum_fusion.1), channel_id=1, source_target_pairs={{0,8},{1,9},{16,24},{17,25},{32,40},{33,41},{48,56},{49,57},{64,72... | collective-permute-start | bytes 393224 | tf_op jit(solution)/shard_map/ppermute | solution.py:88
  27.7 4.0 %collective-permute-start.13 = (f32[192,64]{1,0:T(8,128)S(1)}, f32[192,64]{1,0:T(8,128)S(1)}, u32[]{:S(2)}, u32[]{:S(2)}) collective-permute-start(f32[192,64]{1,0:T(8,128)S(1)} %select_select_fusion.1), channel_id=1, source_target_pairs={{0,34},{1,35},{4,38},{5,39},{8,42},{9,43},{12,46},{13,47},{16,50},... | collective-permute-start | bytes 147464 | tf_op jit(solution)/shard_map/ppermute | solution.py:12
  28.4 39.5 %collective-permute-start.14 = (f32[192,64]{1,0:T(8,128)S(1)}, f32[192,64]{1,0:T(8,128)S(1)}, u32[]{:S(2)}, u32[]{:S(2)}) collective-permute-start(f32[192,64]{1,0:T(8,128)S(1)} %select_select_fusion.1), channel_id=1, source_target_pairs={{0,2},{1,3},{4,6},{5,7},{8,10},{9,11},{12,14},{13,15},{16,18},{17,... | collective-permute-start | bytes 147464 | tf_op jit(solution)/shard_map/ppermute | solution.py:12
  29.7 38.2 %collective-permute-start.15 = (f32[192,64]{1,0:T(8,128)S(1)}, f32[192,64]{1,0:T(8,128)S(1)}, u32[]{:S(2)}, u32[]{:S(2)}) collective-permute-start(f32[192,64]{1,0:T(8,128)S(1)} %select_select_fusion.1), channel_id=1, source_target_pairs={{0,32},{1,33},{4,36},{5,37},{8,40},{9,41},{12,44},{13,45},{16,48},... | collective-permute-start | bytes 147464 | tf_op jit(solution)/shard_map/ppermute | solution.py:12
  31.1 62.6 %collective-permute-start.17 = (f32[512,64]{1,0:T(8,128)S(1)}, f32[512,64]{1,0:T(8,128)S(1)}, u32[]{:S(2)}, u32[]{:S(2)}) collective-permute-start(f32[512,64]{1,0:T(8,128)S(1)} %broadcast_select_fusion.2), channel_id=1, source_target_pairs={{0,4},{1,5},{8,12},{9,13},{16,20},{17,21},{24,28},{25,29},{32,36},... | collective-permute-start | bytes 393224 | tf_op jit(solution)/shard_map/ppermute | solution.py:88
  94.3 8.3 %collective-permute-start.18 = (f32[512,64]{1,0:T(8,128)S(1)}, f32[512,64]{1,0:T(8,128)S(1)}, u32[]{:S(2)}, u32[]{:S(2)}) collective-permute-start(f32[512,64]{1,0:T(8,128)S(1)} %broadcast_select_fusion.3), channel_id=1, source_target_pairs={{0,2},{1,3},{8,10},{9,11},{4,6},{5,7},{12,14},{13,15},{16,18},{17,... | collective-permute-start | bytes 393224 | tf_op jit(solution)/shard_map/ppermute | solution.py:88
  103.6 0.6 copy-start.1
  104.2 48.0 %collective-permute-start.19 = (f32[512,64]{1,0:T(8,128)S(1)}, f32[512,64]{1,0:T(8,128)S(1)}, u32[]{:S(2)}, u32[]{:S(2)}) collective-permute-start(f32[512,64]{1,0:T(8,128)S(1)} %broadcast_select_fusion.4), channel_id=1, source_target_pairs={{0,0},{16,1},{32,2},{48,3},{64,4},{80,5},{96,6},{112,7},{128,8},{1... | collective-permute-start | bytes 393224 | tf_op jit(solution)/shard_map/ppermute | solution.py:12
  106.1 46.1 %collective-permute-start.20 = (f32[512,64]{1,0:T(8,128)S(1)}, f32[512,64]{1,0:T(8,128)S(1)}, u32[]{:S(2)}, u32[]{:S(2)}) collective-permute-start(f32[512,64]{1,0:T(8,128)S(1)} %broadcast_select_fusion.4), channel_id=1, source_target_pairs={{0,256},{16,257},{32,258},{48,259},{64,260},{80,261},{96,262},{112... | collective-permute-start | bytes 393224 | tf_op jit(solution)/shard_map/ppermute | solution.py:12
  108.4 0.8 slice-start
  110.5 0.8 copy-start.2

commit v3 on v2

--- a/solution.py
+++ b/solution.py
@@ -1,6 +1,5 @@
 import jax
 import jax.numpy as jnp
-import numpy as np
 from jax import lax
 from jax.sharding import PartitionSpec as P
 
@@ -31,21 +30,14 @@
     return jnp.concatenate([a00, a10, a11], axis=0)
 
 
-def spread_round(value, holders, offsets, p, q, nrows, ncols):
-    pick = np.full((nrows, ncols), -1, np.int32)
-    received = []
+def spread_round(value, holders, offsets, ncols):
     grown = set(holders)
-    for k, (dr, dc) in enumerate(offsets):
-        pairs = []
-        for r, c in sorted(holders):
-            pairs.append((r * ncols + c, (r + dr) * ncols + c + dc))
-            pick[r + dr, c + dc] = k
-            grown.add((r + dr, c + dc))
-        received.append(both_axes(value, pairs))
-    choice = jnp.asarray(pick)[p, q]
-    for k, got in enumerate(received):
-        value = jnp.where(choice == k, got, value)
-    return value, grown
+    total = value
+    for dr, dc in offsets:
+        pairs = [(r * ncols + c, (r + dr) * ncols + c + dc) for r, c in sorted(holders)]
+        total = total + both_axes(value, pairs)
+        grown.update((r + dr, c + dc) for r, c in holders)
+    return total, grown
 
 
 def interleave(a, b, count):
@@ -75,7 +67,8 @@
     panel = jnp.concatenate(
         [jnp.where(q == 0, mine, swapped), jnp.where(q == 0, swapped, mine)], axis=0
     )
-    corner = gather_corner(stored, swapped, p, q, ncols)
+    panel = jnp.where(q < 2, panel, 0.0)
+    corner = jnp.where((p < 2) & (q < 2), gather_corner(stored, swapped, p, q, ncols), 0.0)
 
     holders_col = [0, 1]
     holders_k = {(0, 0), (0, 1), (1, 0), (1, 1)}
@@ -85,12 +78,10 @@
         [(2, 0), (0, 2), (2, 2)],
     ]
     for step, offsets in zip((8, 4, 2), corner_offsets):
-        got = lax.ppermute(panel, "col", [(c, c + step) for c in holders_col])
-        reached = np.zeros((ncols,), bool)
-        reached[[c + step for c in holders_col]] = True
-        panel = jnp.where(jnp.asarray(reached)[q], got, panel)
+        panel = panel + lax.ppermute(panel, "col", [(c, c + step) for c in holders_col])
         holders_col = holders_col + [c + step for c in holders_col]
-        corner, holders_k = spread_round(corner, holders_k, offsets, p, q, nrows, ncols)
+        corner, holders_k = spread_round(corner, holders_k, offsets, ncols)
+    corner, panel = lax.optimization_barrier((corner, panel))
 
     lin = lambda r, c: r * ncols + c
     first_pairs = [(lin(c, r), lin(r, c)) for r in range(half) for c in range(ncols)]

time: 157 us -> 121 us (0.77)
  the two profiles are of different devices: /device:TPU:80 before, /device:TPU:214 now
where the time goes in v3:
time: 121 us; the launch traced here: 120 us
  waiting for transfers between devices  63.2 us (52%)
  other arithmetic  28.2 us (23%)
  starting transfers between devices  19.6 us (16%)
  local copies, waits for them, and re-layouts  5.29 us (4%)
  matrix products  3.25 us (3%)
    ppermute x17, waiting for transfers between devices, both_axes(): return lax.ppermute(x, ('row', 'col'), pairs)  63.2 us
    ppermute x17, starting transfers between devices, both_axes(): return lax.ppermute(x, ('row', 'col'), pairs)  16.3 us
    another operation x4, other arithmetic, lower_inverse(): return jax.scipy.linalg.solve_triangular(factor, eye, lower=True)  11.1 us
    another operation x3, other arithmetic, per_device(): c0 = jnp.linalg.cholesky(a00)  6.61 us
    another operation x3, other arithmetic, per_device(): c1 = jnp.linalg.cholesky(a11 - mm(x1, x1.T))  6.53 us
    dot_general x9, matrix products, mm(): return jnp.dot(a, b, precision=HIGH, preferred_element_type=jnp.float32)  2.75 us
    ppermute x3, starting transfers between devices, per_device(): lax.ppermute(panel, 'col', [(c, c + step) for c in holders_col])  2.65 us
  transfers between devices with their start and end apart: 21, of which 2 were waited for; matrix products, arithmetic and copies ran while one was open for 14% of the time, Pallas kernels for 0%

profile of v3, /device:TPU:214, one launch (start us, length us, event | category | flops | bytes accessed | tf_op | source)
XLA Modules:
  0.0 120.3 jit_solution(10657140611474179329)
XLA Ops:
  0.0 0.8 slice.62
  2.2 0.9 slice.63
  3.1 0.7 collective-permute-start
  3.8 0.8 broadcast_select_fusion.7
  4.7 0.7 collective-permute-start.3
  5.4 0.7 collective-permute-start.4
  6.1 0.7 collective-permute-start.5
  6.8 0.7 collective-permute-start.6
  7.4 0.7 collective-permute-start.7
  8.1 0.7 collective-permute-start.8
  8.8 0.7 collective-permute-start.9
  9.6 0.7 collective-permute-start.16
  10.3 0.7 collective-permute-start.10
  11.0 0.7 collective-permute-start.11
  11.7 0.7 collective-permute-start.12
  12.4 0.7 collective-permute-start.17
  14.5 1.3 %collective-permute-start.15 = (f32[192,64]{1,0:T(8,128)S(1)}, f32[192,64]{1,0:T(8,128)S(1)}, u32[]{:S(2)}, u32[]{:S(2)}) collective-permute-start(f32[192,64]{1,0:T(8,128)S(1)} %add_add_fusion.1), channel_id=1, source_target_pairs={{0,34},{1,35},{4,38},{5,39},{8,42},{9,43},{12,46},{13,47},{16,50},... | collective-permute-start | bytes 147464 | tf_op jit(solution)/shard_map/ppermute | solution.py:11
  15.9 1.3 %collective-permute-start.18 = (f32[512,64]{1,0:T(8,128)S(1)}, f32[512,64]{1,0:T(8,128)S(1)}, u32[]{:S(2)}, u32[]{:S(2)}) collective-permute-start(f32[512,64]{1,0:T(8,128)S(1)} %add.109), channel_id=1, source_target_pairs={{0,2},{1,3},{8,10},{9,11},{4,6},{5,7},{12,14},{13,15},{16,18},{17,... | collective-permute-start | bytes 393224 | tf_op jit(solution)/shard_map/ppermute | solution.py:81
  17.2 30.8 %collective-permute-done.15 = f32[192,64]{1,0:T(8,128)S(1)} collective-permute-done((f32[192,64]{1,0:T(8,128)S(1)}, f32[192,64]{1,0:T(8,128)S(1)}, u32[]{:S(2)}, u32[]{:S(2)}) %collective-permute-start.15) | collective-permute-done | bytes 49184 | tf_op jit(solution)/shard_map/ppermute | solution.py:11
  48.2 5.9 %cholesky.44 = f32[64,64]{1,0:T(8,128)S(1)} custom-call(f32[64,64]{1,0:T(8,128)S(1)} %copy.13), custom_call_target="Cholesky" | custom-call | tf_op jit(solution)/shard_map/jit(cholesky)/cholesky | solution.py:99
  54.1 0.7 compare_reduce_fusion.1
  54.8 0.7 select_bitcast_fusion.1
  55.6 4.9 %custom-call.6 = f32[1,64,64]{1,2,0:T(8,128)S(1)} custom-call(f32[1,64,64]{2,1,0:T(8,128)S(1)} %select_bitcast_fusion.1), custom_call_target="InvertDiagBlocksLowerTriangular" | custom-call | tf_op jit(solution)/shard_map/jit(_solve_triangular)/triangular_solve | solution.py:50
  61.8 1.9 %collective-permute-start.19 = (f32[512,64]{1,0:T(8,128)S(1)}, f32[512,64]{1,0:T(8,128)S(1)}, u32[]{:S(2)}, u32[]{:S(2)}) collective-permute-start(f32[512,64]{1,0:T(8,128)S(1)} %add.110), channel_id=1, source_target_pairs={{0,0},{16,1},{32,2},{48,3},{64,4},{80,5},{96,6},{112,7},{128,8},{1... | collective-permute-start | bytes 393224 | tf_op jit(solution)/shard_map/ppermute | solution.py:11
  63.7 3.8 %collective-permute-start.20 = (f32[512,64]{1,0:T(8,128)S(1)}, f32[512,64]{1,0:T(8,128)S(1)}, u32[]{:S(2)}, u32[]{:S(2)}) collective-permute-start(f32[512,64]{1,0:T(8,128)S(1)} %add.110), channel_id=1, source_target_pairs={{0,256},{16,257},{32,258},{48,259},{64,260},{80,261},{96,262},{112... | collective-permute-start | bytes 393224 | tf_op jit(solution)/shard_map/ppermute | solution.py:11
  67.9 5.9 %cholesky.55 = f32[64,64]{1,0:T(8,128)S(1)} custom-call(f32[64,64]{1,0:T(8,128)S(1)} %copy.17), custom_call_target="Cholesky" | custom-call | tf_op jit(solution)/shard_map/jit(cholesky)/cholesky | solution.py:102
  75.0 4.9 %custom-call.7 = f32[1,64,64]{1,2,0:T(8,128)S(1)} custom-call(f32[1,64,64]{2,1,0:T(8,128)S(1)} %select_bitcast_fusion), custom_call_target="InvertDiagBlocksLowerTriangular" | custom-call | tf_op jit(solution)/shard_map/jit(_solve_triangular)/triangular_solve | solution.py:50
  80.5 0.7 slice-done
  81.3 1.3 %select_select_fusion.2 = (f32[64,64]{1,0:T(8,128)S(1)}, f32[64,64]{1,0:T(8,128)S(1)}) fusion(f32[64,64]{1,0:T(8,128)S(1)} %copy.26, f32[64,64]{1,0:T(8,128)S(1)} %cholesky.55, pred[]{:T(512)} %compare_reduce_fusion, pred[]{:T(512)S(6)} %eq.13, pred[]{:T(512)S(6)} %eq.11, f32[64,64]{1,0:T(8,128)S(1)} %copy.24, f32[64,64]{1,0:T(8,128)S(1)} %cholesky.44, ...), kind=kLoop, calls=%fused_computation.55 | loop fusion | flops 32768 | bytes 98308 | tf_op jit(solution)/shard_map/jit(_where)/select_n | solution.py:128
  82.8 0.8 copy-done.2
  84.3 32.4 %collective-permute-done.19 = f32[512,64]{1,0:T(8,128)S(1)} collective-permute-done((f32[512,64]{1,0:T(8,128)S(1)}, f32[512,64]{1,0:T(8,128)S(1)}, u32[]{:S(2)}, u32[]{:S(2)}) %collective-permute-start.19) | collective-permute-done | bytes 131104 | tf_op jit(solution)/shard_map/ppermute | solution.py:11
  119.3 1.0 pad_maximum_fusion
  (84 shorter events, 10.3 us)
Async XLA Ops:
  0.0 4.7 %copy-start = (f32[256,512]{1,0:T(8,128)S(1)}, f32[256,512]{1,0:T(8,128)}, u32[]{:S(2)}) copy-start(f32[256,512]{1,0:T(8,128)} %param.4) | copy-start | bytes 1572868
  0.8 3.0 %collective-permute-start.1 = (f32[64,64]{1,0:T(8,128)S(1)}, f32[64,64]{1,0:T(8,128)S(1)}, u32[]{:S(2)}, u32[]{:S(2)}) collective-permute-start(f32[64,64]{1,0:T(8,128)S(1)} %slice.62), channel_id=1, source_target_pairs={{17,0},{0,16}} | collective-permute-start | bytes 49160 | tf_op jit(solution)/shard_map/ppermute | solution.py:11
  1.5 2.3 %collective-permute-start.2 = (f32[64,64]{1,0:T(8,128)S(1)}, f32[64,64]{1,0:T(8,128)S(1)}, u32[]{:S(2)}, u32[]{:S(2)}) collective-permute-start(f32[64,64]{1,0:T(8,128)S(1)} %slice.62), channel_id=1, source_target_pairs={{17,1},{0,17}} | collective-permute-start | bytes 49160 | tf_op jit(solution)/shard_map/ppermute | solution.py:11
  3.1 0.7 collective-permute-start
  4.7 3.4 %collective-permute-start.3 = (f32[192,64]{1,0:T(8,128)S(1)}, f32[192,64]{1,0:T(8,128)S(1)}, u32[]{:S(2)}, u32[]{:S(2)}) collective-permute-start(f32[192,64]{1,0:T(8,128)S(1)} %maximum_select_fusion.2), channel_id=1, source_target_pairs={{0,8},{1,9},{16,24},{17,25}} | collective-permute-start | bytes 147464 | tf_op jit(solution)/shard_map/ppermute | solution.py:11
  5.4 3.4 %collective-permute-start.4 = (f32[192,64]{1,0:T(8,128)S(1)}, f32[192,64]{1,0:T(8,128)S(1)}, u32[]{:S(2)}, u32[]{:S(2)}) collective-permute-start(f32[192,64]{1,0:T(8,128)S(1)} %maximum_select_fusion.2), channel_id=1, source_target_pairs={{0,128},{1,129},{16,144},{17,145}} | collective-permute-start | bytes 147464 | tf_op jit(solution)/shard_map/ppermute | solution.py:11
  6.1 3.5 %collective-permute-start.5 = (f32[192,64]{1,0:T(8,128)S(1)}, f32[192,64]{1,0:T(8,128)S(1)}, u32[]{:S(2)}, u32[]{:S(2)}) collective-permute-start(f32[192,64]{1,0:T(8,128)S(1)} %maximum_select_fusion.2), channel_id=1, source_target_pairs={{0,136},{1,137},{16,152},{17,153}} | collective-permute-start | bytes 147464 | tf_op jit(solution)/shard_map/ppermute | solution.py:11
  6.8 3.5 %collective-permute-start.6 = (f32[192,64]{1,0:T(8,128)S(1)}, f32[192,64]{1,0:T(8,128)S(1)}, u32[]{:S(2)}, u32[]{:S(2)}) collective-permute-start(f32[192,64]{1,0:T(8,128)S(1)} %maximum_select_fusion.2), channel_id=1, source_target_pairs={{0,256},{1,257},{16,272},{17,273}} | collective-permute-start | bytes 147464 | tf_op jit(solution)/shard_map/ppermute | solution.py:11
  7.4 2.8 %collective-permute-start.7 = (f32[192,64]{1,0:T(8,128)S(1)}, f32[192,64]{1,0:T(8,128)S(1)}, u32[]{:S(2)}, u32[]{:S(2)}) collective-permute-start(f32[192,64]{1,0:T(8,128)S(1)} %maximum_select_fusion.2), channel_id=1, source_target_pairs={{0,264},{1,265},{16,280},{17,281}} | collective-permute-start | bytes 147464 | tf_op jit(solution)/shard_map/ppermute | solution.py:11
  8.1 2.1 %collective-permute-start.8 = (f32[192,64]{1,0:T(8,128)S(1)}, f32[192,64]{1,0:T(8,128)S(1)}, u32[]{:S(2)}, u32[]{:S(2)}) collective-permute-start(f32[192,64]{1,0:T(8,128)S(1)} %maximum_select_fusion.2), channel_id=1, source_target_pairs={{0,384},{1,385},{16,400},{17,401}} | collective-permute-start | bytes 147464 | tf_op jit(solution)/shard_map/ppermute | solution.py:11
  8.8 1.4 %collective-permute-start.9 = (f32[192,64]{1,0:T(8,128)S(1)}, f32[192,64]{1,0:T(8,128)S(1)}, u32[]{:S(2)}, u32[]{:S(2)}) collective-permute-start(f32[192,64]{1,0:T(8,128)S(1)} %maximum_select_fusion.2), channel_id=1, source_target_pairs={{0,392},{1,393},{16,408},{17,409}} | collective-permute-start | bytes 147464 | tf_op jit(solution)/shard_map/ppermute | solution.py:11
  9.6 2.8 %collective-permute-start.16 = (f32[512,64]{1,0:T(8,128)S(1)}, f32[512,64]{1,0:T(8,128)S(1)}, u32[]{:S(2)}, u32[]{:S(2)}) collective-permute-start(f32[512,64]{1,0:T(8,128)S(1)} %maximum_select_fusion), channel_id=1, source_target_pairs={{0,8},{1,9},{16,24},{17,25},{32,40},{33,41},{48,56},{49,57},{64,72... | collective-permute-start | bytes 393224 | tf_op jit(solution)/shard_map/ppermute | solution.py:81
  10.3 2.8 %collective-permute-start.10 = (f32[192,64]{1,0:T(8,128)S(1)}, f32[192,64]{1,0:T(8,128)S(1)}, u32[]{:S(2)}, u32[]{:S(2)}) collective-permute-start(f32[192,64]{1,0:T(8,128)S(1)} %add_add_fusion.2), channel_id=1, source_target_pairs={{0,64},{1,65},{8,72},{9,73},{16,80},{17,81},{24,88},{25,89},{128,1... | collective-permute-start | bytes 147464 | tf_op jit(solution)/shard_map/ppermute | solution.py:11
  11.0 2.1 %collective-permute-start.11 = (f32[192,64]{1,0:T(8,128)S(1)}, f32[192,64]{1,0:T(8,128)S(1)}, u32[]{:S(2)}, u32[]{:S(2)}) collective-permute-start(f32[192,64]{1,0:T(8,128)S(1)} %add_add_fusion.2), channel_id=1, source_target_pairs={{0,4},{1,5},{8,12},{9,13},{16,20},{17,21},{24,28},{25,29},{128,132... | collective-permute-start | bytes 147464 | tf_op jit(solution)/shard_map/ppermute | solution.py:11
  11.7 1.4 %collective-permute-start.12 = (f32[192,64]{1,0:T(8,128)S(1)}, f32[192,64]{1,0:T(8,128)S(1)}, u32[]{:S(2)}, u32[]{:S(2)}) collective-permute-start(f32[192,64]{1,0:T(8,128)S(1)} %add_add_fusion.2), channel_id=1, source_target_pairs={{0,68},{1,69},{8,76},{9,77},{16,84},{17,85},{24,92},{25,93},{128,1... | collective-permute-start | bytes 147464 | tf_op jit(solution)/shard_map/ppermute | solution.py:11
  12.4 3.4 %collective-permute-start.17 = (f32[512,64]{1,0:T(8,128)S(1)}, f32[512,64]{1,0:T(8,128)S(1)}, u32[]{:S(2)}, u32[]{:S(2)}) collective-permute-start(f32[512,64]{1,0:T(8,128)S(1)} %add.108), channel_id=1, source_target_pairs={{0,4},{1,5},{8,12},{9,13},{16,20},{17,21},{24,28},{25,29},{32,36},... | collective-permute-start | bytes 393224 | tf_op jit(solution)/shard_map/ppermute | solution.py:81
  13.2 4.0 %collective-permute-start.13 = (f32[192,64]{1,0:T(8,128)S(1)}, f32[192,64]{1,0:T(8,128)S(1)}, u32[]{:S(2)}, u32[]{:S(2)}) collective-permute-start(f32[192,64]{1,0:T(8,128)S(1)} %add_add_fusion.1), channel_id=1, source_target_pairs={{0,32},{1,33},{4,36},{5,37},{8,40},{9,41},{12,44},{13,45},{16,48},... | collective-permute-start | bytes 147464 | tf_op jit(solution)/shard_map/ppermute | solution.py:11
  13.8 3.4 %collective-permute-start.14 = (f32[192,64]{1,0:T(8,128)S(1)}, f32[192,64]{1,0:T(8,128)S(1)}, u32[]{:S(2)}, u32[]{:S(2)}) collective-permute-start(f32[192,64]{1,0:T(8,128)S(1)} %add_add_fusion.1), channel_id=1, source_target_pairs={{0,2},{1,3},{4,6},{5,7},{8,10},{9,11},{12,14},{13,15},{16,18},{17,... | collective-permute-start | bytes 147464 | tf_op jit(solution)/shard_map/ppermute | solution.py:11
  14.5 33.5 %collective-permute-start.15 = (f32[192,64]{1,0:T(8,128)S(1)}, f32[192,64]{1,0:T(8,128)S(1)}, u32[]{:S(2)}, u32[]{:S(2)}) collective-permute-start(f32[192,64]{1,0:T(8,128)S(1)} %add_add_fusion.1), channel_id=1, source_target_pairs={{0,34},{1,35},{4,38},{5,39},{8,42},{9,43},{12,46},{13,47},{16,50},... | collective-permute-start | bytes 147464 | tf_op jit(solution)/shard_map/ppermute | solution.py:11
  15.9 32.1 %collective-permute-start.18 = (f32[512,64]{1,0:T(8,128)S(1)}, f32[512,64]{1,0:T(8,128)S(1)}, u32[]{:S(2)}, u32[]{:S(2)}) collective-permute-start(f32[512,64]{1,0:T(8,128)S(1)} %add.109), channel_id=1, source_target_pairs={{0,2},{1,3},{8,10},{9,11},{4,6},{5,7},{12,14},{13,15},{16,18},{17,... | collective-permute-start | bytes 393224 | tf_op jit(solution)/shard_map/ppermute | solution.py:81
  61.2 0.6 copy-start.1
  61.8 54.9 %collective-permute-start.19 = (f32[512,64]{1,0:T(8,128)S(1)}, f32[512,64]{1,0:T(8,128)S(1)}, u32[]{:S(2)}, u32[]{:S(2)}) collective-permute-start(f32[512,64]{1,0:T(8,128)S(1)} %add.110), channel_id=1, source_target_pairs={{0,0},{16,1},{32,2},{48,3},{64,4},{80,5},{96,6},{112,7},{128,8},{1... | collective-permute-start | bytes 393224 | tf_op jit(solution)/shard_map/ppermute | solution.py:11
  63.7 53.0 %collective-permute-start.20 = (f32[512,64]{1,0:T(8,128)S(1)}, f32[512,64]{1,0:T(8,128)S(1)}, u32[]{:S(2)}, u32[]{:S(2)}) collective-permute-start(f32[512,64]{1,0:T(8,128)S(1)} %add.110), channel_id=1, source_target_pairs={{0,256},{16,257},{32,258},{48,259},{64,260},{80,261},{96,262},{112... | collective-permute-start | bytes 393224 | tf_op jit(solution)/shard_map/ppermute | solution.py:11
  80.4 0.8 slice-start
  82.7 0.8 copy-start.2

commit v4 on v3

--- a/solution.py
+++ b/solution.py
@@ -46,7 +46,7 @@
 
 
 def lower_inverse(factor):
-    eye = jnp.eye(NB, dtype=jnp.float32)
+    eye = jnp.eye(factor.shape[0], dtype=jnp.float32)
     return jax.scipy.linalg.solve_triangular(factor, eye, lower=True)
 
 
@@ -94,22 +94,18 @@
     a00 = corner[:NB]
     a10 = corner[NB : 2 * NB]
     a11 = corner[2 * NB :]
-    rows0 = panel[:rows_len]
-    rows1 = panel[rows_len:]
-    c0 = jnp.linalg.cholesky(a00)
-    inv0_t = lower_inverse(c0).T
-    x1 = mm(a10, inv0_t)
-    c1 = jnp.linalg.cholesky(a11 - mm(x1, x1.T))
-    inv1_t = lower_inverse(c1).T
-    x_rows = mm(rows0, inv0_t)
-    y_rows = mm(rows1 - mm(x_rows, x1.T), inv1_t)
-    cross = -mm(mm(inv0_t, x1.T), inv1_t)
+    lead_block = jnp.concatenate(
+        [jnp.concatenate([a00, a10.T], axis=1), jnp.concatenate([a10, a11], axis=1)], axis=0
+    )
+    factor = jnp.linalg.cholesky(lead_block)
+    inv_t = lower_inverse(factor).T
+    c0 = factor[:NB, :NB]
+    c1 = factor[NB:, NB:]
+    w_rows = mm(jnp.concatenate([panel[:rows_len], panel[rows_len:]], axis=1), inv_t)
+    x_rows = w_rows[:, :NB]
+    y_rows = w_rows[:, NB:]
+    v = mm(w_rows, inv_t.T)
     zero_block = jnp.zeros((NB, NB), jnp.float32)
-    h = jnp.concatenate(
-        [jnp.concatenate([inv0_t, cross], axis=1), jnp.concatenate([zero_block, inv1_t], axis=1)], axis=0
-    )
-    w_rows = jnp.concatenate([x_rows, y_rows], axis=1)
-    v = mm(w_rows, h.T)
 
     low = p < half
     near = jnp.where(low, first, second)

time: 121 us -> 107 us (0.88)
  waiting for transfers between devices: 63.2 us -> 55.1 us
  other arithmetic: 28.2 us -> 25.8 us
  matrix products: 3.25 us -> 1.63 us
  local copies, waits for them, and re-layouts: 5.29 us -> 3.82 us
    ppermute x17, waiting for transfers between devices: 63.2 us -> 55.1 us  [both_axes(): return lax.ppermute(x, ('row', 'col'), pairs)]
    dot_general x9 -> x3, matrix products: 2.75 us -> 1.38 us  [mm(): return jnp.dot(a, b, precision=HIGH, preferred_element_type=jnp.float32)]
    another operation x6 -> x3, other arithmetic: 13.1 us -> 12.4 us  [per_device(): factor = jnp.linalg.cholesky(lead_block)]
    another operation x4 -> x2, other arithmetic: 11.1 us -> 10.5 us  [lower_inverse(): return jax.scipy.linalg.solve_triangular(factor, eye, lower=True)]
  transfers between devices with their start and end apart: 21 -> 21, of which waited for: 2 -> 2; matrix products, arithmetic and copies ran while one was open for 14% -> 24% of each run, Pallas kernels for 0% -> 0%
where the time goes in v4:
time: 107 us
  waiting for transfers between devices  55.1 us (51%)
  other arithmetic  25.8 us (24%)
  starting transfers between devices  19.6 us (18%)
  local copies, waits for them, and re-layouts  3.82 us (4%)
  matrix products  1.63 us (2%)
    ppermute x17, waiting for transfers between devices, both_axes(): return lax.ppermute(x, ('row', 'col'), pairs)  55.1 us
    ppermute x17, starting transfers between devices, both_axes(): return lax.ppermute(x, ('row', 'col'), pairs)  16.3 us
    another operation x3, other arithmetic, per_device(): factor = jnp.linalg.cholesky(lead_block)  12.4 us
    another operation x2, other arithmetic, lower_inverse(): return jax.scipy.linalg.solve_triangular(factor, eye, lower=True)  10.5 us
    ppermute x3, starting transfers between devices, per_device(): lax.ppermute(panel, 'col', [(c, c + step) for c in holders_col])  2.65 us
  transfers between devices with their start and end apart: 21, of which 2 were waited for; matrix products, arithmetic and copies ran while one was open for 24% of the time, Pallas kernels for 0%

profile of v4, /device:TPU:214, one launch (start us, length us, event | category | flops | bytes accessed | tf_op | source)
XLA Modules:
  0.0 106.7 jit_solution(16369149345849382619)
XLA Ops:
  0.0 0.8 slice.78
  0.8 0.7 collective-permute-start.1
  1.5 0.7 collective-permute-start.2
  2.2 0.9 slice.79
  3.1 0.7 collective-permute-start
  3.8 0.8 broadcast_select_fusion.7
  4.7 0.7 collective-permute-start.3
  5.4 0.7 collective-permute-start.4
  6.1 0.7 collective-permute-start.5
  6.8 0.7 collective-permute-start.6
  7.4 0.7 collective-permute-start.7
  8.1 0.7 collective-permute-start.8
  8.8 0.7 collective-permute-start.9
  9.6 0.7 collective-permute-start.16
  10.3 0.7 collective-permute-start.10
  11.0 0.7 collective-permute-start.11
  11.7 0.7 collective-permute-start.12
  12.4 0.7 collective-permute-start.17
  13.2 0.7 collective-permute-start.13
  13.8 0.7 collective-permute-start.14
  14.5 1.3 %collective-permute-start.15 = (f32[192,64]{1,0:T(8,128)S(1)}, f32[192,64]{1,0:T(8,128)S(1)}, u32[]{:S(2)}, u32[]{:S(2)}) collective-permute-start(f32[192,64]{1,0:T(8,128)S(1)} %add_add_fusion.1), channel_id=1, source_target_pairs={{0,34},{1,35},{4,38},{5,39},{8,42},{9,43},{12,46},{13,47},{16,50},... | collective-permute-start | bytes 147464 | tf_op jit(solution)/shard_map/ppermute | solution.py:11
  15.9 1.3 %collective-permute-start.18 = (f32[512,64]{1,0:T(8,128)S(1)}, f32[512,64]{1,0:T(8,128)S(1)}, u32[]{:S(2)}, u32[]{:S(2)}) collective-permute-start(f32[512,64]{1,0:T(8,128)S(1)} %add.110), channel_id=1, source_target_pairs={{0,2},{1,3},{8,10},{9,11},{4,6},{5,7},{12,14},{13,15},{16,18},{17,... | collective-permute-start | bytes 393224 | tf_op jit(solution)/shard_map/ppermute | solution.py:81
  17.2 30.8 %collective-permute-done.15 = f32[192,64]{1,0:T(8,128)S(1)} collective-permute-done((f32[192,64]{1,0:T(8,128)S(1)}, f32[192,64]{1,0:T(8,128)S(1)}, u32[]{:S(2)}, u32[]{:S(2)}) %collective-permute-start.15) | collective-permute-done | bytes 49184 | tf_op jit(solution)/shard_map/ppermute | solution.py:11
  48.2 1.9 %collective-permute-start.19 = (f32[512,64]{1,0:T(8,128)S(1)}, f32[512,64]{1,0:T(8,128)S(1)}, u32[]{:S(2)}, u32[]{:S(2)}) collective-permute-start(f32[512,64]{1,0:T(8,128)S(1)} %add.111), channel_id=1, source_target_pairs={{0,0},{16,1},{32,2},{48,3},{64,4},{80,5},{96,6},{112,7},{128,8},{1... | collective-permute-start | bytes 393224 | tf_op jit(solution)/shard_map/ppermute | solution.py:11
  50.1 3.8 %collective-permute-start.20 = (f32[512,64]{1,0:T(8,128)S(1)}, f32[512,64]{1,0:T(8,128)S(1)}, u32[]{:S(2)}, u32[]{:S(2)}) collective-permute-start(f32[512,64]{1,0:T(8,128)S(1)} %add.111), channel_id=1, source_target_pairs={{0,256},{16,257},{32,258},{48,259},{64,260},{80,261},{96,262},{112... | collective-permute-start | bytes 393224 | tf_op jit(solution)/shard_map/ppermute | solution.py:11
  54.3 11.7 %cholesky.20 = f32[128,128]{1,0:T(8,128)S(1)} custom-call(f32[128,128]{1,0:T(8,128)S(1)} %fusion.10), custom_call_target="Cholesky" | custom-call | tf_op jit(solution)/shard_map/jit(cholesky)/cholesky | solution.py:100
  66.1 0.6 compare_reduce_fusion
  66.7 0.7 select_bitcast_fusion
  67.4 9.8 %custom-call.7 = f32[1,128,128]{1,2,0:T(8,128)S(1)} custom-call(f32[1,128,128]{2,1,0:T(8,128)S(1)} %get-tuple-element.9), custom_call_target="InvertDiagBlocksLowerTriangular" | custom-call | tf_op jit(solution)/shard_map/jit(_solve_triangular)/triangular_solve | solution.py:50
  78.8 24.3 %collective-permute-done.19 = f32[512,64]{1,0:T(8,128)S(1)} collective-permute-done((f32[512,64]{1,0:T(8,128)S(1)}, f32[512,64]{1,0:T(8,128)S(1)}, u32[]{:S(2)}, u32[]{:S(2)}) %collective-permute-start.19) | collective-permute-done | bytes 131104 | tf_op jit(solution)/shard_map/ppermute | solution.py:11
  104.8 0.6 fusion
  105.7 1.0 pad_maximum_fusion
  (66 shorter events, 4.4 us)
Async XLA Ops:
  0.0 4.7 %copy-start = (f32[256,512]{1,0:T(8,128)S(1)}, f32[256,512]{1,0:T(8,128)}, u32[]{:S(2)}) copy-start(f32[256,512]{1,0:T(8,128)} %param.1) | copy-start | bytes 1572868
  0.8 3.0 %collective-permute-start.1 = (f32[64,64]{1,0:T(8,128)S(1)}, f32[64,64]{1,0:T(8,128)S(1)}, u32[]{:S(2)}, u32[]{:S(2)}) collective-permute-start(f32[64,64]{1,0:T(8,128)S(1)} %slice.78), channel_id=1, source_target_pairs={{17,0},{0,16}} | collective-permute-start | bytes 49160 | tf_op jit(solution)/shard_map/ppermute | solution.py:11
  1.5 2.3 %collective-permute-start.2 = (f32[64,64]{1,0:T(8,128)S(1)}, f32[64,64]{1,0:T(8,128)S(1)}, u32[]{:S(2)}, u32[]{:S(2)}) collective-permute-start(f32[64,64]{1,0:T(8,128)S(1)} %slice.78), channel_id=1, source_target_pairs={{17,1},{0,17}} | collective-permute-start | bytes 49160 | tf_op jit(solution)/shard_map/ppermute | solution.py:11
  3.1 0.7 collective-permute-start
  4.7 3.4 %collective-permute-start.3 = (f32[192,64]{1,0:T(8,128)S(1)}, f32[192,64]{1,0:T(8,128)S(1)}, u32[]{:S(2)}, u32[]{:S(2)}) collective-permute-start(f32[192,64]{1,0:T(8,128)S(1)} %maximum_select_fusion.2), channel_id=1, source_target_pairs={{0,8},{1,9},{16,24},{17,25}} | collective-permute-start | bytes 147464 | tf_op jit(solution)/shard_map/ppermute | solution.py:11
  5.4 3.4 %collective-permute-start.4 = (f32[192,64]{1,0:T(8,128)S(1)}, f32[192,64]{1,0:T(8,128)S(1)}, u32[]{:S(2)}, u32[]{:S(2)}) collective-permute-start(f32[192,64]{1,0:T(8,128)S(1)} %maximum_select_fusion.2), channel_id=1, source_target_pairs={{0,128},{1,129},{16,144},{17,145}} | collective-permute-start | bytes 147464 | tf_op jit(solution)/shard_map/ppermute | solution.py:11
  6.1 3.5 %collective-permute-start.5 = (f32[192,64]{1,0:T(8,128)S(1)}, f32[192,64]{1,0:T(8,128)S(1)}, u32[]{:S(2)}, u32[]{:S(2)}) collective-permute-start(f32[192,64]{1,0:T(8,128)S(1)} %maximum_select_fusion.2), channel_id=1, source_target_pairs={{0,136},{1,137},{16,152},{17,153}} | collective-permute-start | bytes 147464 | tf_op jit(solution)/shard_map/ppermute | solution.py:11
  6.8 3.5 %collective-permute-start.6 = (f32[192,64]{1,0:T(8,128)S(1)}, f32[192,64]{1,0:T(8,128)S(1)}, u32[]{:S(2)}, u32[]{:S(2)}) collective-permute-start(f32[192,64]{1,0:T(8,128)S(1)} %maximum_select_fusion.2), channel_id=1, source_target_pairs={{0,256},{1,257},{16,272},{17,273}} | collective-permute-start | bytes 147464 | tf_op jit(solution)/shard_map/ppermute | solution.py:11
  7.4 2.8 %collective-permute-start.7 = (f32[192,64]{1,0:T(8,128)S(1)}, f32[192,64]{1,0:T(8,128)S(1)}, u32[]{:S(2)}, u32[]{:S(2)}) collective-permute-start(f32[192,64]{1,0:T(8,128)S(1)} %maximum_select_fusion.2), channel_id=1, source_target_pairs={{0,264},{1,265},{16,280},{17,281}} | collective-permute-start | bytes 147464 | tf_op jit(solution)/shard_map/ppermute | solution.py:11
  8.1 2.1 %collective-permute-start.8 = (f32[192,64]{1,0:T(8,128)S(1)}, f32[192,64]{1,0:T(8,128)S(1)}, u32[]{:S(2)}, u32[]{:S(2)}) collective-permute-start(f32[192,64]{1,0:T(8,128)S(1)} %maximum_select_fusion.2), channel_id=1, source_target_pairs={{0,384},{1,385},{16,400},{17,401}} | collective-permute-start | bytes 147464 | tf_op jit(solution)/shard_map/ppermute | solution.py:11
  8.8 1.4 %collective-permute-start.9 = (f32[192,64]{1,0:T(8,128)S(1)}, f32[192,64]{1,0:T(8,128)S(1)}, u32[]{:S(2)}, u32[]{:S(2)}) collective-permute-start(f32[192,64]{1,0:T(8,128)S(1)} %maximum_select_fusion.2), channel_id=1, source_target_pairs={{0,392},{1,393},{16,408},{17,409}} | collective-permute-start | bytes 147464 | tf_op jit(solution)/shard_map/ppermute | solution.py:11
  9.6 2.8 %collective-permute-start.16 = (f32[512,64]{1,0:T(8,128)S(1)}, f32[512,64]{1,0:T(8,128)S(1)}, u32[]{:S(2)}, u32[]{:S(2)}) collective-permute-start(f32[512,64]{1,0:T(8,128)S(1)} %maximum_select_fusion), channel_id=1, source_target_pairs={{0,8},{1,9},{16,24},{17,25},{32,40},{33,41},{48,56},{49,57},{64,72... | collective-permute-start | bytes 393224 | tf_op jit(solution)/shard_map/ppermute | solution.py:81
  10.3 2.8 %collective-permute-start.10 = (f32[192,64]{1,0:T(8,128)S(1)}, f32[192,64]{1,0:T(8,128)S(1)}, u32[]{:S(2)}, u32[]{:S(2)}) collective-permute-start(f32[192,64]{1,0:T(8,128)S(1)} %add_add_fusion.2), channel_id=1, source_target_pairs={{0,64},{1,65},{8,72},{9,73},{16,80},{17,81},{24,88},{25,89},{128,1... | collective-permute-start | bytes 147464 | tf_op jit(solution)/shard_map/ppermute | solution.py:11
  11.0 2.1 %collective-permute-start.11 = (f32[192,64]{1,0:T(8,128)S(1)}, f32[192,64]{1,0:T(8,128)S(1)}, u32[]{:S(2)}, u32[]{:S(2)}) collective-permute-start(f32[192,64]{1,0:T(8,128)S(1)} %add_add_fusion.2), channel_id=1, source_target_pairs={{0,4},{1,5},{8,12},{9,13},{16,20},{17,21},{24,28},{25,29},{128,132... | collective-permute-start | bytes 147464 | tf_op jit(solution)/shard_map/ppermute | solution.py:11
  11.7 1.4 %collective-permute-start.12 = (f32[192,64]{1,0:T(8,128)S(1)}, f32[192,64]{1,0:T(8,128)S(1)}, u32[]{:S(2)}, u32[]{:S(2)}) collective-permute-start(f32[192,64]{1,0:T(8,128)S(1)} %add_add_fusion.2), channel_id=1, source_target_pairs={{0,68},{1,69},{8,76},{9,77},{16,84},{17,85},{24,92},{25,93},{128,1... | collective-permute-start | bytes 147464 | tf_op jit(solution)/shard_map/ppermute | solution.py:11
  12.4 3.4 %collective-permute-start.17 = (f32[512,64]{1,0:T(8,128)S(1)}, f32[512,64]{1,0:T(8,128)S(1)}, u32[]{:S(2)}, u32[]{:S(2)}) collective-permute-start(f32[512,64]{1,0:T(8,128)S(1)} %add.109), channel_id=1, source_target_pairs={{0,4},{1,5},{8,12},{9,13},{16,20},{17,21},{24,28},{25,29},{32,36},... | collective-permute-start | bytes 393224 | tf_op jit(solution)/shard_map/ppermute | solution.py:81
  13.2 4.0 %collective-permute-start.13 = (f32[192,64]{1,0:T(8,128)S(1)}, f32[192,64]{1,0:T(8,128)S(1)}, u32[]{:S(2)}, u32[]{:S(2)}) collective-permute-start(f32[192,64]{1,0:T(8,128)S(1)} %add_add_fusion.1), channel_id=1, source_target_pairs={{0,32},{1,33},{4,36},{5,37},{8,40},{9,41},{12,44},{13,45},{16,48},... | collective-permute-start | bytes 147464 | tf_op jit(solution)/shard_map/ppermute | solution.py:11
  13.8 3.4 %collective-permute-start.14 = (f32[192,64]{1,0:T(8,128)S(1)}, f32[192,64]{1,0:T(8,128)S(1)}, u32[]{:S(2)}, u32[]{:S(2)}) collective-permute-start(f32[192,64]{1,0:T(8,128)S(1)} %add_add_fusion.1), channel_id=1, source_target_pairs={{0,2},{1,3},{4,6},{5,7},{8,10},{9,11},{12,14},{13,15},{16,18},{17,... | collective-permute-start | bytes 147464 | tf_op jit(solution)/shard_map/ppermute | solution.py:11
  14.5 33.5 %collective-permute-start.15 = (f32[192,64]{1,0:T(8,128)S(1)}, f32[192,64]{1,0:T(8,128)S(1)}, u32[]{:S(2)}, u32[]{:S(2)}) collective-permute-start(f32[192,64]{1,0:T(8,128)S(1)} %add_add_fusion.1), channel_id=1, source_target_pairs={{0,34},{1,35},{4,38},{5,39},{8,42},{9,43},{12,46},{13,47},{16,50},... | collective-permute-start | bytes 147464 | tf_op jit(solution)/shard_map/ppermute | solution.py:11
  15.9 32.1 %collective-permute-start.18 = (f32[512,64]{1,0:T(8,128)S(1)}, f32[512,64]{1,0:T(8,128)S(1)}, u32[]{:S(2)}, u32[]{:S(2)}) collective-permute-start(f32[512,64]{1,0:T(8,128)S(1)} %add.110), channel_id=1, source_target_pairs={{0,2},{1,3},{8,10},{9,11},{4,6},{5,7},{12,14},{13,15},{16,18},{17,... | collective-permute-start | bytes 393224 | tf_op jit(solution)/shard_map/ppermute | solution.py:81
  48.2 54.9 %collective-permute-start.19 = (f32[512,64]{1,0:T(8,128)S(1)}, f32[512,64]{1,0:T(8,128)S(1)}, u32[]{:S(2)}, u32[]{:S(2)}) collective-permute-start(f32[512,64]{1,0:T(8,128)S(1)} %add.111), channel_id=1, source_target_pairs={{0,0},{16,1},{32,2},{48,3},{64,4},{80,5},{96,6},{112,7},{128,8},{1... | collective-permute-start | bytes 393224 | tf_op jit(solution)/shard_map/ppermute | solution.py:11
  50.1 53.0 %collective-permute-start.20 = (f32[512,64]{1,0:T(8,128)S(1)}, f32[512,64]{1,0:T(8,128)S(1)}, u32[]{:S(2)}, u32[]{:S(2)}) collective-permute-start(f32[512,64]{1,0:T(8,128)S(1)} %add.111), channel_id=1, source_target_pairs={{0,256},{16,257},{32,258},{48,259},{64,260},{80,261},{96,262},{112... | collective-permute-start | bytes 393224 | tf_op jit(solution)/shard_map/ppermute | solution.py:11

commit v5 on v4

--- a/solution.py
+++ b/solution.py
@@ -70,18 +70,18 @@
     panel = jnp.where(q < 2, panel, 0.0)
     corner = jnp.where((p < 2) & (q < 2), gather_corner(stored, swapped, p, q, ncols), 0.0)
 
-    holders_col = [0, 1]
+    sent = panel
+    for t in range((ncols - 2) // 2):
+        panel = panel + lax.ppermute(sent, "col", [(0, 2 + 2 * t), (1, 3 + 2 * t)])
     holders_k = {(0, 0), (0, 1), (1, 0), (1, 1)}
     corner_offsets = [
-        [(a * 16 + b * 8, c * 8) for a in (0, 1) for b in (0, 1) for c in (0, 1)][1:],
-        [(4, 0), (0, 4), (4, 4)],
+        [(16, 0), (0, 8), (16, 8)],
+        [(a * 8 + b * 4, c * 4) for a in (0, 1) for b in (0, 1) for c in (0, 1)][1:],
         [(2, 0), (0, 2), (2, 2)],
     ]
-    for step, offsets in zip((8, 4, 2), corner_offsets):
-        panel = panel + lax.ppermute(panel, "col", [(c, c + step) for c in holders_col])
-        holders_col = holders_col + [c + step for c in holders_col]
+    for offsets in corner_offsets:
         corner, holders_k = spread_round(corner, holders_k, offsets, ncols)
-    corner, panel = lax.optimization_barrier((corner, panel))
+    assert len(holders_k) == nrows * ncols
 
     lin = lambda r, c: r * ncols + c
     first_pairs = [(lin(c, r), lin(r, c)) for r in range(half) for c in range(ncols)]

time: 107 us -> 140 us (1.31)
  the two profiles are of different devices: /device:TPU:214 before, /device:TPU:17 now
where the time goes in v5:
time: 140 us
  starting transfers between devices  83.7 us (60%)
  other arithmetic  25.8 us (18%)
  waiting for transfers between devices  24.2 us (17%)
  local copies, waits for them, and re-layouts  3.67 us (3%)
  matrix products  1.63 us (1%)
    ppermute x17, starting transfers between devices, both_axes(): return lax.ppermute(x, ('row', 'col'), pairs)  67.3 us
    ppermute x17, waiting for transfers between devices, both_axes(): return lax.ppermute(x, ('row', 'col'), pairs)  18 us
    ppermute x7, starting transfers between devices, per_device(): panel = panel + lax.ppermute(sent, 'col', [(0, 2 + 2 * t), (1, 3 + 2 * t)])  13.8 us
    another operation x3, other arithmetic, per_device(): factor = jnp.linalg.cholesky(lead_block)  12.4 us
    another operation x2, other arithmetic, lower_inverse(): return jax.scipy.linalg.solve_triangular(factor, eye, lower=True)  10.5 us
    ppermute x7, waiting for transfers between devices, per_device(): panel = panel + lax.ppermute(sent, 'col', [(0, 2 + 2 * t), (1, 3 + 2 * t)])  5.32 us
  transfers between devices with their start and end apart: 25, of which 3 were waited for; matrix products, arithmetic and copies ran while one was open for 19% of the time, Pallas kernels for 0%

profile of v5, /device:TPU:17, one launch (start us, length us, event | category | flops | bytes accessed | tf_op | source)
XLA Modules:
  0.0 139.7 jit_solution(15156920346315975504)
XLA Ops:
  0.0 0.8 slice.78
  2.2 0.9 slice.79
  3.1 2.6 %collective-permute-start = (f32[256,64]{1,0:T(8,128)S(1)}, f32[256,64]{1,0:T(8,128)S(1)}, u32[]{:S(2)}, u32[]{:S(2)}) collective-permute-start(f32[256,64]{1,0:T(8,128)S(1)} %slice.79), channel_id=1, source_target_pairs={{0,1},{1,0},{16,17},{17,16},{32,33},{33,32},{48,49},{49,48},{64,65... | collective-permute-start | bytes 196616 | tf_op jit(solution)/shard_map/ppermute | solution.py:66
  5.7 0.9 collective-permute-done
  6.6 0.8 broadcast_select_fusion.7
  7.5 0.7 collective-permute-start.3
  8.2 0.7 collective-permute-start.4
  8.9 0.7 collective-permute-start.5
  9.7 0.7 collective-permute-start.10
  10.4 1.3 collective-permute-start.16
  11.7 3.0 %collective-permute-start.17 = (f32[512,64]{1,0:T(8,128)S(1)}, f32[512,64]{1,0:T(8,128)S(1)}, u32[]{:S(2)}, u32[]{:S(2)}) collective-permute-start(f32[512,64]{1,0:T(8,128)S(1)} %maximum_select_fusion), channel_id=1, source_target_pairs={{0,4},{1,5},{16,20},{17,21},{32,36},{33,37},{48,52},{49,53},{64,68... | collective-permute-start | bytes 393224 | tf_op jit(solution)/shard_map/ppermute | solution.py:75
  14.7 0.7 collective-permute-start.11
  15.4 0.7 collective-permute-start.12
  16.1 0.7 collective-permute-start.6
  16.8 0.7 collective-permute-start.7
  17.4 0.7 collective-permute-start.8
  18.1 1.3 collective-permute-start.9
  19.5 1.3 collective-permute-start.18
  20.8 4.3 %collective-permute-start.19 = (f32[512,64]{1,0:T(8,128)S(1)}, f32[512,64]{1,0:T(8,128)S(1)}, u32[]{:S(2)}, u32[]{:S(2)}) collective-permute-start(f32[512,64]{1,0:T(8,128)S(1)} %maximum_select_fusion), channel_id=1, source_target_pairs={{0,8},{1,9},{16,24},{17,25},{32,40},{33,41},{48,56},{49,57},{64,72... | collective-permute-start | bytes 393224 | tf_op jit(solution)/shard_map/ppermute | solution.py:75
  25.0 18.0 %collective-permute-done.9 = f32[192,64]{1,0:T(8,128)S(1)} collective-permute-done((f32[192,64]{1,0:T(8,128)S(1)}, f32[192,64]{1,0:T(8,128)S(1)}, u32[]{:S(2)}, u32[]{:S(2)}) %collective-permute-start.9) | collective-permute-done | bytes 49184 | tf_op jit(solution)/shard_map/ppermute | solution.py:11
  43.0 1.3 collective-permute-start.20
  44.3 1.3 collective-permute-start.21
  45.6 1.3 collective-permute-start.22
  47.0 1.3 collective-permute-start.13
  48.3 1.3 collective-permute-start.14
  49.6 1.3 collective-permute-start.15
  51.0 5.3 %collective-permute-done.22 = f32[512,64]{1,0:T(8,128)S(1)} collective-permute-done((f32[512,64]{1,0:T(8,128)S(1)}, f32[512,64]{1,0:T(8,128)S(1)}, u32[]{:S(2)}, u32[]{:S(2)}) %collective-permute-start.22) | collective-permute-done | bytes 131104 | tf_op jit(solution)/shard_map/ppermute | solution.py:75
  56.4 52.9 %collective-permute-start.23 = (f32[512,64]{1,0:T(8,128)S(1)}, f32[512,64]{1,0:T(8,128)S(1)}, u32[]{:S(2)}, u32[]{:S(2)}) collective-permute-start(f32[512,64]{1,0:T(8,128)S(1)} %add_add_fusion), channel_id=1, source_target_pairs={{0,0},{16,1},{32,2},{48,3},{64,4},{80,5},{96,6},{112,7},{128,8},{1... | collective-permute-start | bytes 393224 | tf_op jit(solution)/shard_map/ppermute | solution.py:11
  109.3 1.9 %collective-permute-start.24 = (f32[512,64]{1,0:T(8,128)S(1)}, f32[512,64]{1,0:T(8,128)S(1)}, u32[]{:S(2)}, u32[]{:S(2)}) collective-permute-start(f32[512,64]{1,0:T(8,128)S(1)} %add_add_fusion), channel_id=1, source_target_pairs={{0,256},{16,257},{32,258},{48,259},{64,260},{80,261},{96,262},{112... | collective-permute-start | bytes 393224 | tf_op jit(solution)/shard_map/ppermute | solution.py:11
  111.7 11.7 %cholesky.20 = f32[128,128]{1,0:T(8,128)S(1)} custom-call(f32[128,128]{1,0:T(8,128)S(1)} %fusion.10), custom_call_target="Cholesky" | custom-call | tf_op jit(solution)/shard_map/jit(cholesky)/cholesky | solution.py:100
  124.7 9.8 %custom-call.7 = f32[1,128,128]{1,2,0:T(8,128)S(1)} custom-call(f32[1,128,128]{2,1,0:T(8,128)S(1)} %get-tuple-element.5), custom_call_target="InvertDiagBlocksLowerTriangular" | custom-call | tf_op jit(solution)/shard_map/jit(_solve_triangular)/triangular_solve | solution.py:50
  138.7 1.0 pad_maximum_fusion
  (70 shorter events, 7.5 us)
Async XLA Ops:
  0.0 7.5 %copy-start = (f32[256,512]{1,0:T(8,128)S(1)}, f32[256,512]{1,0:T(8,128)}, u32[]{:S(2)}) copy-start(f32[256,512]{1,0:T(8,128)} %param.1) | copy-start | bytes 1572868
  0.8 4.9 %collective-permute-start.1 = (f32[64,64]{1,0:T(8,128)S(1)}, f32[64,64]{1,0:T(8,128)S(1)}, u32[]{:S(2)}, u32[]{:S(2)}) collective-permute-start(f32[64,64]{1,0:T(8,128)S(1)} %slice.78), channel_id=1, source_target_pairs={{17,0},{0,16}} | collective-permute-start | bytes 49160 | tf_op jit(solution)/shard_map/ppermute | solution.py:11
  1.5 4.2 %collective-permute-start.2 = (f32[64,64]{1,0:T(8,128)S(1)}, f32[64,64]{1,0:T(8,128)S(1)}, u32[]{:S(2)}, u32[]{:S(2)}) collective-permute-start(f32[64,64]{1,0:T(8,128)S(1)} %slice.78), channel_id=1, source_target_pairs={{17,1},{0,17}} | collective-permute-start | bytes 49160 | tf_op jit(solution)/shard_map/ppermute | solution.py:11
  3.1 3.6 %collective-permute-start = (f32[256,64]{1,0:T(8,128)S(1)}, f32[256,64]{1,0:T(8,128)S(1)}, u32[]{:S(2)}, u32[]{:S(2)}) collective-permute-start(f32[256,64]{1,0:T(8,128)S(1)} %slice.79), channel_id=1, source_target_pairs={{0,1},{1,0},{16,17},{17,16},{32,33},{33,32},{48,49},{49,48},{64,65... | collective-permute-start | bytes 196616 | tf_op jit(solution)/shard_map/ppermute | solution.py:66
  7.5 2.1 %collective-permute-start.3 = (f32[192,64]{1,0:T(8,128)S(1)}, f32[192,64]{1,0:T(8,128)S(1)}, u32[]{:S(2)}, u32[]{:S(2)}) collective-permute-start(f32[192,64]{1,0:T(8,128)S(1)} %maximum_select_fusion.2), channel_id=1, source_target_pairs={{0,256},{1,257},{16,272},{17,273}} | collective-permute-start | bytes 147464 | tf_op jit(solution)/shard_map/ppermute | solution.py:11
  8.2 1.4 collective-permute-start.4
  8.9 0.7 collective-permute-start.5
  9.7 6.4 %collective-permute-start.10 = (f32[192,64]{1,0:T(8,128)S(1)}, f32[192,64]{1,0:T(8,128)S(1)}, u32[]{:S(2)}, u32[]{:S(2)}) collective-permute-start(f32[192,64]{1,0:T(8,128)S(1)} %add_add_fusion.3), channel_id=1, source_target_pairs={{0,132},{1,133},{8,140},{9,141},{16,148},{17,149},{24,156},{25,157... | collective-permute-start | bytes 147464 | tf_op jit(solution)/shard_map/ppermute | solution.py:11
  10.4 33.9 %collective-permute-start.16 = (f32[512,64]{1,0:T(8,128)S(1)}, f32[512,64]{1,0:T(8,128)S(1)}, u32[]{:S(2)}, u32[]{:S(2)}) collective-permute-start(f32[512,64]{1,0:T(8,128)S(1)} %maximum_select_fusion), channel_id=1, source_target_pairs={{0,2},{1,3},{16,18},{17,19},{32,34},{33,35},{48,50},{49,51},{64,66... | collective-permute-start | bytes 393224 | tf_op jit(solution)/shard_map/ppermute | solution.py:75
  11.7 34.0 %collective-permute-start.17 = (f32[512,64]{1,0:T(8,128)S(1)}, f32[512,64]{1,0:T(8,128)S(1)}, u32[]{:S(2)}, u32[]{:S(2)}) collective-permute-start(f32[512,64]{1,0:T(8,128)S(1)} %maximum_select_fusion), channel_id=1, source_target_pairs={{0,4},{1,5},{16,20},{17,21},{32,36},{33,37},{48,52},{49,53},{64,68... | collective-permute-start | bytes 393224 | tf_op jit(solution)/shard_map/ppermute | solution.py:75
  14.7 2.0 %collective-permute-start.11 = (f32[192,64]{1,0:T(8,128)S(1)}, f32[192,64]{1,0:T(8,128)S(1)}, u32[]{:S(2)}, u32[]{:S(2)}) collective-permute-start(f32[192,64]{1,0:T(8,128)S(1)} %add_add_fusion.3), channel_id=1, source_target_pairs={{0,192},{1,193},{8,200},{9,201},{16,208},{17,209},{24,216},{25,217... | collective-permute-start | bytes 147464 | tf_op jit(solution)/shard_map/ppermute | solution.py:11
  15.4 2.1 %collective-permute-start.12 = (f32[192,64]{1,0:T(8,128)S(1)}, f32[192,64]{1,0:T(8,128)S(1)}, u32[]{:S(2)}, u32[]{:S(2)}) collective-permute-start(f32[192,64]{1,0:T(8,128)S(1)} %add_add_fusion.3), channel_id=1, source_target_pairs={{0,196},{1,197},{8,204},{9,205},{16,212},{17,213},{24,220},{25,221... | collective-permute-start | bytes 147464 | tf_op jit(solution)/shard_map/ppermute | solution.py:11
  16.1 2.1 %collective-permute-start.6 = (f32[192,64]{1,0:T(8,128)S(1)}, f32[192,64]{1,0:T(8,128)S(1)}, u32[]{:S(2)}, u32[]{:S(2)}) collective-permute-start(f32[192,64]{1,0:T(8,128)S(1)} %add_add_fusion.3), channel_id=1, source_target_pairs={{0,4},{1,5},{8,12},{9,13},{16,20},{17,21},{24,28},{25,29},{256,260... | collective-permute-start | bytes 147464 | tf_op jit(solution)/shard_map/ppermute | solution.py:11
  16.8 2.7 %collective-permute-start.7 = (f32[192,64]{1,0:T(8,128)S(1)}, f32[192,64]{1,0:T(8,128)S(1)}, u32[]{:S(2)}, u32[]{:S(2)}) collective-permute-start(f32[192,64]{1,0:T(8,128)S(1)} %add_add_fusion.3), channel_id=1, source_target_pairs={{0,64},{1,65},{8,72},{9,73},{16,80},{17,81},{24,88},{25,89},{256,3... | collective-permute-start | bytes 147464 | tf_op jit(solution)/shard_map/ppermute | solution.py:11
  17.4 3.3 %collective-permute-start.8 = (f32[192,64]{1,0:T(8,128)S(1)}, f32[192,64]{1,0:T(8,128)S(1)}, u32[]{:S(2)}, u32[]{:S(2)}) collective-permute-start(f32[192,64]{1,0:T(8,128)S(1)} %add_add_fusion.3), channel_id=1, source_target_pairs={{0,68},{1,69},{8,76},{9,77},{16,84},{17,85},{24,92},{25,93},{256,3... | collective-permute-start | bytes 147464 | tf_op jit(solution)/shard_map/ppermute | solution.py:11
  18.1 24.9 %collective-permute-start.9 = (f32[192,64]{1,0:T(8,128)S(1)}, f32[192,64]{1,0:T(8,128)S(1)}, u32[]{:S(2)}, u32[]{:S(2)}) collective-permute-start(f32[192,64]{1,0:T(8,128)S(1)} %add_add_fusion.3), channel_id=1, source_target_pairs={{0,128},{1,129},{8,136},{9,137},{16,144},{17,145},{24,152},{25,153... | collective-permute-start | bytes 147464 | tf_op jit(solution)/shard_map/ppermute | solution.py:11
  19.5 27.5 %collective-permute-start.18 = (f32[512,64]{1,0:T(8,128)S(1)}, f32[512,64]{1,0:T(8,128)S(1)}, u32[]{:S(2)}, u32[]{:S(2)}) collective-permute-start(f32[512,64]{1,0:T(8,128)S(1)} %maximum_select_fusion), channel_id=1, source_target_pairs={{0,6},{1,7},{16,22},{17,23},{32,38},{33,39},{48,54},{49,55},{64,70... | collective-permute-start | bytes 393224 | tf_op jit(solution)/shard_map/ppermute | solution.py:75
  20.8 27.5 %collective-permute-start.19 = (f32[512,64]{1,0:T(8,128)S(1)}, f32[512,64]{1,0:T(8,128)S(1)}, u32[]{:S(2)}, u32[]{:S(2)}) collective-permute-start(f32[512,64]{1,0:T(8,128)S(1)} %maximum_select_fusion), channel_id=1, source_target_pairs={{0,8},{1,9},{16,24},{17,25},{32,40},{33,41},{48,56},{49,57},{64,72... | collective-permute-start | bytes 393224 | tf_op jit(solution)/shard_map/ppermute | solution.py:75
  43.0 6.6 %collective-permute-start.20 = (f32[512,64]{1,0:T(8,128)S(1)}, f32[512,64]{1,0:T(8,128)S(1)}, u32[]{:S(2)}, u32[]{:S(2)}) collective-permute-start(f32[512,64]{1,0:T(8,128)S(1)} %maximum_select_fusion), channel_id=1, source_target_pairs={{0,10},{1,11},{16,26},{17,27},{32,42},{33,43},{48,58},{49,59},{64,... | collective-permute-start | bytes 393224 | tf_op jit(solution)/shard_map/ppermute | solution.py:75
  44.3 6.6 %collective-permute-start.21 = (f32[512,64]{1,0:T(8,128)S(1)}, f32[512,64]{1,0:T(8,128)S(1)}, u32[]{:S(2)}, u32[]{:S(2)}) collective-permute-start(f32[512,64]{1,0:T(8,128)S(1)} %maximum_select_fusion), channel_id=1, source_target_pairs={{0,12},{1,13},{16,28},{17,29},{32,44},{33,45},{48,60},{49,61},{64,... | collective-permute-start | bytes 393224 | tf_op jit(solution)/shard_map/ppermute | solution.py:75
  45.6 10.6 %collective-permute-start.22 = (f32[512,64]{1,0:T(8,128)S(1)}, f32[512,64]{1,0:T(8,128)S(1)}, u32[]{:S(2)}, u32[]{:S(2)}) collective-permute-start(f32[512,64]{1,0:T(8,128)S(1)} %maximum_select_fusion), channel_id=1, source_target_pairs={{0,14},{1,15},{16,30},{17,31},{32,46},{33,47},{48,62},{49,63},{64,... | collective-permute-start | bytes 393224 | tf_op jit(solution)/shard_map/ppermute | solution.py:75
  47.0 64.2 %collective-permute-start.13 = (f32[192,64]{1,0:T(8,128)S(1)}, f32[192,64]{1,0:T(8,128)S(1)}, u32[]{:S(2)}, u32[]{:S(2)}) collective-permute-start(f32[192,64]{1,0:T(8,128)S(1)} %add_add_fusion.2), channel_id=1, source_target_pairs={{0,32},{1,33},{4,36},{5,37},{8,40},{9,41},{12,44},{13,45},{16,48},... | collective-permute-start | bytes 147464 | tf_op jit(solution)/shard_map/ppermute | solution.py:11
  48.3 62.9 %collective-permute-start.14 = (f32[192,64]{1,0:T(8,128)S(1)}, f32[192,64]{1,0:T(8,128)S(1)}, u32[]{:S(2)}, u32[]{:S(2)}) collective-permute-start(f32[192,64]{1,0:T(8,128)S(1)} %add_add_fusion.2), channel_id=1, source_target_pairs={{0,2},{1,3},{4,6},{5,7},{8,10},{9,11},{12,14},{13,15},{16,18},{17,... | collective-permute-start | bytes 147464 | tf_op jit(solution)/shard_map/ppermute | solution.py:11
  49.6 61.6 %collective-permute-start.15 = (f32[192,64]{1,0:T(8,128)S(1)}, f32[192,64]{1,0:T(8,128)S(1)}, u32[]{:S(2)}, u32[]{:S(2)}) collective-permute-start(f32[192,64]{1,0:T(8,128)S(1)} %add_add_fusion.2), channel_id=1, source_target_pairs={{0,34},{1,35},{4,38},{5,39},{8,42},{9,43},{12,46},{13,47},{16,50},... | collective-permute-start | bytes 147464 | tf_op jit(solution)/shard_map/ppermute | solution.py:11
  56.4 79.7 %collective-permute-start.23 = (f32[512,64]{1,0:T(8,128)S(1)}, f32[512,64]{1,0:T(8,128)S(1)}, u32[]{:S(2)}, u32[]{:S(2)}) collective-permute-start(f32[512,64]{1,0:T(8,128)S(1)} %add_add_fusion), channel_id=1, source_target_pairs={{0,0},{16,1},{32,2},{48,3},{64,4},{80,5},{96,6},{112,7},{128,8},{1... | collective-permute-start | bytes 393224 | tf_op jit(solution)/shard_map/ppermute | solution.py:11
  109.3 26.8 %collective-permute-start.24 = (f32[512,64]{1,0:T(8,128)S(1)}, f32[512,64]{1,0:T(8,128)S(1)}, u32[]{:S(2)}, u32[]{:S(2)}) collective-permute-start(f32[512,64]{1,0:T(8,128)S(1)} %add_add_fusion), channel_id=1, source_target_pairs={{0,256},{16,257},{32,258},{48,259},{64,260},{80,261},{96,262},{112... | collective-permute-start | bytes 393224 | tf_op jit(solution)/shard_map/ppermute | solution.py:11

commit v6 on v4

--- a/solution.py
+++ b/solution.py
@@ -80,8 +80,10 @@
     for step, offsets in zip((8, 4, 2), corner_offsets):
         panel = panel + lax.ppermute(panel, "col", [(c, c + step) for c in holders_col])
         holders_col = holders_col + [c + step for c in holders_col]
+        if step == 2:
+            corner, panel = lax.optimization_barrier((corner, panel))
         corner, holders_k = spread_round(corner, holders_k, offsets, ncols)
-    corner, panel = lax.optimization_barrier((corner, panel))
+    corner, panel_held = lax.optimization_barrier((corner, panel))
 
     lin = lambda r, c: r * ncols + c
     first_pairs = [(lin(c, r), lin(r, c)) for r in range(half) for c in range(ncols)]
@@ -101,7 +103,7 @@
     inv_t = lower_inverse(factor).T
     c0 = factor[:NB, :NB]
     c1 = factor[NB:, NB:]
-    w_rows = mm(jnp.concatenate([panel[:rows_len], panel[rows_len:]], axis=1), inv_t)
+    w_rows = mm(jnp.concatenate([panel_held[:rows_len], panel_held[rows_len:]], axis=1), inv_t)
     x_rows = w_rows[:, :NB]
     y_rows = w_rows[:, NB:]
     v = mm(w_rows, inv_t.T)

time: 107 us -> 98.5 us (0.921)
  the two profiles are of different devices: /device:TPU:214 before, /device:TPU:17 now
where the time goes in v6:
time: 98.5 us; the launch traced here: 97.9 us
  starting transfers between devices  49 us (50%)
  other arithmetic  26 us (26%)
  waiting for transfers between devices  16.9 us (17%)
  local copies, waits for them, and re-layouts  3.75 us (4%)
  matrix products  1.62 us (2%)
    ppermute x17, starting transfers between devices, both_axes(): return lax.ppermute(x, ('row', 'col'), pairs)  35 us
    ppermute x17, waiting for transfers between devices, both_axes(): return lax.ppermute(x, ('row', 'col'), pairs)  13.7 us
    another operation x3, other arithmetic, per_device(): factor = jnp.linalg.cholesky(lead_block)  12.4 us
    ppermute x3, starting transfers between devices, per_device(): lax.ppermute(panel, 'col', [(c, c + step) for c in holders_col])  11.3 us
    another operation x2, other arithmetic, lower_inverse(): return jax.scipy.linalg.solve_triangular(factor, eye, lower=True)  10.5 us
    ppermute x3, waiting for transfers between devices, per_device(): lax.ppermute(panel, 'col', [(c, c + step) for c in holders_col])  3.27 us
    ppermute x1, starting transfers between devices, per_device(): swapped = lax.ppermute(mine, 'col', [(0, 1), (1, 0)])  2.58 us
  transfers between devices with their start and end apart: 21, of which 5 were waited for; matrix products, arithmetic and copies ran while one was open for 28% of the time, Pallas kernels for 0%

profile of v6, /device:TPU:17, one launch (start us, length us, event | category | flops | bytes accessed | tf_op | source)
XLA Modules:
  0.0 97.9 jit_solution(9920582736784706200)
XLA Ops:
  0.0 0.9 slice.79
  0.9 2.6 %collective-permute-start = (f32[256,64]{1,0:T(8,128)S(1)}, f32[256,64]{1,0:T(8,128)S(1)}, u32[]{:S(2)}, u32[]{:S(2)}) collective-permute-start(f32[256,64]{1,0:T(8,128)S(1)} %slice.79), channel_id=1, source_target_pairs={{0,1},{1,0},{16,17},{17,16},{32,33},{33,32},{48,49},{49,48},{64,65... | collective-permute-start | bytes 196616 | tf_op jit(solution)/shard_map/ppermute | solution.py:66
  3.5 0.8 slice.78
  4.9 0.7 collective-permute-start.2
  5.6 1.0 %broadcast_select_fusion.3 = (f32[256,64]{1,0:T(8,128)S(1)}, f32[256,64]{1,0:T(8,128)S(1)}) fusion(f32[256,64]{1,0:T(8,128)S(1)} %collective-permute-done, pred[]{:T(512)S(6)} %eq.6, f32[256,512]{1,0:T(8,128)} %param.1), kind=kLoop, calls=%fused_computation.32 | loop fusion | flops 32768 | bytes 262145 | tf_op jit(solution)/shard_map/jit(_where)/select_n | solution.py:68
  6.7 8.7 %collective-permute-start.13 = (f32[512,64]{1,0:T(8,128)S(1)}, f32[512,64]{1,0:T(8,128)S(1)}, u32[]{:S(2)}, u32[]{:S(2)}) collective-permute-start(f32[512,64]{1,0:T(8,128)S(1)} %maximum_select_fusion), channel_id=1, source_target_pairs={{0,8},{1,9},{16,24},{17,25},{32,40},{33,41},{48,56},{49,57},{64,72... | collective-permute-start | bytes 393224 | tf_op jit(solution)/shard_map/ppermute | solution.py:81
  15.6 0.7 collective-permute-start.3
  16.2 1.3 %collective-permute-start.4 = (f32[192,64]{1,0:T(8,128)S(1)}, f32[192,64]{1,0:T(8,128)S(1)}, u32[]{:S(2)}, u32[]{:S(2)}) collective-permute-start(f32[192,64]{1,0:T(8,128)S(1)} %maximum_select_fusion.2), channel_id=1, source_target_pairs={{0,128},{1,129},{16,144},{17,145}} | collective-permute-start | bytes 147464 | tf_op jit(solution)/shard_map/ppermute | solution.py:11
  17.5 0.7 collective-permute-start.5
  18.2 0.7 collective-permute-start.6
  18.9 0.7 collective-permute-start.7
  19.6 2.9 %collective-permute-done.4 = f32[192,64]{1,0:T(8,128)S(1)} collective-permute-done((f32[192,64]{1,0:T(8,128)S(1)}, f32[192,64]{1,0:T(8,128)S(1)}, u32[]{:S(2)}, u32[]{:S(2)}) %collective-permute-start.4) | collective-permute-done | bytes 49184 | tf_op jit(solution)/shard_map/ppermute | solution.py:11
  22.5 0.7 collective-permute-start.8
  23.2 0.7 collective-permute-start.9
  23.9 1.3 %collective-permute-start.14 = (f32[512,64]{1,0:T(8,128)S(1)}, f32[512,64]{1,0:T(8,128)S(1)}, u32[]{:S(2)}, u32[]{:S(2)}) collective-permute-start(f32[512,64]{1,0:T(8,128)S(1)} %add.106), channel_id=1, source_target_pairs={{0,4},{1,5},{8,12},{9,13},{16,20},{17,21},{24,28},{25,29},{32,36},... | collective-permute-start | bytes 393224 | tf_op jit(solution)/shard_map/ppermute | solution.py:81
  25.3 1.3 %collective-permute-start.10 = (f32[192,64]{1,0:T(8,128)S(1)}, f32[192,64]{1,0:T(8,128)S(1)}, u32[]{:S(2)}, u32[]{:S(2)}) collective-permute-start(f32[192,64]{1,0:T(8,128)S(1)} %add_add_fusion.2), channel_id=1, source_target_pairs={{0,64},{1,65},{8,72},{9,73},{16,80},{17,81},{24,88},{25,89},{128,1... | collective-permute-start | bytes 147464 | tf_op jit(solution)/shard_map/ppermute | solution.py:11
  26.6 1.3 %collective-permute-start.11 = (f32[192,64]{1,0:T(8,128)S(1)}, f32[192,64]{1,0:T(8,128)S(1)}, u32[]{:S(2)}, u32[]{:S(2)}) collective-permute-start(f32[192,64]{1,0:T(8,128)S(1)} %add_add_fusion.2), channel_id=1, source_target_pairs={{0,4},{1,5},{8,12},{9,13},{16,20},{17,21},{24,28},{25,29},{128,132... | collective-permute-start | bytes 147464 | tf_op jit(solution)/shard_map/ppermute | solution.py:11
  27.9 1.3 %collective-permute-start.12 = (f32[192,64]{1,0:T(8,128)S(1)}, f32[192,64]{1,0:T(8,128)S(1)}, u32[]{:S(2)}, u32[]{:S(2)}) collective-permute-start(f32[192,64]{1,0:T(8,128)S(1)} %add_add_fusion.2), channel_id=1, source_target_pairs={{0,68},{1,69},{8,76},{9,77},{16,84},{17,85},{24,92},{25,93},{128,1... | collective-permute-start | bytes 147464 | tf_op jit(solution)/shard_map/ppermute | solution.py:11
  29.3 1.3 %collective-permute-start.15 = (f32[512,64]{1,0:T(8,128)S(1)}, f32[512,64]{1,0:T(8,128)S(1)}, u32[]{:S(2)}, u32[]{:S(2)}) collective-permute-start(f32[512,64]{1,0:T(8,128)S(1)} %add.107), channel_id=1, source_target_pairs={{0,2},{1,3},{8,10},{9,11},{4,6},{5,7},{12,14},{13,15},{16,18},{17,... | collective-permute-start | bytes 393224 | tf_op jit(solution)/shard_map/ppermute | solution.py:81
  30.6 0.7 collective-permute-done.10
  31.3 1.7 %collective-permute-done.12 = f32[192,64]{1,0:T(8,128)S(1)} collective-permute-done((f32[192,64]{1,0:T(8,128)S(1)}, f32[192,64]{1,0:T(8,128)S(1)}, u32[]{:S(2)}, u32[]{:S(2)}) %collective-permute-start.12) | collective-permute-done | bytes 49184 | tf_op jit(solution)/shard_map/ppermute | solution.py:11
  33.0 3.3 %collective-permute-done.15 = f32[512,64]{1,0:T(8,128)S(1)} collective-permute-done((f32[512,64]{1,0:T(8,128)S(1)}, f32[512,64]{1,0:T(8,128)S(1)}, u32[]{:S(2)}, u32[]{:S(2)}) %collective-permute-start.15) | collective-permute-done | bytes 131104 | tf_op jit(solution)/shard_map/ppermute | solution.py:81
  36.3 1.3 %collective-permute-start.16 = (f32[192,64]{1,0:T(8,128)S(1)}, f32[192,64]{1,0:T(8,128)S(1)}, u32[]{:S(2)}, u32[]{:S(2)}) collective-permute-start(f32[192,64]{1,0:T(8,128)S(1)} %add_add_fusion.1), channel_id=1, source_target_pairs={{0,32},{1,33},{4,36},{5,37},{8,40},{9,41},{12,44},{13,45},{16,48},... | collective-permute-start | bytes 147464 | tf_op jit(solution)/shard_map/ppermute | solution.py:11
  37.6 3.7 %collective-permute-start.17 = (f32[192,64]{1,0:T(8,128)S(1)}, f32[192,64]{1,0:T(8,128)S(1)}, u32[]{:S(2)}, u32[]{:S(2)}) collective-permute-start(f32[192,64]{1,0:T(8,128)S(1)} %add_add_fusion.1), channel_id=1, source_target_pairs={{0,2},{1,3},{4,6},{5,7},{8,10},{9,11},{12,14},{13,15},{16,18},{17,... | collective-permute-start | bytes 147464 | tf_op jit(solution)/shard_map/ppermute | solution.py:11
  41.2 1.3 %collective-permute-start.18 = (f32[192,64]{1,0:T(8,128)S(1)}, f32[192,64]{1,0:T(8,128)S(1)}, u32[]{:S(2)}, u32[]{:S(2)}) collective-permute-start(f32[192,64]{1,0:T(8,128)S(1)} %add_add_fusion.1), channel_id=1, source_target_pairs={{0,34},{1,35},{4,38},{5,39},{8,42},{9,43},{12,46},{13,47},{16,50},... | collective-permute-start | bytes 147464 | tf_op jit(solution)/shard_map/ppermute | solution.py:11
  42.6 13.8 %collective-permute-start.19 = (f32[512,64]{1,0:T(8,128)S(1)}, f32[512,64]{1,0:T(8,128)S(1)}, u32[]{:S(2)}, u32[]{:S(2)}) collective-permute-start(f32[512,64]{1,0:T(8,128)S(1)} %add.108), channel_id=1, source_target_pairs={{0,0},{16,1},{32,2},{48,3},{64,4},{80,5},{96,6},{112,7},{128,8},{1... | collective-permute-start | bytes 393224 | tf_op jit(solution)/shard_map/ppermute | solution.py:11
  56.4 4.5 %collective-permute-start.20 = (f32[512,64]{1,0:T(8,128)S(1)}, f32[512,64]{1,0:T(8,128)S(1)}, u32[]{:S(2)}, u32[]{:S(2)}) collective-permute-start(f32[512,64]{1,0:T(8,128)S(1)} %add.108), channel_id=1, source_target_pairs={{0,256},{16,257},{32,258},{48,259},{64,260},{80,261},{96,262},{112... | collective-permute-start | bytes 393224 | tf_op jit(solution)/shard_map/ppermute | solution.py:11
  61.5 11.7 %cholesky.20 = f32[128,128]{1,0:T(8,128)S(1)} custom-call(f32[128,128]{1,0:T(8,128)S(1)} %fusion.10), custom_call_target="Cholesky" | custom-call | tf_op jit(solution)/shard_map/jit(cholesky)/cholesky | solution.py:102
  73.9 0.7 select_bitcast_fusion
  74.6 9.8 %custom-call.7 = f32[1,128,128]{1,2,0:T(8,128)S(1)} custom-call(f32[1,128,128]{2,1,0:T(8,128)S(1)} %get-tuple-element.13), custom_call_target="InvertDiagBlocksLowerTriangular" | custom-call | tf_op jit(solution)/shard_map/jit(_solve_triangular)/triangular_solve | solution.py:50
  86.0 8.4 %collective-permute-done.19 = f32[512,64]{1,0:T(8,128)S(1)} collective-permute-done((f32[512,64]{1,0:T(8,128)S(1)}, f32[512,64]{1,0:T(8,128)S(1)}, u32[]{:S(2)}, u32[]{:S(2)}) %collective-permute-start.19) | collective-permute-done | bytes 131104 | tf_op jit(solution)/shard_map/ppermute | solution.py:11
  96.9 1.0 %pad_maximum_fusion = f32[256,512]{1,0:T(8,128)} fusion(f32[256,448]{1,0:T(8,128)S(1)} %slice.111, f32[256,64]{1,0:T(8,128)S(1)} %slice_select_fusion), kind=kLoop, calls=%fused_computation.2 | loop fusion | flops 131072 | bytes 1048576 | tf_op jit(solution)/shard_map/concatenate | solution.py:130
  (66 shorter events, 6.3 us)
Async XLA Ops:
  0.9 4.7 %collective-permute-start = (f32[256,64]{1,0:T(8,128)S(1)}, f32[256,64]{1,0:T(8,128)S(1)}, u32[]{:S(2)}, u32[]{:S(2)}) collective-permute-start(f32[256,64]{1,0:T(8,128)S(1)} %slice.79), channel_id=1, source_target_pairs={{0,1},{1,0},{16,17},{17,16},{32,33},{33,32},{48,49},{49,48},{64,65... | collective-permute-start | bytes 196616 | tf_op jit(solution)/shard_map/ppermute | solution.py:66
  4.3 11.1 %collective-permute-start.1 = (f32[64,64]{1,0:T(8,128)S(1)}, f32[64,64]{1,0:T(8,128)S(1)}, u32[]{:S(2)}, u32[]{:S(2)}) collective-permute-start(f32[64,64]{1,0:T(8,128)S(1)} %slice.78), channel_id=1, source_target_pairs={{17,0},{0,16}} | collective-permute-start | bytes 49160 | tf_op jit(solution)/shard_map/ppermute | solution.py:11
  4.9 10.5 %collective-permute-start.2 = (f32[64,64]{1,0:T(8,128)S(1)}, f32[64,64]{1,0:T(8,128)S(1)}, u32[]{:S(2)}, u32[]{:S(2)}) collective-permute-start(f32[64,64]{1,0:T(8,128)S(1)} %slice.78), channel_id=1, source_target_pairs={{17,1},{0,17}} | collective-permute-start | bytes 49160 | tf_op jit(solution)/shard_map/ppermute | solution.py:11
  5.6 9.8 %copy-start = (f32[256,512]{1,0:T(8,128)S(1)}, f32[256,512]{1,0:T(8,128)}, u32[]{:S(2)}) copy-start(f32[256,512]{1,0:T(8,128)} %param.1) | copy-start | bytes 1572868
  6.7 16.5 %collective-permute-start.13 = (f32[512,64]{1,0:T(8,128)S(1)}, f32[512,64]{1,0:T(8,128)S(1)}, u32[]{:S(2)}, u32[]{:S(2)}) collective-permute-start(f32[512,64]{1,0:T(8,128)S(1)} %maximum_select_fusion), channel_id=1, source_target_pairs={{0,8},{1,9},{16,24},{17,25},{32,40},{33,41},{48,56},{49,57},{64,72... | collective-permute-start | bytes 393224 | tf_op jit(solution)/shard_map/ppermute | solution.py:81
  15.6 3.3 %collective-permute-start.3 = (f32[192,64]{1,0:T(8,128)S(1)}, f32[192,64]{1,0:T(8,128)S(1)}, u32[]{:S(2)}, u32[]{:S(2)}) collective-permute-start(f32[192,64]{1,0:T(8,128)S(1)} %maximum_select_fusion.2), channel_id=1, source_target_pairs={{0,8},{1,9},{16,24},{17,25}} | collective-permute-start | bytes 147464 | tf_op jit(solution)/shard_map/ppermute | solution.py:11
  16.2 6.3 %collective-permute-start.4 = (f32[192,64]{1,0:T(8,128)S(1)}, f32[192,64]{1,0:T(8,128)S(1)}, u32[]{:S(2)}, u32[]{:S(2)}) collective-permute-start(f32[192,64]{1,0:T(8,128)S(1)} %maximum_select_fusion.2), channel_id=1, source_target_pairs={{0,128},{1,129},{16,144},{17,145}} | collective-permute-start | bytes 147464 | tf_op jit(solution)/shard_map/ppermute | solution.py:11
  17.5 6.4 %collective-permute-start.5 = (f32[192,64]{1,0:T(8,128)S(1)}, f32[192,64]{1,0:T(8,128)S(1)}, u32[]{:S(2)}, u32[]{:S(2)}) collective-permute-start(f32[192,64]{1,0:T(8,128)S(1)} %maximum_select_fusion.2), channel_id=1, source_target_pairs={{0,136},{1,137},{16,152},{17,153}} | collective-permute-start | bytes 147464 | tf_op jit(solution)/shard_map/ppermute | solution.py:11
  18.2 7.0 %collective-permute-start.6 = (f32[192,64]{1,0:T(8,128)S(1)}, f32[192,64]{1,0:T(8,128)S(1)}, u32[]{:S(2)}, u32[]{:S(2)}) collective-permute-start(f32[192,64]{1,0:T(8,128)S(1)} %maximum_select_fusion.2), channel_id=1, source_target_pairs={{0,256},{1,257},{16,272},{17,273}} | collective-permute-start | bytes 147464 | tf_op jit(solution)/shard_map/ppermute | solution.py:11
  18.9 6.3 %collective-permute-start.7 = (f32[192,64]{1,0:T(8,128)S(1)}, f32[192,64]{1,0:T(8,128)S(1)}, u32[]{:S(2)}, u32[]{:S(2)}) collective-permute-start(f32[192,64]{1,0:T(8,128)S(1)} %maximum_select_fusion.2), channel_id=1, source_target_pairs={{0,264},{1,265},{16,280},{17,281}} | collective-permute-start | bytes 147464 | tf_op jit(solution)/shard_map/ppermute | solution.py:11
  22.5 2.7 %collective-permute-start.8 = (f32[192,64]{1,0:T(8,128)S(1)}, f32[192,64]{1,0:T(8,128)S(1)}, u32[]{:S(2)}, u32[]{:S(2)}) collective-permute-start(f32[192,64]{1,0:T(8,128)S(1)} %maximum_select_fusion.2), channel_id=1, source_target_pairs={{0,384},{1,385},{16,400},{17,401}} | collective-permute-start | bytes 147464 | tf_op jit(solution)/shard_map/ppermute | solution.py:11
  23.2 2.1 %collective-permute-start.9 = (f32[192,64]{1,0:T(8,128)S(1)}, f32[192,64]{1,0:T(8,128)S(1)}, u32[]{:S(2)}, u32[]{:S(2)}) collective-permute-start(f32[192,64]{1,0:T(8,128)S(1)} %maximum_select_fusion.2), channel_id=1, source_target_pairs={{0,392},{1,393},{16,408},{17,409}} | collective-permute-start | bytes 147464 | tf_op jit(solution)/shard_map/ppermute | solution.py:11
  23.9 5.3 %collective-permute-start.14 = (f32[512,64]{1,0:T(8,128)S(1)}, f32[512,64]{1,0:T(8,128)S(1)}, u32[]{:S(2)}, u32[]{:S(2)}) collective-permute-start(f32[512,64]{1,0:T(8,128)S(1)} %add.106), channel_id=1, source_target_pairs={{0,4},{1,5},{8,12},{9,13},{16,20},{17,21},{24,28},{25,29},{32,36},... | collective-permute-start | bytes 393224 | tf_op jit(solution)/shard_map/ppermute | solution.py:81
  25.3 6.0 %collective-permute-start.10 = (f32[192,64]{1,0:T(8,128)S(1)}, f32[192,64]{1,0:T(8,128)S(1)}, u32[]{:S(2)}, u32[]{:S(2)}) collective-permute-start(f32[192,64]{1,0:T(8,128)S(1)} %add_add_fusion.2), channel_id=1, source_target_pairs={{0,64},{1,65},{8,72},{9,73},{16,80},{17,81},{24,88},{25,89},{128,1... | collective-permute-start | bytes 147464 | tf_op jit(solution)/shard_map/ppermute | solution.py:11
  26.6 4.7 %collective-permute-start.11 = (f32[192,64]{1,0:T(8,128)S(1)}, f32[192,64]{1,0:T(8,128)S(1)}, u32[]{:S(2)}, u32[]{:S(2)}) collective-permute-start(f32[192,64]{1,0:T(8,128)S(1)} %add_add_fusion.2), channel_id=1, source_target_pairs={{0,4},{1,5},{8,12},{9,13},{16,20},{17,21},{24,28},{25,29},{128,132... | collective-permute-start | bytes 147464 | tf_op jit(solution)/shard_map/ppermute | solution.py:11
  27.9 5.0 %collective-permute-start.12 = (f32[192,64]{1,0:T(8,128)S(1)}, f32[192,64]{1,0:T(8,128)S(1)}, u32[]{:S(2)}, u32[]{:S(2)}) collective-permute-start(f32[192,64]{1,0:T(8,128)S(1)} %add_add_fusion.2), channel_id=1, source_target_pairs={{0,68},{1,69},{8,76},{9,77},{16,84},{17,85},{24,92},{25,93},{128,1... | collective-permute-start | bytes 147464 | tf_op jit(solution)/shard_map/ppermute | solution.py:11
  29.3 6.9 %collective-permute-start.15 = (f32[512,64]{1,0:T(8,128)S(1)}, f32[512,64]{1,0:T(8,128)S(1)}, u32[]{:S(2)}, u32[]{:S(2)}) collective-permute-start(f32[512,64]{1,0:T(8,128)S(1)} %add.107), channel_id=1, source_target_pairs={{0,2},{1,3},{8,10},{9,11},{4,6},{5,7},{12,14},{13,15},{16,18},{17,... | collective-permute-start | bytes 393224 | tf_op jit(solution)/shard_map/ppermute | solution.py:81
  36.3 24.6 %collective-permute-start.16 = (f32[192,64]{1,0:T(8,128)S(1)}, f32[192,64]{1,0:T(8,128)S(1)}, u32[]{:S(2)}, u32[]{:S(2)}) collective-permute-start(f32[192,64]{1,0:T(8,128)S(1)} %add_add_fusion.1), channel_id=1, source_target_pairs={{0,32},{1,33},{4,36},{5,37},{8,40},{9,41},{12,44},{13,45},{16,48},... | collective-permute-start | bytes 147464 | tf_op jit(solution)/shard_map/ppermute | solution.py:11
  37.6 23.3 %collective-permute-start.17 = (f32[192,64]{1,0:T(8,128)S(1)}, f32[192,64]{1,0:T(8,128)S(1)}, u32[]{:S(2)}, u32[]{:S(2)}) collective-permute-start(f32[192,64]{1,0:T(8,128)S(1)} %add_add_fusion.1), channel_id=1, source_target_pairs={{0,2},{1,3},{4,6},{5,7},{8,10},{9,11},{12,14},{13,15},{16,18},{17,... | collective-permute-start | bytes 147464 | tf_op jit(solution)/shard_map/ppermute | solution.py:11
  41.2 19.7 %collective-permute-start.18 = (f32[192,64]{1,0:T(8,128)S(1)}, f32[192,64]{1,0:T(8,128)S(1)}, u32[]{:S(2)}, u32[]{:S(2)}) collective-permute-start(f32[192,64]{1,0:T(8,128)S(1)} %add_add_fusion.1), channel_id=1, source_target_pairs={{0,34},{1,35},{4,38},{5,39},{8,42},{9,43},{12,46},{13,47},{16,50},... | collective-permute-start | bytes 147464 | tf_op jit(solution)/shard_map/ppermute | solution.py:11
  42.6 51.8 %collective-permute-start.19 = (f32[512,64]{1,0:T(8,128)S(1)}, f32[512,64]{1,0:T(8,128)S(1)}, u32[]{:S(2)}, u32[]{:S(2)}) collective-permute-start(f32[512,64]{1,0:T(8,128)S(1)} %add.108), channel_id=1, source_target_pairs={{0,0},{16,1},{32,2},{48,3},{64,4},{80,5},{96,6},{112,7},{128,8},{1... | collective-permute-start | bytes 393224 | tf_op jit(solution)/shard_map/ppermute | solution.py:11
  56.4 37.9 %collective-permute-start.20 = (f32[512,64]{1,0:T(8,128)S(1)}, f32[512,64]{1,0:T(8,128)S(1)}, u32[]{:S(2)}, u32[]{:S(2)}) collective-permute-start(f32[512,64]{1,0:T(8,128)S(1)} %add.108), channel_id=1, source_target_pairs={{0,256},{16,257},{32,258},{48,259},{64,260},{80,261},{96,262},{112... | collective-permute-start | bytes 393224 | tf_op jit(solution)/shard_map/ppermute | solution.py:11

commit v7 on v6

--- a/solution.py
+++ b/solution.py
@@ -80,18 +80,31 @@
     for step, offsets in zip((8, 4, 2), corner_offsets):
         panel = panel + lax.ppermute(panel, "col", [(c, c + step) for c in holders_col])
         holders_col = holders_col + [c + step for c in holders_col]
-        if step == 2:
+        corner, holders_k = spread_round(corner, holders_k, offsets, ncols)
+        if step == 4:
             corner, panel = lax.optimization_barrier((corner, panel))
-        corner, holders_k = spread_round(corner, holders_k, offsets, ncols)
+            early_panel, early_cols = panel, list(holders_col)
     corner, panel_held = lax.optimization_barrier((corner, panel))
 
-    lin = lambda r, c: r * ncols + c
-    first_pairs = [(lin(c, r), lin(r, c)) for r in range(half) for c in range(ncols)]
-    first_pairs += [(lin(c + half, r - half), lin(r, c)) for r in range(half, nrows) for c in range(ncols)]
-    second_pairs = [(lin(c, r - half), lin(r, c)) for r in range(half, nrows) for c in range(ncols)]
-    second_pairs += [(lin(c + half, r), lin(r, c)) for r in range(half) for c in range(ncols)]
-    first = both_axes(panel, first_pairs)
-    second = both_axes(panel, second_pairs)
+    width = len(early_cols)
+    groups = nrows // width
+    arrivals = []
+    for k in range(groups):
+        other = (k + groups // 2) % groups
+        pairs = []
+        for r in range(k * width, (k + 1) * width):
+            for c in range(ncols):
+                pairs.append((c * ncols + early_cols[r % width], r * ncols + c))
+        for r in range(other * width, (other + 1) * width):
+            for c in range(ncols):
+                pairs.append(((c + half) * ncols + early_cols[r % width], r * ncols + c))
+        arrivals.append(both_axes(early_panel, pairs))
+    group = p // width
+    near = arrivals[0]
+    far = arrivals[groups // 2]
+    for k in range(groups):
+        near = jnp.where(group == k, arrivals[k], near)
+        far = jnp.where(group == (k + groups // 2) % groups, arrivals[k], far)
 
     a00 = corner[:NB]
     a10 = corner[NB : 2 * NB]
@@ -109,9 +122,6 @@
     v = mm(w_rows, inv_t.T)
     zero_block = jnp.zeros((NB, NB), jnp.float32)
 
-    low = p < half
-    near = jnp.where(low, first, second)
-    far = jnp.where(low, second, first)
     col0 = interleave(near[:rows_len], far[:rows_len], row_count)
     col1 = interleave(near[rows_len:], far[rows_len:], row_count)
     cols = jnp.concatenate([col0, col1], axis=1)

time: 98.5 us -> 111 us (1.13)
  the two profiles are of different devices: /device:TPU:17 before, /device:TPU:21 now
where the time goes in v7:
time: 111 us; the launch traced here: 110 us
  starting transfers between devices  59.8 us (54%)
  other arithmetic  25.9 us (23%)
  waiting for transfers between devices  18.2 us (16%)
  local copies, waits for them, and re-layouts  3.82 us (3%)
  matrix products  1.63 us (1%)
    ppermute x19, starting transfers between devices, both_axes(): return lax.ppermute(x, ('row', 'col'), pairs)  46.7 us
    another operation x3, other arithmetic, per_device(): factor = jnp.linalg.cholesky(lead_block)  12.4 us
    another operation x2, other arithmetic, lower_inverse(): return jax.scipy.linalg.solve_triangular(factor, eye, lower=True)  10.5 us
    ppermute x3, starting transfers between devices, per_device(): lax.ppermute(panel, 'col', [(c, c + step) for c in holders_col])  10.5 us
    ppermute x19, waiting for transfers between devices, both_axes(): return lax.ppermute(x, ('row', 'col'), pairs)  10.2 us
    ppermute x3, waiting for transfers between devices, per_device(): lax.ppermute(panel, 'col', [(c, c + step) for c in holders_col])  7.05 us
    ppermute x1, starting transfers between devices, per_device(): swapped = lax.ppermute(mine, 'col', [(0, 1), (1, 0)])  2.58 us
  transfers between devices with their start and end apart: 23, of which 4 were waited for; matrix products, arithmetic and copies ran while one was open for 23% of the time, Pallas kernels for 0%

profile of v7, /device:TPU:21, one launch (start us, length us, event | category | flops | bytes accessed | tf_op | source)
XLA Modules:
  0.0 109.9 jit_solution(15978873381896214900)
XLA Ops:
  0.0 0.8 slice.78
  1.5 0.7 collective-permute-start.2
  2.2 0.9 slice.79
  3.1 2.6 %collective-permute-start = (f32[256,64]{1,0:T(8,128)S(1)}, f32[256,64]{1,0:T(8,128)S(1)}, u32[]{:S(2)}, u32[]{:S(2)}) collective-permute-start(f32[256,64]{1,0:T(8,128)S(1)} %slice.79), channel_id=1, source_target_pairs={{0,1},{1,0},{16,17},{17,16},{32,33},{33,32},{48,49},{49,48},{64,65... | collective-permute-start | bytes 196616 | tf_op jit(solution)/shard_map/ppermute | solution.py:66
  5.7 0.9 collective-permute-done
  6.6 0.8 broadcast_select_fusion.5
  7.5 0.7 collective-permute-start.3
  8.2 0.7 collective-permute-start.4
  8.9 0.7 collective-permute-start.5
  9.6 0.7 collective-permute-start.6
  10.2 0.7 collective-permute-start.7
  11.0 0.7 collective-permute-start.8
  11.6 0.7 collective-permute-start.9
  12.4 7.8 %collective-permute-start.13 = (f32[512,64]{1,0:T(8,128)S(1)}, f32[512,64]{1,0:T(8,128)S(1)}, u32[]{:S(2)}, u32[]{:S(2)}) collective-permute-start(f32[512,64]{1,0:T(8,128)S(1)} %maximum_select_fusion), channel_id=1, source_target_pairs={{0,8},{1,9},{16,24},{17,25},{32,40},{33,41},{48,56},{49,57},{64,72... | collective-permute-start | bytes 393224 | tf_op jit(solution)/shard_map/ppermute | solution.py:81
  20.3 0.7 collective-permute-start.10
  21.0 0.7 collective-permute-start.11
  21.7 0.7 collective-permute-start.12
  22.3 2.8 %collective-permute-done.13 = f32[512,64]{1,0:T(8,128)S(1)} collective-permute-done((f32[512,64]{1,0:T(8,128)S(1)}, f32[512,64]{1,0:T(8,128)S(1)}, u32[]{:S(2)}, u32[]{:S(2)}) %collective-permute-start.13) | collective-permute-done | bytes 131104 | tf_op jit(solution)/shard_map/ppermute | solution.py:81
  25.2 1.3 %collective-permute-start.14 = (f32[512,64]{1,0:T(8,128)S(1)}, f32[512,64]{1,0:T(8,128)S(1)}, u32[]{:S(2)}, u32[]{:S(2)}) collective-permute-start(f32[512,64]{1,0:T(8,128)S(1)} %add.107), channel_id=1, source_target_pairs={{0,4},{1,5},{8,12},{9,13},{16,20},{17,21},{24,28},{25,29},{32,36},... | collective-permute-start | bytes 393224 | tf_op jit(solution)/shard_map/ppermute | solution.py:81
  26.6 4.2 %collective-permute-done.14 = f32[512,64]{1,0:T(8,128)S(1)} collective-permute-done((f32[512,64]{1,0:T(8,128)S(1)}, f32[512,64]{1,0:T(8,128)S(1)}, u32[]{:S(2)}, u32[]{:S(2)}) %collective-permute-start.14) | collective-permute-done | bytes 131104 | tf_op jit(solution)/shard_map/ppermute | solution.py:81
  30.8 1.3 %collective-permute-start.15 = (f32[192,64]{1,0:T(8,128)S(1)}, f32[192,64]{1,0:T(8,128)S(1)}, u32[]{:S(2)}, u32[]{:S(2)}) collective-permute-start(f32[192,64]{1,0:T(8,128)S(1)} %add_add_fusion.1), channel_id=1, source_target_pairs={{0,32},{1,33},{4,36},{5,37},{8,40},{9,41},{12,44},{13,45},{16,48},... | collective-permute-start | bytes 147464 | tf_op jit(solution)/shard_map/ppermute | solution.py:11
  32.1 0.7 collective-permute-start.16
  32.8 0.7 collective-permute-start.17
  33.5 1.3 %collective-permute-start.18 = (f32[512,64]{1,0:T(8,128)S(1)}, f32[512,64]{1,0:T(8,128)S(1)}, u32[]{:S(2)}, u32[]{:S(2)}) collective-permute-start(f32[512,64]{1,0:T(8,128)S(1)} %add.108), channel_id=1, source_target_pairs={{0,2},{1,3},{8,10},{9,11},{4,6},{5,7},{12,14},{13,15},{16,18},{17,... | collective-permute-start | bytes 393224 | tf_op jit(solution)/shard_map/ppermute | solution.py:81
  34.8 1.9 %collective-permute-start.19 = (f32[512,64]{1,0:T(8,128)S(1)}, f32[512,64]{1,0:T(8,128)S(1)}, u32[]{:S(2)}, u32[]{:S(2)}) collective-permute-start(f32[512,64]{1,0:T(8,128)S(1)} %add.108), channel_id=1, source_target_pairs={{0,384},{16,385},{32,386},{48,387},{64,388},{80,389},{96,390},{112... | collective-permute-start | bytes 393224 | tf_op jit(solution)/shard_map/ppermute | solution.py:11
  36.8 10.1 %collective-permute-done.15 = f32[192,64]{1,0:T(8,128)S(1)} collective-permute-done((f32[192,64]{1,0:T(8,128)S(1)}, f32[192,64]{1,0:T(8,128)S(1)}, u32[]{:S(2)}, u32[]{:S(2)}) %collective-permute-start.15) | collective-permute-done | bytes 49184 | tf_op jit(solution)/shard_map/ppermute | solution.py:11
  46.9 1.3 %collective-permute-start.20 = (f32[512,64]{1,0:T(8,128)S(1)}, f32[512,64]{1,0:T(8,128)S(1)}, u32[]{:S(2)}, u32[]{:S(2)}) collective-permute-start(f32[512,64]{1,0:T(8,128)S(1)} %add.108), channel_id=1, source_target_pairs={{0,256},{16,257},{32,258},{48,259},{64,260},{80,261},{96,262},{112... | collective-permute-start | bytes 393224 | tf_op jit(solution)/shard_map/ppermute | solution.py:11
  48.2 31.6 %collective-permute-start.21 = (f32[512,64]{1,0:T(8,128)S(1)}, f32[512,64]{1,0:T(8,128)S(1)}, u32[]{:S(2)}, u32[]{:S(2)}) collective-permute-start(f32[512,64]{1,0:T(8,128)S(1)} %add.108), channel_id=1, source_target_pairs={{0,128},{16,129},{32,130},{48,131},{64,132},{80,133},{96,134},{112... | collective-permute-start | bytes 393224 | tf_op jit(solution)/shard_map/ppermute | solution.py:11
  79.8 1.3 %collective-permute-start.22 = (f32[512,64]{1,0:T(8,128)S(1)}, f32[512,64]{1,0:T(8,128)S(1)}, u32[]{:S(2)}, u32[]{:S(2)}) collective-permute-start(f32[512,64]{1,0:T(8,128)S(1)} %add.108), channel_id=1, source_target_pairs={{0,0},{16,1},{32,2},{48,3},{64,4},{80,5},{96,6},{112,7},{128,8},{1... | collective-permute-start | bytes 393224 | tf_op jit(solution)/shard_map/ppermute | solution.py:11
  81.8 11.7 %cholesky.20 = f32[128,128]{1,0:T(8,128)S(1)} custom-call(f32[128,128]{1,0:T(8,128)S(1)} %fusion.10), custom_call_target="Cholesky" | custom-call | tf_op jit(solution)/shard_map/jit(cholesky)/cholesky | solution.py:115
  94.8 9.8 %custom-call.7 = f32[1,128,128]{1,2,0:T(8,128)S(1)} custom-call(f32[1,128,128]{2,1,0:T(8,128)S(1)} %get-tuple-element.13), custom_call_target="InvertDiagBlocksLowerTriangular" | custom-call | tf_op jit(solution)/shard_map/jit(_solve_triangular)/triangular_solve | solution.py:50
  108.9 1.0 pad_maximum_fusion
  (70 shorter events, 7.0 us)
Async XLA Ops:
  0.0 7.5 %copy-start = (f32[256,512]{1,0:T(8,128)S(1)}, f32[256,512]{1,0:T(8,128)}, u32[]{:S(2)}) copy-start(f32[256,512]{1,0:T(8,128)} %param.1) | copy-start | bytes 1572868
  0.8 4.9 %collective-permute-start.1 = (f32[64,64]{1,0:T(8,128)S(1)}, f32[64,64]{1,0:T(8,128)S(1)}, u32[]{:S(2)}, u32[]{:S(2)}) collective-permute-start(f32[64,64]{1,0:T(8,128)S(1)} %slice.78), channel_id=1, source_target_pairs={{17,0},{0,16}} | collective-permute-start | bytes 49160 | tf_op jit(solution)/shard_map/ppermute | solution.py:11
  1.5 4.2 %collective-permute-start.2 = (f32[64,64]{1,0:T(8,128)S(1)}, f32[64,64]{1,0:T(8,128)S(1)}, u32[]{:S(2)}, u32[]{:S(2)}) collective-permute-start(f32[64,64]{1,0:T(8,128)S(1)} %slice.78), channel_id=1, source_target_pairs={{17,1},{0,17}} | collective-permute-start | bytes 49160 | tf_op jit(solution)/shard_map/ppermute | solution.py:11
  3.1 3.6 %collective-permute-start = (f32[256,64]{1,0:T(8,128)S(1)}, f32[256,64]{1,0:T(8,128)S(1)}, u32[]{:S(2)}, u32[]{:S(2)}) collective-permute-start(f32[256,64]{1,0:T(8,128)S(1)} %slice.79), channel_id=1, source_target_pairs={{0,1},{1,0},{16,17},{17,16},{32,33},{33,32},{48,49},{49,48},{64,65... | collective-permute-start | bytes 196616 | tf_op jit(solution)/shard_map/ppermute | solution.py:66
  7.5 3.4 %collective-permute-start.3 = (f32[192,64]{1,0:T(8,128)S(1)}, f32[192,64]{1,0:T(8,128)S(1)}, u32[]{:S(2)}, u32[]{:S(2)}) collective-permute-start(f32[192,64]{1,0:T(8,128)S(1)} %maximum_select_fusion.2), channel_id=1, source_target_pairs={{0,8},{1,9},{16,24},{17,25}} | collective-permute-start | bytes 147464 | tf_op jit(solution)/shard_map/ppermute | solution.py:11
  8.2 3.4 %collective-permute-start.4 = (f32[192,64]{1,0:T(8,128)S(1)}, f32[192,64]{1,0:T(8,128)S(1)}, u32[]{:S(2)}, u32[]{:S(2)}) collective-permute-start(f32[192,64]{1,0:T(8,128)S(1)} %maximum_select_fusion.2), channel_id=1, source_target_pairs={{0,128},{1,129},{16,144},{17,145}} | collective-permute-start | bytes 147464 | tf_op jit(solution)/shard_map/ppermute | solution.py:11
  8.9 3.5 %collective-permute-start.5 = (f32[192,64]{1,0:T(8,128)S(1)}, f32[192,64]{1,0:T(8,128)S(1)}, u32[]{:S(2)}, u32[]{:S(2)}) collective-permute-start(f32[192,64]{1,0:T(8,128)S(1)} %maximum_select_fusion.2), channel_id=1, source_target_pairs={{0,136},{1,137},{16,152},{17,153}} | collective-permute-start | bytes 147464 | tf_op jit(solution)/shard_map/ppermute | solution.py:11
  9.6 10.6 %collective-permute-start.6 = (f32[192,64]{1,0:T(8,128)S(1)}, f32[192,64]{1,0:T(8,128)S(1)}, u32[]{:S(2)}, u32[]{:S(2)}) collective-permute-start(f32[192,64]{1,0:T(8,128)S(1)} %maximum_select_fusion.2), channel_id=1, source_target_pairs={{0,256},{1,257},{16,272},{17,273}} | collective-permute-start | bytes 147464 | tf_op jit(solution)/shard_map/ppermute | solution.py:11
  10.2 10.0 %collective-permute-start.7 = (f32[192,64]{1,0:T(8,128)S(1)}, f32[192,64]{1,0:T(8,128)S(1)}, u32[]{:S(2)}, u32[]{:S(2)}) collective-permute-start(f32[192,64]{1,0:T(8,128)S(1)} %maximum_select_fusion.2), channel_id=1, source_target_pairs={{0,264},{1,265},{16,280},{17,281}} | collective-permute-start | bytes 147464 | tf_op jit(solution)/shard_map/ppermute | solution.py:11
  11.0 9.3 %collective-permute-start.8 = (f32[192,64]{1,0:T(8,128)S(1)}, f32[192,64]{1,0:T(8,128)S(1)}, u32[]{:S(2)}, u32[]{:S(2)}) collective-permute-start(f32[192,64]{1,0:T(8,128)S(1)} %maximum_select_fusion.2), channel_id=1, source_target_pairs={{0,384},{1,385},{16,400},{17,401}} | collective-permute-start | bytes 147464 | tf_op jit(solution)/shard_map/ppermute | solution.py:11
  11.6 8.6 %collective-permute-start.9 = (f32[192,64]{1,0:T(8,128)S(1)}, f32[192,64]{1,0:T(8,128)S(1)}, u32[]{:S(2)}, u32[]{:S(2)}) collective-permute-start(f32[192,64]{1,0:T(8,128)S(1)} %maximum_select_fusion.2), channel_id=1, source_target_pairs={{0,392},{1,393},{16,408},{17,409}} | collective-permute-start | bytes 147464 | tf_op jit(solution)/shard_map/ppermute | solution.py:11
  12.4 12.8 %collective-permute-start.13 = (f32[512,64]{1,0:T(8,128)S(1)}, f32[512,64]{1,0:T(8,128)S(1)}, u32[]{:S(2)}, u32[]{:S(2)}) collective-permute-start(f32[512,64]{1,0:T(8,128)S(1)} %maximum_select_fusion), channel_id=1, source_target_pairs={{0,8},{1,9},{16,24},{17,25},{32,40},{33,41},{48,56},{49,57},{64,72... | collective-permute-start | bytes 393224 | tf_op jit(solution)/shard_map/ppermute | solution.py:81
  20.3 6.2 %collective-permute-start.10 = (f32[192,64]{1,0:T(8,128)S(1)}, f32[192,64]{1,0:T(8,128)S(1)}, u32[]{:S(2)}, u32[]{:S(2)}) collective-permute-start(f32[192,64]{1,0:T(8,128)S(1)} %add_add_fusion.2), channel_id=1, source_target_pairs={{0,64},{1,65},{8,72},{9,73},{16,80},{17,81},{24,88},{25,89},{128,1... | collective-permute-start | bytes 147464 | tf_op jit(solution)/shard_map/ppermute | solution.py:11
  21.0 5.5 %collective-permute-start.11 = (f32[192,64]{1,0:T(8,128)S(1)}, f32[192,64]{1,0:T(8,128)S(1)}, u32[]{:S(2)}, u32[]{:S(2)}) collective-permute-start(f32[192,64]{1,0:T(8,128)S(1)} %add_add_fusion.2), channel_id=1, source_target_pairs={{0,4},{1,5},{8,12},{9,13},{16,20},{17,21},{24,28},{25,29},{128,132... | collective-permute-start | bytes 147464 | tf_op jit(solution)/shard_map/ppermute | solution.py:11
  21.7 4.9 %collective-permute-start.12 = (f32[192,64]{1,0:T(8,128)S(1)}, f32[192,64]{1,0:T(8,128)S(1)}, u32[]{:S(2)}, u32[]{:S(2)}) collective-permute-start(f32[192,64]{1,0:T(8,128)S(1)} %add_add_fusion.2), channel_id=1, source_target_pairs={{0,68},{1,69},{8,76},{9,77},{16,84},{17,85},{24,92},{25,93},{128,1... | collective-permute-start | bytes 147464 | tf_op jit(solution)/shard_map/ppermute | solution.py:11
  25.2 5.6 %collective-permute-start.14 = (f32[512,64]{1,0:T(8,128)S(1)}, f32[512,64]{1,0:T(8,128)S(1)}, u32[]{:S(2)}, u32[]{:S(2)}) collective-permute-start(f32[512,64]{1,0:T(8,128)S(1)} %add.107), channel_id=1, source_target_pairs={{0,4},{1,5},{8,12},{9,13},{16,20},{17,21},{24,28},{25,29},{32,36},... | collective-permute-start | bytes 393224 | tf_op jit(solution)/shard_map/ppermute | solution.py:81
  30.8 16.1 %collective-permute-start.15 = (f32[192,64]{1,0:T(8,128)S(1)}, f32[192,64]{1,0:T(8,128)S(1)}, u32[]{:S(2)}, u32[]{:S(2)}) collective-permute-start(f32[192,64]{1,0:T(8,128)S(1)} %add_add_fusion.1), channel_id=1, source_target_pairs={{0,32},{1,33},{4,36},{5,37},{8,40},{9,41},{12,44},{13,45},{16,48},... | collective-permute-start | bytes 147464 | tf_op jit(solution)/shard_map/ppermute | solution.py:11
  32.1 16.1 %collective-permute-start.16 = (f32[192,64]{1,0:T(8,128)S(1)}, f32[192,64]{1,0:T(8,128)S(1)}, u32[]{:S(2)}, u32[]{:S(2)}) collective-permute-start(f32[192,64]{1,0:T(8,128)S(1)} %add_add_fusion.1), channel_id=1, source_target_pairs={{0,2},{1,3},{4,6},{5,7},{8,10},{9,11},{12,14},{13,15},{16,18},{17,... | collective-permute-start | bytes 147464 | tf_op jit(solution)/shard_map/ppermute | solution.py:11
  32.8 47.0 %collective-permute-start.17 = (f32[192,64]{1,0:T(8,128)S(1)}, f32[192,64]{1,0:T(8,128)S(1)}, u32[]{:S(2)}, u32[]{:S(2)}) collective-permute-start(f32[192,64]{1,0:T(8,128)S(1)} %add_add_fusion.1), channel_id=1, source_target_pairs={{0,34},{1,35},{4,38},{5,39},{8,42},{9,43},{12,46},{13,47},{16,50},... | collective-permute-start | bytes 147464 | tf_op jit(solution)/shard_map/ppermute | solution.py:11
  33.5 47.7 %collective-permute-start.18 = (f32[512,64]{1,0:T(8,128)S(1)}, f32[512,64]{1,0:T(8,128)S(1)}, u32[]{:S(2)}, u32[]{:S(2)}) collective-permute-start(f32[512,64]{1,0:T(8,128)S(1)} %add.108), channel_id=1, source_target_pairs={{0,2},{1,3},{8,10},{9,11},{4,6},{5,7},{12,14},{13,15},{16,18},{17,... | collective-permute-start | bytes 393224 | tf_op jit(solution)/shard_map/ppermute | solution.py:81
  34.8 71.1 %collective-permute-start.19 = (f32[512,64]{1,0:T(8,128)S(1)}, f32[512,64]{1,0:T(8,128)S(1)}, u32[]{:S(2)}, u32[]{:S(2)}) collective-permute-start(f32[512,64]{1,0:T(8,128)S(1)} %add.108), channel_id=1, source_target_pairs={{0,384},{16,385},{32,386},{48,387},{64,388},{80,389},{96,390},{112... | collective-permute-start | bytes 393224 | tf_op jit(solution)/shard_map/ppermute | solution.py:11
  46.9 59.1 %collective-permute-start.20 = (f32[512,64]{1,0:T(8,128)S(1)}, f32[512,64]{1,0:T(8,128)S(1)}, u32[]{:S(2)}, u32[]{:S(2)}) collective-permute-start(f32[512,64]{1,0:T(8,128)S(1)} %add.108), channel_id=1, source_target_pairs={{0,256},{16,257},{32,258},{48,259},{64,260},{80,261},{96,262},{112... | collective-permute-start | bytes 393224 | tf_op jit(solution)/shard_map/ppermute | solution.py:11
  48.2 57.8 %collective-permute-start.21 = (f32[512,64]{1,0:T(8,128)S(1)}, f32[512,64]{1,0:T(8,128)S(1)}, u32[]{:S(2)}, u32[]{:S(2)}) collective-permute-start(f32[512,64]{1,0:T(8,128)S(1)} %add.108), channel_id=1, source_target_pairs={{0,128},{16,129},{32,130},{48,131},{64,132},{80,133},{96,134},{112... | collective-permute-start | bytes 393224 | tf_op jit(solution)/shard_map/ppermute | solution.py:11
  79.8 26.2 %collective-permute-start.22 = (f32[512,64]{1,0:T(8,128)S(1)}, f32[512,64]{1,0:T(8,128)S(1)}, u32[]{:S(2)}, u32[]{:S(2)}) collective-permute-start(f32[512,64]{1,0:T(8,128)S(1)} %add.108), channel_id=1, source_target_pairs={{0,0},{16,1},{32,2},{48,3},{64,4},{80,5},{96,6},{112,7},{128,8},{1... | collective-permute-start | bytes 393224 | tf_op jit(solution)/shard_map/ppermute | solution.py:11

commit v8 on v6

--- a/solution.py
+++ b/solution.py
@@ -78,11 +78,18 @@
         [(2, 0), (0, 2), (2, 2)],
     ]
     for step, offsets in zip((8, 4, 2), corner_offsets):
-        panel = panel + lax.ppermute(panel, "col", [(c, c + step) for c in holders_col])
+        assert {c for _, c in holders_k} <= set(holders_col) and (0, step) in offsets
+        both = jnp.concatenate([panel, corner], axis=0)
+        got = lax.ppermute(both, "col", [(c, c + step) for c in holders_col])
+        panel = panel + got[: panel.shape[0]]
+        along = got[panel.shape[0] :]
         holders_col = holders_col + [c + step for c in holders_col]
         if step == 2:
-            corner, panel = lax.optimization_barrier((corner, panel))
-        corner, holders_k = spread_round(corner, holders_k, offsets, ncols)
+            corner, panel, along = lax.optimization_barrier((corner, panel, along))
+        moved = {(r, c + step) for r, c in holders_k}
+        corner, holders_k = spread_round(corner, holders_k, [o for o in offsets if o != (0, step)], ncols)
+        corner = corner + along
+        holders_k = holders_k | moved
     corner, panel_held = lax.optimization_barrier((corner, panel))
 
     lin = lambda r, c: r * ncols + c

time: 98.5 us -> 106 us (1.076)
  the two profiles are of different devices: /device:TPU:17 before, /device:TPU:464 now
where the time goes in v8:
time: 106 us; the launch traced here: 105 us
  starting transfers between devices  44.9 us (42%)
  waiting for transfers between devices  28.7 us (27%)
  other arithmetic  25.2 us (24%)
  local copies, waits for them, and re-layouts  4.14 us (4%)
  matrix products  1.63 us (2%)
    ppermute x14, starting transfers between devices, both_axes(): return lax.ppermute(x, ('row', 'col'), pairs)  41.6 us
    ppermute x3, waiting for transfers between devices, per_device(): got = lax.ppermute(both, 'col', [(c, c + step) for c in holders_col])  28.7 us
    another operation x3, other arithmetic, per_device(): factor = jnp.linalg.cholesky(lead_block)  12.4 us
    another operation x2, other arithmetic, lower_inverse(): return jax.scipy.linalg.solve_triangular(factor, eye, lower=True)  10.5 us
    ppermute x3, starting transfers between devices, per_device(): got = lax.ppermute(both, 'col', [(c, c + step) for c in holders_col])  2.66 us
  transfers between devices with their start and end apart: 18, of which 1 were waited for; matrix products, arithmetic and copies ran while one was open for 25% of the time, Pallas kernels for 0%

profile of v8, /device:TPU:464, one launch (start us, length us, event | category | flops | bytes accessed | tf_op | source)
XLA Modules:
  0.0 105.2 jit_solution(17747156431832906716)
XLA Ops:
  0.0 1.0 slice.97
  1.0 0.7 collective-permute-start
  1.7 0.8 slice.96
  2.5 0.7 collective-permute-start.1
  3.2 0.7 collective-permute-start.2
  4.4 0.7 collective-permute-start.9
  5.1 0.7 collective-permute-start.3
  5.8 0.7 collective-permute-start.4
  6.5 0.7 collective-permute-start.5
  7.1 0.7 collective-permute-start.6
  7.8 0.7 collective-permute-start.7
  8.5 0.7 collective-permute-start.8
  9.4 0.7 collective-permute-start.12
  10.0 0.7 collective-permute-start.10
  10.7 0.7 collective-permute-start.11
  11.5 1.3 %collective-permute-start.13 = (f32[704,64]{1,0:T(8,128)S(1)}, f32[704,64]{1,0:T(8,128)S(1)}, u32[]{:S(2)}, u32[]{:S(2)}) collective-permute-start(f32[704,64]{1,0:T(8,128)S(1)} %pad_maximum_fusion.3), channel_id=1, source_target_pairs={{0,2},{1,3},{8,10},{9,11},{4,6},{5,7},{12,14},{13,15},{16,18},{17,... | collective-permute-start | bytes 540680 | tf_op jit(solution)/shard_map/ppermute | solution.py:83
  12.9 28.7 %collective-permute-done.13 = f32[704,64]{1,0:T(8,128)S(1)} collective-permute-done((f32[704,64]{1,0:T(8,128)S(1)}, f32[704,64]{1,0:T(8,128)S(1)}, u32[]{:S(2)}, u32[]{:S(2)}) %collective-permute-start.13) | collective-permute-done | bytes 180256 | tf_op jit(solution)/shard_map/ppermute | solution.py:83
  41.6 0.7 collective-permute-start.14
  42.2 0.7 collective-permute-start.15
  42.9 2.4 %collective-permute-start.16 = (f32[512,64]{1,0:T(8,128)S(1)}, f32[512,64]{1,0:T(8,128)S(1)}, u32[]{:S(2)}, u32[]{:S(2)}) collective-permute-start(f32[512,64]{1,0:T(8,128)S(1)} %slice_add_fusion), channel_id=1, source_target_pairs={{0,0},{16,1},{32,2},{48,3},{64,4},{80,5},{96,6},{112,7},{128,8},{1... | collective-permute-start | bytes 393224 | tf_op jit(solution)/shard_map/ppermute | solution.py:11
  45.4 31.2 %collective-permute-start.17 = (f32[512,64]{1,0:T(8,128)S(1)}, f32[512,64]{1,0:T(8,128)S(1)}, u32[]{:S(2)}, u32[]{:S(2)}) collective-permute-start(f32[512,64]{1,0:T(8,128)S(1)} %slice_add_fusion), channel_id=1, source_target_pairs={{0,256},{16,257},{32,258},{48,259},{64,260},{80,261},{96,262},{112... | collective-permute-start | bytes 393224 | tf_op jit(solution)/shard_map/ppermute | solution.py:11
  77.2 11.7 %cholesky.20 = f32[128,128]{1,0:T(8,128)S(1)} custom-call(f32[128,128]{1,0:T(8,128)S(1)} %fusion.10), custom_call_target="Cholesky" | custom-call | tf_op jit(solution)/shard_map/jit(cholesky)/cholesky | solution.py:109
  88.9 0.6 compare_reduce_fusion
  89.6 0.7 select_bitcast_fusion
  90.2 9.8 %custom-call.7 = f32[1,128,128]{1,2,0:T(8,128)S(1)} custom-call(f32[1,128,128]{2,1,0:T(8,128)S(1)} %get-tuple-element.15), custom_call_target="InvertDiagBlocksLowerTriangular" | custom-call | tf_op jit(solution)/shard_map/jit(_solve_triangular)/triangular_solve | solution.py:50
  100.3 0.4 fusion.4
  100.7 0.4 fusion.27
  102.0 0.3 pad_maximum_fusion.4
  102.3 0.3 reshape.50
  102.8 0.3 pad_maximum_fusion.5
  103.4 0.6 fusion
  104.2 1.0 pad_maximum_fusion
  (69 shorter events, 3.2 us)
Async XLA Ops:
  0.0 4.0 %copy-start = (f32[256,512]{1,0:T(8,128)S(1)}, f32[256,512]{1,0:T(8,128)}, u32[]{:S(2)}) copy-start(f32[256,512]{1,0:T(8,128)} %param.1) | copy-start | bytes 1572868
  1.0 2.9 %collective-permute-start = (f32[256,64]{1,0:T(8,128)S(1)}, f32[256,64]{1,0:T(8,128)S(1)}, u32[]{:S(2)}, u32[]{:S(2)}) collective-permute-start(f32[256,64]{1,0:T(8,128)S(1)} %slice.97), channel_id=1, source_target_pairs={{0,1},{1,0},{16,17},{17,16},{32,33},{33,32},{48,49},{49,48},{64,65... | collective-permute-start | bytes 196616 | tf_op jit(solution)/shard_map/ppermute | solution.py:66
  2.5 1.5 %collective-permute-start.1 = (f32[64,64]{0,1:T(8,128)S(1)}, f32[64,64]{0,1:T(8,128)S(1)}, u32[]{:S(2)}, u32[]{:S(2)}) collective-permute-start(f32[64,64]{0,1:T(8,128)S(1)} %copy.38), channel_id=1, source_target_pairs={{17,0},{0,16}} | collective-permute-start | bytes 49160 | tf_op jit(solution)/shard_map/ppermute | solution.py:11
  3.2 0.8 collective-permute-start.2
  4.4 4.1 %collective-permute-start.9 = (f32[704,64]{1,0:T(8,128)S(1)}, f32[704,64]{1,0:T(8,128)S(1)}, u32[]{:S(2)}, u32[]{:S(2)}) collective-permute-start(f32[704,64]{1,0:T(8,128)S(1)} %pad_maximum_fusion.1), channel_id=1, source_target_pairs={{0,8},{1,9},{16,24},{17,25},{32,40},{33,41},{48,56},{49,57},{64,72... | collective-permute-start | bytes 540680 | tf_op jit(solution)/shard_map/ppermute | solution.py:83
  5.1 2.7 %collective-permute-start.3 = (f32[192,64]{1,0:T(8,128)S(1)}, f32[192,64]{1,0:T(8,128)S(1)}, u32[]{:S(2)}, u32[]{:S(2)}) collective-permute-start(f32[192,64]{1,0:T(8,128)S(1)} %maximum_select_fusion.2), channel_id=1, source_target_pairs={{0,128},{1,129},{16,144},{17,145}} | collective-permute-start | bytes 147464 | tf_op jit(solution)/shard_map/ppermute | solution.py:11
  5.8 3.4 %collective-permute-start.4 = (f32[192,64]{1,0:T(8,128)S(1)}, f32[192,64]{1,0:T(8,128)S(1)}, u32[]{:S(2)}, u32[]{:S(2)}) collective-permute-start(f32[192,64]{1,0:T(8,128)S(1)} %maximum_select_fusion.2), channel_id=1, source_target_pairs={{0,136},{1,137},{16,152},{17,153}} | collective-permute-start | bytes 147464 | tf_op jit(solution)/shard_map/ppermute | solution.py:11
  6.5 2.8 %collective-permute-start.5 = (f32[192,64]{1,0:T(8,128)S(1)}, f32[192,64]{1,0:T(8,128)S(1)}, u32[]{:S(2)}, u32[]{:S(2)}) collective-permute-start(f32[192,64]{1,0:T(8,128)S(1)} %maximum_select_fusion.2), channel_id=1, source_target_pairs={{0,256},{1,257},{16,272},{17,273}} | collective-permute-start | bytes 147464 | tf_op jit(solution)/shard_map/ppermute | solution.py:11
  7.1 2.1 %collective-permute-start.6 = (f32[192,64]{1,0:T(8,128)S(1)}, f32[192,64]{1,0:T(8,128)S(1)}, u32[]{:S(2)}, u32[]{:S(2)}) collective-permute-start(f32[192,64]{1,0:T(8,128)S(1)} %maximum_select_fusion.2), channel_id=1, source_target_pairs={{0,264},{1,265},{16,280},{17,281}} | collective-permute-start | bytes 147464 | tf_op jit(solution)/shard_map/ppermute | solution.py:11
  7.8 1.4 %collective-permute-start.7 = (f32[192,64]{1,0:T(8,128)S(1)}, f32[192,64]{1,0:T(8,128)S(1)}, u32[]{:S(2)}, u32[]{:S(2)}) collective-permute-start(f32[192,64]{1,0:T(8,128)S(1)} %maximum_select_fusion.2), channel_id=1, source_target_pairs={{0,384},{1,385},{16,400},{17,401}} | collective-permute-start | bytes 147464 | tf_op jit(solution)/shard_map/ppermute | solution.py:11
  8.5 0.8 collective-permute-start.8
  9.4 2.0 %collective-permute-start.12 = (f32[704,64]{1,0:T(8,128)S(1)}, f32[704,64]{1,0:T(8,128)S(1)}, u32[]{:S(2)}, u32[]{:S(2)}) collective-permute-start(f32[704,64]{1,0:T(8,128)S(1)} %pad_maximum_fusion.2), channel_id=1, source_target_pairs={{0,4},{1,5},{8,12},{9,13},{16,20},{17,21},{24,28},{25,29},{32,36},... | collective-permute-start | bytes 540680 | tf_op jit(solution)/shard_map/ppermute | solution.py:83
  10.0 1.4 %collective-permute-start.10 = (f32[192,64]{1,0:T(8,128)S(1)}, f32[192,64]{1,0:T(8,128)S(1)}, u32[]{:S(2)}, u32[]{:S(2)}) collective-permute-start(f32[192,64]{1,0:T(8,128)S(1)} %slice_add_fusion.4), channel_id=1, source_target_pairs={{0,64},{1,65},{8,72},{9,73},{16,80},{17,81},{24,88},{25,89},{128,1... | collective-permute-start | bytes 147464 | tf_op jit(solution)/shard_map/ppermute | solution.py:11
  10.7 0.7 collective-permute-start.11
  11.5 30.0 %collective-permute-start.13 = (f32[704,64]{1,0:T(8,128)S(1)}, f32[704,64]{1,0:T(8,128)S(1)}, u32[]{:S(2)}, u32[]{:S(2)}) collective-permute-start(f32[704,64]{1,0:T(8,128)S(1)} %pad_maximum_fusion.3), channel_id=1, source_target_pairs={{0,2},{1,3},{8,10},{9,11},{4,6},{5,7},{12,14},{13,15},{16,18},{17,... | collective-permute-start | bytes 540680 | tf_op jit(solution)/shard_map/ppermute | solution.py:83
  41.6 35.0 %collective-permute-start.14 = (f32[192,64]{1,0:T(8,128)S(1)}, f32[192,64]{1,0:T(8,128)S(1)}, u32[]{:S(2)}, u32[]{:S(2)}) collective-permute-start(f32[192,64]{1,0:T(8,128)S(1)} %slice_add_fusion.3), channel_id=1, source_target_pairs={{0,32},{1,33},{4,36},{5,37},{8,40},{9,41},{12,44},{13,45},{16,48},... | collective-permute-start | bytes 147464 | tf_op jit(solution)/shard_map/ppermute | solution.py:11
  42.2 34.3 %collective-permute-start.15 = (f32[192,64]{1,0:T(8,128)S(1)}, f32[192,64]{1,0:T(8,128)S(1)}, u32[]{:S(2)}, u32[]{:S(2)}) collective-permute-start(f32[192,64]{1,0:T(8,128)S(1)} %slice_add_fusion.3), channel_id=1, source_target_pairs={{0,34},{1,35},{4,38},{5,39},{8,42},{9,43},{12,46},{13,47},{16,50},... | collective-permute-start | bytes 147464 | tf_op jit(solution)/shard_map/ppermute | solution.py:11
  42.9 58.7 %collective-permute-start.16 = (f32[512,64]{1,0:T(8,128)S(1)}, f32[512,64]{1,0:T(8,128)S(1)}, u32[]{:S(2)}, u32[]{:S(2)}) collective-permute-start(f32[512,64]{1,0:T(8,128)S(1)} %slice_add_fusion), channel_id=1, source_target_pairs={{0,0},{16,1},{32,2},{48,3},{64,4},{80,5},{96,6},{112,7},{128,8},{1... | collective-permute-start | bytes 393224 | tf_op jit(solution)/shard_map/ppermute | solution.py:11
  45.4 56.3 %collective-permute-start.17 = (f32[512,64]{1,0:T(8,128)S(1)}, f32[512,64]{1,0:T(8,128)S(1)}, u32[]{:S(2)}, u32[]{:S(2)}) collective-permute-start(f32[512,64]{1,0:T(8,128)S(1)} %slice_add_fusion), channel_id=1, source_target_pairs={{0,256},{16,257},{32,258},{48,259},{64,260},{80,261},{96,262},{112... | collective-permute-start | bytes 393224 | tf_op jit(solution)/shard_map/ppermute | solution.py:11

commit v9 on v6

--- a/solution.py
+++ b/solution.py
@@ -27,7 +27,7 @@
     a00 = jnp.where(p == 0, u, sent)
     a10 = jnp.where(p == 0, t.T, u)
     a11 = jnp.where(p == 0, sent, t)
-    return jnp.concatenate([a00, a10, a11], axis=0)
+    return jnp.concatenate([a00, a10, a11], axis=0).reshape(3 * NB // 2, 2 * NB)
 
 
 def spread_round(value, holders, offsets, ncols):
@@ -41,8 +41,9 @@
 
 
 def interleave(a, b, count):
-    blocks = jnp.stack([a.reshape(count, NB, NB), b.reshape(count, NB, NB)], axis=1)
-    return blocks.reshape(2 * count * NB, NB)
+    width = a.shape[1]
+    blocks = jnp.stack([a.reshape(count, NB, width), b.reshape(count, NB, width)], axis=1)
+    return blocks.reshape(2 * count * NB, width)
 
 
 def lower_inverse(factor):
@@ -65,7 +66,7 @@
     mine = stored[:, :NB]
     swapped = lax.ppermute(mine, "col", [(0, 1), (1, 0)])
     panel = jnp.concatenate(
-        [jnp.where(q == 0, mine, swapped), jnp.where(q == 0, swapped, mine)], axis=0
+        [jnp.where(q == 0, mine, swapped), jnp.where(q == 0, swapped, mine)], axis=1
     )
     panel = jnp.where(q < 2, panel, 0.0)
     corner = jnp.where((p < 2) & (q < 2), gather_corner(stored, swapped, p, q, ncols), 0.0)
@@ -93,6 +94,7 @@
     first = both_axes(panel, first_pairs)
     second = both_axes(panel, second_pairs)
 
+    corner = corner.reshape(3 * NB, NB)
     a00 = corner[:NB]
     a10 = corner[NB : 2 * NB]
     a11 = corner[2 * NB :]
@@ -103,7 +105,7 @@
     inv_t = lower_inverse(factor).T
     c0 = factor[:NB, :NB]
     c1 = factor[NB:, NB:]
-    w_rows = mm(jnp.concatenate([panel_held[:rows_len], panel_held[rows_len:]], axis=1), inv_t)
+    w_rows = mm(panel_held, inv_t)
     x_rows = w_rows[:, :NB]
     y_rows = w_rows[:, NB:]
     v = mm(w_rows, inv_t.T)
@@ -112,9 +114,7 @@
     low = p < half
     near = jnp.where(low, first, second)
     far = jnp.where(low, second, first)
-    col0 = interleave(near[:rows_len], far[:rows_len], row_count)
-    col1 = interleave(near[rows_len:], far[rows_len:], row_count)
-    cols = jnp.concatenate([col0, col1], axis=1)
+    cols = interleave(near, far, row_count)
     update = mm(v, cols.T)
 
     row_ids = jnp.arange(row_count * NB, dtype=jnp.int32) // NB * nrows + p

time: 98.5 us -> 86.6 us (0.88)
  the two profiles are of different devices: /device:TPU:17 before, /device:TPU:18 now
where the time goes in v9:
time: 86.6 us; the launch traced here: 86 us
  starting transfers between devices  48.9 us (56%)
  other arithmetic  25.4 us (29%)
  waiting for transfers between devices  6.48 us (7%)
  local copies, waits for them, and re-layouts  3.03 us (3%)
  matrix products  1.55 us (2%)
    ppermute x17, starting transfers between devices, both_axes(): return lax.ppermute(x, ('row', 'col'), pairs)  34.6 us
    another operation x3, other arithmetic, per_device(): factor = jnp.linalg.cholesky(lead_block)  12.4 us
    ppermute x3, starting transfers between devices, per_device(): lax.ppermute(panel, 'col', [(c, c + step) for c in holders_col])  12.3 us
    another operation x2, other arithmetic, lower_inverse(): return jax.scipy.linalg.solve_triangular(factor, eye, lower=True)  10.5 us
    ppermute x17, waiting for transfers between devices, both_axes(): return lax.ppermute(x, ('row', 'col'), pairs)  4.37 us
    ppermute x3, waiting for transfers between devices, per_device(): lax.ppermute(panel, 'col', [(c, c + step) for c in holders_col])  2.11 us
    ppermute x1, starting transfers between devices, per_device(): swapped = lax.ppermute(mine, 'col', [(0, 1), (1, 0)])  2.05 us
  transfers between devices with their start and end apart: 21, of which 3 were waited for; matrix products, arithmetic and copies ran while one was open for 32% of the time, Pallas kernels for 0%

profile of v9, /device:TPU:18, one launch (start us, length us, event | category | flops | bytes accessed | tf_op | source)
XLA Modules:
  0.0 86.0 jit_solution(13867721036723375991)
XLA Ops:
  0.0 0.9 %slice.70 = f32[256,64]{1,0:T(8,128)S(1)} slice(f32[256,512]{1,0:T(8,128)} %param.1), slice={[0:256], [0:64]} | slice | bytes 131072 | tf_op jit(solution)/shard_map/slice | solution.py:66
  0.9 2.1 %collective-permute-start = (f32[256,64]{1,0:T(8,128)S(1)}, f32[256,64]{1,0:T(8,128)S(1)}, u32[]{:S(2)}, u32[]{:S(2)}) collective-permute-start(f32[256,64]{1,0:T(8,128)S(1)} %slice.70), channel_id=1, source_target_pairs={{0,1},{1,0},{16,17},{17,16},{32,33},{33,32},{48,49},{49,48},{64,65... | collective-permute-start | bytes 196616 | tf_op jit(solution)/shard_map/ppermute | solution.py:67
  3.0 0.8 slice.69
  3.8 0.7 collective-permute-start.1
  4.4 0.7 collective-permute-start.2
  5.1 0.9 %broadcast_select_fusion.3 = (f32[256,64]{1,0:T(8,128)S(1)}, f32[256,64]{1,0:T(8,128)S(1)}) fusion(f32[256,64]{1,0:T(8,128)S(1)} %collective-permute-done, pred[]{:T(512)S(6)} %eq.6, f32[256,512]{1,0:T(8,128)} %param.1), kind=kLoop, calls=%fused_computation.21 | loop fusion | flops 32768 | bytes 262145 | tf_op jit(solution)/shard_map/jit(_where)/select_n | solution.py:69
  6.1 9.7 %collective-permute-start.13 = (f32[256,128]{1,0:T(8,128)S(1)}, f32[256,128]{1,0:T(8,128)S(1)}, u32[]{:S(2)}, u32[]{:S(2)}) collective-permute-start(f32[256,128]{1,0:T(8,128)S(1)} %maximum_select_fusion), channel_id=1, source_target_pairs={{0,8},{1,9},{16,24},{17,25},{32,40},{33,41},{48,56},{49,57},{64,72... | collective-permute-start | bytes 393224 | tf_op jit(solution)/shard_map/ppermute | solution.py:82
  16.1 0.7 collective-permute-start.3
  16.7 1.3 %collective-permute-start.4 = (f32[96,128]{1,0:T(8,128)S(1)}, f32[96,128]{1,0:T(8,128)S(1)}, u32[]{:S(2)}, u32[]{:S(2)}) collective-permute-start(f32[96,128]{1,0:T(8,128)S(1)} %select_n.138), channel_id=1, source_target_pairs={{0,128},{1,129},{16,144},{17,145}} | collective-permute-start | bytes 147464 | tf_op jit(solution)/shard_map/ppermute | solution.py:11
  18.0 0.7 collective-permute-start.5
  18.7 0.7 collective-permute-start.6
  19.4 0.7 collective-permute-start.7
  20.1 4.0 %collective-permute-done.4 = f32[96,128]{1,0:T(8,128)S(1)} collective-permute-done((f32[96,128]{1,0:T(8,128)S(1)}, f32[96,128]{1,0:T(8,128)S(1)}, u32[]{:S(2)}, u32[]{:S(2)}) %collective-permute-start.4) | collective-permute-done | bytes 49184 | tf_op jit(solution)/shard_map/ppermute | solution.py:11
  24.0 0.7 collective-permute-start.8
  24.7 0.7 collective-permute-start.9
  25.4 1.3 %collective-permute-start.14 = (f32[256,128]{1,0:T(8,128)S(1)}, f32[256,128]{1,0:T(8,128)S(1)}, u32[]{:S(2)}, u32[]{:S(2)}) collective-permute-start(f32[256,128]{1,0:T(8,128)S(1)} %add.106), channel_id=1, source_target_pairs={{0,4},{1,5},{8,12},{9,13},{16,20},{17,21},{24,28},{25,29},{32,36},... | collective-permute-start | bytes 393224 | tf_op jit(solution)/shard_map/ppermute | solution.py:82
  26.8 1.3 %collective-permute-start.10 = (f32[96,128]{1,0:T(8,128)S(1)}, f32[96,128]{1,0:T(8,128)S(1)}, u32[]{:S(2)}, u32[]{:S(2)}) collective-permute-start(f32[96,128]{1,0:T(8,128)S(1)} %add_add_fusion.2), channel_id=1, source_target_pairs={{0,64},{1,65},{8,72},{9,73},{16,80},{17,81},{24,88},{25,89},{128,1... | collective-permute-start | bytes 147464 | tf_op jit(solution)/shard_map/ppermute | solution.py:11
  28.1 1.3 %collective-permute-start.11 = (f32[96,128]{1,0:T(8,128)S(1)}, f32[96,128]{1,0:T(8,128)S(1)}, u32[]{:S(2)}, u32[]{:S(2)}) collective-permute-start(f32[96,128]{1,0:T(8,128)S(1)} %add_add_fusion.2), channel_id=1, source_target_pairs={{0,4},{1,5},{8,12},{9,13},{16,20},{17,21},{24,28},{25,29},{128,132... | collective-permute-start | bytes 147464 | tf_op jit(solution)/shard_map/ppermute | solution.py:11
  29.4 1.3 %collective-permute-start.12 = (f32[96,128]{1,0:T(8,128)S(1)}, f32[96,128]{1,0:T(8,128)S(1)}, u32[]{:S(2)}, u32[]{:S(2)}) collective-permute-start(f32[96,128]{1,0:T(8,128)S(1)} %add_add_fusion.2), channel_id=1, source_target_pairs={{0,68},{1,69},{8,76},{9,77},{16,84},{17,85},{24,92},{25,93},{128,1... | collective-permute-start | bytes 147464 | tf_op jit(solution)/shard_map/ppermute | solution.py:11
  30.8 1.3 %collective-permute-start.15 = (f32[256,128]{1,0:T(8,128)S(1)}, f32[256,128]{1,0:T(8,128)S(1)}, u32[]{:S(2)}, u32[]{:S(2)}) collective-permute-start(f32[256,128]{1,0:T(8,128)S(1)} %add.107), channel_id=1, source_target_pairs={{0,2},{1,3},{8,10},{9,11},{4,6},{5,7},{12,14},{13,15},{16,18},{17,... | collective-permute-start | bytes 393224 | tf_op jit(solution)/shard_map/ppermute | solution.py:82
  32.5 2.1 %collective-permute-done.15 = f32[256,128]{1,0:T(8,128)S(1)} collective-permute-done((f32[256,128]{1,0:T(8,128)S(1)}, f32[256,128]{1,0:T(8,128)S(1)}, u32[]{:S(2)}, u32[]{:S(2)}) %collective-permute-start.15) | collective-permute-done | bytes 131104 | tf_op jit(solution)/shard_map/ppermute | solution.py:82
  34.6 1.3 %collective-permute-start.16 = (f32[96,128]{1,0:T(8,128)S(1)}, f32[96,128]{1,0:T(8,128)S(1)}, u32[]{:S(2)}, u32[]{:S(2)}) collective-permute-start(f32[96,128]{1,0:T(8,128)S(1)} %add_add_fusion.1), channel_id=1, source_target_pairs={{0,32},{1,33},{4,36},{5,37},{8,40},{9,41},{12,44},{13,45},{16,48},... | collective-permute-start | bytes 147464 | tf_op jit(solution)/shard_map/ppermute | solution.py:11
  35.9 3.7 %collective-permute-start.17 = (f32[96,128]{1,0:T(8,128)S(1)}, f32[96,128]{1,0:T(8,128)S(1)}, u32[]{:S(2)}, u32[]{:S(2)}) collective-permute-start(f32[96,128]{1,0:T(8,128)S(1)} %add_add_fusion.1), channel_id=1, source_target_pairs={{0,2},{1,3},{4,6},{5,7},{8,10},{9,11},{12,14},{13,15},{16,18},{17,... | collective-permute-start | bytes 147464 | tf_op jit(solution)/shard_map/ppermute | solution.py:11
  39.6 1.3 %collective-permute-start.18 = (f32[96,128]{1,0:T(8,128)S(1)}, f32[96,128]{1,0:T(8,128)S(1)}, u32[]{:S(2)}, u32[]{:S(2)}) collective-permute-start(f32[96,128]{1,0:T(8,128)S(1)} %add_add_fusion.1), channel_id=1, source_target_pairs={{0,34},{1,35},{4,38},{5,39},{8,42},{9,43},{12,46},{13,47},{16,50},... | collective-permute-start | bytes 147464 | tf_op jit(solution)/shard_map/ppermute | solution.py:11
  40.9 2.2 %collective-permute-start.19 = (f32[256,128]{1,0:T(8,128)S(1)}, f32[256,128]{1,0:T(8,128)S(1)}, u32[]{:S(2)}, u32[]{:S(2)}) collective-permute-start(f32[256,128]{1,0:T(8,128)S(1)} %add.108), channel_id=1, source_target_pairs={{0,0},{16,1},{32,2},{48,3},{64,4},{80,5},{96,6},{112,7},{128,8},{1... | collective-permute-start | bytes 393224 | tf_op jit(solution)/shard_map/ppermute | solution.py:11
  43.1 15.7 %collective-permute-start.20 = (f32[256,128]{1,0:T(8,128)S(1)}, f32[256,128]{1,0:T(8,128)S(1)}, u32[]{:S(2)}, u32[]{:S(2)}) collective-permute-start(f32[256,128]{1,0:T(8,128)S(1)} %add.108), channel_id=1, source_target_pairs={{0,256},{16,257},{32,258},{48,259},{64,260},{80,261},{96,262},{112... | collective-permute-start | bytes 393224 | tf_op jit(solution)/shard_map/ppermute | solution.py:11
  59.6 11.7 %cholesky.20 = f32[128,128]{1,0:T(8,128)S(1)} custom-call(f32[128,128]{1,0:T(8,128)S(1)} %fusion.3), custom_call_target="Cholesky" | custom-call | tf_op jit(solution)/shard_map/jit(cholesky)/cholesky | solution.py:104
  71.4 0.6 compare_reduce_fusion
  72.0 0.7 select_bitcast_fusion
  72.7 9.8 %custom-call.7 = f32[1,128,128]{1,2,0:T(8,128)S(1)} custom-call(f32[1,128,128]{2,1,0:T(8,128)S(1)} %get-tuple-element.13), custom_call_target="InvertDiagBlocksLowerTriangular" | custom-call | tf_op jit(solution)/shard_map/jit(_solve_triangular)/triangular_solve | solution.py:51
  84.1 0.6 fusion
  85.0 1.0 %pad_maximum_fusion = f32[256,512]{1,0:T(8,128)} fusion(f32[256,448]{1,0:T(8,128)S(1)} %slice.94, f32[256,64]{1,0:T(8,128)S(1)} %slice_select_fusion), kind=kLoop, calls=%fused_computation.2 | loop fusion | flops 131072 | bytes 1048576 | tf_op jit(solution)/shard_map/concatenate | solution.py:130
  (61 shorter events, 3.3 us)
Async XLA Ops:
  0.9 14.9 %copy-start = (f32[256,512]{1,0:T(8,128)S(1)}, f32[256,512]{1,0:T(8,128)}, u32[]{:S(2)}) copy-start(f32[256,512]{1,0:T(8,128)} %param.1) | copy-start | bytes 1572868
  0.9 4.2 %collective-permute-start = (f32[256,64]{1,0:T(8,128)S(1)}, f32[256,64]{1,0:T(8,128)S(1)}, u32[]{:S(2)}, u32[]{:S(2)}) collective-permute-start(f32[256,64]{1,0:T(8,128)S(1)} %slice.70), channel_id=1, source_target_pairs={{0,1},{1,0},{16,17},{17,16},{32,33},{33,32},{48,49},{49,48},{64,65... | collective-permute-start | bytes 196616 | tf_op jit(solution)/shard_map/ppermute | solution.py:67
  3.8 12.1 %collective-permute-start.1 = (f32[64,64]{1,0:T(8,128)S(1)}, f32[64,64]{1,0:T(8,128)S(1)}, u32[]{:S(2)}, u32[]{:S(2)}) collective-permute-start(f32[64,64]{1,0:T(8,128)S(1)} %slice.69), channel_id=1, source_target_pairs={{17,0},{0,16}} | collective-permute-start | bytes 49160 | tf_op jit(solution)/shard_map/ppermute | solution.py:11
  4.4 11.4 %collective-permute-start.2 = (f32[64,64]{1,0:T(8,128)S(1)}, f32[64,64]{1,0:T(8,128)S(1)}, u32[]{:S(2)}, u32[]{:S(2)}) collective-permute-start(f32[64,64]{1,0:T(8,128)S(1)} %slice.69), channel_id=1, source_target_pairs={{17,1},{0,17}} | collective-permute-start | bytes 49160 | tf_op jit(solution)/shard_map/ppermute | solution.py:11
  6.1 18.6 %collective-permute-start.13 = (f32[256,128]{1,0:T(8,128)S(1)}, f32[256,128]{1,0:T(8,128)S(1)}, u32[]{:S(2)}, u32[]{:S(2)}) collective-permute-start(f32[256,128]{1,0:T(8,128)S(1)} %maximum_select_fusion), channel_id=1, source_target_pairs={{0,8},{1,9},{16,24},{17,25},{32,40},{33,41},{48,56},{49,57},{64,72... | collective-permute-start | bytes 393224 | tf_op jit(solution)/shard_map/ppermute | solution.py:82
  16.1 3.3 %collective-permute-start.3 = (f32[96,128]{1,0:T(8,128)S(1)}, f32[96,128]{1,0:T(8,128)S(1)}, u32[]{:S(2)}, u32[]{:S(2)}) collective-permute-start(f32[96,128]{1,0:T(8,128)S(1)} %select_n.138), channel_id=1, source_target_pairs={{0,8},{1,9},{16,24},{17,25}} | collective-permute-start | bytes 147464 | tf_op jit(solution)/shard_map/ppermute | solution.py:11
  16.7 7.3 %collective-permute-start.4 = (f32[96,128]{1,0:T(8,128)S(1)}, f32[96,128]{1,0:T(8,128)S(1)}, u32[]{:S(2)}, u32[]{:S(2)}) collective-permute-start(f32[96,128]{1,0:T(8,128)S(1)} %select_n.138), channel_id=1, source_target_pairs={{0,128},{1,129},{16,144},{17,145}} | collective-permute-start | bytes 147464 | tf_op jit(solution)/shard_map/ppermute | solution.py:11
  18.0 7.4 %collective-permute-start.5 = (f32[96,128]{1,0:T(8,128)S(1)}, f32[96,128]{1,0:T(8,128)S(1)}, u32[]{:S(2)}, u32[]{:S(2)}) collective-permute-start(f32[96,128]{1,0:T(8,128)S(1)} %select_n.138), channel_id=1, source_target_pairs={{0,136},{1,137},{16,152},{17,153}} | collective-permute-start | bytes 147464 | tf_op jit(solution)/shard_map/ppermute | solution.py:11
  18.7 8.0 %collective-permute-start.6 = (f32[96,128]{1,0:T(8,128)S(1)}, f32[96,128]{1,0:T(8,128)S(1)}, u32[]{:S(2)}, u32[]{:S(2)}) collective-permute-start(f32[96,128]{1,0:T(8,128)S(1)} %select_n.138), channel_id=1, source_target_pairs={{0,256},{1,257},{16,272},{17,273}} | collective-permute-start | bytes 147464 | tf_op jit(solution)/shard_map/ppermute | solution.py:11
  19.4 7.3 %collective-permute-start.7 = (f32[96,128]{1,0:T(8,128)S(1)}, f32[96,128]{1,0:T(8,128)S(1)}, u32[]{:S(2)}, u32[]{:S(2)}) collective-permute-start(f32[96,128]{1,0:T(8,128)S(1)} %select_n.138), channel_id=1, source_target_pairs={{0,264},{1,265},{16,280},{17,281}} | collective-permute-start | bytes 147464 | tf_op jit(solution)/shard_map/ppermute | solution.py:11
  24.0 2.7 %collective-permute-start.8 = (f32[96,128]{1,0:T(8,128)S(1)}, f32[96,128]{1,0:T(8,128)S(1)}, u32[]{:S(2)}, u32[]{:S(2)}) collective-permute-start(f32[96,128]{1,0:T(8,128)S(1)} %select_n.138), channel_id=1, source_target_pairs={{0,384},{1,385},{16,400},{17,401}} | collective-permute-start | bytes 147464 | tf_op jit(solution)/shard_map/ppermute | solution.py:11
  24.7 2.1 %collective-permute-start.9 = (f32[96,128]{1,0:T(8,128)S(1)}, f32[96,128]{1,0:T(8,128)S(1)}, u32[]{:S(2)}, u32[]{:S(2)}) collective-permute-start(f32[96,128]{1,0:T(8,128)S(1)} %select_n.138), channel_id=1, source_target_pairs={{0,392},{1,393},{16,408},{17,409}} | collective-permute-start | bytes 147464 | tf_op jit(solution)/shard_map/ppermute | solution.py:11
  25.4 5.3 %collective-permute-start.14 = (f32[256,128]{1,0:T(8,128)S(1)}, f32[256,128]{1,0:T(8,128)S(1)}, u32[]{:S(2)}, u32[]{:S(2)}) collective-permute-start(f32[256,128]{1,0:T(8,128)S(1)} %add.106), channel_id=1, source_target_pairs={{0,4},{1,5},{8,12},{9,13},{16,20},{17,21},{24,28},{25,29},{32,36},... | collective-permute-start | bytes 393224 | tf_op jit(solution)/shard_map/ppermute | solution.py:82
  26.8 5.3 %collective-permute-start.10 = (f32[96,128]{1,0:T(8,128)S(1)}, f32[96,128]{1,0:T(8,128)S(1)}, u32[]{:S(2)}, u32[]{:S(2)}) collective-permute-start(f32[96,128]{1,0:T(8,128)S(1)} %add_add_fusion.2), channel_id=1, source_target_pairs={{0,64},{1,65},{8,72},{9,73},{16,80},{17,81},{24,88},{25,89},{128,1... | collective-permute-start | bytes 147464 | tf_op jit(solution)/shard_map/ppermute | solution.py:11
  28.1 4.0 %collective-permute-start.11 = (f32[96,128]{1,0:T(8,128)S(1)}, f32[96,128]{1,0:T(8,128)S(1)}, u32[]{:S(2)}, u32[]{:S(2)}) collective-permute-start(f32[96,128]{1,0:T(8,128)S(1)} %add_add_fusion.2), channel_id=1, source_target_pairs={{0,4},{1,5},{8,12},{9,13},{16,20},{17,21},{24,28},{25,29},{128,132... | collective-permute-start | bytes 147464 | tf_op jit(solution)/shard_map/ppermute | solution.py:11
  29.4 3.0 %collective-permute-start.12 = (f32[96,128]{1,0:T(8,128)S(1)}, f32[96,128]{1,0:T(8,128)S(1)}, u32[]{:S(2)}, u32[]{:S(2)}) collective-permute-start(f32[96,128]{1,0:T(8,128)S(1)} %add_add_fusion.2), channel_id=1, source_target_pairs={{0,68},{1,69},{8,76},{9,77},{16,84},{17,85},{24,92},{25,93},{128,1... | collective-permute-start | bytes 147464 | tf_op jit(solution)/shard_map/ppermute | solution.py:11
  30.8 3.8 %collective-permute-start.15 = (f32[256,128]{1,0:T(8,128)S(1)}, f32[256,128]{1,0:T(8,128)S(1)}, u32[]{:S(2)}, u32[]{:S(2)}) collective-permute-start(f32[256,128]{1,0:T(8,128)S(1)} %add.107), channel_id=1, source_target_pairs={{0,2},{1,3},{8,10},{9,11},{4,6},{5,7},{12,14},{13,15},{16,18},{17,... | collective-permute-start | bytes 393224 | tf_op jit(solution)/shard_map/ppermute | solution.py:82
  34.6 24.2 %collective-permute-start.16 = (f32[96,128]{1,0:T(8,128)S(1)}, f32[96,128]{1,0:T(8,128)S(1)}, u32[]{:S(2)}, u32[]{:S(2)}) collective-permute-start(f32[96,128]{1,0:T(8,128)S(1)} %add_add_fusion.1), channel_id=1, source_target_pairs={{0,32},{1,33},{4,36},{5,37},{8,40},{9,41},{12,44},{13,45},{16,48},... | collective-permute-start | bytes 147464 | tf_op jit(solution)/shard_map/ppermute | solution.py:11
  35.9 23.0 %collective-permute-start.17 = (f32[96,128]{1,0:T(8,128)S(1)}, f32[96,128]{1,0:T(8,128)S(1)}, u32[]{:S(2)}, u32[]{:S(2)}) collective-permute-start(f32[96,128]{1,0:T(8,128)S(1)} %add_add_fusion.1), channel_id=1, source_target_pairs={{0,2},{1,3},{4,6},{5,7},{8,10},{9,11},{12,14},{13,15},{16,18},{17,... | collective-permute-start | bytes 147464 | tf_op jit(solution)/shard_map/ppermute | solution.py:11
  39.6 19.2 %collective-permute-start.18 = (f32[96,128]{1,0:T(8,128)S(1)}, f32[96,128]{1,0:T(8,128)S(1)}, u32[]{:S(2)}, u32[]{:S(2)}) collective-permute-start(f32[96,128]{1,0:T(8,128)S(1)} %add_add_fusion.1), channel_id=1, source_target_pairs={{0,34},{1,35},{4,38},{5,39},{8,42},{9,43},{12,46},{13,47},{16,50},... | collective-permute-start | bytes 147464 | tf_op jit(solution)/shard_map/ppermute | solution.py:11
  40.9 43.1 %collective-permute-start.19 = (f32[256,128]{1,0:T(8,128)S(1)}, f32[256,128]{1,0:T(8,128)S(1)}, u32[]{:S(2)}, u32[]{:S(2)}) collective-permute-start(f32[256,128]{1,0:T(8,128)S(1)} %add.108), channel_id=1, source_target_pairs={{0,0},{16,1},{32,2},{48,3},{64,4},{80,5},{96,6},{112,7},{128,8},{1... | collective-permute-start | bytes 393224 | tf_op jit(solution)/shard_map/ppermute | solution.py:11
  43.1 40.9 %collective-permute-start.20 = (f32[256,128]{1,0:T(8,128)S(1)}, f32[256,128]{1,0:T(8,128)S(1)}, u32[]{:S(2)}, u32[]{:S(2)}) collective-permute-start(f32[256,128]{1,0:T(8,128)S(1)} %add.108), channel_id=1, source_target_pairs={{0,256},{16,257},{32,258},{48,259},{64,260},{80,261},{96,262},{112... | collective-permute-start | bytes 393224 | tf_op jit(solution)/shard_map/ppermute | solution.py:11

commit v10 on v9

--- a/solution.py
+++ b/solution.py
@@ -78,12 +78,20 @@
         [(4, 0), (0, 4), (4, 4)],
         [(2, 0), (0, 2), (2, 2)],
     ]
-    for step, offsets in zip((8, 4, 2), corner_offsets):
-        panel = panel + lax.ppermute(panel, "col", [(c, c + step) for c in holders_col])
-        holders_col = holders_col + [c + step for c in holders_col]
-        if step == 2:
-            corner, panel = lax.optimization_barrier((corner, panel))
+    panel_rounds = [
+        [[(0, 8), (1, 9)], [(0, 4), (1, 5)]],
+        [[(0, 2), (1, 3), (4, 6), (5, 7), (8, 10), (9, 11)], [(8, 12), (9, 13), (4, 14), (5, 15)]],
+    ]
+    for pairs_list, offsets in zip(panel_rounds, corner_offsets[:2]):
+        sent = panel
+        for pairs in pairs_list:
+            panel = panel + lax.ppermute(sent, "col", pairs)
+            holders_col = holders_col + [dst for _, dst in pairs]
         corner, holders_k = spread_round(corner, holders_k, offsets, ncols)
+    assert sorted(holders_col) == list(range(ncols))
+    corner, panel = lax.optimization_barrier((corner, panel))
+    corner, holders_k = spread_round(corner, holders_k, corner_offsets[2], ncols)
+    assert len(holders_k) == nrows * ncols
     corner, panel_held = lax.optimization_barrier((corner, panel))
 
     lin = lambda r, c: r * ncols + c

time: 86.6 us -> 85.1 us (0.983)
  the two profiles are of different devices: /device:TPU:18 before, /device:TPU:48 now
where the time goes in v10:
time: 85.1 us; the launch traced here: 84.5 us
  starting transfers between devices  46.4 us (55%)
  other arithmetic  25.3 us (30%)
  waiting for transfers between devices  7.56 us (9%)
  local copies, waits for them, and re-layouts  3.1 us (4%)
  matrix products  1.56 us (2%)
    ppermute x17, starting transfers between devices, both_axes(): return lax.ppermute(x, ('row', 'col'), pairs)  32.8 us
    another operation x3, other arithmetic, per_device(): factor = jnp.linalg.cholesky(lead_block)  12.4 us
    ppermute x4, starting transfers between devices, per_device(): panel = panel + lax.ppermute(sent, 'col', pairs)  11.7 us
    another operation x2, other arithmetic, lower_inverse(): return jax.scipy.linalg.solve_triangular(factor, eye, lower=True)  10.5 us
    ppermute x17, waiting for transfers between devices, both_axes(): return lax.ppermute(x, ('row', 'col'), pairs)  4.54 us
    ppermute x1, starting transfers between devices, per_device(): swapped = lax.ppermute(mine, 'col', [(0, 1), (1, 0)])  1.92 us
    ppermute x4, waiting for transfers between devices, per_device(): panel = panel + lax.ppermute(sent, 'col', pairs)  1.77 us
  transfers between devices with their start and end apart: 22, of which 3 were waited for; matrix products, arithmetic and copies ran while one was open for 31% of the time, Pallas kernels for 0%

profile of v10, /device:TPU:48, one launch (start us, length us, event | category | flops | bytes accessed | tf_op | source)
XLA Modules:
  0.0 84.5 jit_solution(10877475211761987444)
XLA Ops:
  0.0 0.8 slice.69
  0.8 0.7 collective-permute-start.1
  1.5 0.7 collective-permute-start.2
  2.2 0.9 %slice.70 = f32[256,64]{1,0:T(8,128)S(1)} slice(f32[256,512]{1,0:T(8,128)} %param.1), slice={[0:256], [0:64]} | slice | bytes 131072 | tf_op jit(solution)/shard_map/slice | solution.py:66
  3.1 1.9 %collective-permute-start = (f32[256,64]{1,0:T(8,128)S(1)}, f32[256,64]{1,0:T(8,128)S(1)}, u32[]{:S(2)}, u32[]{:S(2)}) collective-permute-start(f32[256,64]{1,0:T(8,128)S(1)} %slice.70), channel_id=1, source_target_pairs={{0,1},{1,0},{16,17},{17,16},{32,33},{33,32},{48,49},{49,48},{64,65... | collective-permute-start | bytes 196616 | tf_op jit(solution)/shard_map/ppermute | solution.py:67
  5.1 1.2 %collective-permute-done = f32[256,64]{1,0:T(8,128)S(1)} collective-permute-done((f32[256,64]{1,0:T(8,128)S(1)}, f32[256,64]{1,0:T(8,128)S(1)}, u32[]{:S(2)}, u32[]{:S(2)}) %collective-permute-start) | collective-permute-done | bytes 65568 | tf_op jit(solution)/shard_map/ppermute | solution.py:67
  6.3 0.8 broadcast_select_fusion.7
  7.3 0.7 collective-permute-start.3
  8.0 0.7 collective-permute-start.4
  8.6 0.7 collective-permute-start.5
  9.3 0.7 collective-permute-start.6
  10.0 0.7 collective-permute-start.7
  10.7 1.3 %collective-permute-start.8 = (f32[96,128]{1,0:T(8,128)S(1)}, f32[96,128]{1,0:T(8,128)S(1)}, u32[]{:S(2)}, u32[]{:S(2)}) collective-permute-start(f32[96,128]{1,0:T(8,128)S(1)} %select_n.138), channel_id=1, source_target_pairs={{0,384},{1,385},{16,400},{17,401}} | collective-permute-start | bytes 147464 | tf_op jit(solution)/shard_map/ppermute | solution.py:11
  12.0 0.7 collective-permute-start.9
  12.8 8.4 %collective-permute-start.13 = (f32[256,128]{1,0:T(8,128)S(1)}, f32[256,128]{1,0:T(8,128)S(1)}, u32[]{:S(2)}, u32[]{:S(2)}) collective-permute-start(f32[256,128]{1,0:T(8,128)S(1)} %maximum_select_fusion), channel_id=1, source_target_pairs={{0,8},{1,9},{16,24},{17,25},{32,40},{33,41},{48,56},{49,57},{64,72... | collective-permute-start | bytes 393224 | tf_op jit(solution)/shard_map/ppermute | solution.py:88
  21.3 1.3 %collective-permute-start.14 = (f32[256,128]{1,0:T(8,128)S(1)}, f32[256,128]{1,0:T(8,128)S(1)}, u32[]{:S(2)}, u32[]{:S(2)}) collective-permute-start(f32[256,128]{1,0:T(8,128)S(1)} %maximum_select_fusion), channel_id=1, source_target_pairs={{0,4},{1,5},{16,20},{17,21},{32,36},{33,37},{48,52},{49,53},{64,68... | collective-permute-start | bytes 393224 | tf_op jit(solution)/shard_map/ppermute | solution.py:88
  22.6 4.5 %collective-permute-done.8 = f32[96,128]{1,0:T(8,128)S(1)} collective-permute-done((f32[96,128]{1,0:T(8,128)S(1)}, f32[96,128]{1,0:T(8,128)S(1)}, u32[]{:S(2)}, u32[]{:S(2)}) %collective-permute-start.8) | collective-permute-done | bytes 49184 | tf_op jit(solution)/shard_map/ppermute | solution.py:11
  27.1 1.3 %collective-permute-start.10 = (f32[96,128]{1,0:T(8,128)S(1)}, f32[96,128]{1,0:T(8,128)S(1)}, u32[]{:S(2)}, u32[]{:S(2)}) collective-permute-start(f32[96,128]{1,0:T(8,128)S(1)} %add_add_fusion.4), channel_id=1, source_target_pairs={{0,64},{1,65},{8,72},{9,73},{16,80},{17,81},{24,88},{25,89},{128,1... | collective-permute-start | bytes 147464 | tf_op jit(solution)/shard_map/ppermute | solution.py:11
  28.4 1.3 %collective-permute-start.11 = (f32[96,128]{1,0:T(8,128)S(1)}, f32[96,128]{1,0:T(8,128)S(1)}, u32[]{:S(2)}, u32[]{:S(2)}) collective-permute-start(f32[96,128]{1,0:T(8,128)S(1)} %add_add_fusion.4), channel_id=1, source_target_pairs={{0,4},{1,5},{8,12},{9,13},{16,20},{17,21},{24,28},{25,29},{128,132... | collective-permute-start | bytes 147464 | tf_op jit(solution)/shard_map/ppermute | solution.py:11
  29.7 1.3 %collective-permute-start.12 = (f32[96,128]{1,0:T(8,128)S(1)}, f32[96,128]{1,0:T(8,128)S(1)}, u32[]{:S(2)}, u32[]{:S(2)}) collective-permute-start(f32[96,128]{1,0:T(8,128)S(1)} %add_add_fusion.4), channel_id=1, source_target_pairs={{0,68},{1,69},{8,76},{9,77},{16,84},{17,85},{24,92},{25,93},{128,1... | collective-permute-start | bytes 147464 | tf_op jit(solution)/shard_map/ppermute | solution.py:11
  31.1 1.3 %collective-permute-start.15 = (f32[256,128]{1,0:T(8,128)S(1)}, f32[256,128]{1,0:T(8,128)S(1)}, u32[]{:S(2)}, u32[]{:S(2)}) collective-permute-start(f32[256,128]{1,0:T(8,128)S(1)} %add_add_fusion.1), channel_id=1, source_target_pairs={{0,2},{1,3},{4,6},{5,7},{8,10},{9,11},{16,18},{17,19},{20,22},{21,... | collective-permute-start | bytes 393224 | tf_op jit(solution)/shard_map/ppermute | solution.py:88
  32.4 0.7 collective-permute-start.16
  33.1 1.8 %collective-permute-done.15 = f32[256,128]{1,0:T(8,128)S(1)} collective-permute-done((f32[256,128]{1,0:T(8,128)S(1)}, f32[256,128]{1,0:T(8,128)S(1)}, u32[]{:S(2)}, u32[]{:S(2)}) %collective-permute-start.15) | collective-permute-done | bytes 131104 | tf_op jit(solution)/shard_map/ppermute | solution.py:88
  34.9 1.3 %collective-permute-start.17 = (f32[96,128]{1,0:T(8,128)S(1)}, f32[96,128]{1,0:T(8,128)S(1)}, u32[]{:S(2)}, u32[]{:S(2)}) collective-permute-start(f32[96,128]{1,0:T(8,128)S(1)} %add_add_fusion.3), channel_id=1, source_target_pairs={{0,32},{1,33},{4,36},{5,37},{8,40},{9,41},{12,44},{13,45},{16,48},... | collective-permute-start | bytes 147464 | tf_op jit(solution)/shard_map/ppermute | solution.py:11
  36.2 3.7 %collective-permute-start.18 = (f32[96,128]{1,0:T(8,128)S(1)}, f32[96,128]{1,0:T(8,128)S(1)}, u32[]{:S(2)}, u32[]{:S(2)}) collective-permute-start(f32[96,128]{1,0:T(8,128)S(1)} %add_add_fusion.3), channel_id=1, source_target_pairs={{0,2},{1,3},{4,6},{5,7},{8,10},{9,11},{12,14},{13,15},{16,18},{17,... | collective-permute-start | bytes 147464 | tf_op jit(solution)/shard_map/ppermute | solution.py:11
  39.9 1.3 %collective-permute-start.19 = (f32[96,128]{1,0:T(8,128)S(1)}, f32[96,128]{1,0:T(8,128)S(1)}, u32[]{:S(2)}, u32[]{:S(2)}) collective-permute-start(f32[96,128]{1,0:T(8,128)S(1)} %add_add_fusion.3), channel_id=1, source_target_pairs={{0,34},{1,35},{4,38},{5,39},{8,42},{9,43},{12,46},{13,47},{16,50},... | collective-permute-start | bytes 147464 | tf_op jit(solution)/shard_map/ppermute | solution.py:11
  41.2 8.8 %collective-permute-start.20 = (f32[256,128]{1,0:T(8,128)S(1)}, f32[256,128]{1,0:T(8,128)S(1)}, u32[]{:S(2)}, u32[]{:S(2)}) collective-permute-start(f32[256,128]{1,0:T(8,128)S(1)} %add_add_fusion), channel_id=1, source_target_pairs={{0,0},{16,1},{32,2},{48,3},{64,4},{80,5},{96,6},{112,7},{128,8},{1... | collective-permute-start | bytes 393224 | tf_op jit(solution)/shard_map/ppermute | solution.py:11
  50.1 7.2 %collective-permute-start.21 = (f32[256,128]{1,0:T(8,128)S(1)}, f32[256,128]{1,0:T(8,128)S(1)}, u32[]{:S(2)}, u32[]{:S(2)}) collective-permute-start(f32[256,128]{1,0:T(8,128)S(1)} %add_add_fusion), channel_id=1, source_target_pairs={{0,256},{16,257},{32,258},{48,259},{64,260},{80,261},{96,262},{112... | collective-permute-start | bytes 393224 | tf_op jit(solution)/shard_map/ppermute | solution.py:11
  58.1 11.7 %cholesky.20 = f32[128,128]{1,0:T(8,128)S(1)} custom-call(f32[128,128]{1,0:T(8,128)S(1)} %fusion.3), custom_call_target="Cholesky" | custom-call | tf_op jit(solution)/shard_map/jit(cholesky)/cholesky | solution.py:112
  70.5 0.7 select_bitcast_fusion
  71.2 9.8 %custom-call.7 = f32[1,128,128]{1,2,0:T(8,128)S(1)} custom-call(f32[1,128,128]{2,1,0:T(8,128)S(1)} %get-tuple-element.13), custom_call_target="InvertDiagBlocksLowerTriangular" | custom-call | tf_op jit(solution)/shard_map/jit(_solve_triangular)/triangular_solve | solution.py:51
  83.5 1.0 %pad_maximum_fusion = f32[256,512]{1,0:T(8,128)} fusion(f32[256,448]{1,0:T(8,128)S(1)} %slice.94, f32[256,64]{1,0:T(8,128)S(1)} %slice_select_fusion), kind=kLoop, calls=%fused_computation.2 | loop fusion | flops 131072 | bytes 1048576 | tf_op jit(solution)/shard_map/concatenate | solution.py:138
  (62 shorter events, 4.3 us)
Async XLA Ops:
  0.0 7.2 %copy-start = (f32[256,512]{1,0:T(8,128)S(1)}, f32[256,512]{1,0:T(8,128)}, u32[]{:S(2)}) copy-start(f32[256,512]{1,0:T(8,128)} %param.1) | copy-start | bytes 1572868
  0.8 4.2 %collective-permute-start.1 = (f32[64,64]{1,0:T(8,128)S(1)}, f32[64,64]{1,0:T(8,128)S(1)}, u32[]{:S(2)}, u32[]{:S(2)}) collective-permute-start(f32[64,64]{1,0:T(8,128)S(1)} %slice.69), channel_id=1, source_target_pairs={{17,0},{0,16}} | collective-permute-start | bytes 49160 | tf_op jit(solution)/shard_map/ppermute | solution.py:11
  1.5 3.6 %collective-permute-start.2 = (f32[64,64]{1,0:T(8,128)S(1)}, f32[64,64]{1,0:T(8,128)S(1)}, u32[]{:S(2)}, u32[]{:S(2)}) collective-permute-start(f32[64,64]{1,0:T(8,128)S(1)} %slice.69), channel_id=1, source_target_pairs={{17,1},{0,17}} | collective-permute-start | bytes 49160 | tf_op jit(solution)/shard_map/ppermute | solution.py:11
  3.1 3.2 %collective-permute-start = (f32[256,64]{1,0:T(8,128)S(1)}, f32[256,64]{1,0:T(8,128)S(1)}, u32[]{:S(2)}, u32[]{:S(2)}) collective-permute-start(f32[256,64]{1,0:T(8,128)S(1)} %slice.70), channel_id=1, source_target_pairs={{0,1},{1,0},{16,17},{17,16},{32,33},{33,32},{48,49},{49,48},{64,65... | collective-permute-start | bytes 196616 | tf_op jit(solution)/shard_map/ppermute | solution.py:67
  7.3 3.4 %collective-permute-start.3 = (f32[96,128]{1,0:T(8,128)S(1)}, f32[96,128]{1,0:T(8,128)S(1)}, u32[]{:S(2)}, u32[]{:S(2)}) collective-permute-start(f32[96,128]{1,0:T(8,128)S(1)} %select_n.138), channel_id=1, source_target_pairs={{0,8},{1,9},{16,24},{17,25}} | collective-permute-start | bytes 147464 | tf_op jit(solution)/shard_map/ppermute | solution.py:11
  8.0 4.0 %collective-permute-start.4 = (f32[96,128]{1,0:T(8,128)S(1)}, f32[96,128]{1,0:T(8,128)S(1)}, u32[]{:S(2)}, u32[]{:S(2)}) collective-permute-start(f32[96,128]{1,0:T(8,128)S(1)} %select_n.138), channel_id=1, source_target_pairs={{0,128},{1,129},{16,144},{17,145}} | collective-permute-start | bytes 147464 | tf_op jit(solution)/shard_map/ppermute | solution.py:11
  8.6 4.2 %collective-permute-start.5 = (f32[96,128]{1,0:T(8,128)S(1)}, f32[96,128]{1,0:T(8,128)S(1)}, u32[]{:S(2)}, u32[]{:S(2)}) collective-permute-start(f32[96,128]{1,0:T(8,128)S(1)} %select_n.138), channel_id=1, source_target_pairs={{0,136},{1,137},{16,152},{17,153}} | collective-permute-start | bytes 147464 | tf_op jit(solution)/shard_map/ppermute | solution.py:11
  9.3 11.9 %collective-permute-start.6 = (f32[96,128]{1,0:T(8,128)S(1)}, f32[96,128]{1,0:T(8,128)S(1)}, u32[]{:S(2)}, u32[]{:S(2)}) collective-permute-start(f32[96,128]{1,0:T(8,128)S(1)} %select_n.138), channel_id=1, source_target_pairs={{0,256},{1,257},{16,272},{17,273}} | collective-permute-start | bytes 147464 | tf_op jit(solution)/shard_map/ppermute | solution.py:11
  10.0 12.6 %collective-permute-start.7 = (f32[96,128]{1,0:T(8,128)S(1)}, f32[96,128]{1,0:T(8,128)S(1)}, u32[]{:S(2)}, u32[]{:S(2)}) collective-permute-start(f32[96,128]{1,0:T(8,128)S(1)} %select_n.138), channel_id=1, source_target_pairs={{0,264},{1,265},{16,280},{17,281}} | collective-permute-start | bytes 147464 | tf_op jit(solution)/shard_map/ppermute | solution.py:11
  10.7 16.4 %collective-permute-start.8 = (f32[96,128]{1,0:T(8,128)S(1)}, f32[96,128]{1,0:T(8,128)S(1)}, u32[]{:S(2)}, u32[]{:S(2)}) collective-permute-start(f32[96,128]{1,0:T(8,128)S(1)} %select_n.138), channel_id=1, source_target_pairs={{0,384},{1,385},{16,400},{17,401}} | collective-permute-start | bytes 147464 | tf_op jit(solution)/shard_map/ppermute | solution.py:11
  12.0 15.1 %collective-permute-start.9 = (f32[96,128]{1,0:T(8,128)S(1)}, f32[96,128]{1,0:T(8,128)S(1)}, u32[]{:S(2)}, u32[]{:S(2)}) collective-permute-start(f32[96,128]{1,0:T(8,128)S(1)} %select_n.138), channel_id=1, source_target_pairs={{0,392},{1,393},{16,408},{17,409}} | collective-permute-start | bytes 147464 | tf_op jit(solution)/shard_map/ppermute | solution.py:11
  12.8 18.2 %collective-permute-start.13 = (f32[256,128]{1,0:T(8,128)S(1)}, f32[256,128]{1,0:T(8,128)S(1)}, u32[]{:S(2)}, u32[]{:S(2)}) collective-permute-start(f32[256,128]{1,0:T(8,128)S(1)} %maximum_select_fusion), channel_id=1, source_target_pairs={{0,8},{1,9},{16,24},{17,25},{32,40},{33,41},{48,56},{49,57},{64,72... | collective-permute-start | bytes 393224 | tf_op jit(solution)/shard_map/ppermute | solution.py:88
  21.3 9.8 %collective-permute-start.14 = (f32[256,128]{1,0:T(8,128)S(1)}, f32[256,128]{1,0:T(8,128)S(1)}, u32[]{:S(2)}, u32[]{:S(2)}) collective-permute-start(f32[256,128]{1,0:T(8,128)S(1)} %maximum_select_fusion), channel_id=1, source_target_pairs={{0,4},{1,5},{16,20},{17,21},{32,36},{33,37},{48,52},{49,53},{64,68... | collective-permute-start | bytes 393224 | tf_op jit(solution)/shard_map/ppermute | solution.py:88
  27.1 5.9 %collective-permute-start.10 = (f32[96,128]{1,0:T(8,128)S(1)}, f32[96,128]{1,0:T(8,128)S(1)}, u32[]{:S(2)}, u32[]{:S(2)}) collective-permute-start(f32[96,128]{1,0:T(8,128)S(1)} %add_add_fusion.4), channel_id=1, source_target_pairs={{0,64},{1,65},{8,72},{9,73},{16,80},{17,81},{24,88},{25,89},{128,1... | collective-permute-start | bytes 147464 | tf_op jit(solution)/shard_map/ppermute | solution.py:11
  28.4 4.6 %collective-permute-start.11 = (f32[96,128]{1,0:T(8,128)S(1)}, f32[96,128]{1,0:T(8,128)S(1)}, u32[]{:S(2)}, u32[]{:S(2)}) collective-permute-start(f32[96,128]{1,0:T(8,128)S(1)} %add_add_fusion.4), channel_id=1, source_target_pairs={{0,4},{1,5},{8,12},{9,13},{16,20},{17,21},{24,28},{25,29},{128,132... | collective-permute-start | bytes 147464 | tf_op jit(solution)/shard_map/ppermute | solution.py:11
  29.7 3.4 %collective-permute-start.12 = (f32[96,128]{1,0:T(8,128)S(1)}, f32[96,128]{1,0:T(8,128)S(1)}, u32[]{:S(2)}, u32[]{:S(2)}) collective-permute-start(f32[96,128]{1,0:T(8,128)S(1)} %add_add_fusion.4), channel_id=1, source_target_pairs={{0,68},{1,69},{8,76},{9,77},{16,84},{17,85},{24,92},{25,93},{128,1... | collective-permute-start | bytes 147464 | tf_op jit(solution)/shard_map/ppermute | solution.py:11
  31.1 3.8 %collective-permute-start.15 = (f32[256,128]{1,0:T(8,128)S(1)}, f32[256,128]{1,0:T(8,128)S(1)}, u32[]{:S(2)}, u32[]{:S(2)}) collective-permute-start(f32[256,128]{1,0:T(8,128)S(1)} %add_add_fusion.1), channel_id=1, source_target_pairs={{0,2},{1,3},{4,6},{5,7},{8,10},{9,11},{16,18},{17,19},{20,22},{21,... | collective-permute-start | bytes 393224 | tf_op jit(solution)/shard_map/ppermute | solution.py:88
  32.4 2.5 %collective-permute-start.16 = (f32[256,128]{1,0:T(8,128)S(1)}, f32[256,128]{1,0:T(8,128)S(1)}, u32[]{:S(2)}, u32[]{:S(2)}) collective-permute-start(f32[256,128]{1,0:T(8,128)S(1)} %add_add_fusion.1), channel_id=1, source_target_pairs={{8,12},{9,13},{4,14},{5,15},{24,28},{25,29},{20,30},{21,31},{40,44... | collective-permute-start | bytes 393224 | tf_op jit(solution)/shard_map/ppermute | solution.py:88
  34.9 22.4 %collective-permute-start.17 = (f32[96,128]{1,0:T(8,128)S(1)}, f32[96,128]{1,0:T(8,128)S(1)}, u32[]{:S(2)}, u32[]{:S(2)}) collective-permute-start(f32[96,128]{1,0:T(8,128)S(1)} %add_add_fusion.3), channel_id=1, source_target_pairs={{0,32},{1,33},{4,36},{5,37},{8,40},{9,41},{12,44},{13,45},{16,48},... | collective-permute-start | bytes 147464 | tf_op jit(solution)/shard_map/ppermute | solution.py:11
  36.2 21.1 %collective-permute-start.18 = (f32[96,128]{1,0:T(8,128)S(1)}, f32[96,128]{1,0:T(8,128)S(1)}, u32[]{:S(2)}, u32[]{:S(2)}) collective-permute-start(f32[96,128]{1,0:T(8,128)S(1)} %add_add_fusion.3), channel_id=1, source_target_pairs={{0,2},{1,3},{4,6},{5,7},{8,10},{9,11},{12,14},{13,15},{16,18},{17,... | collective-permute-start | bytes 147464 | tf_op jit(solution)/shard_map/ppermute | solution.py:11
  39.9 17.4 %collective-permute-start.19 = (f32[96,128]{1,0:T(8,128)S(1)}, f32[96,128]{1,0:T(8,128)S(1)}, u32[]{:S(2)}, u32[]{:S(2)}) collective-permute-start(f32[96,128]{1,0:T(8,128)S(1)} %add_add_fusion.3), channel_id=1, source_target_pairs={{0,34},{1,35},{4,38},{5,39},{8,42},{9,43},{12,46},{13,47},{16,50},... | collective-permute-start | bytes 147464 | tf_op jit(solution)/shard_map/ppermute | solution.py:11
  41.2 41.2 %collective-permute-start.20 = (f32[256,128]{1,0:T(8,128)S(1)}, f32[256,128]{1,0:T(8,128)S(1)}, u32[]{:S(2)}, u32[]{:S(2)}) collective-permute-start(f32[256,128]{1,0:T(8,128)S(1)} %add_add_fusion), channel_id=1, source_target_pairs={{0,0},{16,1},{32,2},{48,3},{64,4},{80,5},{96,6},{112,7},{128,8},{1... | collective-permute-start | bytes 393224 | tf_op jit(solution)/shard_map/ppermute | solution.py:11
  50.1 32.4 %collective-permute-start.21 = (f32[256,128]{1,0:T(8,128)S(1)}, f32[256,128]{1,0:T(8,128)S(1)}, u32[]{:S(2)}, u32[]{:S(2)}) collective-permute-start(f32[256,128]{1,0:T(8,128)S(1)} %add_add_fusion), channel_id=1, source_target_pairs={{0,256},{16,257},{32,258},{48,259},{64,260},{80,261},{96,262},{112... | collective-permute-start | bytes 393224 | tf_op jit(solution)/shard_map/ppermute | solution.py:11

commit v11 on v10

--- a/solution.py
+++ b/solution.py
@@ -79,8 +79,8 @@
         [(2, 0), (0, 2), (2, 2)],
     ]
     panel_rounds = [
-        [[(0, 8), (1, 9)], [(0, 4), (1, 5)]],
-        [[(0, 2), (1, 3), (4, 6), (5, 7), (8, 10), (9, 11)], [(8, 12), (9, 13), (4, 14), (5, 15)]],
+        [[(0, 8), (1, 9)], [(0, 12), (1, 13)]],
+        [[(0, 2), (1, 3), (8, 10), (9, 11), (12, 14), (13, 15)], [(8, 6), (9, 7), (0, 4), (1, 5)]],
     ]
     for pairs_list, offsets in zip(panel_rounds, corner_offsets[:2]):
         sent = panel

time: 85.1 us -> 86 us (1.011)
  waiting for transfers between devices: 7.56 us -> 9.3 us
    ppermute x4, waiting for transfers between devices: 1.77 us -> 3.51 us  [per_device(): panel = panel + lax.ppermute(sent, 'col', pairs)]
    ppermute x17, starting transfers between devices: 32.8 us -> 31.4 us  [both_axes(): return lax.ppermute(x, ('row', 'col'), pairs)]
  transfers between devices with their start and end apart: 22 -> 22, of which waited for: 3 -> 4; matrix products, arithmetic and copies ran while one was open for 31% -> 31% of each run, Pallas kernels for 0% -> 0%
where the time goes in v11:
time: 86 us; the launch traced here: 85.4 us
  starting transfers between devices  45.6 us (53%)
  other arithmetic  25.3 us (29%)
  waiting for transfers between devices  9.3 us (11%)
  local copies, waits for them, and re-layouts  3.1 us (4%)
  matrix products  1.55 us (2%)
    ppermute x17, starting transfers between devices, both_axes(): return lax.ppermute(x, ('row', 'col'), pairs)  31.4 us
    another operation x3, other arithmetic, per_device(): factor = jnp.linalg.cholesky(lead_block)  12.4 us
    ppermute x4, starting transfers between devices, per_device(): panel = panel + lax.ppermute(sent, 'col', pairs)  12.3 us
    another operation x2, other arithmetic, lower_inverse(): return jax.scipy.linalg.solve_triangular(factor, eye, lower=True)  10.5 us
    ppermute x17, waiting for transfers between devices, both_axes(): return lax.ppermute(x, ('row', 'col'), pairs)  4.54 us
    ppermute x4, waiting for transfers between devices, per_device(): panel = panel + lax.ppermute(sent, 'col', pairs)  3.51 us
    ppermute x1, starting transfers between devices, per_device(): swapped = lax.ppermute(mine, 'col', [(0, 1), (1, 0)])  1.92 us
  transfers between devices with their start and end apart: 22, of which 4 were waited for; matrix products, arithmetic and copies ran while one was open for 31% of the time, Pallas kernels for 0%

profile of v11, /device:TPU:48, one launch (start us, length us, event | category | flops | bytes accessed | tf_op | source)
XLA Modules:
  0.0 85.4 jit_solution(14765818086710323272)
XLA Ops:
  0.0 0.8 slice.69
  1.5 0.7 collective-permute-start.2
  2.2 0.9 %slice.70 = f32[256,64]{1,0:T(8,128)S(1)} slice(f32[256,512]{1,0:T(8,128)} %param.1), slice={[0:256], [0:64]} | slice | bytes 131072 | tf_op jit(solution)/shard_map/slice | solution.py:66
  3.1 1.9 %collective-permute-start = (f32[256,64]{1,0:T(8,128)S(1)}, f32[256,64]{1,0:T(8,128)S(1)}, u32[]{:S(2)}, u32[]{:S(2)}) collective-permute-start(f32[256,64]{1,0:T(8,128)S(1)} %slice.70), channel_id=1, source_target_pairs={{0,1},{1,0},{16,17},{17,16},{32,33},{33,32},{48,49},{49,48},{64,65... | collective-permute-start | bytes 196616 | tf_op jit(solution)/shard_map/ppermute | solution.py:67
  5.1 1.2 %collective-permute-done = f32[256,64]{1,0:T(8,128)S(1)} collective-permute-done((f32[256,64]{1,0:T(8,128)S(1)}, f32[256,64]{1,0:T(8,128)S(1)}, u32[]{:S(2)}, u32[]{:S(2)}) %collective-permute-start) | collective-permute-done | bytes 65568 | tf_op jit(solution)/shard_map/ppermute | solution.py:67
  6.3 0.8 broadcast_select_fusion.7
  7.3 0.7 collective-permute-start.3
  8.0 0.7 collective-permute-start.4
  8.6 0.7 collective-permute-start.5
  9.3 0.7 collective-permute-start.6
  10.0 0.7 collective-permute-start.7
  10.7 1.3 %collective-permute-start.8 = (f32[96,128]{1,0:T(8,128)S(1)}, f32[96,128]{1,0:T(8,128)S(1)}, u32[]{:S(2)}, u32[]{:S(2)}) collective-permute-start(f32[96,128]{1,0:T(8,128)S(1)} %select_n.138), channel_id=1, source_target_pairs={{0,384},{1,385},{16,400},{17,401}} | collective-permute-start | bytes 147464 | tf_op jit(solution)/shard_map/ppermute | solution.py:11
  12.0 0.7 collective-permute-start.9
  12.8 8.4 %collective-permute-start.13 = (f32[256,128]{1,0:T(8,128)S(1)}, f32[256,128]{1,0:T(8,128)S(1)}, u32[]{:S(2)}, u32[]{:S(2)}) collective-permute-start(f32[256,128]{1,0:T(8,128)S(1)} %maximum_select_fusion), channel_id=1, source_target_pairs={{0,8},{1,9},{16,24},{17,25},{32,40},{33,41},{48,56},{49,57},{64,72... | collective-permute-start | bytes 393224 | tf_op jit(solution)/shard_map/ppermute | solution.py:88
  21.3 1.3 %collective-permute-start.14 = (f32[256,128]{1,0:T(8,128)S(1)}, f32[256,128]{1,0:T(8,128)S(1)}, u32[]{:S(2)}, u32[]{:S(2)}) collective-permute-start(f32[256,128]{1,0:T(8,128)S(1)} %maximum_select_fusion), channel_id=1, source_target_pairs={{0,12},{1,13},{16,28},{17,29},{32,44},{33,45},{48,60},{49,61},{64,... | collective-permute-start | bytes 393224 | tf_op jit(solution)/shard_map/ppermute | solution.py:88
  22.6 4.5 %collective-permute-done.8 = f32[96,128]{1,0:T(8,128)S(1)} collective-permute-done((f32[96,128]{1,0:T(8,128)S(1)}, f32[96,128]{1,0:T(8,128)S(1)}, u32[]{:S(2)}, u32[]{:S(2)}) %collective-permute-start.8) | collective-permute-done | bytes 49184 | tf_op jit(solution)/shard_map/ppermute | solution.py:11
  27.1 1.3 %collective-permute-start.10 = (f32[96,128]{1,0:T(8,128)S(1)}, f32[96,128]{1,0:T(8,128)S(1)}, u32[]{:S(2)}, u32[]{:S(2)}) collective-permute-start(f32[96,128]{1,0:T(8,128)S(1)} %add_add_fusion.4), channel_id=1, source_target_pairs={{0,64},{1,65},{8,72},{9,73},{16,80},{17,81},{24,88},{25,89},{128,1... | collective-permute-start | bytes 147464 | tf_op jit(solution)/shard_map/ppermute | solution.py:11
  28.4 1.3 %collective-permute-start.11 = (f32[96,128]{1,0:T(8,128)S(1)}, f32[96,128]{1,0:T(8,128)S(1)}, u32[]{:S(2)}, u32[]{:S(2)}) collective-permute-start(f32[96,128]{1,0:T(8,128)S(1)} %add_add_fusion.4), channel_id=1, source_target_pairs={{0,4},{1,5},{8,12},{9,13},{16,20},{17,21},{24,28},{25,29},{128,132... | collective-permute-start | bytes 147464 | tf_op jit(solution)/shard_map/ppermute | solution.py:11
  29.7 1.3 %collective-permute-start.12 = (f32[96,128]{1,0:T(8,128)S(1)}, f32[96,128]{1,0:T(8,128)S(1)}, u32[]{:S(2)}, u32[]{:S(2)}) collective-permute-start(f32[96,128]{1,0:T(8,128)S(1)} %add_add_fusion.4), channel_id=1, source_target_pairs={{0,68},{1,69},{8,76},{9,77},{16,84},{17,85},{24,92},{25,93},{128,1... | collective-permute-start | bytes 147464 | tf_op jit(solution)/shard_map/ppermute | solution.py:11
  31.1 1.3 %collective-permute-start.15 = (f32[256,128]{1,0:T(8,128)S(1)}, f32[256,128]{1,0:T(8,128)S(1)}, u32[]{:S(2)}, u32[]{:S(2)}) collective-permute-start(f32[256,128]{1,0:T(8,128)S(1)} %add_add_fusion.1), channel_id=1, source_target_pairs={{0,2},{1,3},{8,10},{9,11},{12,14},{13,15},{16,18},{17,19},{24,26},... | collective-permute-start | bytes 393224 | tf_op jit(solution)/shard_map/ppermute | solution.py:88
  32.4 1.3 %collective-permute-start.16 = (f32[256,128]{1,0:T(8,128)S(1)}, f32[256,128]{1,0:T(8,128)S(1)}, u32[]{:S(2)}, u32[]{:S(2)}) collective-permute-start(f32[256,128]{1,0:T(8,128)S(1)} %add_add_fusion.1), channel_id=1, source_target_pairs={{8,6},{9,7},{0,4},{1,5},{24,22},{25,23},{16,20},{17,21},{40,38},{4... | collective-permute-start | bytes 393224 | tf_op jit(solution)/shard_map/ppermute | solution.py:88
  33.7 2.1 %collective-permute-done.15 = f32[256,128]{1,0:T(8,128)S(1)} collective-permute-done((f32[256,128]{1,0:T(8,128)S(1)}, f32[256,128]{1,0:T(8,128)S(1)}, u32[]{:S(2)}, u32[]{:S(2)}) %collective-permute-start.15) | collective-permute-done | bytes 131104 | tf_op jit(solution)/shard_map/ppermute | solution.py:88
  35.8 1.4 %collective-permute-done.16 = f32[256,128]{1,0:T(8,128)S(1)} collective-permute-done((f32[256,128]{1,0:T(8,128)S(1)}, f32[256,128]{1,0:T(8,128)S(1)}, u32[]{:S(2)}, u32[]{:S(2)}) %collective-permute-start.16) | collective-permute-done | bytes 131104 | tf_op jit(solution)/shard_map/ppermute | solution.py:88
  37.3 1.3 %collective-permute-start.17 = (f32[96,128]{1,0:T(8,128)S(1)}, f32[96,128]{1,0:T(8,128)S(1)}, u32[]{:S(2)}, u32[]{:S(2)}) collective-permute-start(f32[96,128]{1,0:T(8,128)S(1)} %add_add_fusion.3), channel_id=1, source_target_pairs={{0,32},{1,33},{4,36},{5,37},{8,40},{9,41},{12,44},{13,45},{16,48},... | collective-permute-start | bytes 147464 | tf_op jit(solution)/shard_map/ppermute | solution.py:11
  38.6 2.4 %collective-permute-start.18 = (f32[96,128]{1,0:T(8,128)S(1)}, f32[96,128]{1,0:T(8,128)S(1)}, u32[]{:S(2)}, u32[]{:S(2)}) collective-permute-start(f32[96,128]{1,0:T(8,128)S(1)} %add_add_fusion.3), channel_id=1, source_target_pairs={{0,2},{1,3},{4,6},{5,7},{8,10},{9,11},{12,14},{13,15},{16,18},{17,... | collective-permute-start | bytes 147464 | tf_op jit(solution)/shard_map/ppermute | solution.py:11
  40.9 1.3 %collective-permute-start.19 = (f32[96,128]{1,0:T(8,128)S(1)}, f32[96,128]{1,0:T(8,128)S(1)}, u32[]{:S(2)}, u32[]{:S(2)}) collective-permute-start(f32[96,128]{1,0:T(8,128)S(1)} %add_add_fusion.3), channel_id=1, source_target_pairs={{0,34},{1,35},{4,38},{5,39},{8,42},{9,43},{12,46},{13,47},{16,50},... | collective-permute-start | bytes 147464 | tf_op jit(solution)/shard_map/ppermute | solution.py:11
  42.2 6.6 %collective-permute-start.20 = (f32[256,128]{1,0:T(8,128)S(1)}, f32[256,128]{1,0:T(8,128)S(1)}, u32[]{:S(2)}, u32[]{:S(2)}) collective-permute-start(f32[256,128]{1,0:T(8,128)S(1)} %add_add_fusion), channel_id=1, source_target_pairs={{0,0},{16,1},{32,2},{48,3},{64,4},{80,5},{96,6},{112,7},{128,8},{1... | collective-permute-start | bytes 393224 | tf_op jit(solution)/shard_map/ppermute | solution.py:11
  48.9 9.3 %collective-permute-start.21 = (f32[256,128]{1,0:T(8,128)S(1)}, f32[256,128]{1,0:T(8,128)S(1)}, u32[]{:S(2)}, u32[]{:S(2)}) collective-permute-start(f32[256,128]{1,0:T(8,128)S(1)} %add_add_fusion), channel_id=1, source_target_pairs={{0,256},{16,257},{32,258},{48,259},{64,260},{80,261},{96,262},{112... | collective-permute-start | bytes 393224 | tf_op jit(solution)/shard_map/ppermute | solution.py:11
  59.0 11.7 %cholesky.20 = f32[128,128]{1,0:T(8,128)S(1)} custom-call(f32[128,128]{1,0:T(8,128)S(1)} %fusion.3), custom_call_target="Cholesky" | custom-call | tf_op jit(solution)/shard_map/jit(cholesky)/cholesky | solution.py:112
  71.4 0.7 select_bitcast_fusion
  72.1 9.8 %custom-call.7 = f32[1,128,128]{1,2,0:T(8,128)S(1)} custom-call(f32[1,128,128]{2,1,0:T(8,128)S(1)} %get-tuple-element.13), custom_call_target="InvertDiagBlocksLowerTriangular" | custom-call | tf_op jit(solution)/shard_map/jit(_solve_triangular)/triangular_solve | solution.py:51
  84.4 1.0 %pad_maximum_fusion = f32[256,512]{1,0:T(8,128)} fusion(f32[256,448]{1,0:T(8,128)S(1)} %slice.94, f32[256,64]{1,0:T(8,128)S(1)} %slice_select_fusion), kind=kLoop, calls=%fused_computation.2 | loop fusion | flops 131072 | bytes 1048576 | tf_op jit(solution)/shard_map/concatenate | solution.py:138
  (62 shorter events, 4.9 us)
Async XLA Ops:
  0.0 7.2 %copy-start = (f32[256,512]{1,0:T(8,128)S(1)}, f32[256,512]{1,0:T(8,128)}, u32[]{:S(2)}) copy-start(f32[256,512]{1,0:T(8,128)} %param.1) | copy-start | bytes 1572868
  0.8 4.2 %collective-permute-start.1 = (f32[64,64]{1,0:T(8,128)S(1)}, f32[64,64]{1,0:T(8,128)S(1)}, u32[]{:S(2)}, u32[]{:S(2)}) collective-permute-start(f32[64,64]{1,0:T(8,128)S(1)} %slice.69), channel_id=1, source_target_pairs={{17,0},{0,16}} | collective-permute-start | bytes 49160 | tf_op jit(solution)/shard_map/ppermute | solution.py:11
  1.5 3.6 %collective-permute-start.2 = (f32[64,64]{1,0:T(8,128)S(1)}, f32[64,64]{1,0:T(8,128)S(1)}, u32[]{:S(2)}, u32[]{:S(2)}) collective-permute-start(f32[64,64]{1,0:T(8,128)S(1)} %slice.69), channel_id=1, source_target_pairs={{17,1},{0,17}} | collective-permute-start | bytes 49160 | tf_op jit(solution)/shard_map/ppermute | solution.py:11
  3.1 3.2 %collective-permute-start = (f32[256,64]{1,0:T(8,128)S(1)}, f32[256,64]{1,0:T(8,128)S(1)}, u32[]{:S(2)}, u32[]{:S(2)}) collective-permute-start(f32[256,64]{1,0:T(8,128)S(1)} %slice.70), channel_id=1, source_target_pairs={{0,1},{1,0},{16,17},{17,16},{32,33},{33,32},{48,49},{49,48},{64,65... | collective-permute-start | bytes 196616 | tf_op jit(solution)/shard_map/ppermute | solution.py:67
  7.3 3.4 %collective-permute-start.3 = (f32[96,128]{1,0:T(8,128)S(1)}, f32[96,128]{1,0:T(8,128)S(1)}, u32[]{:S(2)}, u32[]{:S(2)}) collective-permute-start(f32[96,128]{1,0:T(8,128)S(1)} %select_n.138), channel_id=1, source_target_pairs={{0,8},{1,9},{16,24},{17,25}} | collective-permute-start | bytes 147464 | tf_op jit(solution)/shard_map/ppermute | solution.py:11
  8.0 4.0 %collective-permute-start.4 = (f32[96,128]{1,0:T(8,128)S(1)}, f32[96,128]{1,0:T(8,128)S(1)}, u32[]{:S(2)}, u32[]{:S(2)}) collective-permute-start(f32[96,128]{1,0:T(8,128)S(1)} %select_n.138), channel_id=1, source_target_pairs={{0,128},{1,129},{16,144},{17,145}} | collective-permute-start | bytes 147464 | tf_op jit(solution)/shard_map/ppermute | solution.py:11
  8.6 4.2 %collective-permute-start.5 = (f32[96,128]{1,0:T(8,128)S(1)}, f32[96,128]{1,0:T(8,128)S(1)}, u32[]{:S(2)}, u32[]{:S(2)}) collective-permute-start(f32[96,128]{1,0:T(8,128)S(1)} %select_n.138), channel_id=1, source_target_pairs={{0,136},{1,137},{16,152},{17,153}} | collective-permute-start | bytes 147464 | tf_op jit(solution)/shard_map/ppermute | solution.py:11
  9.3 11.9 %collective-permute-start.6 = (f32[96,128]{1,0:T(8,128)S(1)}, f32[96,128]{1,0:T(8,128)S(1)}, u32[]{:S(2)}, u32[]{:S(2)}) collective-permute-start(f32[96,128]{1,0:T(8,128)S(1)} %select_n.138), channel_id=1, source_target_pairs={{0,256},{1,257},{16,272},{17,273}} | collective-permute-start | bytes 147464 | tf_op jit(solution)/shard_map/ppermute | solution.py:11
  10.0 12.6 %collective-permute-start.7 = (f32[96,128]{1,0:T(8,128)S(1)}, f32[96,128]{1,0:T(8,128)S(1)}, u32[]{:S(2)}, u32[]{:S(2)}) collective-permute-start(f32[96,128]{1,0:T(8,128)S(1)} %select_n.138), channel_id=1, source_target_pairs={{0,264},{1,265},{16,280},{17,281}} | collective-permute-start | bytes 147464 | tf_op jit(solution)/shard_map/ppermute | solution.py:11
  10.7 16.4 %collective-permute-start.8 = (f32[96,128]{1,0:T(8,128)S(1)}, f32[96,128]{1,0:T(8,128)S(1)}, u32[]{:S(2)}, u32[]{:S(2)}) collective-permute-start(f32[96,128]{1,0:T(8,128)S(1)} %select_n.138), channel_id=1, source_target_pairs={{0,384},{1,385},{16,400},{17,401}} | collective-permute-start | bytes 147464 | tf_op jit(solution)/shard_map/ppermute | solution.py:11
  12.0 15.1 %collective-permute-start.9 = (f32[96,128]{1,0:T(8,128)S(1)}, f32[96,128]{1,0:T(8,128)S(1)}, u32[]{:S(2)}, u32[]{:S(2)}) collective-permute-start(f32[96,128]{1,0:T(8,128)S(1)} %select_n.138), channel_id=1, source_target_pairs={{0,392},{1,393},{16,408},{17,409}} | collective-permute-start | bytes 147464 | tf_op jit(solution)/shard_map/ppermute | solution.py:11
  12.8 18.2 %collective-permute-start.13 = (f32[256,128]{1,0:T(8,128)S(1)}, f32[256,128]{1,0:T(8,128)S(1)}, u32[]{:S(2)}, u32[]{:S(2)}) collective-permute-start(f32[256,128]{1,0:T(8,128)S(1)} %maximum_select_fusion), channel_id=1, source_target_pairs={{0,8},{1,9},{16,24},{17,25},{32,40},{33,41},{48,56},{49,57},{64,72... | collective-permute-start | bytes 393224 | tf_op jit(solution)/shard_map/ppermute | solution.py:88
  21.3 9.8 %collective-permute-start.14 = (f32[256,128]{1,0:T(8,128)S(1)}, f32[256,128]{1,0:T(8,128)S(1)}, u32[]{:S(2)}, u32[]{:S(2)}) collective-permute-start(f32[256,128]{1,0:T(8,128)S(1)} %maximum_select_fusion), channel_id=1, source_target_pairs={{0,12},{1,13},{16,28},{17,29},{32,44},{33,45},{48,60},{49,61},{64,... | collective-permute-start | bytes 393224 | tf_op jit(solution)/shard_map/ppermute | solution.py:88
  27.1 6.6 %collective-permute-start.10 = (f32[96,128]{1,0:T(8,128)S(1)}, f32[96,128]{1,0:T(8,128)S(1)}, u32[]{:S(2)}, u32[]{:S(2)}) collective-permute-start(f32[96,128]{1,0:T(8,128)S(1)} %add_add_fusion.4), channel_id=1, source_target_pairs={{0,64},{1,65},{8,72},{9,73},{16,80},{17,81},{24,88},{25,89},{128,1... | collective-permute-start | bytes 147464 | tf_op jit(solution)/shard_map/ppermute | solution.py:11
  28.4 5.3 %collective-permute-start.11 = (f32[96,128]{1,0:T(8,128)S(1)}, f32[96,128]{1,0:T(8,128)S(1)}, u32[]{:S(2)}, u32[]{:S(2)}) collective-permute-start(f32[96,128]{1,0:T(8,128)S(1)} %add_add_fusion.4), channel_id=1, source_target_pairs={{0,4},{1,5},{8,12},{9,13},{16,20},{17,21},{24,28},{25,29},{128,132... | collective-permute-start | bytes 147464 | tf_op jit(solution)/shard_map/ppermute | solution.py:11
  29.7 4.0 %collective-permute-start.12 = (f32[96,128]{1,0:T(8,128)S(1)}, f32[96,128]{1,0:T(8,128)S(1)}, u32[]{:S(2)}, u32[]{:S(2)}) collective-permute-start(f32[96,128]{1,0:T(8,128)S(1)} %add_add_fusion.4), channel_id=1, source_target_pairs={{0,68},{1,69},{8,76},{9,77},{16,84},{17,85},{24,92},{25,93},{128,1... | collective-permute-start | bytes 147464 | tf_op jit(solution)/shard_map/ppermute | solution.py:11
  31.1 4.8 %collective-permute-start.15 = (f32[256,128]{1,0:T(8,128)S(1)}, f32[256,128]{1,0:T(8,128)S(1)}, u32[]{:S(2)}, u32[]{:S(2)}) collective-permute-start(f32[256,128]{1,0:T(8,128)S(1)} %add_add_fusion.1), channel_id=1, source_target_pairs={{0,2},{1,3},{8,10},{9,11},{12,14},{13,15},{16,18},{17,19},{24,26},... | collective-permute-start | bytes 393224 | tf_op jit(solution)/shard_map/ppermute | solution.py:88
  32.4 4.9 %collective-permute-start.16 = (f32[256,128]{1,0:T(8,128)S(1)}, f32[256,128]{1,0:T(8,128)S(1)}, u32[]{:S(2)}, u32[]{:S(2)}) collective-permute-start(f32[256,128]{1,0:T(8,128)S(1)} %add_add_fusion.1), channel_id=1, source_target_pairs={{8,6},{9,7},{0,4},{1,5},{24,22},{25,23},{16,20},{17,21},{40,38},{4... | collective-permute-start | bytes 393224 | tf_op jit(solution)/shard_map/ppermute | solution.py:88
  37.3 21.0 %collective-permute-start.17 = (f32[96,128]{1,0:T(8,128)S(1)}, f32[96,128]{1,0:T(8,128)S(1)}, u32[]{:S(2)}, u32[]{:S(2)}) collective-permute-start(f32[96,128]{1,0:T(8,128)S(1)} %add_add_fusion.3), channel_id=1, source_target_pairs={{0,32},{1,33},{4,36},{5,37},{8,40},{9,41},{12,44},{13,45},{16,48},... | collective-permute-start | bytes 147464 | tf_op jit(solution)/shard_map/ppermute | solution.py:11
  38.6 19.7 %collective-permute-start.18 = (f32[96,128]{1,0:T(8,128)S(1)}, f32[96,128]{1,0:T(8,128)S(1)}, u32[]{:S(2)}, u32[]{:S(2)}) collective-permute-start(f32[96,128]{1,0:T(8,128)S(1)} %add_add_fusion.3), channel_id=1, source_target_pairs={{0,2},{1,3},{4,6},{5,7},{8,10},{9,11},{12,14},{13,15},{16,18},{17,... | collective-permute-start | bytes 147464 | tf_op jit(solution)/shard_map/ppermute | solution.py:11
  40.9 17.3 %collective-permute-start.19 = (f32[96,128]{1,0:T(8,128)S(1)}, f32[96,128]{1,0:T(8,128)S(1)}, u32[]{:S(2)}, u32[]{:S(2)}) collective-permute-start(f32[96,128]{1,0:T(8,128)S(1)} %add_add_fusion.3), channel_id=1, source_target_pairs={{0,34},{1,35},{4,38},{5,39},{8,42},{9,43},{12,46},{13,47},{16,50},... | collective-permute-start | bytes 147464 | tf_op jit(solution)/shard_map/ppermute | solution.py:11
  42.2 41.2 %collective-permute-start.20 = (f32[256,128]{1,0:T(8,128)S(1)}, f32[256,128]{1,0:T(8,128)S(1)}, u32[]{:S(2)}, u32[]{:S(2)}) collective-permute-start(f32[256,128]{1,0:T(8,128)S(1)} %add_add_fusion), channel_id=1, source_target_pairs={{0,0},{16,1},{32,2},{48,3},{64,4},{80,5},{96,6},{112,7},{128,8},{1... | collective-permute-start | bytes 393224 | tf_op jit(solution)/shard_map/ppermute | solution.py:11
  48.9 34.5 %collective-permute-start.21 = (f32[256,128]{1,0:T(8,128)S(1)}, f32[256,128]{1,0:T(8,128)S(1)}, u32[]{:S(2)}, u32[]{:S(2)}) collective-permute-start(f32[256,128]{1,0:T(8,128)S(1)} %add_add_fusion), channel_id=1, source_target_pairs={{0,256},{16,257},{32,258},{48,259},{64,260},{80,261},{96,262},{112... | collective-permute-start | bytes 393224 | tf_op jit(solution)/shard_map/ppermute | solution.py:11

commit v12 on v10

--- a/solution.py
+++ b/solution.py
@@ -135,7 +135,7 @@
     lead1 = jnp.concatenate([lead1_top, y_rows[NB:]], axis=0)
     lead = jnp.where(q == 0, lead0, lead1)
     head = jnp.where(q < 2, lead, result[:, :NB])
-    return jnp.concatenate([head, result[:, NB:]], axis=1)
+    return lax.dynamic_update_slice(result, head, (0, 0))
 
 
 def solution(mesh):

time: 85.1 us -> 86.3 us (1.014)
  local copies, waits for them, and re-layouts: 3.1 us -> 5.31 us
  other arithmetic: 25.3 us -> 24.2 us
    dynamic_update_slice x0 -> x1, local copies, waits for them, and re-layouts: none -> 1.65 us  [per_device(): return lax.dynamic_update_slice(result, head, (0, 0))]
    concatenate x1 -> x0, other arithmetic: 1 us -> none  [per_device(): return jnp.concatenate([head, result[:, NB:]], axis=1)]
where the time goes in v12:
time: 86.3 us; the launch traced here: 85.7 us
  starting transfers between devices  46.4 us (54%)
  other arithmetic  24.2 us (28%)
  waiting for transfers between devices  7.56 us (9%)
  local copies, waits for them, and re-layouts  5.31 us (6%)
  matrix products  1.55 us (2%)
    ppermute x17, starting transfers between devices, both_axes(): return lax.ppermute(x, ('row', 'col'), pairs)  32.8 us
    another operation x3, other arithmetic, per_device(): factor = jnp.linalg.cholesky(lead_block)  12.4 us
    ppermute x4, starting transfers between devices, per_device(): panel = panel + lax.ppermute(sent, 'col', pairs)  11.7 us
    another operation x2, other arithmetic, lower_inverse(): return jax.scipy.linalg.solve_triangular(factor, eye, lower=True)  10.5 us
    ppermute x17, waiting for transfers between devices, both_axes(): return lax.ppermute(x, ('row', 'col'), pairs)  4.54 us
    ppermute x1, starting transfers between devices, per_device(): swapped = lax.ppermute(mine, 'col', [(0, 1), (1, 0)])  1.92 us
    ppermute x4, waiting for transfers between devices, per_device(): panel = panel + lax.ppermute(sent, 'col', pairs)  1.77 us
  transfers between devices with their start and end apart: 22, of which 3 were waited for; matrix products, arithmetic and copies ran while one was open for 31% of the time, Pallas kernels for 0%

profile of v12, /device:TPU:48, one launch (start us, length us, event | category | flops | bytes accessed | tf_op | source)
XLA Modules:
  0.0 85.7 jit_solution(2210773379343887595)
XLA Ops:
  0.0 0.8 slice.66
  1.5 0.7 collective-permute-start.2
  2.2 0.9 %slice.67 = f32[256,64]{1,0:T(8,128)S(1)} slice(f32[256,512]{1,0:T(8,128)} %param.1), slice={[0:256], [0:64]} | slice | bytes 131072 | tf_op jit(solution)/shard_map/slice | solution.py:66
  3.1 1.9 %collective-permute-start = (f32[256,64]{1,0:T(8,128)S(1)}, f32[256,64]{1,0:T(8,128)S(1)}, u32[]{:S(2)}, u32[]{:S(2)}) collective-permute-start(f32[256,64]{1,0:T(8,128)S(1)} %slice.67), channel_id=1, source_target_pairs={{0,1},{1,0},{16,17},{17,16},{32,33},{33,32},{48,49},{49,48},{64,65... | collective-permute-start | bytes 196616 | tf_op jit(solution)/shard_map/ppermute | solution.py:67
  5.1 1.2 %collective-permute-done = f32[256,64]{1,0:T(8,128)S(1)} collective-permute-done((f32[256,64]{1,0:T(8,128)S(1)}, f32[256,64]{1,0:T(8,128)S(1)}, u32[]{:S(2)}, u32[]{:S(2)}) %collective-permute-start) | collective-permute-done | bytes 65568 | tf_op jit(solution)/shard_map/ppermute | solution.py:67
  6.3 0.8 broadcast_select_fusion.7
  7.3 0.7 collective-permute-start.3
  8.0 0.7 collective-permute-start.4
  8.6 0.7 collective-permute-start.5
  9.3 0.7 collective-permute-start.6
  10.0 0.7 collective-permute-start.7
  10.7 1.3 %collective-permute-start.8 = (f32[96,128]{1,0:T(8,128)S(1)}, f32[96,128]{1,0:T(8,128)S(1)}, u32[]{:S(2)}, u32[]{:S(2)}) collective-permute-start(f32[96,128]{1,0:T(8,128)S(1)} %select_n.138), channel_id=1, source_target_pairs={{0,384},{1,385},{16,400},{17,401}} | collective-permute-start | bytes 147464 | tf_op jit(solution)/shard_map/ppermute | solution.py:11
  12.0 0.7 collective-permute-start.9
  12.8 8.4 %collective-permute-start.13 = (f32[256,128]{1,0:T(8,128)S(1)}, f32[256,128]{1,0:T(8,128)S(1)}, u32[]{:S(2)}, u32[]{:S(2)}) collective-permute-start(f32[256,128]{1,0:T(8,128)S(1)} %maximum_select_fusion), channel_id=1, source_target_pairs={{0,8},{1,9},{16,24},{17,25},{32,40},{33,41},{48,56},{49,57},{64,72... | collective-permute-start | bytes 393224 | tf_op jit(solution)/shard_map/ppermute | solution.py:88
  21.3 1.3 %collective-permute-start.14 = (f32[256,128]{1,0:T(8,128)S(1)}, f32[256,128]{1,0:T(8,128)S(1)}, u32[]{:S(2)}, u32[]{:S(2)}) collective-permute-start(f32[256,128]{1,0:T(8,128)S(1)} %maximum_select_fusion), channel_id=1, source_target_pairs={{0,4},{1,5},{16,20},{17,21},{32,36},{33,37},{48,52},{49,53},{64,68... | collective-permute-start | bytes 393224 | tf_op jit(solution)/shard_map/ppermute | solution.py:88
  22.6 4.5 %collective-permute-done.8 = f32[96,128]{1,0:T(8,128)S(1)} collective-permute-done((f32[96,128]{1,0:T(8,128)S(1)}, f32[96,128]{1,0:T(8,128)S(1)}, u32[]{:S(2)}, u32[]{:S(2)}) %collective-permute-start.8) | collective-permute-done | bytes 49184 | tf_op jit(solution)/shard_map/ppermute | solution.py:11
  27.1 1.3 %collective-permute-start.10 = (f32[96,128]{1,0:T(8,128)S(1)}, f32[96,128]{1,0:T(8,128)S(1)}, u32[]{:S(2)}, u32[]{:S(2)}) collective-permute-start(f32[96,128]{1,0:T(8,128)S(1)} %add_add_fusion.4), channel_id=1, source_target_pairs={{0,64},{1,65},{8,72},{9,73},{16,80},{17,81},{24,88},{25,89},{128,1... | collective-permute-start | bytes 147464 | tf_op jit(solution)/shard_map/ppermute | solution.py:11
  28.4 1.3 %collective-permute-start.11 = (f32[96,128]{1,0:T(8,128)S(1)}, f32[96,128]{1,0:T(8,128)S(1)}, u32[]{:S(2)}, u32[]{:S(2)}) collective-permute-start(f32[96,128]{1,0:T(8,128)S(1)} %add_add_fusion.4), channel_id=1, source_target_pairs={{0,4},{1,5},{8,12},{9,13},{16,20},{17,21},{24,28},{25,29},{128,132... | collective-permute-start | bytes 147464 | tf_op jit(solution)/shard_map/ppermute | solution.py:11
  29.7 1.3 %collective-permute-start.12 = (f32[96,128]{1,0:T(8,128)S(1)}, f32[96,128]{1,0:T(8,128)S(1)}, u32[]{:S(2)}, u32[]{:S(2)}) collective-permute-start(f32[96,128]{1,0:T(8,128)S(1)} %add_add_fusion.4), channel_id=1, source_target_pairs={{0,68},{1,69},{8,76},{9,77},{16,84},{17,85},{24,92},{25,93},{128,1... | collective-permute-start | bytes 147464 | tf_op jit(solution)/shard_map/ppermute | solution.py:11
  31.1 1.3 %collective-permute-start.15 = (f32[256,128]{1,0:T(8,128)S(1)}, f32[256,128]{1,0:T(8,128)S(1)}, u32[]{:S(2)}, u32[]{:S(2)}) collective-permute-start(f32[256,128]{1,0:T(8,128)S(1)} %add_add_fusion.1), channel_id=1, source_target_pairs={{0,2},{1,3},{4,6},{5,7},{8,10},{9,11},{16,18},{17,19},{20,22},{21,... | collective-permute-start | bytes 393224 | tf_op jit(solution)/shard_map/ppermute | solution.py:88
  32.4 0.7 collective-permute-start.16
  33.1 1.8 %collective-permute-done.15 = f32[256,128]{1,0:T(8,128)S(1)} collective-permute-done((f32[256,128]{1,0:T(8,128)S(1)}, f32[256,128]{1,0:T(8,128)S(1)}, u32[]{:S(2)}, u32[]{:S(2)}) %collective-permute-start.15) | collective-permute-done | bytes 131104 | tf_op jit(solution)/shard_map/ppermute | solution.py:88
  34.9 1.3 %collective-permute-start.17 = (f32[96,128]{1,0:T(8,128)S(1)}, f32[96,128]{1,0:T(8,128)S(1)}, u32[]{:S(2)}, u32[]{:S(2)}) collective-permute-start(f32[96,128]{1,0:T(8,128)S(1)} %add_add_fusion.3), channel_id=1, source_target_pairs={{0,32},{1,33},{4,36},{5,37},{8,40},{9,41},{12,44},{13,45},{16,48},... | collective-permute-start | bytes 147464 | tf_op jit(solution)/shard_map/ppermute | solution.py:11
  36.2 3.7 %collective-permute-start.18 = (f32[96,128]{1,0:T(8,128)S(1)}, f32[96,128]{1,0:T(8,128)S(1)}, u32[]{:S(2)}, u32[]{:S(2)}) collective-permute-start(f32[96,128]{1,0:T(8,128)S(1)} %add_add_fusion.3), channel_id=1, source_target_pairs={{0,2},{1,3},{4,6},{5,7},{8,10},{9,11},{12,14},{13,15},{16,18},{17,... | collective-permute-start | bytes 147464 | tf_op jit(solution)/shard_map/ppermute | solution.py:11
  39.9 1.3 %collective-permute-start.19 = (f32[96,128]{1,0:T(8,128)S(1)}, f32[96,128]{1,0:T(8,128)S(1)}, u32[]{:S(2)}, u32[]{:S(2)}) collective-permute-start(f32[96,128]{1,0:T(8,128)S(1)} %add_add_fusion.3), channel_id=1, source_target_pairs={{0,34},{1,35},{4,38},{5,39},{8,42},{9,43},{12,46},{13,47},{16,50},... | collective-permute-start | bytes 147464 | tf_op jit(solution)/shard_map/ppermute | solution.py:11
  41.2 8.8 %collective-permute-start.20 = (f32[256,128]{1,0:T(8,128)S(1)}, f32[256,128]{1,0:T(8,128)S(1)}, u32[]{:S(2)}, u32[]{:S(2)}) collective-permute-start(f32[256,128]{1,0:T(8,128)S(1)} %add_add_fusion), channel_id=1, source_target_pairs={{0,0},{16,1},{32,2},{48,3},{64,4},{80,5},{96,6},{112,7},{128,8},{1... | collective-permute-start | bytes 393224 | tf_op jit(solution)/shard_map/ppermute | solution.py:11
  50.1 7.2 %collective-permute-start.21 = (f32[256,128]{1,0:T(8,128)S(1)}, f32[256,128]{1,0:T(8,128)S(1)}, u32[]{:S(2)}, u32[]{:S(2)}) collective-permute-start(f32[256,128]{1,0:T(8,128)S(1)} %add_add_fusion), channel_id=1, source_target_pairs={{0,256},{16,257},{32,258},{48,259},{64,260},{80,261},{96,262},{112... | collective-permute-start | bytes 393224 | tf_op jit(solution)/shard_map/ppermute | solution.py:11
  58.1 11.7 %cholesky.17 = f32[128,128]{1,0:T(8,128)S(1)} custom-call(f32[128,128]{1,0:T(8,128)S(1)} %fusion.3), custom_call_target="Cholesky" | custom-call | tf_op jit(solution)/shard_map/jit(cholesky)/cholesky | solution.py:112
  70.5 0.7 select_bitcast_fusion
  71.2 9.8 %custom-call.7 = f32[1,128,128]{1,2,0:T(8,128)S(1)} custom-call(f32[1,128,128]{2,1,0:T(8,128)S(1)} %get-tuple-element.13), custom_call_target="InvertDiagBlocksLowerTriangular" | custom-call | tf_op jit(solution)/shard_map/jit(_solve_triangular)/triangular_solve | solution.py:51
  83.3 0.7 copy-done.1
  84.0 1.6 %dynamic_update_slice.3 = f32[256,512]{1,0:T(8,128)} dynamic-update-slice(f32[256,512]{1,0:T(8,128)} %copy-done.1, f32[256,64]{1,0:T(8,128)S(1)} %slice_select_fusion, s32[]{:T(128)} %constant.82.clone.1, s32[]{:T(128)} %constant.82.clone.1) | dynamic-update-slice | bytes 131076 | tf_op jit(solution)/shard_map/dynamic_update_slice | solution.py:138
  (63 shorter events, 4.7 us)
Async XLA Ops:
  0.0 7.2 %copy-start = (f32[256,512]{1,0:T(8,128)S(1)}, f32[256,512]{1,0:T(8,128)}, u32[]{:S(2)}) copy-start(f32[256,512]{1,0:T(8,128)} %param.1) | copy-start | bytes 1572868
  0.8 4.2 %collective-permute-start.1 = (f32[64,64]{1,0:T(8,128)S(1)}, f32[64,64]{1,0:T(8,128)S(1)}, u32[]{:S(2)}, u32[]{:S(2)}) collective-permute-start(f32[64,64]{1,0:T(8,128)S(1)} %slice.66), channel_id=1, source_target_pairs={{17,0},{0,16}} | collective-permute-start | bytes 49160 | tf_op jit(solution)/shard_map/ppermute | solution.py:11
  1.5 3.6 %collective-permute-start.2 = (f32[64,64]{1,0:T(8,128)S(1)}, f32[64,64]{1,0:T(8,128)S(1)}, u32[]{:S(2)}, u32[]{:S(2)}) collective-permute-start(f32[64,64]{1,0:T(8,128)S(1)} %slice.66), channel_id=1, source_target_pairs={{17,1},{0,17}} | collective-permute-start | bytes 49160 | tf_op jit(solution)/shard_map/ppermute | solution.py:11
  3.1 3.2 %collective-permute-start = (f32[256,64]{1,0:T(8,128)S(1)}, f32[256,64]{1,0:T(8,128)S(1)}, u32[]{:S(2)}, u32[]{:S(2)}) collective-permute-start(f32[256,64]{1,0:T(8,128)S(1)} %slice.67), channel_id=1, source_target_pairs={{0,1},{1,0},{16,17},{17,16},{32,33},{33,32},{48,49},{49,48},{64,65... | collective-permute-start | bytes 196616 | tf_op jit(solution)/shard_map/ppermute | solution.py:67
  7.3 3.4 %collective-permute-start.3 = (f32[96,128]{1,0:T(8,128)S(1)}, f32[96,128]{1,0:T(8,128)S(1)}, u32[]{:S(2)}, u32[]{:S(2)}) collective-permute-start(f32[96,128]{1,0:T(8,128)S(1)} %select_n.138), channel_id=1, source_target_pairs={{0,8},{1,9},{16,24},{17,25}} | collective-permute-start | bytes 147464 | tf_op jit(solution)/shard_map/ppermute | solution.py:11
  8.0 4.0 %collective-permute-start.4 = (f32[96,128]{1,0:T(8,128)S(1)}, f32[96,128]{1,0:T(8,128)S(1)}, u32[]{:S(2)}, u32[]{:S(2)}) collective-permute-start(f32[96,128]{1,0:T(8,128)S(1)} %select_n.138), channel_id=1, source_target_pairs={{0,128},{1,129},{16,144},{17,145}} | collective-permute-start | bytes 147464 | tf_op jit(solution)/shard_map/ppermute | solution.py:11
  8.6 4.2 %collective-permute-start.5 = (f32[96,128]{1,0:T(8,128)S(1)}, f32[96,128]{1,0:T(8,128)S(1)}, u32[]{:S(2)}, u32[]{:S(2)}) collective-permute-start(f32[96,128]{1,0:T(8,128)S(1)} %select_n.138), channel_id=1, source_target_pairs={{0,136},{1,137},{16,152},{17,153}} | collective-permute-start | bytes 147464 | tf_op jit(solution)/shard_map/ppermute | solution.py:11
  9.3 11.9 %collective-permute-start.6 = (f32[96,128]{1,0:T(8,128)S(1)}, f32[96,128]{1,0:T(8,128)S(1)}, u32[]{:S(2)}, u32[]{:S(2)}) collective-permute-start(f32[96,128]{1,0:T(8,128)S(1)} %select_n.138), channel_id=1, source_target_pairs={{0,256},{1,257},{16,272},{17,273}} | collective-permute-start | bytes 147464 | tf_op jit(solution)/shard_map/ppermute | solution.py:11
  10.0 12.6 %collective-permute-start.7 = (f32[96,128]{1,0:T(8,128)S(1)}, f32[96,128]{1,0:T(8,128)S(1)}, u32[]{:S(2)}, u32[]{:S(2)}) collective-permute-start(f32[96,128]{1,0:T(8,128)S(1)} %select_n.138), channel_id=1, source_target_pairs={{0,264},{1,265},{16,280},{17,281}} | collective-permute-start | bytes 147464 | tf_op jit(solution)/shard_map/ppermute | solution.py:11
  10.7 16.4 %collective-permute-start.8 = (f32[96,128]{1,0:T(8,128)S(1)}, f32[96,128]{1,0:T(8,128)S(1)}, u32[]{:S(2)}, u32[]{:S(2)}) collective-permute-start(f32[96,128]{1,0:T(8,128)S(1)} %select_n.138), channel_id=1, source_target_pairs={{0,384},{1,385},{16,400},{17,401}} | collective-permute-start | bytes 147464 | tf_op jit(solution)/shard_map/ppermute | solution.py:11
  12.0 15.1 %collective-permute-start.9 = (f32[96,128]{1,0:T(8,128)S(1)}, f32[96,128]{1,0:T(8,128)S(1)}, u32[]{:S(2)}, u32[]{:S(2)}) collective-permute-start(f32[96,128]{1,0:T(8,128)S(1)} %select_n.138), channel_id=1, source_target_pairs={{0,392},{1,393},{16,408},{17,409}} | collective-permute-start | bytes 147464 | tf_op jit(solution)/shard_map/ppermute | solution.py:11
  12.8 18.2 %collective-permute-start.13 = (f32[256,128]{1,0:T(8,128)S(1)}, f32[256,128]{1,0:T(8,128)S(1)}, u32[]{:S(2)}, u32[]{:S(2)}) collective-permute-start(f32[256,128]{1,0:T(8,128)S(1)} %maximum_select_fusion), channel_id=1, source_target_pairs={{0,8},{1,9},{16,24},{17,25},{32,40},{33,41},{48,56},{49,57},{64,72... | collective-permute-start | bytes 393224 | tf_op jit(solution)/shard_map/ppermute | solution.py:88
  21.3 9.8 %collective-permute-start.14 = (f32[256,128]{1,0:T(8,128)S(1)}, f32[256,128]{1,0:T(8,128)S(1)}, u32[]{:S(2)}, u32[]{:S(2)}) collective-permute-start(f32[256,128]{1,0:T(8,128)S(1)} %maximum_select_fusion), channel_id=1, source_target_pairs={{0,4},{1,5},{16,20},{17,21},{32,36},{33,37},{48,52},{49,53},{64,68... | collective-permute-start | bytes 393224 | tf_op jit(solution)/shard_map/ppermute | solution.py:88
  27.1 5.9 %collective-permute-start.10 = (f32[96,128]{1,0:T(8,128)S(1)}, f32[96,128]{1,0:T(8,128)S(1)}, u32[]{:S(2)}, u32[]{:S(2)}) collective-permute-start(f32[96,128]{1,0:T(8,128)S(1)} %add_add_fusion.4), channel_id=1, source_target_pairs={{0,64},{1,65},{8,72},{9,73},{16,80},{17,81},{24,88},{25,89},{128,1... | collective-permute-start | bytes 147464 | tf_op jit(solution)/shard_map/ppermute | solution.py:11
  28.4 4.6 %collective-permute-start.11 = (f32[96,128]{1,0:T(8,128)S(1)}, f32[96,128]{1,0:T(8,128)S(1)}, u32[]{:S(2)}, u32[]{:S(2)}) collective-permute-start(f32[96,128]{1,0:T(8,128)S(1)} %add_add_fusion.4), channel_id=1, source_target_pairs={{0,4},{1,5},{8,12},{9,13},{16,20},{17,21},{24,28},{25,29},{128,132... | collective-permute-start | bytes 147464 | tf_op jit(solution)/shard_map/ppermute | solution.py:11
  29.7 3.4 %collective-permute-start.12 = (f32[96,128]{1,0:T(8,128)S(1)}, f32[96,128]{1,0:T(8,128)S(1)}, u32[]{:S(2)}, u32[]{:S(2)}) collective-permute-start(f32[96,128]{1,0:T(8,128)S(1)} %add_add_fusion.4), channel_id=1, source_target_pairs={{0,68},{1,69},{8,76},{9,77},{16,84},{17,85},{24,92},{25,93},{128,1... | collective-permute-start | bytes 147464 | tf_op jit(solution)/shard_map/ppermute | solution.py:11
  31.1 3.8 %collective-permute-start.15 = (f32[256,128]{1,0:T(8,128)S(1)}, f32[256,128]{1,0:T(8,128)S(1)}, u32[]{:S(2)}, u32[]{:S(2)}) collective-permute-start(f32[256,128]{1,0:T(8,128)S(1)} %add_add_fusion.1), channel_id=1, source_target_pairs={{0,2},{1,3},{4,6},{5,7},{8,10},{9,11},{16,18},{17,19},{20,22},{21,... | collective-permute-start | bytes 393224 | tf_op jit(solution)/shard_map/ppermute | solution.py:88
  32.4 2.5 %collective-permute-start.16 = (f32[256,128]{1,0:T(8,128)S(1)}, f32[256,128]{1,0:T(8,128)S(1)}, u32[]{:S(2)}, u32[]{:S(2)}) collective-permute-start(f32[256,128]{1,0:T(8,128)S(1)} %add_add_fusion.1), channel_id=1, source_target_pairs={{8,12},{9,13},{4,14},{5,15},{24,28},{25,29},{20,30},{21,31},{40,44... | collective-permute-start | bytes 393224 | tf_op jit(solution)/shard_map/ppermute | solution.py:88
  34.9 22.4 %collective-permute-start.17 = (f32[96,128]{1,0:T(8,128)S(1)}, f32[96,128]{1,0:T(8,128)S(1)}, u32[]{:S(2)}, u32[]{:S(2)}) collective-permute-start(f32[96,128]{1,0:T(8,128)S(1)} %add_add_fusion.3), channel_id=1, source_target_pairs={{0,32},{1,33},{4,36},{5,37},{8,40},{9,41},{12,44},{13,45},{16,48},... | collective-permute-start | bytes 147464 | tf_op jit(solution)/shard_map/ppermute | solution.py:11
  36.2 21.1 %collective-permute-start.18 = (f32[96,128]{1,0:T(8,128)S(1)}, f32[96,128]{1,0:T(8,128)S(1)}, u32[]{:S(2)}, u32[]{:S(2)}) collective-permute-start(f32[96,128]{1,0:T(8,128)S(1)} %add_add_fusion.3), channel_id=1, source_target_pairs={{0,2},{1,3},{4,6},{5,7},{8,10},{9,11},{12,14},{13,15},{16,18},{17,... | collective-permute-start | bytes 147464 | tf_op jit(solution)/shard_map/ppermute | solution.py:11
  39.9 17.4 %collective-permute-start.19 = (f32[96,128]{1,0:T(8,128)S(1)}, f32[96,128]{1,0:T(8,128)S(1)}, u32[]{:S(2)}, u32[]{:S(2)}) collective-permute-start(f32[96,128]{1,0:T(8,128)S(1)} %add_add_fusion.3), channel_id=1, source_target_pairs={{0,34},{1,35},{4,38},{5,39},{8,42},{9,43},{12,46},{13,47},{16,50},... | collective-permute-start | bytes 147464 | tf_op jit(solution)/shard_map/ppermute | solution.py:11
  41.2 41.3 %collective-permute-start.20 = (f32[256,128]{1,0:T(8,128)S(1)}, f32[256,128]{1,0:T(8,128)S(1)}, u32[]{:S(2)}, u32[]{:S(2)}) collective-permute-start(f32[256,128]{1,0:T(8,128)S(1)} %add_add_fusion), channel_id=1, source_target_pairs={{0,0},{16,1},{32,2},{48,3},{64,4},{80,5},{96,6},{112,7},{128,8},{1... | collective-permute-start | bytes 393224 | tf_op jit(solution)/shard_map/ppermute | solution.py:11
  50.1 32.4 %collective-permute-start.21 = (f32[256,128]{1,0:T(8,128)S(1)}, f32[256,128]{1,0:T(8,128)S(1)}, u32[]{:S(2)}, u32[]{:S(2)}) collective-permute-start(f32[256,128]{1,0:T(8,128)S(1)} %add_add_fusion), channel_id=1, source_target_pairs={{0,256},{16,257},{32,258},{48,259},{64,260},{80,261},{96,262},{112... | collective-permute-start | bytes 393224 | tf_op jit(solution)/shard_map/ppermute | solution.py:11
  83.2 0.8 copy-start.1

commit v13 on v10

--- a/solution.py
+++ b/solution.py
@@ -75,8 +75,8 @@
     holders_k = {(0, 0), (0, 1), (1, 0), (1, 1)}
     corner_offsets = [
         [(a * 16 + b * 8, c * 8) for a in (0, 1) for b in (0, 1) for c in (0, 1)][1:],
-        [(4, 0), (0, 4), (4, 4)],
-        [(2, 0), (0, 2), (2, 2)],
+        [(a * 4 + b * 2, c * 4) for a in (0, 1) for b in (0, 1) for c in (0, 1)][1:],
+        [(0, 2)],
     ]
     panel_rounds = [
         [[(0, 8), (1, 9)], [(0, 4), (1, 5)]],

time: 85.1 us -> 89.4 us (1.051)
  starting transfers between devices: 46.4 us -> 50.7 us
    ppermute x17 -> x19, starting transfers between devices: 32.8 us -> 37.1 us  [both_axes(): return lax.ppermute(x, ('row', 'col'), pairs)]
    ppermute x17 -> x19, waiting for transfers between devices: 4.54 us -> 4.53 us  [both_axes(): return lax.ppermute(x, ('row', 'col'), pairs)]
  transfers between devices with their start and end apart: 22 -> 24, of which waited for: 3 -> 3; matrix products, arithmetic and copies ran while one was open for 31% -> 30% of each run, Pallas kernels for 0% -> 0%
where the time goes in v13:
time: 89.4 us; the launch traced here: 88.7 us
  starting transfers between devices  50.7 us (57%)
  other arithmetic  25.3 us (28%)
  waiting for transfers between devices  7.54 us (8%)
  local copies, waits for them, and re-layouts  3.1 us (3%)
  matrix products  1.55 us (2%)
    ppermute x19, starting transfers between devices, both_axes(): return lax.ppermute(x, ('row', 'col'), pairs)  37.1 us
    another operation x3, other arithmetic, per_device(): factor = jnp.linalg.cholesky(lead_block)  12.4 us
    ppermute x4, starting transfers between devices, per_device(): panel = panel + lax.ppermute(sent, 'col', pairs)  11.7 us
    another operation x2, other arithmetic, lower_inverse(): return jax.scipy.linalg.solve_triangular(factor, eye, lower=True)  10.5 us
    ppermute x19, waiting for transfers between devices, both_axes(): return lax.ppermute(x, ('row', 'col'), pairs)  4.53 us
    ppermute x1, starting transfers between devices, per_device(): swapped = lax.ppermute(mine, 'col', [(0, 1), (1, 0)])  1.92 us
  transfers between devices with their start and end apart: 24, of which 3 were waited for; matrix products, arithmetic and copies ran while one was open for 30% of the time, Pallas kernels for 0%

profile of v13, /device:TPU:48, one launch (start us, length us, event | category | flops | bytes accessed | tf_op | source)
XLA Modules:
  0.0 88.7 jit_solution(13085653386653367224)
XLA Ops:
  0.0 0.8 slice.69
  1.5 0.7 collective-permute-start.2
  2.2 0.9 %slice.70 = f32[256,64]{1,0:T(8,128)S(1)} slice(f32[256,512]{1,0:T(8,128)} %param.1), slice={[0:256], [0:64]} | slice | bytes 131072 | tf_op jit(solution)/shard_map/slice | solution.py:66
  3.1 1.9 %collective-permute-start = (f32[256,64]{1,0:T(8,128)S(1)}, f32[256,64]{1,0:T(8,128)S(1)}, u32[]{:S(2)}, u32[]{:S(2)}) collective-permute-start(f32[256,64]{1,0:T(8,128)S(1)} %slice.70), channel_id=1, source_target_pairs={{0,1},{1,0},{16,17},{17,16},{32,33},{33,32},{48,49},{49,48},{64,65... | collective-permute-start | bytes 196616 | tf_op jit(solution)/shard_map/ppermute | solution.py:67
  5.1 1.3 %collective-permute-done = f32[256,64]{1,0:T(8,128)S(1)} collective-permute-done((f32[256,64]{1,0:T(8,128)S(1)}, f32[256,64]{1,0:T(8,128)S(1)}, u32[]{:S(2)}, u32[]{:S(2)}) %collective-permute-start) | collective-permute-done | bytes 65568 | tf_op jit(solution)/shard_map/ppermute | solution.py:67
  6.3 0.8 broadcast_select_fusion.7
  7.3 0.7 collective-permute-start.3
  8.0 0.7 collective-permute-start.4
  8.6 0.7 collective-permute-start.5
  9.3 0.7 collective-permute-start.6
  10.0 0.7 collective-permute-start.7
  10.7 1.3 %collective-permute-start.8 = (f32[96,128]{1,0:T(8,128)S(1)}, f32[96,128]{1,0:T(8,128)S(1)}, u32[]{:S(2)}, u32[]{:S(2)}) collective-permute-start(f32[96,128]{1,0:T(8,128)S(1)} %select_n.138), channel_id=1, source_target_pairs={{0,384},{1,385},{16,400},{17,401}} | collective-permute-start | bytes 147464 | tf_op jit(solution)/shard_map/ppermute | solution.py:11
  12.0 0.7 collective-permute-start.9
  12.8 8.4 %collective-permute-start.17 = (f32[256,128]{1,0:T(8,128)S(1)}, f32[256,128]{1,0:T(8,128)S(1)}, u32[]{:S(2)}, u32[]{:S(2)}) collective-permute-start(f32[256,128]{1,0:T(8,128)S(1)} %maximum_select_fusion), channel_id=1, source_target_pairs={{0,8},{1,9},{16,24},{17,25},{32,40},{33,41},{48,56},{49,57},{64,72... | collective-permute-start | bytes 393224 | tf_op jit(solution)/shard_map/ppermute | solution.py:88
  21.2 1.3 %collective-permute-start.18 = (f32[256,128]{1,0:T(8,128)S(1)}, f32[256,128]{1,0:T(8,128)S(1)}, u32[]{:S(2)}, u32[]{:S(2)}) collective-permute-start(f32[256,128]{1,0:T(8,128)S(1)} %maximum_select_fusion), channel_id=1, source_target_pairs={{0,4},{1,5},{16,20},{17,21},{32,36},{33,37},{48,52},{49,53},{64,68... | collective-permute-start | bytes 393224 | tf_op jit(solution)/shard_map/ppermute | solution.py:88
  22.6 4.5 %collective-permute-done.8 = f32[96,128]{1,0:T(8,128)S(1)} collective-permute-done((f32[96,128]{1,0:T(8,128)S(1)}, f32[96,128]{1,0:T(8,128)S(1)}, u32[]{:S(2)}, u32[]{:S(2)}) %collective-permute-start.8) | collective-permute-done | bytes 49184 | tf_op jit(solution)/shard_map/ppermute | solution.py:11
  27.1 1.3 %collective-permute-start.10 = (f32[96,128]{1,0:T(8,128)S(1)}, f32[96,128]{1,0:T(8,128)S(1)}, u32[]{:S(2)}, u32[]{:S(2)}) collective-permute-start(f32[96,128]{1,0:T(8,128)S(1)} %add_add_fusion.3), channel_id=1, source_target_pairs={{0,4},{1,5},{8,12},{9,13},{16,20},{17,21},{24,28},{25,29},{128,132... | collective-permute-start | bytes 147464 | tf_op jit(solution)/shard_map/ppermute | solution.py:11
  28.4 1.3 %collective-permute-start.11 = (f32[96,128]{1,0:T(8,128)S(1)}, f32[96,128]{1,0:T(8,128)S(1)}, u32[]{:S(2)}, u32[]{:S(2)}) collective-permute-start(f32[96,128]{1,0:T(8,128)S(1)} %add_add_fusion.3), channel_id=1, source_target_pairs={{0,32},{1,33},{8,40},{9,41},{16,48},{17,49},{24,56},{25,57},{128,1... | collective-permute-start | bytes 147464 | tf_op jit(solution)/shard_map/ppermute | solution.py:11
  29.7 1.3 %collective-permute-start.12 = (f32[96,128]{1,0:T(8,128)S(1)}, f32[96,128]{1,0:T(8,128)S(1)}, u32[]{:S(2)}, u32[]{:S(2)}) collective-permute-start(f32[96,128]{1,0:T(8,128)S(1)} %add_add_fusion.3), channel_id=1, source_target_pairs={{0,36},{1,37},{8,44},{9,45},{16,52},{17,53},{24,60},{25,61},{128,1... | collective-permute-start | bytes 147464 | tf_op jit(solution)/shard_map/ppermute | solution.py:11
  31.0 1.3 %collective-permute-start.13 = (f32[96,128]{1,0:T(8,128)S(1)}, f32[96,128]{1,0:T(8,128)S(1)}, u32[]{:S(2)}, u32[]{:S(2)}) collective-permute-start(f32[96,128]{1,0:T(8,128)S(1)} %add_add_fusion.3), channel_id=1, source_target_pairs={{0,64},{1,65},{8,72},{9,73},{16,80},{17,81},{24,88},{25,89},{128,1... | collective-permute-start | bytes 147464 | tf_op jit(solution)/shard_map/ppermute | solution.py:11
  32.3 1.3 %collective-permute-start.14 = (f32[96,128]{1,0:T(8,128)S(1)}, f32[96,128]{1,0:T(8,128)S(1)}, u32[]{:S(2)}, u32[]{:S(2)}) collective-permute-start(f32[96,128]{1,0:T(8,128)S(1)} %add_add_fusion.3), channel_id=1, source_target_pairs={{0,68},{1,69},{8,76},{9,77},{16,84},{17,85},{24,92},{25,93},{128,1... | collective-permute-start | bytes 147464 | tf_op jit(solution)/shard_map/ppermute | solution.py:11
  33.6 1.3 %collective-permute-start.15 = (f32[96,128]{1,0:T(8,128)S(1)}, f32[96,128]{1,0:T(8,128)S(1)}, u32[]{:S(2)}, u32[]{:S(2)}) collective-permute-start(f32[96,128]{1,0:T(8,128)S(1)} %add_add_fusion.3), channel_id=1, source_target_pairs={{0,96},{1,97},{8,104},{9,105},{16,112},{17,113},{24,120},{25,121},... | collective-permute-start | bytes 147464 | tf_op jit(solution)/shard_map/ppermute | solution.py:11
  34.9 1.3 %collective-permute-start.16 = (f32[96,128]{1,0:T(8,128)S(1)}, f32[96,128]{1,0:T(8,128)S(1)}, u32[]{:S(2)}, u32[]{:S(2)}) collective-permute-start(f32[96,128]{1,0:T(8,128)S(1)} %add_add_fusion.3), channel_id=1, source_target_pairs={{0,100},{1,101},{8,108},{9,109},{16,116},{17,117},{24,124},{25,125... | collective-permute-start | bytes 147464 | tf_op jit(solution)/shard_map/ppermute | solution.py:11
  36.3 1.3 %collective-permute-start.19 = (f32[256,128]{1,0:T(8,128)S(1)}, f32[256,128]{1,0:T(8,128)S(1)}, u32[]{:S(2)}, u32[]{:S(2)}) collective-permute-start(f32[256,128]{1,0:T(8,128)S(1)} %add_add_fusion.1), channel_id=1, source_target_pairs={{0,2},{1,3},{4,6},{5,7},{8,10},{9,11},{16,18},{17,19},{20,22},{21,... | collective-permute-start | bytes 393224 | tf_op jit(solution)/shard_map/ppermute | solution.py:88
  37.6 0.7 collective-permute-start.20
  38.3 1.7 %collective-permute-done.19 = f32[256,128]{1,0:T(8,128)S(1)} collective-permute-done((f32[256,128]{1,0:T(8,128)S(1)}, f32[256,128]{1,0:T(8,128)S(1)}, u32[]{:S(2)}, u32[]{:S(2)}) %collective-permute-start.19) | collective-permute-done | bytes 131104 | tf_op jit(solution)/shard_map/ppermute | solution.py:88
  40.1 4.4 %collective-permute-start.21 = (f32[96,128]{1,0:T(8,128)S(1)}, f32[96,128]{1,0:T(8,128)S(1)}, u32[]{:S(2)}, u32[]{:S(2)}) collective-permute-start(f32[96,128]{1,0:T(8,128)S(1)} %add_add_fusion.2), channel_id=1, source_target_pairs={{0,2},{1,3},{4,6},{5,7},{8,10},{9,11},{12,14},{13,15},{16,18},{17,... | collective-permute-start | bytes 147464 | tf_op jit(solution)/shard_map/ppermute | solution.py:11
  44.5 8.9 %collective-permute-start.22 = (f32[256,128]{1,0:T(8,128)S(1)}, f32[256,128]{1,0:T(8,128)S(1)}, u32[]{:S(2)}, u32[]{:S(2)}) collective-permute-start(f32[256,128]{1,0:T(8,128)S(1)} %add_add_fusion), channel_id=1, source_target_pairs={{0,0},{16,1},{32,2},{48,3},{64,4},{80,5},{96,6},{112,7},{128,8},{1... | collective-permute-start | bytes 393224 | tf_op jit(solution)/shard_map/ppermute | solution.py:11
  53.4 8.2 %collective-permute-start.23 = (f32[256,128]{1,0:T(8,128)S(1)}, f32[256,128]{1,0:T(8,128)S(1)}, u32[]{:S(2)}, u32[]{:S(2)}) collective-permute-start(f32[256,128]{1,0:T(8,128)S(1)} %add_add_fusion), channel_id=1, source_target_pairs={{0,256},{16,257},{32,258},{48,259},{64,260},{80,261},{96,262},{112... | collective-permute-start | bytes 393224 | tf_op jit(solution)/shard_map/ppermute | solution.py:11
  62.4 11.7 %cholesky.20 = f32[128,128]{1,0:T(8,128)S(1)} custom-call(f32[128,128]{1,0:T(8,128)S(1)} %fusion.3), custom_call_target="Cholesky" | custom-call | tf_op jit(solution)/shard_map/jit(cholesky)/cholesky | solution.py:112
  75.5 9.8 %custom-call.7 = f32[1,128,128]{1,2,0:T(8,128)S(1)} custom-call(f32[1,128,128]{2,1,0:T(8,128)S(1)} %get-tuple-element.13), custom_call_target="InvertDiagBlocksLowerTriangular" | custom-call | tf_op jit(solution)/shard_map/jit(_solve_triangular)/triangular_solve | solution.py:51
  87.7 1.0 %pad_maximum_fusion = f32[256,512]{1,0:T(8,128)} fusion(f32[256,448]{1,0:T(8,128)S(1)} %slice.94, f32[256,64]{1,0:T(8,128)S(1)} %slice_select_fusion), kind=kLoop, calls=%fused_computation.2 | loop fusion | flops 131072 | bytes 1048576 | tf_op jit(solution)/shard_map/concatenate | solution.py:138
  (66 shorter events, 5.6 us)
Async XLA Ops:
  0.0 7.2 %copy-start = (f32[256,512]{1,0:T(8,128)S(1)}, f32[256,512]{1,0:T(8,128)}, u32[]{:S(2)}) copy-start(f32[256,512]{1,0:T(8,128)} %param.1) | copy-start | bytes 1572868
  0.8 4.2 %collective-permute-start.1 = (f32[64,64]{1,0:T(8,128)S(1)}, f32[64,64]{1,0:T(8,128)S(1)}, u32[]{:S(2)}, u32[]{:S(2)}) collective-permute-start(f32[64,64]{1,0:T(8,128)S(1)} %slice.69), channel_id=1, source_target_pairs={{17,0},{0,16}} | collective-permute-start | bytes 49160 | tf_op jit(solution)/shard_map/ppermute | solution.py:11
  1.5 3.6 %collective-permute-start.2 = (f32[64,64]{1,0:T(8,128)S(1)}, f32[64,64]{1,0:T(8,128)S(1)}, u32[]{:S(2)}, u32[]{:S(2)}) collective-permute-start(f32[64,64]{1,0:T(8,128)S(1)} %slice.69), channel_id=1, source_target_pairs={{17,1},{0,17}} | collective-permute-start | bytes 49160 | tf_op jit(solution)/shard_map/ppermute | solution.py:11
  3.1 3.2 %collective-permute-start = (f32[256,64]{1,0:T(8,128)S(1)}, f32[256,64]{1,0:T(8,128)S(1)}, u32[]{:S(2)}, u32[]{:S(2)}) collective-permute-start(f32[256,64]{1,0:T(8,128)S(1)} %slice.70), channel_id=1, source_target_pairs={{0,1},{1,0},{16,17},{17,16},{32,33},{33,32},{48,49},{49,48},{64,65... | collective-permute-start | bytes 196616 | tf_op jit(solution)/shard_map/ppermute | solution.py:67
  7.3 3.4 %collective-permute-start.3 = (f32[96,128]{1,0:T(8,128)S(1)}, f32[96,128]{1,0:T(8,128)S(1)}, u32[]{:S(2)}, u32[]{:S(2)}) collective-permute-start(f32[96,128]{1,0:T(8,128)S(1)} %select_n.138), channel_id=1, source_target_pairs={{0,8},{1,9},{16,24},{17,25}} | collective-permute-start | bytes 147464 | tf_op jit(solution)/shard_map/ppermute | solution.py:11
  8.0 4.0 %collective-permute-start.4 = (f32[96,128]{1,0:T(8,128)S(1)}, f32[96,128]{1,0:T(8,128)S(1)}, u32[]{:S(2)}, u32[]{:S(2)}) collective-permute-start(f32[96,128]{1,0:T(8,128)S(1)} %select_n.138), channel_id=1, source_target_pairs={{0,128},{1,129},{16,144},{17,145}} | collective-permute-start | bytes 147464 | tf_op jit(solution)/shard_map/ppermute | solution.py:11
  8.6 4.2 %collective-permute-start.5 = (f32[96,128]{1,0:T(8,128)S(1)}, f32[96,128]{1,0:T(8,128)S(1)}, u32[]{:S(2)}, u32[]{:S(2)}) collective-permute-start(f32[96,128]{1,0:T(8,128)S(1)} %select_n.138), channel_id=1, source_target_pairs={{0,136},{1,137},{16,152},{17,153}} | collective-permute-start | bytes 147464 | tf_op jit(solution)/shard_map/ppermute | solution.py:11
  9.3 11.9 %collective-permute-start.6 = (f32[96,128]{1,0:T(8,128)S(1)}, f32[96,128]{1,0:T(8,128)S(1)}, u32[]{:S(2)}, u32[]{:S(2)}) collective-permute-start(f32[96,128]{1,0:T(8,128)S(1)} %select_n.138), channel_id=1, source_target_pairs={{0,256},{1,257},{16,272},{17,273}} | collective-permute-start | bytes 147464 | tf_op jit(solution)/shard_map/ppermute | solution.py:11
  10.0 12.6 %collective-permute-start.7 = (f32[96,128]{1,0:T(8,128)S(1)}, f32[96,128]{1,0:T(8,128)S(1)}, u32[]{:S(2)}, u32[]{:S(2)}) collective-permute-start(f32[96,128]{1,0:T(8,128)S(1)} %select_n.138), channel_id=1, source_target_pairs={{0,264},{1,265},{16,280},{17,281}} | collective-permute-start | bytes 147464 | tf_op jit(solution)/shard_map/ppermute | solution.py:11
  10.7 16.3 %collective-permute-start.8 = (f32[96,128]{1,0:T(8,128)S(1)}, f32[96,128]{1,0:T(8,128)S(1)}, u32[]{:S(2)}, u32[]{:S(2)}) collective-permute-start(f32[96,128]{1,0:T(8,128)S(1)} %select_n.138), channel_id=1, source_target_pairs={{0,384},{1,385},{16,400},{17,401}} | collective-permute-start | bytes 147464 | tf_op jit(solution)/shard_map/ppermute | solution.py:11
  12.0 15.0 %collective-permute-start.9 = (f32[96,128]{1,0:T(8,128)S(1)}, f32[96,128]{1,0:T(8,128)S(1)}, u32[]{:S(2)}, u32[]{:S(2)}) collective-permute-start(f32[96,128]{1,0:T(8,128)S(1)} %select_n.138), channel_id=1, source_target_pairs={{0,392},{1,393},{16,408},{17,409}} | collective-permute-start | bytes 147464 | tf_op jit(solution)/shard_map/ppermute | solution.py:11
  12.8 20.8 %collective-permute-start.17 = (f32[256,128]{1,0:T(8,128)S(1)}, f32[256,128]{1,0:T(8,128)S(1)}, u32[]{:S(2)}, u32[]{:S(2)}) collective-permute-start(f32[256,128]{1,0:T(8,128)S(1)} %maximum_select_fusion), channel_id=1, source_target_pairs={{0,8},{1,9},{16,24},{17,25},{32,40},{33,41},{48,56},{49,57},{64,72... | collective-permute-start | bytes 393224 | tf_op jit(solution)/shard_map/ppermute | solution.py:88
  21.2 13.7 %collective-permute-start.18 = (f32[256,128]{1,0:T(8,128)S(1)}, f32[256,128]{1,0:T(8,128)S(1)}, u32[]{:S(2)}, u32[]{:S(2)}) collective-permute-start(f32[256,128]{1,0:T(8,128)S(1)} %maximum_select_fusion), channel_id=1, source_target_pairs={{0,4},{1,5},{16,20},{17,21},{32,36},{33,37},{48,52},{49,53},{64,68... | collective-permute-start | bytes 393224 | tf_op jit(solution)/shard_map/ppermute | solution.py:88
  27.1 3.9 %collective-permute-start.10 = (f32[96,128]{1,0:T(8,128)S(1)}, f32[96,128]{1,0:T(8,128)S(1)}, u32[]{:S(2)}, u32[]{:S(2)}) collective-permute-start(f32[96,128]{1,0:T(8,128)S(1)} %add_add_fusion.3), channel_id=1, source_target_pairs={{0,4},{1,5},{8,12},{9,13},{16,20},{17,21},{24,28},{25,29},{128,132... | collective-permute-start | bytes 147464 | tf_op jit(solution)/shard_map/ppermute | solution.py:11
  28.4 3.9 %collective-permute-start.11 = (f32[96,128]{1,0:T(8,128)S(1)}, f32[96,128]{1,0:T(8,128)S(1)}, u32[]{:S(2)}, u32[]{:S(2)}) collective-permute-start(f32[96,128]{1,0:T(8,128)S(1)} %add_add_fusion.3), channel_id=1, source_target_pairs={{0,32},{1,33},{8,40},{9,41},{16,48},{17,49},{24,56},{25,57},{128,1... | collective-permute-start | bytes 147464 | tf_op jit(solution)/shard_map/ppermute | solution.py:11
  29.7 6.6 %collective-permute-start.12 = (f32[96,128]{1,0:T(8,128)S(1)}, f32[96,128]{1,0:T(8,128)S(1)}, u32[]{:S(2)}, u32[]{:S(2)}) collective-permute-start(f32[96,128]{1,0:T(8,128)S(1)} %add_add_fusion.3), channel_id=1, source_target_pairs={{0,36},{1,37},{8,44},{9,45},{16,52},{17,53},{24,60},{25,61},{128,1... | collective-permute-start | bytes 147464 | tf_op jit(solution)/shard_map/ppermute | solution.py:11
  31.0 6.6 %collective-permute-start.13 = (f32[96,128]{1,0:T(8,128)S(1)}, f32[96,128]{1,0:T(8,128)S(1)}, u32[]{:S(2)}, u32[]{:S(2)}) collective-permute-start(f32[96,128]{1,0:T(8,128)S(1)} %add_add_fusion.3), channel_id=1, source_target_pairs={{0,64},{1,65},{8,72},{9,73},{16,80},{17,81},{24,88},{25,89},{128,1... | collective-permute-start | bytes 147464 | tf_op jit(solution)/shard_map/ppermute | solution.py:11
  32.3 6.0 %collective-permute-start.14 = (f32[96,128]{1,0:T(8,128)S(1)}, f32[96,128]{1,0:T(8,128)S(1)}, u32[]{:S(2)}, u32[]{:S(2)}) collective-permute-start(f32[96,128]{1,0:T(8,128)S(1)} %add_add_fusion.3), channel_id=1, source_target_pairs={{0,68},{1,69},{8,76},{9,77},{16,84},{17,85},{24,92},{25,93},{128,1... | collective-permute-start | bytes 147464 | tf_op jit(solution)/shard_map/ppermute | solution.py:11
  33.6 4.7 %collective-permute-start.15 = (f32[96,128]{1,0:T(8,128)S(1)}, f32[96,128]{1,0:T(8,128)S(1)}, u32[]{:S(2)}, u32[]{:S(2)}) collective-permute-start(f32[96,128]{1,0:T(8,128)S(1)} %add_add_fusion.3), channel_id=1, source_target_pairs={{0,96},{1,97},{8,104},{9,105},{16,112},{17,113},{24,120},{25,121},... | collective-permute-start | bytes 147464 | tf_op jit(solution)/shard_map/ppermute | solution.py:11
  34.9 3.4 %collective-permute-start.16 = (f32[96,128]{1,0:T(8,128)S(1)}, f32[96,128]{1,0:T(8,128)S(1)}, u32[]{:S(2)}, u32[]{:S(2)}) collective-permute-start(f32[96,128]{1,0:T(8,128)S(1)} %add_add_fusion.3), channel_id=1, source_target_pairs={{0,100},{1,101},{8,108},{9,109},{16,116},{17,117},{24,124},{25,125... | collective-permute-start | bytes 147464 | tf_op jit(solution)/shard_map/ppermute | solution.py:11
  36.3 3.8 %collective-permute-start.19 = (f32[256,128]{1,0:T(8,128)S(1)}, f32[256,128]{1,0:T(8,128)S(1)}, u32[]{:S(2)}, u32[]{:S(2)}) collective-permute-start(f32[256,128]{1,0:T(8,128)S(1)} %add_add_fusion.1), channel_id=1, source_target_pairs={{0,2},{1,3},{4,6},{5,7},{8,10},{9,11},{16,18},{17,19},{20,22},{21,... | collective-permute-start | bytes 393224 | tf_op jit(solution)/shard_map/ppermute | solution.py:88
  37.6 2.5 %collective-permute-start.20 = (f32[256,128]{1,0:T(8,128)S(1)}, f32[256,128]{1,0:T(8,128)S(1)}, u32[]{:S(2)}, u32[]{:S(2)}) collective-permute-start(f32[256,128]{1,0:T(8,128)S(1)} %add_add_fusion.1), channel_id=1, source_target_pairs={{8,12},{9,13},{4,14},{5,15},{24,28},{25,29},{20,30},{21,31},{40,44... | collective-permute-start | bytes 393224 | tf_op jit(solution)/shard_map/ppermute | solution.py:88
  40.1 21.5 %collective-permute-start.21 = (f32[96,128]{1,0:T(8,128)S(1)}, f32[96,128]{1,0:T(8,128)S(1)}, u32[]{:S(2)}, u32[]{:S(2)}) collective-permute-start(f32[96,128]{1,0:T(8,128)S(1)} %add_add_fusion.2), channel_id=1, source_target_pairs={{0,2},{1,3},{4,6},{5,7},{8,10},{9,11},{12,14},{13,15},{16,18},{17,... | collective-permute-start | bytes 147464 | tf_op jit(solution)/shard_map/ppermute | solution.py:11
  44.5 42.3 %collective-permute-start.22 = (f32[256,128]{1,0:T(8,128)S(1)}, f32[256,128]{1,0:T(8,128)S(1)}, u32[]{:S(2)}, u32[]{:S(2)}) collective-permute-start(f32[256,128]{1,0:T(8,128)S(1)} %add_add_fusion), channel_id=1, source_target_pairs={{0,0},{16,1},{32,2},{48,3},{64,4},{80,5},{96,6},{112,7},{128,8},{1... | collective-permute-start | bytes 393224 | tf_op jit(solution)/shard_map/ppermute | solution.py:11
  53.4 33.4 %collective-permute-start.23 = (f32[256,128]{1,0:T(8,128)S(1)}, f32[256,128]{1,0:T(8,128)S(1)}, u32[]{:S(2)}, u32[]{:S(2)}) collective-permute-start(f32[256,128]{1,0:T(8,128)S(1)} %add_add_fusion), channel_id=1, source_target_pairs={{0,256},{16,257},{32,258},{48,259},{64,260},{80,261},{96,262},{112... | collective-permute-start | bytes 393224 | tf_op jit(solution)/shard_map/ppermute | solution.py:11

commit v14 on v10

--- a/solution.py
+++ b/solution.py
@@ -110,14 +110,21 @@
         [jnp.concatenate([a00, a10.T], axis=1), jnp.concatenate([a10, a11], axis=1)], axis=0
     )
     factor = jnp.linalg.cholesky(lead_block)
-    inv_t = lower_inverse(factor).T
     c0 = factor[:NB, :NB]
     c1 = factor[NB:, NB:]
+    eye = jnp.broadcast_to(jnp.eye(NB, dtype=jnp.float32), (2, NB, NB))
+    diag_inv = jax.scipy.linalg.solve_triangular(jnp.stack([c0, c1]), eye, lower=True)
+    inv0, inv1 = diag_inv[0], diag_inv[1]
+    off = -mm(mm(inv1, factor[NB:, :NB]), inv0)
+    zero_block = jnp.zeros((NB, NB), jnp.float32)
+    inv_lower = jnp.concatenate(
+        [jnp.concatenate([inv0, zero_block], axis=1), jnp.concatenate([off, inv1], axis=1)], axis=0
+    )
+    inv_t = inv_lower.T
     w_rows = mm(panel_held, inv_t)
     x_rows = w_rows[:, :NB]
     y_rows = w_rows[:, NB:]
     v = mm(w_rows, inv_t.T)
-    zero_block = jnp.zeros((NB, NB), jnp.float32)
 
     low = p < half
     near = jnp.where(low, first, second)

time: 85.1 us -> 85.6 us (level)
    another operation x2 -> x3, other arithmetic: 10.5 us -> 9.85 us  [per_device(): jax.scipy.linalg.solve_triangular(jnp.stack([c0, c1]), eye, lower=True)]
where the time goes in v14:
time: 85.6 us; the launch traced here: 85 us
  starting transfers between devices  46.4 us (54%)
  other arithmetic  25.3 us (30%)
  waiting for transfers between devices  7.56 us (9%)
  local copies, waits for them, and re-layouts  3.18 us (4%)
  matrix products  1.99 us (2%)
    ppermute x17, starting transfers between devices, both_axes(): return lax.ppermute(x, ('row', 'col'), pairs)  32.7 us
    another operation x3, other arithmetic, per_device(): factor = jnp.linalg.cholesky(lead_block)  12.4 us
    ppermute x4, starting transfers between devices, per_device(): panel = panel + lax.ppermute(sent, 'col', pairs)  11.7 us
    another operation x3, other arithmetic, per_device(): jax.scipy.linalg.solve_triangular(jnp.stack([c0, c1]), eye, lower=True)  9.85 us
    ppermute x17, waiting for transfers between devices, both_axes(): return lax.ppermute(x, ('row', 'col'), pairs)  4.57 us
    ppermute x1, starting transfers between devices, per_device(): swapped = lax.ppermute(mine, 'col', [(0, 1), (1, 0)])  1.92 us
    ppermute x4, waiting for transfers between devices, per_device(): panel = panel + lax.ppermute(sent, 'col', pairs)  1.77 us
  transfers between devices with their start and end apart: 22, of which 3 were waited for; matrix products, arithmetic and copies ran while one was open for 31% of the time, Pallas kernels for 0%

profile of v14, /device:TPU:48, one launch (start us, length us, event | category | flops | bytes accessed | tf_op | source)
XLA Modules:
  0.0 85.0 jit_solution(11741028799423484405)
XLA Ops:
  0.0 0.8 slice.78
  0.8 0.7 collective-permute-start.1
  1.5 0.7 collective-permute-start.2
  2.2 0.9 %slice.79 = f32[256,64]{1,0:T(8,128)S(1)} slice(f32[256,512]{1,0:T(8,128)} %param.1), slice={[0:256], [0:64]} | slice | bytes 131072 | tf_op jit(solution)/shard_map/slice | solution.py:66
  3.1 1.9 %collective-permute-start = (f32[256,64]{1,0:T(8,128)S(1)}, f32[256,64]{1,0:T(8,128)S(1)}, u32[]{:S(2)}, u32[]{:S(2)}) collective-permute-start(f32[256,64]{1,0:T(8,128)S(1)} %slice.79), channel_id=1, source_target_pairs={{0,1},{1,0},{16,17},{17,16},{32,33},{33,32},{48,49},{49,48},{64,65... | collective-permute-start | bytes 196616 | tf_op jit(solution)/shard_map/ppermute | solution.py:67
  5.1 1.2 %collective-permute-done = f32[256,64]{1,0:T(8,128)S(1)} collective-permute-done((f32[256,64]{1,0:T(8,128)S(1)}, f32[256,64]{1,0:T(8,128)S(1)}, u32[]{:S(2)}, u32[]{:S(2)}) %collective-permute-start) | collective-permute-done | bytes 65568 | tf_op jit(solution)/shard_map/ppermute | solution.py:67
  6.3 0.8 broadcast_select_fusion.7
  7.3 0.7 collective-permute-start.3
  8.0 0.7 collective-permute-start.4
  8.6 0.7 collective-permute-start.5
  9.3 0.7 collective-permute-start.6
  10.0 0.7 collective-permute-start.7
  10.7 1.3 %collective-permute-start.8 = (f32[96,128]{1,0:T(8,128)S(1)}, f32[96,128]{1,0:T(8,128)S(1)}, u32[]{:S(2)}, u32[]{:S(2)}) collective-permute-start(f32[96,128]{1,0:T(8,128)S(1)} %select_n.138), channel_id=1, source_target_pairs={{0,384},{1,385},{16,400},{17,401}} | collective-permute-start | bytes 147464 | tf_op jit(solution)/shard_map/ppermute | solution.py:11
  12.0 0.7 collective-permute-start.9
  12.8 8.5 %collective-permute-start.13 = (f32[256,128]{1,0:T(8,128)S(1)}, f32[256,128]{1,0:T(8,128)S(1)}, u32[]{:S(2)}, u32[]{:S(2)}) collective-permute-start(f32[256,128]{1,0:T(8,128)S(1)} %maximum_select_fusion), channel_id=1, source_target_pairs={{0,8},{1,9},{16,24},{17,25},{32,40},{33,41},{48,56},{49,57},{64,72... | collective-permute-start | bytes 393224 | tf_op jit(solution)/shard_map/ppermute | solution.py:88
  21.3 1.3 %collective-permute-start.14 = (f32[256,128]{1,0:T(8,128)S(1)}, f32[256,128]{1,0:T(8,128)S(1)}, u32[]{:S(2)}, u32[]{:S(2)}) collective-permute-start(f32[256,128]{1,0:T(8,128)S(1)} %maximum_select_fusion), channel_id=1, source_target_pairs={{0,4},{1,5},{16,20},{17,21},{32,36},{33,37},{48,52},{49,53},{64,68... | collective-permute-start | bytes 393224 | tf_op jit(solution)/shard_map/ppermute | solution.py:88
  22.6 4.5 %collective-permute-done.8 = f32[96,128]{1,0:T(8,128)S(1)} collective-permute-done((f32[96,128]{1,0:T(8,128)S(1)}, f32[96,128]{1,0:T(8,128)S(1)}, u32[]{:S(2)}, u32[]{:S(2)}) %collective-permute-start.8) | collective-permute-done | bytes 49184 | tf_op jit(solution)/shard_map/ppermute | solution.py:11
  27.2 1.3 %collective-permute-start.10 = (f32[96,128]{1,0:T(8,128)S(1)}, f32[96,128]{1,0:T(8,128)S(1)}, u32[]{:S(2)}, u32[]{:S(2)}) collective-permute-start(f32[96,128]{1,0:T(8,128)S(1)} %add_add_fusion.4), channel_id=1, source_target_pairs={{0,64},{1,65},{8,72},{9,73},{16,80},{17,81},{24,88},{25,89},{128,1... | collective-permute-start | bytes 147464 | tf_op jit(solution)/shard_map/ppermute | solution.py:11
  28.5 1.3 %collective-permute-start.11 = (f32[96,128]{1,0:T(8,128)S(1)}, f32[96,128]{1,0:T(8,128)S(1)}, u32[]{:S(2)}, u32[]{:S(2)}) collective-permute-start(f32[96,128]{1,0:T(8,128)S(1)} %add_add_fusion.4), channel_id=1, source_target_pairs={{0,4},{1,5},{8,12},{9,13},{16,20},{17,21},{24,28},{25,29},{128,132... | collective-permute-start | bytes 147464 | tf_op jit(solution)/shard_map/ppermute | solution.py:11
  29.8 1.3 %collective-permute-start.12 = (f32[96,128]{1,0:T(8,128)S(1)}, f32[96,128]{1,0:T(8,128)S(1)}, u32[]{:S(2)}, u32[]{:S(2)}) collective-permute-start(f32[96,128]{1,0:T(8,128)S(1)} %add_add_fusion.4), channel_id=1, source_target_pairs={{0,68},{1,69},{8,76},{9,77},{16,84},{17,85},{24,92},{25,93},{128,1... | collective-permute-start | bytes 147464 | tf_op jit(solution)/shard_map/ppermute | solution.py:11
  31.1 1.3 %collective-permute-start.15 = (f32[256,128]{1,0:T(8,128)S(1)}, f32[256,128]{1,0:T(8,128)S(1)}, u32[]{:S(2)}, u32[]{:S(2)}) collective-permute-start(f32[256,128]{1,0:T(8,128)S(1)} %add_add_fusion.1), channel_id=1, source_target_pairs={{0,2},{1,3},{4,6},{5,7},{8,10},{9,11},{16,18},{17,19},{20,22},{21,... | collective-permute-start | bytes 393224 | tf_op jit(solution)/shard_map/ppermute | solution.py:88
  32.4 0.7 collective-permute-start.16
  33.2 1.8 %collective-permute-done.15 = f32[256,128]{1,0:T(8,128)S(1)} collective-permute-done((f32[256,128]{1,0:T(8,128)S(1)}, f32[256,128]{1,0:T(8,128)S(1)}, u32[]{:S(2)}, u32[]{:S(2)}) %collective-permute-start.15) | collective-permute-done | bytes 131104 | tf_op jit(solution)/shard_map/ppermute | solution.py:88
  35.0 1.3 %collective-permute-start.17 = (f32[96,128]{1,0:T(8,128)S(1)}, f32[96,128]{1,0:T(8,128)S(1)}, u32[]{:S(2)}, u32[]{:S(2)}) collective-permute-start(f32[96,128]{1,0:T(8,128)S(1)} %add_add_fusion.3), channel_id=1, source_target_pairs={{0,32},{1,33},{4,36},{5,37},{8,40},{9,41},{12,44},{13,45},{16,48},... | collective-permute-start | bytes 147464 | tf_op jit(solution)/shard_map/ppermute | solution.py:11
  36.3 3.7 %collective-permute-start.18 = (f32[96,128]{1,0:T(8,128)S(1)}, f32[96,128]{1,0:T(8,128)S(1)}, u32[]{:S(2)}, u32[]{:S(2)}) collective-permute-start(f32[96,128]{1,0:T(8,128)S(1)} %add_add_fusion.3), channel_id=1, source_target_pairs={{0,2},{1,3},{4,6},{5,7},{8,10},{9,11},{12,14},{13,15},{16,18},{17,... | collective-permute-start | bytes 147464 | tf_op jit(solution)/shard_map/ppermute | solution.py:11
  40.0 1.3 %collective-permute-start.19 = (f32[96,128]{1,0:T(8,128)S(1)}, f32[96,128]{1,0:T(8,128)S(1)}, u32[]{:S(2)}, u32[]{:S(2)}) collective-permute-start(f32[96,128]{1,0:T(8,128)S(1)} %add_add_fusion.3), channel_id=1, source_target_pairs={{0,34},{1,35},{4,38},{5,39},{8,42},{9,43},{12,46},{13,47},{16,50},... | collective-permute-start | bytes 147464 | tf_op jit(solution)/shard_map/ppermute | solution.py:11
  41.3 8.8 %collective-permute-start.20 = (f32[256,128]{1,0:T(8,128)S(1)}, f32[256,128]{1,0:T(8,128)S(1)}, u32[]{:S(2)}, u32[]{:S(2)}) collective-permute-start(f32[256,128]{1,0:T(8,128)S(1)} %add_add_fusion), channel_id=1, source_target_pairs={{0,0},{16,1},{32,2},{48,3},{64,4},{80,5},{96,6},{112,7},{128,8},{1... | collective-permute-start | bytes 393224 | tf_op jit(solution)/shard_map/ppermute | solution.py:11
  50.1 7.2 %collective-permute-start.21 = (f32[256,128]{1,0:T(8,128)S(1)}, f32[256,128]{1,0:T(8,128)S(1)}, u32[]{:S(2)}, u32[]{:S(2)}) collective-permute-start(f32[256,128]{1,0:T(8,128)S(1)} %add_add_fusion), channel_id=1, source_target_pairs={{0,256},{16,257},{32,258},{48,259},{64,260},{80,261},{96,262},{112... | collective-permute-start | bytes 393224 | tf_op jit(solution)/shard_map/ppermute | solution.py:11
  58.1 11.7 %cholesky.18 = f32[128,128]{1,0:T(8,128)S(1)} custom-call(f32[128,128]{1,0:T(8,128)S(1)} %fusion.3), custom_call_target="Cholesky" | custom-call | tf_op jit(solution)/shard_map/jit(cholesky)/cholesky | solution.py:112
  70.5 0.7 select_select_fusion
  71.3 9.8 %custom-call.7 = f32[2,1,64,64]{2,3,1,0:T(8,128)S(1)} custom-call(f32[2,1,64,64]{3,2,1,0:T(8,128)S(1)} %maximum_select_fusion.3), custom_call_target="InvertDiagBlocksLowerTriangular" | custom-call | tf_op jit(solution)/shard_map/jit(_solve_triangular)/vmap()/triangular_solve | solution.py:116
  84.0 1.0 %pad_maximum_fusion = f32[256,512]{1,0:T(8,128)} fusion(f32[256,448]{1,0:T(8,128)S(1)} %slice.109, f32[256,64]{1,0:T(8,128)S(1)} %slice_select_fusion), kind=kLoop, calls=%fused_computation.3 | loop fusion | flops 131072 | bytes 1048576 | tf_op jit(solution)/shard_map/concatenate | solution.py:145
  (69 shorter events, 4.8 us)
Async XLA Ops:
  0.0 7.2 %copy-start = (f32[256,512]{1,0:T(8,128)S(1)}, f32[256,512]{1,0:T(8,128)}, u32[]{:S(2)}) copy-start(f32[256,512]{1,0:T(8,128)} %param.1) | copy-start | bytes 1572868
  0.8 4.3 %collective-permute-start.1 = (f32[64,64]{1,0:T(8,128)S(1)}, f32[64,64]{1,0:T(8,128)S(1)}, u32[]{:S(2)}, u32[]{:S(2)}) collective-permute-start(f32[64,64]{1,0:T(8,128)S(1)} %slice.78), channel_id=1, source_target_pairs={{17,0},{0,16}} | collective-permute-start | bytes 49160 | tf_op jit(solution)/shard_map/ppermute | solution.py:11
  1.5 3.6 %collective-permute-start.2 = (f32[64,64]{1,0:T(8,128)S(1)}, f32[64,64]{1,0:T(8,128)S(1)}, u32[]{:S(2)}, u32[]{:S(2)}) collective-permute-start(f32[64,64]{1,0:T(8,128)S(1)} %slice.78), channel_id=1, source_target_pairs={{17,1},{0,17}} | collective-permute-start | bytes 49160 | tf_op jit(solution)/shard_map/ppermute | solution.py:11
  3.1 3.2 %collective-permute-start = (f32[256,64]{1,0:T(8,128)S(1)}, f32[256,64]{1,0:T(8,128)S(1)}, u32[]{:S(2)}, u32[]{:S(2)}) collective-permute-start(f32[256,64]{1,0:T(8,128)S(1)} %slice.79), channel_id=1, source_target_pairs={{0,1},{1,0},{16,17},{17,16},{32,33},{33,32},{48,49},{49,48},{64,65... | collective-permute-start | bytes 196616 | tf_op jit(solution)/shard_map/ppermute | solution.py:67
  7.3 3.4 %collective-permute-start.3 = (f32[96,128]{1,0:T(8,128)S(1)}, f32[96,128]{1,0:T(8,128)S(1)}, u32[]{:S(2)}, u32[]{:S(2)}) collective-permute-start(f32[96,128]{1,0:T(8,128)S(1)} %select_n.138), channel_id=1, source_target_pairs={{0,8},{1,9},{16,24},{17,25}} | collective-permute-start | bytes 147464 | tf_op jit(solution)/shard_map/ppermute | solution.py:11
  8.0 4.0 %collective-permute-start.4 = (f32[96,128]{1,0:T(8,128)S(1)}, f32[96,128]{1,0:T(8,128)S(1)}, u32[]{:S(2)}, u32[]{:S(2)}) collective-permute-start(f32[96,128]{1,0:T(8,128)S(1)} %select_n.138), channel_id=1, source_target_pairs={{0,128},{1,129},{16,144},{17,145}} | collective-permute-start | bytes 147464 | tf_op jit(solution)/shard_map/ppermute | solution.py:11
  8.6 4.2 %collective-permute-start.5 = (f32[96,128]{1,0:T(8,128)S(1)}, f32[96,128]{1,0:T(8,128)S(1)}, u32[]{:S(2)}, u32[]{:S(2)}) collective-permute-start(f32[96,128]{1,0:T(8,128)S(1)} %select_n.138), channel_id=1, source_target_pairs={{0,136},{1,137},{16,152},{17,153}} | collective-permute-start | bytes 147464 | tf_op jit(solution)/shard_map/ppermute | solution.py:11
  9.3 12.0 %collective-permute-start.6 = (f32[96,128]{1,0:T(8,128)S(1)}, f32[96,128]{1,0:T(8,128)S(1)}, u32[]{:S(2)}, u32[]{:S(2)}) collective-permute-start(f32[96,128]{1,0:T(8,128)S(1)} %select_n.138), channel_id=1, source_target_pairs={{0,256},{1,257},{16,272},{17,273}} | collective-permute-start | bytes 147464 | tf_op jit(solution)/shard_map/ppermute | solution.py:11
  10.0 12.6 %collective-permute-start.7 = (f32[96,128]{1,0:T(8,128)S(1)}, f32[96,128]{1,0:T(8,128)S(1)}, u32[]{:S(2)}, u32[]{:S(2)}) collective-permute-start(f32[96,128]{1,0:T(8,128)S(1)} %select_n.138), channel_id=1, source_target_pairs={{0,264},{1,265},{16,280},{17,281}} | collective-permute-start | bytes 147464 | tf_op jit(solution)/shard_map/ppermute | solution.py:11
  10.7 16.4 %collective-permute-start.8 = (f32[96,128]{1,0:T(8,128)S(1)}, f32[96,128]{1,0:T(8,128)S(1)}, u32[]{:S(2)}, u32[]{:S(2)}) collective-permute-start(f32[96,128]{1,0:T(8,128)S(1)} %select_n.138), channel_id=1, source_target_pairs={{0,384},{1,385},{16,400},{17,401}} | collective-permute-start | bytes 147464 | tf_op jit(solution)/shard_map/ppermute | solution.py:11
  12.0 15.1 %collective-permute-start.9 = (f32[96,128]{1,0:T(8,128)S(1)}, f32[96,128]{1,0:T(8,128)S(1)}, u32[]{:S(2)}, u32[]{:S(2)}) collective-permute-start(f32[96,128]{1,0:T(8,128)S(1)} %select_n.138), channel_id=1, source_target_pairs={{0,392},{1,393},{16,408},{17,409}} | collective-permute-start | bytes 147464 | tf_op jit(solution)/shard_map/ppermute | solution.py:11
  12.8 18.3 %collective-permute-start.13 = (f32[256,128]{1,0:T(8,128)S(1)}, f32[256,128]{1,0:T(8,128)S(1)}, u32[]{:S(2)}, u32[]{:S(2)}) collective-permute-start(f32[256,128]{1,0:T(8,128)S(1)} %maximum_select_fusion), channel_id=1, source_target_pairs={{0,8},{1,9},{16,24},{17,25},{32,40},{33,41},{48,56},{49,57},{64,72... | collective-permute-start | bytes 393224 | tf_op jit(solution)/shard_map/ppermute | solution.py:88
  21.3 9.8 %collective-permute-start.14 = (f32[256,128]{1,0:T(8,128)S(1)}, f32[256,128]{1,0:T(8,128)S(1)}, u32[]{:S(2)}, u32[]{:S(2)}) collective-permute-start(f32[256,128]{1,0:T(8,128)S(1)} %maximum_select_fusion), channel_id=1, source_target_pairs={{0,4},{1,5},{16,20},{17,21},{32,36},{33,37},{48,52},{49,53},{64,68... | collective-permute-start | bytes 393224 | tf_op jit(solution)/shard_map/ppermute | solution.py:88
  27.2 5.9 %collective-permute-start.10 = (f32[96,128]{1,0:T(8,128)S(1)}, f32[96,128]{1,0:T(8,128)S(1)}, u32[]{:S(2)}, u32[]{:S(2)}) collective-permute-start(f32[96,128]{1,0:T(8,128)S(1)} %add_add_fusion.4), channel_id=1, source_target_pairs={{0,64},{1,65},{8,72},{9,73},{16,80},{17,81},{24,88},{25,89},{128,1... | collective-permute-start | bytes 147464 | tf_op jit(solution)/shard_map/ppermute | solution.py:11
  28.5 4.6 %collective-permute-start.11 = (f32[96,128]{1,0:T(8,128)S(1)}, f32[96,128]{1,0:T(8,128)S(1)}, u32[]{:S(2)}, u32[]{:S(2)}) collective-permute-start(f32[96,128]{1,0:T(8,128)S(1)} %add_add_fusion.4), channel_id=1, source_target_pairs={{0,4},{1,5},{8,12},{9,13},{16,20},{17,21},{24,28},{25,29},{128,132... | collective-permute-start | bytes 147464 | tf_op jit(solution)/shard_map/ppermute | solution.py:11
  29.8 3.4 %collective-permute-start.12 = (f32[96,128]{1,0:T(8,128)S(1)}, f32[96,128]{1,0:T(8,128)S(1)}, u32[]{:S(2)}, u32[]{:S(2)}) collective-permute-start(f32[96,128]{1,0:T(8,128)S(1)} %add_add_fusion.4), channel_id=1, source_target_pairs={{0,68},{1,69},{8,76},{9,77},{16,84},{17,85},{24,92},{25,93},{128,1... | collective-permute-start | bytes 147464 | tf_op jit(solution)/shard_map/ppermute | solution.py:11
  31.1 3.8 %collective-permute-start.15 = (f32[256,128]{1,0:T(8,128)S(1)}, f32[256,128]{1,0:T(8,128)S(1)}, u32[]{:S(2)}, u32[]{:S(2)}) collective-permute-start(f32[256,128]{1,0:T(8,128)S(1)} %add_add_fusion.1), channel_id=1, source_target_pairs={{0,2},{1,3},{4,6},{5,7},{8,10},{9,11},{16,18},{17,19},{20,22},{21,... | collective-permute-start | bytes 393224 | tf_op jit(solution)/shard_map/ppermute | solution.py:88
  32.4 2.5 %collective-permute-start.16 = (f32[256,128]{1,0:T(8,128)S(1)}, f32[256,128]{1,0:T(8,128)S(1)}, u32[]{:S(2)}, u32[]{:S(2)}) collective-permute-start(f32[256,128]{1,0:T(8,128)S(1)} %add_add_fusion.1), channel_id=1, source_target_pairs={{8,12},{9,13},{4,14},{5,15},{24,28},{25,29},{20,30},{21,31},{40,44... | collective-permute-start | bytes 393224 | tf_op jit(solution)/shard_map/ppermute | solution.py:88
  35.0 22.3 %collective-permute-start.17 = (f32[96,128]{1,0:T(8,128)S(1)}, f32[96,128]{1,0:T(8,128)S(1)}, u32[]{:S(2)}, u32[]{:S(2)}) collective-permute-start(f32[96,128]{1,0:T(8,128)S(1)} %add_add_fusion.3), channel_id=1, source_target_pairs={{0,32},{1,33},{4,36},{5,37},{8,40},{9,41},{12,44},{13,45},{16,48},... | collective-permute-start | bytes 147464 | tf_op jit(solution)/shard_map/ppermute | solution.py:11
  36.3 21.0 %collective-permute-start.18 = (f32[96,128]{1,0:T(8,128)S(1)}, f32[96,128]{1,0:T(8,128)S(1)}, u32[]{:S(2)}, u32[]{:S(2)}) collective-permute-start(f32[96,128]{1,0:T(8,128)S(1)} %add_add_fusion.3), channel_id=1, source_target_pairs={{0,2},{1,3},{4,6},{5,7},{8,10},{9,11},{12,14},{13,15},{16,18},{17,... | collective-permute-start | bytes 147464 | tf_op jit(solution)/shard_map/ppermute | solution.py:11
  40.0 17.3 %collective-permute-start.19 = (f32[96,128]{1,0:T(8,128)S(1)}, f32[96,128]{1,0:T(8,128)S(1)}, u32[]{:S(2)}, u32[]{:S(2)}) collective-permute-start(f32[96,128]{1,0:T(8,128)S(1)} %add_add_fusion.3), channel_id=1, source_target_pairs={{0,34},{1,35},{4,38},{5,39},{8,42},{9,43},{12,46},{13,47},{16,50},... | collective-permute-start | bytes 147464 | tf_op jit(solution)/shard_map/ppermute | solution.py:11
  41.3 41.8 %collective-permute-start.20 = (f32[256,128]{1,0:T(8,128)S(1)}, f32[256,128]{1,0:T(8,128)S(1)}, u32[]{:S(2)}, u32[]{:S(2)}) collective-permute-start(f32[256,128]{1,0:T(8,128)S(1)} %add_add_fusion), channel_id=1, source_target_pairs={{0,0},{16,1},{32,2},{48,3},{64,4},{80,5},{96,6},{112,7},{128,8},{1... | collective-permute-start | bytes 393224 | tf_op jit(solution)/shard_map/ppermute | solution.py:11
  50.1 33.0 %collective-permute-start.21 = (f32[256,128]{1,0:T(8,128)S(1)}, f32[256,128]{1,0:T(8,128)S(1)}, u32[]{:S(2)}, u32[]{:S(2)}) collective-permute-start(f32[256,128]{1,0:T(8,128)S(1)} %add_add_fusion), channel_id=1, source_target_pairs={{0,256},{16,257},{32,258},{48,259},{64,260},{80,261},{96,262},{112... | collective-permute-start | bytes 393224 | tf_op jit(solution)/shard_map/ppermute | solution.py:11

commit v15 on v10

--- a/solution.py
+++ b/solution.py
@@ -27,7 +27,27 @@
     a00 = jnp.where(p == 0, u, sent)
     a10 = jnp.where(p == 0, t.T, u)
     a11 = jnp.where(p == 0, sent, t)
-    return jnp.concatenate([a00, a10, a11], axis=0).reshape(3 * NB // 2, 2 * NB)
+    return pack_corner(a00, a10, a11)
+
+
+def pack_corner(a00, a10, a11):
+    r = lax.broadcasted_iota(jnp.int32, (NB, NB), 0)
+    c = lax.broadcasted_iota(jnp.int32, (NB, NB), 1)
+    shared = jnp.where(r >= c, a00, a11)
+    diag = jnp.sum(jnp.where(r == c, a11, 0.0), axis=0, keepdims=True)
+    last = jnp.concatenate([diag, jnp.zeros((1, NB), jnp.float32)], axis=1)
+    return jnp.concatenate([jnp.concatenate([shared, a10], axis=1), last], axis=0)
+
+
+def unpack_corner(packed):
+    r = lax.broadcasted_iota(jnp.int32, (NB, NB), 0)
+    c = lax.broadcasted_iota(jnp.int32, (NB, NB), 1)
+    shared = packed[:NB, :NB]
+    a10 = packed[:NB, NB:]
+    diag = packed[NB:, :NB]
+    a00 = jnp.where(r >= c, shared, shared.T)
+    a11 = jnp.where(r == c, diag, jnp.where(r < c, shared, shared.T))
+    return a00, a10, a11
 
 
 def spread_round(value, holders, offsets, ncols):
@@ -102,10 +122,7 @@
     first = both_axes(panel, first_pairs)
     second = both_axes(panel, second_pairs)
 
-    corner = corner.reshape(3 * NB, NB)
-    a00 = corner[:NB]
-    a10 = corner[NB : 2 * NB]
-    a11 = corner[2 * NB :]
+    a00, a10, a11 = unpack_corner(corner)
     lead_block = jnp.concatenate(
         [jnp.concatenate([a00, a10.T], axis=1), jnp.concatenate([a10, a11], axis=1)], axis=0
     )

time: 85.1 us -> 84.6 us (level)
  no operation moved by 1% of the time
where the time goes in v15:
time: 84.6 us; the launch traced here: 84 us
  starting transfers between devices  46.4 us (55%)
  other arithmetic  25.4 us (30%)
  waiting for transfers between devices  7.32 us (9%)
  local copies, waits for them, and re-layouts  2.72 us (3%)
  matrix products  1.56 us (2%)
    ppermute x17, starting transfers between devices, both_axes(): return lax.ppermute(x, ('row', 'col'), pairs)  32.8 us
    another operation x3, other arithmetic, per_device(): factor = jnp.linalg.cholesky(lead_block)  12.4 us
    ppermute x4, starting transfers between devices, per_device(): panel = panel + lax.ppermute(sent, 'col', pairs)  11.7 us
    another operation x2, other arithmetic, lower_inverse(): return jax.scipy.linalg.solve_triangular(factor, eye, lower=True)  10.5 us
    ppermute x17, waiting for transfers between devices, both_axes(): return lax.ppermute(x, ('row', 'col'), pairs)  4.29 us
    ppermute x1, starting transfers between devices, per_device(): swapped = lax.ppermute(mine, 'col', [(0, 1), (1, 0)])  1.92 us
    ppermute x4, waiting for transfers between devices, per_device(): panel = panel + lax.ppermute(sent, 'col', pairs)  1.78 us
  transfers between devices with their start and end apart: 22, of which 3 were waited for; matrix products, arithmetic and copies ran while one was open for 31% of the time, Pallas kernels for 0%

profile of v15, /device:TPU:48, one launch (start us, length us, event | category | flops | bytes accessed | tf_op | source)
XLA Modules:
  0.0 84.0 jit_solution(14189843120002672207)
XLA Ops:
  0.0 0.8 slice.60
  0.8 0.7 collective-permute-start.1
  1.5 0.7 collective-permute-start.2
  2.2 0.9 %slice.61 = f32[256,64]{1,0:T(8,128)S(1)} slice(f32[256,512]{1,0:T(8,128)} %param.1), slice={[0:256], [0:64]} | slice | bytes 131072 | tf_op jit(solution)/shard_map/slice | solution.py:86
  3.1 1.9 %collective-permute-start = (f32[256,64]{1,0:T(8,128)S(1)}, f32[256,64]{1,0:T(8,128)S(1)}, u32[]{:S(2)}, u32[]{:S(2)}) collective-permute-start(f32[256,64]{1,0:T(8,128)S(1)} %slice.61), channel_id=1, source_target_pairs={{0,1},{1,0},{16,17},{17,16},{32,33},{33,32},{48,49},{49,48},{64,65... | collective-permute-start | bytes 196616 | tf_op jit(solution)/shard_map/ppermute | solution.py:87
  5.1 1.2 %collective-permute-done = f32[256,64]{1,0:T(8,128)S(1)} collective-permute-done((f32[256,64]{1,0:T(8,128)S(1)}, f32[256,64]{1,0:T(8,128)S(1)}, u32[]{:S(2)}, u32[]{:S(2)}) %collective-permute-start) | collective-permute-done | bytes 65568 | tf_op jit(solution)/shard_map/ppermute | solution.py:87
  6.3 0.8 select_select_fusion.1
  7.3 0.7 collective-permute-start.3
  8.0 0.7 collective-permute-start.4
  8.6 0.7 collective-permute-start.5
  9.3 0.7 collective-permute-start.6
  10.0 0.7 collective-permute-start.7
  10.7 1.3 %collective-permute-start.8 = (f32[65,128]{1,0:T(8,128)S(1)}, f32[65,128]{1,0:T(8,128)S(1)}, u32[]{:S(2)}, u32[]{:S(2)}) collective-permute-start(f32[65,128]{1,0:T(8,128)S(1)} %fusion.4), channel_id=1, source_target_pairs={{0,384},{1,385},{16,400},{17,401}} | collective-permute-start | bytes 99848 | tf_op jit(solution)/shard_map/ppermute | solution.py:11
  12.0 0.7 collective-permute-start.9
  12.8 8.4 %collective-permute-start.13 = (f32[256,128]{1,0:T(8,128)S(1)}, f32[256,128]{1,0:T(8,128)S(1)}, u32[]{:S(2)}, u32[]{:S(2)}) collective-permute-start(f32[256,128]{1,0:T(8,128)S(1)} %maximum_select_fusion), channel_id=1, source_target_pairs={{0,8},{1,9},{16,24},{17,25},{32,40},{33,41},{48,56},{49,57},{64,72... | collective-permute-start | bytes 393224 | tf_op jit(solution)/shard_map/ppermute | solution.py:108
  21.2 1.3 %collective-permute-start.14 = (f32[256,128]{1,0:T(8,128)S(1)}, f32[256,128]{1,0:T(8,128)S(1)}, u32[]{:S(2)}, u32[]{:S(2)}) collective-permute-start(f32[256,128]{1,0:T(8,128)S(1)} %maximum_select_fusion), channel_id=1, source_target_pairs={{0,4},{1,5},{16,20},{17,21},{32,36},{33,37},{48,52},{49,53},{64,68... | collective-permute-start | bytes 393224 | tf_op jit(solution)/shard_map/ppermute | solution.py:108
  22.6 4.3 %collective-permute-done.8 = f32[65,128]{1,0:T(8,128)S(1)} collective-permute-done((f32[65,128]{1,0:T(8,128)S(1)}, f32[65,128]{1,0:T(8,128)S(1)}, u32[]{:S(2)}, u32[]{:S(2)}) %collective-permute-start.8) | collective-permute-done | bytes 33312 | tf_op jit(solution)/shard_map/ppermute | solution.py:11
  26.8 1.3 %collective-permute-start.10 = (f32[65,128]{1,0:T(8,128)S(1)}, f32[65,128]{1,0:T(8,128)S(1)}, u32[]{:S(2)}, u32[]{:S(2)}) collective-permute-start(f32[65,128]{1,0:T(8,128)S(1)} %add_add_fusion.4), channel_id=1, source_target_pairs={{0,64},{1,65},{8,72},{9,73},{16,80},{17,81},{24,88},{25,89},{128,1... | collective-permute-start | bytes 99848 | tf_op jit(solution)/shard_map/ppermute | solution.py:11
  28.1 1.3 %collective-permute-start.11 = (f32[65,128]{1,0:T(8,128)S(1)}, f32[65,128]{1,0:T(8,128)S(1)}, u32[]{:S(2)}, u32[]{:S(2)}) collective-permute-start(f32[65,128]{1,0:T(8,128)S(1)} %add_add_fusion.4), channel_id=1, source_target_pairs={{0,4},{1,5},{8,12},{9,13},{16,20},{17,21},{24,28},{25,29},{128,132... | collective-permute-start | bytes 99848 | tf_op jit(solution)/shard_map/ppermute | solution.py:11
  29.4 1.3 %collective-permute-start.12 = (f32[65,128]{1,0:T(8,128)S(1)}, f32[65,128]{1,0:T(8,128)S(1)}, u32[]{:S(2)}, u32[]{:S(2)}) collective-permute-start(f32[65,128]{1,0:T(8,128)S(1)} %add_add_fusion.4), channel_id=1, source_target_pairs={{0,68},{1,69},{8,76},{9,77},{16,84},{17,85},{24,92},{25,93},{128,1... | collective-permute-start | bytes 99848 | tf_op jit(solution)/shard_map/ppermute | solution.py:11
  30.8 1.3 %collective-permute-start.15 = (f32[256,128]{1,0:T(8,128)S(1)}, f32[256,128]{1,0:T(8,128)S(1)}, u32[]{:S(2)}, u32[]{:S(2)}) collective-permute-start(f32[256,128]{1,0:T(8,128)S(1)} %add_add_fusion.1), channel_id=1, source_target_pairs={{0,2},{1,3},{4,6},{5,7},{8,10},{9,11},{16,18},{17,19},{20,22},{21,... | collective-permute-start | bytes 393224 | tf_op jit(solution)/shard_map/ppermute | solution.py:108
  32.1 0.7 collective-permute-start.16
  32.8 1.8 %collective-permute-done.15 = f32[256,128]{1,0:T(8,128)S(1)} collective-permute-done((f32[256,128]{1,0:T(8,128)S(1)}, f32[256,128]{1,0:T(8,128)S(1)}, u32[]{:S(2)}, u32[]{:S(2)}) %collective-permute-start.15) | collective-permute-done | bytes 131104 | tf_op jit(solution)/shard_map/ppermute | solution.py:108
  34.6 1.3 %collective-permute-start.17 = (f32[65,128]{1,0:T(8,128)S(1)}, f32[65,128]{1,0:T(8,128)S(1)}, u32[]{:S(2)}, u32[]{:S(2)}) collective-permute-start(f32[65,128]{1,0:T(8,128)S(1)} %add_add_fusion.3), channel_id=1, source_target_pairs={{0,32},{1,33},{4,36},{5,37},{8,40},{9,41},{12,44},{13,45},{16,48},... | collective-permute-start | bytes 99848 | tf_op jit(solution)/shard_map/ppermute | solution.py:11
  35.9 3.7 %collective-permute-start.18 = (f32[65,128]{1,0:T(8,128)S(1)}, f32[65,128]{1,0:T(8,128)S(1)}, u32[]{:S(2)}, u32[]{:S(2)}) collective-permute-start(f32[65,128]{1,0:T(8,128)S(1)} %add_add_fusion.3), channel_id=1, source_target_pairs={{0,2},{1,3},{4,6},{5,7},{8,10},{9,11},{12,14},{13,15},{16,18},{17,... | collective-permute-start | bytes 99848 | tf_op jit(solution)/shard_map/ppermute | solution.py:11
  39.7 1.3 %collective-permute-start.19 = (f32[65,128]{1,0:T(8,128)S(1)}, f32[65,128]{1,0:T(8,128)S(1)}, u32[]{:S(2)}, u32[]{:S(2)}) collective-permute-start(f32[65,128]{1,0:T(8,128)S(1)} %add_add_fusion.3), channel_id=1, source_target_pairs={{0,34},{1,35},{4,38},{5,39},{8,42},{9,43},{12,46},{13,47},{16,50},... | collective-permute-start | bytes 99848 | tf_op jit(solution)/shard_map/ppermute | solution.py:11
  41.0 9.0 %collective-permute-start.20 = (f32[256,128]{1,0:T(8,128)S(1)}, f32[256,128]{1,0:T(8,128)S(1)}, u32[]{:S(2)}, u32[]{:S(2)}) collective-permute-start(f32[256,128]{1,0:T(8,128)S(1)} %add_add_fusion), channel_id=1, source_target_pairs={{0,0},{16,1},{32,2},{48,3},{64,4},{80,5},{96,6},{112,7},{128,8},{1... | collective-permute-start | bytes 393224 | tf_op jit(solution)/shard_map/ppermute | solution.py:11
  49.9 7.1 %collective-permute-start.21 = (f32[256,128]{1,0:T(8,128)S(1)}, f32[256,128]{1,0:T(8,128)S(1)}, u32[]{:S(2)}, u32[]{:S(2)}) collective-permute-start(f32[256,128]{1,0:T(8,128)S(1)} %add_add_fusion), channel_id=1, source_target_pairs={{0,256},{16,257},{32,258},{48,259},{64,260},{80,261},{96,262},{112... | collective-permute-start | bytes 393224 | tf_op jit(solution)/shard_map/ppermute | solution.py:11
  57.6 11.7 %cholesky.20 = f32[128,128]{1,0:T(8,128)S(1)} custom-call(f32[128,128]{1,0:T(8,128)S(1)} %fusion.3), custom_call_target="Cholesky" | custom-call | tf_op jit(solution)/shard_map/jit(cholesky)/cholesky | solution.py:129
  70.0 0.7 select_bitcast_fusion
  70.7 9.8 %custom-call.7 = f32[1,128,128]{1,2,0:T(8,128)S(1)} custom-call(f32[1,128,128]{2,1,0:T(8,128)S(1)} %get-tuple-element.13), custom_call_target="InvertDiagBlocksLowerTriangular" | custom-call | tf_op jit(solution)/shard_map/jit(_solve_triangular)/triangular_solve | solution.py:71
  83.0 1.0 %pad_maximum_fusion = f32[256,512]{1,0:T(8,128)} fusion(f32[256,448]{1,0:T(8,128)S(1)} %slice.82, f32[256,64]{1,0:T(8,128)S(1)} %slice_select_fusion), kind=kLoop, calls=%fused_computation.2 | loop fusion | flops 131072 | bytes 1048576 | tf_op jit(solution)/shard_map/concatenate | solution.py:155
  (59 shorter events, 4.0 us)
Async XLA Ops:
  0.0 7.2 %copy-start = (f32[256,512]{1,0:T(8,128)S(1)}, f32[256,512]{1,0:T(8,128)}, u32[]{:S(2)}) copy-start(f32[256,512]{1,0:T(8,128)} %param.1) | copy-start | bytes 1572868
  0.8 4.2 %collective-permute-start.1 = (f32[64,64]{1,0:T(8,128)S(1)}, f32[64,64]{1,0:T(8,128)S(1)}, u32[]{:S(2)}, u32[]{:S(2)}) collective-permute-start(f32[64,64]{1,0:T(8,128)S(1)} %slice.60), channel_id=1, source_target_pairs={{17,0},{0,16}} | collective-permute-start | bytes 49160 | tf_op jit(solution)/shard_map/ppermute | solution.py:11
  1.5 3.6 %collective-permute-start.2 = (f32[64,64]{1,0:T(8,128)S(1)}, f32[64,64]{1,0:T(8,128)S(1)}, u32[]{:S(2)}, u32[]{:S(2)}) collective-permute-start(f32[64,64]{1,0:T(8,128)S(1)} %slice.60), channel_id=1, source_target_pairs={{17,1},{0,17}} | collective-permute-start | bytes 49160 | tf_op jit(solution)/shard_map/ppermute | solution.py:11
  3.1 3.2 %collective-permute-start = (f32[256,64]{1,0:T(8,128)S(1)}, f32[256,64]{1,0:T(8,128)S(1)}, u32[]{:S(2)}, u32[]{:S(2)}) collective-permute-start(f32[256,64]{1,0:T(8,128)S(1)} %slice.61), channel_id=1, source_target_pairs={{0,1},{1,0},{16,17},{17,16},{32,33},{33,32},{48,49},{49,48},{64,65... | collective-permute-start | bytes 196616 | tf_op jit(solution)/shard_map/ppermute | solution.py:87
  7.3 3.4 %collective-permute-start.3 = (f32[65,128]{1,0:T(8,128)S(1)}, f32[65,128]{1,0:T(8,128)S(1)}, u32[]{:S(2)}, u32[]{:S(2)}) collective-permute-start(f32[65,128]{1,0:T(8,128)S(1)} %fusion.4), channel_id=1, source_target_pairs={{0,8},{1,9},{16,24},{17,25}} | collective-permute-start | bytes 99848 | tf_op jit(solution)/shard_map/ppermute | solution.py:11
  8.0 4.0 %collective-permute-start.4 = (f32[65,128]{1,0:T(8,128)S(1)}, f32[65,128]{1,0:T(8,128)S(1)}, u32[]{:S(2)}, u32[]{:S(2)}) collective-permute-start(f32[65,128]{1,0:T(8,128)S(1)} %fusion.4), channel_id=1, source_target_pairs={{0,128},{1,129},{16,144},{17,145}} | collective-permute-start | bytes 99848 | tf_op jit(solution)/shard_map/ppermute | solution.py:11
  8.6 4.2 %collective-permute-start.5 = (f32[65,128]{1,0:T(8,128)S(1)}, f32[65,128]{1,0:T(8,128)S(1)}, u32[]{:S(2)}, u32[]{:S(2)}) collective-permute-start(f32[65,128]{1,0:T(8,128)S(1)} %fusion.4), channel_id=1, source_target_pairs={{0,136},{1,137},{16,152},{17,153}} | collective-permute-start | bytes 99848 | tf_op jit(solution)/shard_map/ppermute | solution.py:11
  9.3 11.9 %collective-permute-start.6 = (f32[65,128]{1,0:T(8,128)S(1)}, f32[65,128]{1,0:T(8,128)S(1)}, u32[]{:S(2)}, u32[]{:S(2)}) collective-permute-start(f32[65,128]{1,0:T(8,128)S(1)} %fusion.4), channel_id=1, source_target_pairs={{0,256},{1,257},{16,272},{17,273}} | collective-permute-start | bytes 99848 | tf_op jit(solution)/shard_map/ppermute | solution.py:11
  10.0 12.6 %collective-permute-start.7 = (f32[65,128]{1,0:T(8,128)S(1)}, f32[65,128]{1,0:T(8,128)S(1)}, u32[]{:S(2)}, u32[]{:S(2)}) collective-permute-start(f32[65,128]{1,0:T(8,128)S(1)} %fusion.4), channel_id=1, source_target_pairs={{0,264},{1,265},{16,280},{17,281}} | collective-permute-start | bytes 99848 | tf_op jit(solution)/shard_map/ppermute | solution.py:11
  10.7 16.1 %collective-permute-start.8 = (f32[65,128]{1,0:T(8,128)S(1)}, f32[65,128]{1,0:T(8,128)S(1)}, u32[]{:S(2)}, u32[]{:S(2)}) collective-permute-start(f32[65,128]{1,0:T(8,128)S(1)} %fusion.4), channel_id=1, source_target_pairs={{0,384},{1,385},{16,400},{17,401}} | collective-permute-start | bytes 99848 | tf_op jit(solution)/shard_map/ppermute | solution.py:11
  12.0 14.8 %collective-permute-start.9 = (f32[65,128]{1,0:T(8,128)S(1)}, f32[65,128]{1,0:T(8,128)S(1)}, u32[]{:S(2)}, u32[]{:S(2)}) collective-permute-start(f32[65,128]{1,0:T(8,128)S(1)} %fusion.4), channel_id=1, source_target_pairs={{0,392},{1,393},{16,408},{17,409}} | collective-permute-start | bytes 99848 | tf_op jit(solution)/shard_map/ppermute | solution.py:11
  12.8 18.0 %collective-permute-start.13 = (f32[256,128]{1,0:T(8,128)S(1)}, f32[256,128]{1,0:T(8,128)S(1)}, u32[]{:S(2)}, u32[]{:S(2)}) collective-permute-start(f32[256,128]{1,0:T(8,128)S(1)} %maximum_select_fusion), channel_id=1, source_target_pairs={{0,8},{1,9},{16,24},{17,25},{32,40},{33,41},{48,56},{49,57},{64,72... | collective-permute-start | bytes 393224 | tf_op jit(solution)/shard_map/ppermute | solution.py:108
  21.2 9.5 %collective-permute-start.14 = (f32[256,128]{1,0:T(8,128)S(1)}, f32[256,128]{1,0:T(8,128)S(1)}, u32[]{:S(2)}, u32[]{:S(2)}) collective-permute-start(f32[256,128]{1,0:T(8,128)S(1)} %maximum_select_fusion), channel_id=1, source_target_pairs={{0,4},{1,5},{16,20},{17,21},{32,36},{33,37},{48,52},{49,53},{64,68... | collective-permute-start | bytes 393224 | tf_op jit(solution)/shard_map/ppermute | solution.py:108
  26.8 5.9 %collective-permute-start.10 = (f32[65,128]{1,0:T(8,128)S(1)}, f32[65,128]{1,0:T(8,128)S(1)}, u32[]{:S(2)}, u32[]{:S(2)}) collective-permute-start(f32[65,128]{1,0:T(8,128)S(1)} %add_add_fusion.4), channel_id=1, source_target_pairs={{0,64},{1,65},{8,72},{9,73},{16,80},{17,81},{24,88},{25,89},{128,1... | collective-permute-start | bytes 99848 | tf_op jit(solution)/shard_map/ppermute | solution.py:11
  28.1 4.6 %collective-permute-start.11 = (f32[65,128]{1,0:T(8,128)S(1)}, f32[65,128]{1,0:T(8,128)S(1)}, u32[]{:S(2)}, u32[]{:S(2)}) collective-permute-start(f32[65,128]{1,0:T(8,128)S(1)} %add_add_fusion.4), channel_id=1, source_target_pairs={{0,4},{1,5},{8,12},{9,13},{16,20},{17,21},{24,28},{25,29},{128,132... | collective-permute-start | bytes 99848 | tf_op jit(solution)/shard_map/ppermute | solution.py:11
  29.4 3.4 %collective-permute-start.12 = (f32[65,128]{1,0:T(8,128)S(1)}, f32[65,128]{1,0:T(8,128)S(1)}, u32[]{:S(2)}, u32[]{:S(2)}) collective-permute-start(f32[65,128]{1,0:T(8,128)S(1)} %add_add_fusion.4), channel_id=1, source_target_pairs={{0,68},{1,69},{8,76},{9,77},{16,84},{17,85},{24,92},{25,93},{128,1... | collective-permute-start | bytes 99848 | tf_op jit(solution)/shard_map/ppermute | solution.py:11
  30.8 3.8 %collective-permute-start.15 = (f32[256,128]{1,0:T(8,128)S(1)}, f32[256,128]{1,0:T(8,128)S(1)}, u32[]{:S(2)}, u32[]{:S(2)}) collective-permute-start(f32[256,128]{1,0:T(8,128)S(1)} %add_add_fusion.1), channel_id=1, source_target_pairs={{0,2},{1,3},{4,6},{5,7},{8,10},{9,11},{16,18},{17,19},{20,22},{21,... | collective-permute-start | bytes 393224 | tf_op jit(solution)/shard_map/ppermute | solution.py:108
  32.1 2.5 %collective-permute-start.16 = (f32[256,128]{1,0:T(8,128)S(1)}, f32[256,128]{1,0:T(8,128)S(1)}, u32[]{:S(2)}, u32[]{:S(2)}) collective-permute-start(f32[256,128]{1,0:T(8,128)S(1)} %add_add_fusion.1), channel_id=1, source_target_pairs={{8,12},{9,13},{4,14},{5,15},{24,28},{25,29},{20,30},{21,31},{40,44... | collective-permute-start | bytes 393224 | tf_op jit(solution)/shard_map/ppermute | solution.py:108
  34.6 22.4 %collective-permute-start.17 = (f32[65,128]{1,0:T(8,128)S(1)}, f32[65,128]{1,0:T(8,128)S(1)}, u32[]{:S(2)}, u32[]{:S(2)}) collective-permute-start(f32[65,128]{1,0:T(8,128)S(1)} %add_add_fusion.3), channel_id=1, source_target_pairs={{0,32},{1,33},{4,36},{5,37},{8,40},{9,41},{12,44},{13,45},{16,48},... | collective-permute-start | bytes 99848 | tf_op jit(solution)/shard_map/ppermute | solution.py:11
  35.9 21.1 %collective-permute-start.18 = (f32[65,128]{1,0:T(8,128)S(1)}, f32[65,128]{1,0:T(8,128)S(1)}, u32[]{:S(2)}, u32[]{:S(2)}) collective-permute-start(f32[65,128]{1,0:T(8,128)S(1)} %add_add_fusion.3), channel_id=1, source_target_pairs={{0,2},{1,3},{4,6},{5,7},{8,10},{9,11},{12,14},{13,15},{16,18},{17,... | collective-permute-start | bytes 99848 | tf_op jit(solution)/shard_map/ppermute | solution.py:11
  39.7 17.4 %collective-permute-start.19 = (f32[65,128]{1,0:T(8,128)S(1)}, f32[65,128]{1,0:T(8,128)S(1)}, u32[]{:S(2)}, u32[]{:S(2)}) collective-permute-start(f32[65,128]{1,0:T(8,128)S(1)} %add_add_fusion.3), channel_id=1, source_target_pairs={{0,34},{1,35},{4,38},{5,39},{8,42},{9,43},{12,46},{13,47},{16,50},... | collective-permute-start | bytes 99848 | tf_op jit(solution)/shard_map/ppermute | solution.py:11
  41.0 41.0 %collective-permute-start.20 = (f32[256,128]{1,0:T(8,128)S(1)}, f32[256,128]{1,0:T(8,128)S(1)}, u32[]{:S(2)}, u32[]{:S(2)}) collective-permute-start(f32[256,128]{1,0:T(8,128)S(1)} %add_add_fusion), channel_id=1, source_target_pairs={{0,0},{16,1},{32,2},{48,3},{64,4},{80,5},{96,6},{112,7},{128,8},{1... | collective-permute-start | bytes 393224 | tf_op jit(solution)/shard_map/ppermute | solution.py:11
  49.9 32.1 %collective-permute-start.21 = (f32[256,128]{1,0:T(8,128)S(1)}, f32[256,128]{1,0:T(8,128)S(1)}, u32[]{:S(2)}, u32[]{:S(2)}) collective-permute-start(f32[256,128]{1,0:T(8,128)S(1)} %add_add_fusion), channel_id=1, source_target_pairs={{0,256},{16,257},{32,258},{48,259},{64,260},{80,261},{96,262},{112... | collective-permute-start | bytes 393224 | tf_op jit(solution)/shard_map/ppermute | solution.py:11

commit v16 on v15

--- a/solution.py
+++ b/solution.py
@@ -151,8 +151,9 @@
     lead1_top = jnp.where(p == 0, zero_block, jnp.where(p == 1, c1, y_rows[:NB]))
     lead1 = jnp.concatenate([lead1_top, y_rows[NB:]], axis=0)
     lead = jnp.where(q == 0, lead0, lead1)
-    head = jnp.where(q < 2, lead, result[:, :NB])
-    return jnp.concatenate([head, result[:, NB:]], axis=1)
+    lead_wide = jnp.pad(lead, ((0, 0), (0, (col_count - 1) * NB)))
+    in_lead = (q < 2) & (jnp.arange(col_count * NB, dtype=jnp.int32)[None, :] < NB)
+    return jnp.where(in_lead, lead_wide, result)
 
 
 def solution(mesh):

time: 84.6 us -> 89.3 us (1.056)
  the two profiles are of different devices: /device:TPU:48 before, /device:TPU:17 now
where the time goes in v16:
time: 89.3 us; the launch traced here: 88.6 us
  starting transfers between devices  50.1 us (56%)
  other arithmetic  24.4 us (27%)
  waiting for transfers between devices  8.7 us (10%)
  local copies, waits for them, and re-layouts  2.51 us (3%)
  matrix products  2.37 us (3%)
    ppermute x17, starting transfers between devices, both_axes(): return lax.ppermute(x, ('row', 'col'), pairs)  37 us
    another operation x3, other arithmetic, per_device(): factor = jnp.linalg.cholesky(lead_block)  12.4 us
    ppermute x4, starting transfers between devices, per_device(): panel = panel + lax.ppermute(sent, 'col', pairs)  10.5 us
    another operation x2, other arithmetic, lower_inverse(): return jax.scipy.linalg.solve_triangular(factor, eye, lower=True)  10.5 us
    ppermute x17, waiting for transfers between devices, both_axes(): return lax.ppermute(x, ('row', 'col'), pairs)  5.95 us
    ppermute x1, starting transfers between devices, per_device(): swapped = lax.ppermute(mine, 'col', [(0, 1), (1, 0)])  2.58 us
    dot_general x3, matrix products, mm(): return jnp.dot(a, b, precision=HIGH, preferred_element_type=jnp.float32)  2.12 us
    ppermute x4, waiting for transfers between devices, per_device(): panel = panel + lax.ppermute(sent, 'col', pairs)  1.87 us
  transfers between devices with their start and end apart: 22, of which 3 were waited for; matrix products, arithmetic and copies ran while one was open for 29% of the time, Pallas kernels for 0%

profile of v16, /device:TPU:17, one launch (start us, length us, event | category | flops | bytes accessed | tf_op | source)
XLA Modules:
  0.0 88.6 jit_solution(2906396645433389478)
XLA Ops:
  0.0 0.8 slice.54
  0.8 0.7 collective-permute-start.1
  1.5 0.7 collective-permute-start.2
  2.2 0.9 %slice.55 = f32[256,64]{1,0:T(8,128)S(1)} slice(f32[256,512]{1,0:T(8,128)} %param.1), slice={[0:256], [0:64]} | slice | bytes 131072 | tf_op jit(solution)/shard_map/slice | solution.py:86
  3.1 2.6 %collective-permute-start = (f32[256,64]{1,0:T(8,128)S(1)}, f32[256,64]{1,0:T(8,128)S(1)}, u32[]{:S(2)}, u32[]{:S(2)}) collective-permute-start(f32[256,64]{1,0:T(8,128)S(1)} %slice.55), channel_id=1, source_target_pairs={{0,1},{1,0},{16,17},{17,16},{32,33},{33,32},{48,49},{49,48},{64,65... | collective-permute-start | bytes 196616 | tf_op jit(solution)/shard_map/ppermute | solution.py:87
  5.8 0.9 collective-permute-done
  6.6 0.8 select_select_fusion.1
  7.6 0.7 collective-permute-start.9
  8.3 0.7 collective-permute-start.8
  8.9 0.7 collective-permute-start.7
  9.6 0.7 collective-permute-start.6
  10.3 0.7 collective-permute-start.5
  11.0 1.3 %collective-permute-start.4 = (f32[65,128]{1,0:T(8,128)S(1)}, f32[65,128]{1,0:T(8,128)S(1)}, u32[]{:S(2)}, u32[]{:S(2)}) collective-permute-start(f32[65,128]{1,0:T(8,128)S(1)} %fusion.5), channel_id=1, source_target_pairs={{0,128},{1,129},{16,144},{17,145}} | collective-permute-start | bytes 99848 | tf_op jit(solution)/shard_map/ppermute | solution.py:11
  12.3 0.7 collective-permute-start.3
  13.1 2.4 %collective-permute-start.14 = (f32[256,128]{1,0:T(8,128)S(1)}, f32[256,128]{1,0:T(8,128)S(1)}, u32[]{:S(2)}, u32[]{:S(2)}) collective-permute-start(f32[256,128]{1,0:T(8,128)S(1)} %maximum_select_fusion), channel_id=1, source_target_pairs={{0,4},{1,5},{16,20},{17,21},{32,36},{33,37},{48,52},{49,53},{64,68... | collective-permute-start | bytes 393224 | tf_op jit(solution)/shard_map/ppermute | solution.py:108
  15.5 6.1 %collective-permute-start.13 = (f32[256,128]{1,0:T(8,128)S(1)}, f32[256,128]{1,0:T(8,128)S(1)}, u32[]{:S(2)}, u32[]{:S(2)}) collective-permute-start(f32[256,128]{1,0:T(8,128)S(1)} %maximum_select_fusion), channel_id=1, source_target_pairs={{0,8},{1,9},{16,24},{17,25},{32,40},{33,41},{48,56},{49,57},{64,72... | collective-permute-start | bytes 393224 | tf_op jit(solution)/shard_map/ppermute | solution.py:108
  21.7 5.9 %collective-permute-done.4 = f32[65,128]{1,0:T(8,128)S(1)} collective-permute-done((f32[65,128]{1,0:T(8,128)S(1)}, f32[65,128]{1,0:T(8,128)S(1)}, u32[]{:S(2)}, u32[]{:S(2)}) %collective-permute-start.4) | collective-permute-done | bytes 33312 | tf_op jit(solution)/shard_map/ppermute | solution.py:11
  27.6 1.3 %collective-permute-start.12 = (f32[65,128]{1,0:T(8,128)S(1)}, f32[65,128]{1,0:T(8,128)S(1)}, u32[]{:S(2)}, u32[]{:S(2)}) collective-permute-start(f32[65,128]{1,0:T(8,128)S(1)} %add_add_fusion.4), channel_id=1, source_target_pairs={{0,68},{1,69},{8,76},{9,77},{16,84},{17,85},{24,92},{25,93},{128,1... | collective-permute-start | bytes 99848 | tf_op jit(solution)/shard_map/ppermute | solution.py:11
  28.9 1.3 %collective-permute-start.11 = (f32[65,128]{1,0:T(8,128)S(1)}, f32[65,128]{1,0:T(8,128)S(1)}, u32[]{:S(2)}, u32[]{:S(2)}) collective-permute-start(f32[65,128]{1,0:T(8,128)S(1)} %add_add_fusion.4), channel_id=1, source_target_pairs={{0,4},{1,5},{8,12},{9,13},{16,20},{17,21},{24,28},{25,29},{128,132... | collective-permute-start | bytes 99848 | tf_op jit(solution)/shard_map/ppermute | solution.py:11
  30.2 1.3 %collective-permute-start.10 = (f32[65,128]{1,0:T(8,128)S(1)}, f32[65,128]{1,0:T(8,128)S(1)}, u32[]{:S(2)}, u32[]{:S(2)}) collective-permute-start(f32[65,128]{1,0:T(8,128)S(1)} %add_add_fusion.4), channel_id=1, source_target_pairs={{0,64},{1,65},{8,72},{9,73},{16,80},{17,81},{24,88},{25,89},{128,1... | collective-permute-start | bytes 99848 | tf_op jit(solution)/shard_map/ppermute | solution.py:11
  31.6 0.7 collective-permute-start.16
  32.2 1.3 %collective-permute-start.15 = (f32[256,128]{1,0:T(8,128)S(1)}, f32[256,128]{1,0:T(8,128)S(1)}, u32[]{:S(2)}, u32[]{:S(2)}) collective-permute-start(f32[256,128]{1,0:T(8,128)S(1)} %add_add_fusion.1), channel_id=1, source_target_pairs={{0,2},{1,3},{4,6},{5,7},{8,10},{9,11},{16,18},{17,19},{20,22},{21,... | collective-permute-start | bytes 393224 | tf_op jit(solution)/shard_map/ppermute | solution.py:108
  33.6 1.9 %collective-permute-done.15 = f32[256,128]{1,0:T(8,128)S(1)} collective-permute-done((f32[256,128]{1,0:T(8,128)S(1)}, f32[256,128]{1,0:T(8,128)S(1)}, u32[]{:S(2)}, u32[]{:S(2)}) %collective-permute-start.15) | collective-permute-done | bytes 131104 | tf_op jit(solution)/shard_map/ppermute | solution.py:108
  35.5 1.3 %collective-permute-start.19 = (f32[65,128]{1,0:T(8,128)S(1)}, f32[65,128]{1,0:T(8,128)S(1)}, u32[]{:S(2)}, u32[]{:S(2)}) collective-permute-start(f32[65,128]{1,0:T(8,128)S(1)} %add_add_fusion.3), channel_id=1, source_target_pairs={{0,34},{1,35},{4,38},{5,39},{8,42},{9,43},{12,46},{13,47},{16,50},... | collective-permute-start | bytes 99848 | tf_op jit(solution)/shard_map/ppermute | solution.py:11
  36.8 3.1 %collective-permute-start.18 = (f32[65,128]{1,0:T(8,128)S(1)}, f32[65,128]{1,0:T(8,128)S(1)}, u32[]{:S(2)}, u32[]{:S(2)}) collective-permute-start(f32[65,128]{1,0:T(8,128)S(1)} %add_add_fusion.3), channel_id=1, source_target_pairs={{0,2},{1,3},{4,6},{5,7},{8,10},{9,11},{12,14},{13,15},{16,18},{17,... | collective-permute-start | bytes 99848 | tf_op jit(solution)/shard_map/ppermute | solution.py:11
  40.0 1.3 %collective-permute-start.17 = (f32[65,128]{1,0:T(8,128)S(1)}, f32[65,128]{1,0:T(8,128)S(1)}, u32[]{:S(2)}, u32[]{:S(2)}) collective-permute-start(f32[65,128]{1,0:T(8,128)S(1)} %add_add_fusion.3), channel_id=1, source_target_pairs={{0,32},{1,33},{4,36},{5,37},{8,40},{9,41},{12,44},{13,45},{16,48},... | collective-permute-start | bytes 99848 | tf_op jit(solution)/shard_map/ppermute | solution.py:11
  41.3 18.9 %collective-permute-start.21 = (f32[256,128]{1,0:T(8,128)S(1)}, f32[256,128]{1,0:T(8,128)S(1)}, u32[]{:S(2)}, u32[]{:S(2)}) collective-permute-start(f32[256,128]{1,0:T(8,128)S(1)} %add_add_fusion), channel_id=1, source_target_pairs={{0,256},{16,257},{32,258},{48,259},{64,260},{80,261},{96,262},{112... | collective-permute-start | bytes 393224 | tf_op jit(solution)/shard_map/ppermute | solution.py:11
  60.2 1.9 %collective-permute-start.20 = (f32[256,128]{1,0:T(8,128)S(1)}, f32[256,128]{1,0:T(8,128)S(1)}, u32[]{:S(2)}, u32[]{:S(2)}) collective-permute-start(f32[256,128]{1,0:T(8,128)S(1)} %add_add_fusion), channel_id=1, source_target_pairs={{0,0},{16,1},{32,2},{48,3},{64,4},{80,5},{96,6},{112,7},{128,8},{1... | collective-permute-start | bytes 393224 | tf_op jit(solution)/shard_map/ppermute | solution.py:11
  62.7 11.7 %cholesky.20 = f32[128,128]{1,0:T(8,128)S(1)} custom-call(f32[128,128]{1,0:T(8,128)S(1)} %fusion.4), custom_call_target="Cholesky" | custom-call | tf_op jit(solution)/shard_map/jit(cholesky)/cholesky | solution.py:129
  75.1 0.7 select_bitcast_fusion
  75.8 9.8 %custom-call.7 = f32[1,128,128]{1,2,0:T(8,128)S(1)} custom-call(f32[1,128,128]{2,1,0:T(8,128)S(1)} %get-tuple-element.13), custom_call_target="InvertDiagBlocksLowerTriangular" | custom-call | tf_op jit(solution)/shard_map/jit(_solve_triangular)/triangular_solve | solution.py:71
  87.2 1.5 %fusion.1 = f32[256,512]{1,0:T(8,128)} fusion(f32[256,512]{1,0:T(8,128)S(1)} %copy-done, f32[256,128]{1,0:T(8,128)S(1)} %fusion.20, f32[512,128]{1,0:T(8,128)S(1)} %bitcast.33, f32[256,64]{1,0:T(8,128)S(1)} %maximum_select_fusion.1, s32[512]{0:T(512)S(1)} %fusion.9, s32[256]{0:T(256)S(1)} %fusion.15, pred[512]{0:T(512)(128)(4,1)S(1)} %broadcast_compare_fusion, ...), kind=kOutput, calls=%fused_computation.2 | convolution fusion | flops 201981952 | bytes 1511424 | tf_op jit(solution)/shard_map/dot_general | solution.py:15
  (58 shorter events, 3.2 us)
Async XLA Ops:
  0.0 7.5 %copy-start = (f32[256,512]{1,0:T(8,128)S(1)}, f32[256,512]{1,0:T(8,128)}, u32[]{:S(2)}) copy-start(f32[256,512]{1,0:T(8,128)} %param.1) | copy-start | bytes 1572868
  0.8 4.9 %collective-permute-start.1 = (f32[64,64]{1,0:T(8,128)S(1)}, f32[64,64]{1,0:T(8,128)S(1)}, u32[]{:S(2)}, u32[]{:S(2)}) collective-permute-start(f32[64,64]{1,0:T(8,128)S(1)} %slice.54), channel_id=1, source_target_pairs={{17,0},{0,16}} | collective-permute-start | bytes 49160 | tf_op jit(solution)/shard_map/ppermute | solution.py:11
  1.5 4.3 %collective-permute-start.2 = (f32[64,64]{1,0:T(8,128)S(1)}, f32[64,64]{1,0:T(8,128)S(1)}, u32[]{:S(2)}, u32[]{:S(2)}) collective-permute-start(f32[64,64]{1,0:T(8,128)S(1)} %slice.54), channel_id=1, source_target_pairs={{17,1},{0,17}} | collective-permute-start | bytes 49160 | tf_op jit(solution)/shard_map/ppermute | solution.py:11
  3.1 3.6 %collective-permute-start = (f32[256,64]{1,0:T(8,128)S(1)}, f32[256,64]{1,0:T(8,128)S(1)}, u32[]{:S(2)}, u32[]{:S(2)}) collective-permute-start(f32[256,64]{1,0:T(8,128)S(1)} %slice.55), channel_id=1, source_target_pairs={{0,1},{1,0},{16,17},{17,16},{32,33},{33,32},{48,49},{49,48},{64,65... | collective-permute-start | bytes 196616 | tf_op jit(solution)/shard_map/ppermute | solution.py:87
  7.6 3.4 %collective-permute-start.9 = (f32[65,128]{1,0:T(8,128)S(1)}, f32[65,128]{1,0:T(8,128)S(1)}, u32[]{:S(2)}, u32[]{:S(2)}) collective-permute-start(f32[65,128]{1,0:T(8,128)S(1)} %fusion.5), channel_id=1, source_target_pairs={{0,392},{1,393},{16,408},{17,409}} | collective-permute-start | bytes 99848 | tf_op jit(solution)/shard_map/ppermute | solution.py:11
  8.3 4.0 %collective-permute-start.8 = (f32[65,128]{1,0:T(8,128)S(1)}, f32[65,128]{1,0:T(8,128)S(1)}, u32[]{:S(2)}, u32[]{:S(2)}) collective-permute-start(f32[65,128]{1,0:T(8,128)S(1)} %fusion.5), channel_id=1, source_target_pairs={{0,384},{1,385},{16,400},{17,401}} | collective-permute-start | bytes 99848 | tf_op jit(solution)/shard_map/ppermute | solution.py:11
  8.9 4.2 %collective-permute-start.7 = (f32[65,128]{1,0:T(8,128)S(1)}, f32[65,128]{1,0:T(8,128)S(1)}, u32[]{:S(2)}, u32[]{:S(2)}) collective-permute-start(f32[65,128]{1,0:T(8,128)S(1)} %fusion.5), channel_id=1, source_target_pairs={{0,264},{1,265},{16,280},{17,281}} | collective-permute-start | bytes 99848 | tf_op jit(solution)/shard_map/ppermute | solution.py:11
  9.6 5.9 %collective-permute-start.6 = (f32[65,128]{1,0:T(8,128)S(1)}, f32[65,128]{1,0:T(8,128)S(1)}, u32[]{:S(2)}, u32[]{:S(2)}) collective-permute-start(f32[65,128]{1,0:T(8,128)S(1)} %fusion.5), channel_id=1, source_target_pairs={{0,256},{1,257},{16,272},{17,273}} | collective-permute-start | bytes 99848 | tf_op jit(solution)/shard_map/ppermute | solution.py:11
  10.3 11.4 %collective-permute-start.5 = (f32[65,128]{1,0:T(8,128)S(1)}, f32[65,128]{1,0:T(8,128)S(1)}, u32[]{:S(2)}, u32[]{:S(2)}) collective-permute-start(f32[65,128]{1,0:T(8,128)S(1)} %fusion.5), channel_id=1, source_target_pairs={{0,136},{1,137},{16,152},{17,153}} | collective-permute-start | bytes 99848 | tf_op jit(solution)/shard_map/ppermute | solution.py:11
  11.0 16.6 %collective-permute-start.4 = (f32[65,128]{1,0:T(8,128)S(1)}, f32[65,128]{1,0:T(8,128)S(1)}, u32[]{:S(2)}, u32[]{:S(2)}) collective-permute-start(f32[65,128]{1,0:T(8,128)S(1)} %fusion.5), channel_id=1, source_target_pairs={{0,128},{1,129},{16,144},{17,145}} | collective-permute-start | bytes 99848 | tf_op jit(solution)/shard_map/ppermute | solution.py:11
  12.3 15.3 %collective-permute-start.3 = (f32[65,128]{1,0:T(8,128)S(1)}, f32[65,128]{1,0:T(8,128)S(1)}, u32[]{:S(2)}, u32[]{:S(2)}) collective-permute-start(f32[65,128]{1,0:T(8,128)S(1)} %fusion.5), channel_id=1, source_target_pairs={{0,8},{1,9},{16,24},{17,25}} | collective-permute-start | bytes 99848 | tf_op jit(solution)/shard_map/ppermute | solution.py:11
  13.1 18.4 %collective-permute-start.14 = (f32[256,128]{1,0:T(8,128)S(1)}, f32[256,128]{1,0:T(8,128)S(1)}, u32[]{:S(2)}, u32[]{:S(2)}) collective-permute-start(f32[256,128]{1,0:T(8,128)S(1)} %maximum_select_fusion), channel_id=1, source_target_pairs={{0,4},{1,5},{16,20},{17,21},{32,36},{33,37},{48,52},{49,53},{64,68... | collective-permute-start | bytes 393224 | tf_op jit(solution)/shard_map/ppermute | solution.py:108
  15.5 16.0 %collective-permute-start.13 = (f32[256,128]{1,0:T(8,128)S(1)}, f32[256,128]{1,0:T(8,128)S(1)}, u32[]{:S(2)}, u32[]{:S(2)}) collective-permute-start(f32[256,128]{1,0:T(8,128)S(1)} %maximum_select_fusion), channel_id=1, source_target_pairs={{0,8},{1,9},{16,24},{17,25},{32,40},{33,41},{48,56},{49,57},{64,72... | collective-permute-start | bytes 393224 | tf_op jit(solution)/shard_map/ppermute | solution.py:108
  27.6 5.9 %collective-permute-start.12 = (f32[65,128]{1,0:T(8,128)S(1)}, f32[65,128]{1,0:T(8,128)S(1)}, u32[]{:S(2)}, u32[]{:S(2)}) collective-permute-start(f32[65,128]{1,0:T(8,128)S(1)} %add_add_fusion.4), channel_id=1, source_target_pairs={{0,68},{1,69},{8,76},{9,77},{16,84},{17,85},{24,92},{25,93},{128,1... | collective-permute-start | bytes 99848 | tf_op jit(solution)/shard_map/ppermute | solution.py:11
  28.9 4.6 %collective-permute-start.11 = (f32[65,128]{1,0:T(8,128)S(1)}, f32[65,128]{1,0:T(8,128)S(1)}, u32[]{:S(2)}, u32[]{:S(2)}) collective-permute-start(f32[65,128]{1,0:T(8,128)S(1)} %add_add_fusion.4), channel_id=1, source_target_pairs={{0,4},{1,5},{8,12},{9,13},{16,20},{17,21},{24,28},{25,29},{128,132... | collective-permute-start | bytes 99848 | tf_op jit(solution)/shard_map/ppermute | solution.py:11
  30.2 3.4 %collective-permute-start.10 = (f32[65,128]{1,0:T(8,128)S(1)}, f32[65,128]{1,0:T(8,128)S(1)}, u32[]{:S(2)}, u32[]{:S(2)}) collective-permute-start(f32[65,128]{1,0:T(8,128)S(1)} %add_add_fusion.4), channel_id=1, source_target_pairs={{0,64},{1,65},{8,72},{9,73},{16,80},{17,81},{24,88},{25,89},{128,1... | collective-permute-start | bytes 99848 | tf_op jit(solution)/shard_map/ppermute | solution.py:11
  31.6 2.0 %collective-permute-start.16 = (f32[256,128]{1,0:T(8,128)S(1)}, f32[256,128]{1,0:T(8,128)S(1)}, u32[]{:S(2)}, u32[]{:S(2)}) collective-permute-start(f32[256,128]{1,0:T(8,128)S(1)} %add_add_fusion.1), channel_id=1, source_target_pairs={{8,12},{9,13},{4,14},{5,15},{24,28},{25,29},{20,30},{21,31},{40,44... | collective-permute-start | bytes 393224 | tf_op jit(solution)/shard_map/ppermute | solution.py:108
  32.2 3.2 %collective-permute-start.15 = (f32[256,128]{1,0:T(8,128)S(1)}, f32[256,128]{1,0:T(8,128)S(1)}, u32[]{:S(2)}, u32[]{:S(2)}) collective-permute-start(f32[256,128]{1,0:T(8,128)S(1)} %add_add_fusion.1), channel_id=1, source_target_pairs={{0,2},{1,3},{4,6},{5,7},{8,10},{9,11},{16,18},{17,19},{20,22},{21,... | collective-permute-start | bytes 393224 | tf_op jit(solution)/shard_map/ppermute | solution.py:108
  35.5 26.6 %collective-permute-start.19 = (f32[65,128]{1,0:T(8,128)S(1)}, f32[65,128]{1,0:T(8,128)S(1)}, u32[]{:S(2)}, u32[]{:S(2)}) collective-permute-start(f32[65,128]{1,0:T(8,128)S(1)} %add_add_fusion.3), channel_id=1, source_target_pairs={{0,34},{1,35},{4,38},{5,39},{8,42},{9,43},{12,46},{13,47},{16,50},... | collective-permute-start | bytes 99848 | tf_op jit(solution)/shard_map/ppermute | solution.py:11
  36.8 25.3 %collective-permute-start.18 = (f32[65,128]{1,0:T(8,128)S(1)}, f32[65,128]{1,0:T(8,128)S(1)}, u32[]{:S(2)}, u32[]{:S(2)}) collective-permute-start(f32[65,128]{1,0:T(8,128)S(1)} %add_add_fusion.3), channel_id=1, source_target_pairs={{0,2},{1,3},{4,6},{5,7},{8,10},{9,11},{12,14},{13,15},{16,18},{17,... | collective-permute-start | bytes 99848 | tf_op jit(solution)/shard_map/ppermute | solution.py:11
  40.0 22.2 %collective-permute-start.17 = (f32[65,128]{1,0:T(8,128)S(1)}, f32[65,128]{1,0:T(8,128)S(1)}, u32[]{:S(2)}, u32[]{:S(2)}) collective-permute-start(f32[65,128]{1,0:T(8,128)S(1)} %add_add_fusion.3), channel_id=1, source_target_pairs={{0,32},{1,33},{4,36},{5,37},{8,40},{9,41},{12,44},{13,45},{16,48},... | collective-permute-start | bytes 99848 | tf_op jit(solution)/shard_map/ppermute | solution.py:11
  41.3 45.8 %collective-permute-start.21 = (f32[256,128]{1,0:T(8,128)S(1)}, f32[256,128]{1,0:T(8,128)S(1)}, u32[]{:S(2)}, u32[]{:S(2)}) collective-permute-start(f32[256,128]{1,0:T(8,128)S(1)} %add_add_fusion), channel_id=1, source_target_pairs={{0,256},{16,257},{32,258},{48,259},{64,260},{80,261},{96,262},{112... | collective-permute-start | bytes 393224 | tf_op jit(solution)/shard_map/ppermute | solution.py:11
  60.2 26.9 %collective-permute-start.20 = (f32[256,128]{1,0:T(8,128)S(1)}, f32[256,128]{1,0:T(8,128)S(1)}, u32[]{:S(2)}, u32[]{:S(2)}) collective-permute-start(f32[256,128]{1,0:T(8,128)S(1)} %add_add_fusion), channel_id=1, source_target_pairs={{0,0},{16,1},{32,2},{48,3},{64,4},{80,5},{96,6},{112,7},{128,8},{1... | collective-permute-start | bytes 393224 | tf_op jit(solution)/shard_map/ppermute | solution.py:11

commit v17 on v15

--- a/solution.py
+++ b/solution.py
@@ -126,7 +126,7 @@
     lead_block = jnp.concatenate(
         [jnp.concatenate([a00, a10.T], axis=1), jnp.concatenate([a10, a11], axis=1)], axis=0
     )
-    factor = jnp.linalg.cholesky(lead_block)
+    factor = jnp.linalg.cholesky(lead_block, symmetrize_input=False)
     inv_t = lower_inverse(factor).T
     c0 = factor[:NB, :NB]
     c1 = factor[NB:, NB:]

time: 84.6 us -> 84.4 us (level)
  no operation moved by 1% of the time
where the time goes in v17:
time: 84.4 us; the launch traced here: 83.8 us
  starting transfers between devices  46.4 us (55%)
  other arithmetic  25.3 us (30%)
  waiting for transfers between devices  7.32 us (9%)
  local copies, waits for them, and re-layouts  2.63 us (3%)
  matrix products  1.56 us (2%)
    ppermute x17, starting transfers between devices, both_axes(): return lax.ppermute(x, ('row', 'col'), pairs)  32.8 us
    another operation x3, other arithmetic, per_device(): factor = jnp.linalg.cholesky(lead_block, symmetrize_input=False)  12.4 us
    ppermute x4, starting transfers between devices, per_device(): panel = panel + lax.ppermute(sent, 'col', pairs)  11.7 us
    another operation x2, other arithmetic, lower_inverse(): return jax.scipy.linalg.solve_triangular(factor, eye, lower=True)  10.5 us
    ppermute x17, waiting for transfers between devices, both_axes(): return lax.ppermute(x, ('row', 'col'), pairs)  4.29 us
    ppermute x1, starting transfers between devices, per_device(): swapped = lax.ppermute(mine, 'col', [(0, 1), (1, 0)])  1.92 us
    ppermute x4, waiting for transfers between devices, per_device(): panel = panel + lax.ppermute(sent, 'col', pairs)  1.78 us
  transfers between devices with their start and end apart: 22, of which 3 were waited for; matrix products, arithmetic and copies ran while one was open for 31% of the time, Pallas kernels for 0%

profile of v17, /device:TPU:48, one launch (start us, length us, event | category | flops | bytes accessed | tf_op | source)
XLA Modules:
  0.0 83.8 jit_solution(8382733538068542565)
XLA Ops:
  0.0 0.8 slice.60
  0.8 0.7 collective-permute-start.1
  1.5 0.7 collective-permute-start.2
  2.2 0.9 %slice.61 = f32[256,64]{1,0:T(8,128)S(1)} slice(f32[256,512]{1,0:T(8,128)} %param.1), slice={[0:256], [0:64]} | slice | bytes 131072 | tf_op jit(solution)/shard_map/slice | solution.py:86
  3.1 1.9 %collective-permute-start = (f32[256,64]{1,0:T(8,128)S(1)}, f32[256,64]{1,0:T(8,128)S(1)}, u32[]{:S(2)}, u32[]{:S(2)}) collective-permute-start(f32[256,64]{1,0:T(8,128)S(1)} %slice.61), channel_id=1, source_target_pairs={{0,1},{1,0},{16,17},{17,16},{32,33},{33,32},{48,49},{49,48},{64,65... | collective-permute-start | bytes 196616 | tf_op jit(solution)/shard_map/ppermute | solution.py:87
  5.1 1.2 %collective-permute-done = f32[256,64]{1,0:T(8,128)S(1)} collective-permute-done((f32[256,64]{1,0:T(8,128)S(1)}, f32[256,64]{1,0:T(8,128)S(1)}, u32[]{:S(2)}, u32[]{:S(2)}) %collective-permute-start) | collective-permute-done | bytes 65568 | tf_op jit(solution)/shard_map/ppermute | solution.py:87
  6.3 0.8 select_select_fusion.1
  7.3 0.7 collective-permute-start.3
  8.0 0.7 collective-permute-start.4
  8.6 0.7 collective-permute-start.5
  9.3 0.7 collective-permute-start.6
  10.0 0.7 collective-permute-start.7
  10.7 1.3 %collective-permute-start.8 = (f32[65,128]{1,0:T(8,128)S(1)}, f32[65,128]{1,0:T(8,128)S(1)}, u32[]{:S(2)}, u32[]{:S(2)}) collective-permute-start(f32[65,128]{1,0:T(8,128)S(1)} %fusion.3), channel_id=1, source_target_pairs={{0,384},{1,385},{16,400},{17,401}} | collective-permute-start | bytes 99848 | tf_op jit(solution)/shard_map/ppermute | solution.py:11
  12.0 0.7 collective-permute-start.9
  12.8 8.4 %collective-permute-start.13 = (f32[256,128]{1,0:T(8,128)S(1)}, f32[256,128]{1,0:T(8,128)S(1)}, u32[]{:S(2)}, u32[]{:S(2)}) collective-permute-start(f32[256,128]{1,0:T(8,128)S(1)} %maximum_select_fusion), channel_id=1, source_target_pairs={{0,8},{1,9},{16,24},{17,25},{32,40},{33,41},{48,56},{49,57},{64,72... | collective-permute-start | bytes 393224 | tf_op jit(solution)/shard_map/ppermute | solution.py:108
  21.2 1.3 %collective-permute-start.14 = (f32[256,128]{1,0:T(8,128)S(1)}, f32[256,128]{1,0:T(8,128)S(1)}, u32[]{:S(2)}, u32[]{:S(2)}) collective-permute-start(f32[256,128]{1,0:T(8,128)S(1)} %maximum_select_fusion), channel_id=1, source_target_pairs={{0,4},{1,5},{16,20},{17,21},{32,36},{33,37},{48,52},{49,53},{64,68... | collective-permute-start | bytes 393224 | tf_op jit(solution)/shard_map/ppermute | solution.py:108
  22.6 4.3 %collective-permute-done.8 = f32[65,128]{1,0:T(8,128)S(1)} collective-permute-done((f32[65,128]{1,0:T(8,128)S(1)}, f32[65,128]{1,0:T(8,128)S(1)}, u32[]{:S(2)}, u32[]{:S(2)}) %collective-permute-start.8) | collective-permute-done | bytes 33312 | tf_op jit(solution)/shard_map/ppermute | solution.py:11
  26.8 1.3 %collective-permute-start.10 = (f32[65,128]{1,0:T(8,128)S(1)}, f32[65,128]{1,0:T(8,128)S(1)}, u32[]{:S(2)}, u32[]{:S(2)}) collective-permute-start(f32[65,128]{1,0:T(8,128)S(1)} %add_add_fusion.4), channel_id=1, source_target_pairs={{0,64},{1,65},{8,72},{9,73},{16,80},{17,81},{24,88},{25,89},{128,1... | collective-permute-start | bytes 99848 | tf_op jit(solution)/shard_map/ppermute | solution.py:11
  28.1 1.3 %collective-permute-start.11 = (f32[65,128]{1,0:T(8,128)S(1)}, f32[65,128]{1,0:T(8,128)S(1)}, u32[]{:S(2)}, u32[]{:S(2)}) collective-permute-start(f32[65,128]{1,0:T(8,128)S(1)} %add_add_fusion.4), channel_id=1, source_target_pairs={{0,4},{1,5},{8,12},{9,13},{16,20},{17,21},{24,28},{25,29},{128,132... | collective-permute-start | bytes 99848 | tf_op jit(solution)/shard_map/ppermute | solution.py:11
  29.4 1.3 %collective-permute-start.12 = (f32[65,128]{1,0:T(8,128)S(1)}, f32[65,128]{1,0:T(8,128)S(1)}, u32[]{:S(2)}, u32[]{:S(2)}) collective-permute-start(f32[65,128]{1,0:T(8,128)S(1)} %add_add_fusion.4), channel_id=1, source_target_pairs={{0,68},{1,69},{8,76},{9,77},{16,84},{17,85},{24,92},{25,93},{128,1... | collective-permute-start | bytes 99848 | tf_op jit(solution)/shard_map/ppermute | solution.py:11
  30.8 1.3 %collective-permute-start.15 = (f32[256,128]{1,0:T(8,128)S(1)}, f32[256,128]{1,0:T(8,128)S(1)}, u32[]{:S(2)}, u32[]{:S(2)}) collective-permute-start(f32[256,128]{1,0:T(8,128)S(1)} %add_add_fusion.1), channel_id=1, source_target_pairs={{0,2},{1,3},{4,6},{5,7},{8,10},{9,11},{16,18},{17,19},{20,22},{21,... | collective-permute-start | bytes 393224 | tf_op jit(solution)/shard_map/ppermute | solution.py:108
  32.1 0.7 collective-permute-start.16
  32.8 1.8 %collective-permute-done.15 = f32[256,128]{1,0:T(8,128)S(1)} collective-permute-done((f32[256,128]{1,0:T(8,128)S(1)}, f32[256,128]{1,0:T(8,128)S(1)}, u32[]{:S(2)}, u32[]{:S(2)}) %collective-permute-start.15) | collective-permute-done | bytes 131104 | tf_op jit(solution)/shard_map/ppermute | solution.py:108
  34.6 1.3 %collective-permute-start.17 = (f32[65,128]{1,0:T(8,128)S(1)}, f32[65,128]{1,0:T(8,128)S(1)}, u32[]{:S(2)}, u32[]{:S(2)}) collective-permute-start(f32[65,128]{1,0:T(8,128)S(1)} %add_add_fusion.3), channel_id=1, source_target_pairs={{0,32},{1,33},{4,36},{5,37},{8,40},{9,41},{12,44},{13,45},{16,48},... | collective-permute-start | bytes 99848 | tf_op jit(solution)/shard_map/ppermute | solution.py:11
  35.9 3.7 %collective-permute-start.18 = (f32[65,128]{1,0:T(8,128)S(1)}, f32[65,128]{1,0:T(8,128)S(1)}, u32[]{:S(2)}, u32[]{:S(2)}) collective-permute-start(f32[65,128]{1,0:T(8,128)S(1)} %add_add_fusion.3), channel_id=1, source_target_pairs={{0,2},{1,3},{4,6},{5,7},{8,10},{9,11},{12,14},{13,15},{16,18},{17,... | collective-permute-start | bytes 99848 | tf_op jit(solution)/shard_map/ppermute | solution.py:11
  39.7 1.3 %collective-permute-start.19 = (f32[65,128]{1,0:T(8,128)S(1)}, f32[65,128]{1,0:T(8,128)S(1)}, u32[]{:S(2)}, u32[]{:S(2)}) collective-permute-start(f32[65,128]{1,0:T(8,128)S(1)} %add_add_fusion.3), channel_id=1, source_target_pairs={{0,34},{1,35},{4,38},{5,39},{8,42},{9,43},{12,46},{13,47},{16,50},... | collective-permute-start | bytes 99848 | tf_op jit(solution)/shard_map/ppermute | solution.py:11
  41.0 9.0 %collective-permute-start.20 = (f32[256,128]{1,0:T(8,128)S(1)}, f32[256,128]{1,0:T(8,128)S(1)}, u32[]{:S(2)}, u32[]{:S(2)}) collective-permute-start(f32[256,128]{1,0:T(8,128)S(1)} %add_add_fusion), channel_id=1, source_target_pairs={{0,0},{16,1},{32,2},{48,3},{64,4},{80,5},{96,6},{112,7},{128,8},{1... | collective-permute-start | bytes 393224 | tf_op jit(solution)/shard_map/ppermute | solution.py:11
  49.9 7.1 %collective-permute-start.21 = (f32[256,128]{1,0:T(8,128)S(1)}, f32[256,128]{1,0:T(8,128)S(1)}, u32[]{:S(2)}, u32[]{:S(2)}) collective-permute-start(f32[256,128]{1,0:T(8,128)S(1)} %add_add_fusion), channel_id=1, source_target_pairs={{0,256},{16,257},{32,258},{48,259},{64,260},{80,261},{96,262},{112... | collective-permute-start | bytes 393224 | tf_op jit(solution)/shard_map/ppermute | solution.py:11
  57.4 11.7 %cholesky.20 = f32[128,128]{1,0:T(8,128)S(1)} custom-call(f32[128,128]{1,0:T(8,128)S(1)} %maximum_maximum_fusion), custom_call_target="Cholesky" | custom-call | tf_op jit(solution)/shard_map/jit(cholesky)/cholesky | solution.py:129
  69.8 0.7 select_bitcast_fusion
  70.5 9.8 %custom-call.7 = f32[1,128,128]{1,2,0:T(8,128)S(1)} custom-call(f32[1,128,128]{2,1,0:T(8,128)S(1)} %get-tuple-element.13), custom_call_target="InvertDiagBlocksLowerTriangular" | custom-call | tf_op jit(solution)/shard_map/jit(_solve_triangular)/triangular_solve | solution.py:71
  82.8 1.0 %pad_maximum_fusion = f32[256,512]{1,0:T(8,128)} fusion(f32[256,448]{1,0:T(8,128)S(1)} %slice.82, f32[256,64]{1,0:T(8,128)S(1)} %slice_select_fusion), kind=kLoop, calls=%fused_computation.2 | loop fusion | flops 131072 | bytes 1048576 | tf_op jit(solution)/shard_map/concatenate | solution.py:155
  (57 shorter events, 3.8 us)
Async XLA Ops:
  0.0 7.2 %copy-start = (f32[256,512]{1,0:T(8,128)S(1)}, f32[256,512]{1,0:T(8,128)}, u32[]{:S(2)}) copy-start(f32[256,512]{1,0:T(8,128)} %param.1) | copy-start | bytes 1572868
  0.8 4.2 %collective-permute-start.1 = (f32[64,64]{1,0:T(8,128)S(1)}, f32[64,64]{1,0:T(8,128)S(1)}, u32[]{:S(2)}, u32[]{:S(2)}) collective-permute-start(f32[64,64]{1,0:T(8,128)S(1)} %slice.60), channel_id=1, source_target_pairs={{17,0},{0,16}} | collective-permute-start | bytes 49160 | tf_op jit(solution)/shard_map/ppermute | solution.py:11
  1.5 3.6 %collective-permute-start.2 = (f32[64,64]{1,0:T(8,128)S(1)}, f32[64,64]{1,0:T(8,128)S(1)}, u32[]{:S(2)}, u32[]{:S(2)}) collective-permute-start(f32[64,64]{1,0:T(8,128)S(1)} %slice.60), channel_id=1, source_target_pairs={{17,1},{0,17}} | collective-permute-start | bytes 49160 | tf_op jit(solution)/shard_map/ppermute | solution.py:11
  3.1 3.2 %collective-permute-start = (f32[256,64]{1,0:T(8,128)S(1)}, f32[256,64]{1,0:T(8,128)S(1)}, u32[]{:S(2)}, u32[]{:S(2)}) collective-permute-start(f32[256,64]{1,0:T(8,128)S(1)} %slice.61), channel_id=1, source_target_pairs={{0,1},{1,0},{16,17},{17,16},{32,33},{33,32},{48,49},{49,48},{64,65... | collective-permute-start | bytes 196616 | tf_op jit(solution)/shard_map/ppermute | solution.py:87
  7.3 3.4 %collective-permute-start.3 = (f32[65,128]{1,0:T(8,128)S(1)}, f32[65,128]{1,0:T(8,128)S(1)}, u32[]{:S(2)}, u32[]{:S(2)}) collective-permute-start(f32[65,128]{1,0:T(8,128)S(1)} %fusion.3), channel_id=1, source_target_pairs={{0,8},{1,9},{16,24},{17,25}} | collective-permute-start | bytes 99848 | tf_op jit(solution)/shard_map/ppermute | solution.py:11
  8.0 4.0 %collective-permute-start.4 = (f32[65,128]{1,0:T(8,128)S(1)}, f32[65,128]{1,0:T(8,128)S(1)}, u32[]{:S(2)}, u32[]{:S(2)}) collective-permute-start(f32[65,128]{1,0:T(8,128)S(1)} %fusion.3), channel_id=1, source_target_pairs={{0,128},{1,129},{16,144},{17,145}} | collective-permute-start | bytes 99848 | tf_op jit(solution)/shard_map/ppermute | solution.py:11
  8.6 4.2 %collective-permute-start.5 = (f32[65,128]{1,0:T(8,128)S(1)}, f32[65,128]{1,0:T(8,128)S(1)}, u32[]{:S(2)}, u32[]{:S(2)}) collective-permute-start(f32[65,128]{1,0:T(8,128)S(1)} %fusion.3), channel_id=1, source_target_pairs={{0,136},{1,137},{16,152},{17,153}} | collective-permute-start | bytes 99848 | tf_op jit(solution)/shard_map/ppermute | solution.py:11
  9.3 11.9 %collective-permute-start.6 = (f32[65,128]{1,0:T(8,128)S(1)}, f32[65,128]{1,0:T(8,128)S(1)}, u32[]{:S(2)}, u32[]{:S(2)}) collective-permute-start(f32[65,128]{1,0:T(8,128)S(1)} %fusion.3), channel_id=1, source_target_pairs={{0,256},{1,257},{16,272},{17,273}} | collective-permute-start | bytes 99848 | tf_op jit(solution)/shard_map/ppermute | solution.py:11
  10.0 12.6 %collective-permute-start.7 = (f32[65,128]{1,0:T(8,128)S(1)}, f32[65,128]{1,0:T(8,128)S(1)}, u32[]{:S(2)}, u32[]{:S(2)}) collective-permute-start(f32[65,128]{1,0:T(8,128)S(1)} %fusion.3), channel_id=1, source_target_pairs={{0,264},{1,265},{16,280},{17,281}} | collective-permute-start | bytes 99848 | tf_op jit(solution)/shard_map/ppermute | solution.py:11
  10.7 16.1 %collective-permute-start.8 = (f32[65,128]{1,0:T(8,128)S(1)}, f32[65,128]{1,0:T(8,128)S(1)}, u32[]{:S(2)}, u32[]{:S(2)}) collective-permute-start(f32[65,128]{1,0:T(8,128)S(1)} %fusion.3), channel_id=1, source_target_pairs={{0,384},{1,385},{16,400},{17,401}} | collective-permute-start | bytes 99848 | tf_op jit(solution)/shard_map/ppermute | solution.py:11
  12.0 14.8 %collective-permute-start.9 = (f32[65,128]{1,0:T(8,128)S(1)}, f32[65,128]{1,0:T(8,128)S(1)}, u32[]{:S(2)}, u32[]{:S(2)}) collective-permute-start(f32[65,128]{1,0:T(8,128)S(1)} %fusion.3), channel_id=1, source_target_pairs={{0,392},{1,393},{16,408},{17,409}} | collective-permute-start | bytes 99848 | tf_op jit(solution)/shard_map/ppermute | solution.py:11
  12.8 18.0 %collective-permute-start.13 = (f32[256,128]{1,0:T(8,128)S(1)}, f32[256,128]{1,0:T(8,128)S(1)}, u32[]{:S(2)}, u32[]{:S(2)}) collective-permute-start(f32[256,128]{1,0:T(8,128)S(1)} %maximum_select_fusion), channel_id=1, source_target_pairs={{0,8},{1,9},{16,24},{17,25},{32,40},{33,41},{48,56},{49,57},{64,72... | collective-permute-start | bytes 393224 | tf_op jit(solution)/shard_map/ppermute | solution.py:108
  21.2 9.5 %collective-permute-start.14 = (f32[256,128]{1,0:T(8,128)S(1)}, f32[256,128]{1,0:T(8,128)S(1)}, u32[]{:S(2)}, u32[]{:S(2)}) collective-permute-start(f32[256,128]{1,0:T(8,128)S(1)} %maximum_select_fusion), channel_id=1, source_target_pairs={{0,4},{1,5},{16,20},{17,21},{32,36},{33,37},{48,52},{49,53},{64,68... | collective-permute-start | bytes 393224 | tf_op jit(solution)/shard_map/ppermute | solution.py:108
  26.8 5.9 %collective-permute-start.10 = (f32[65,128]{1,0:T(8,128)S(1)}, f32[65,128]{1,0:T(8,128)S(1)}, u32[]{:S(2)}, u32[]{:S(2)}) collective-permute-start(f32[65,128]{1,0:T(8,128)S(1)} %add_add_fusion.4), channel_id=1, source_target_pairs={{0,64},{1,65},{8,72},{9,73},{16,80},{17,81},{24,88},{25,89},{128,1... | collective-permute-start | bytes 99848 | tf_op jit(solution)/shard_map/ppermute | solution.py:11
  28.1 4.6 %collective-permute-start.11 = (f32[65,128]{1,0:T(8,128)S(1)}, f32[65,128]{1,0:T(8,128)S(1)}, u32[]{:S(2)}, u32[]{:S(2)}) collective-permute-start(f32[65,128]{1,0:T(8,128)S(1)} %add_add_fusion.4), channel_id=1, source_target_pairs={{0,4},{1,5},{8,12},{9,13},{16,20},{17,21},{24,28},{25,29},{128,132... | collective-permute-start | bytes 99848 | tf_op jit(solution)/shard_map/ppermute | solution.py:11
  29.4 3.4 %collective-permute-start.12 = (f32[65,128]{1,0:T(8,128)S(1)}, f32[65,128]{1,0:T(8,128)S(1)}, u32[]{:S(2)}, u32[]{:S(2)}) collective-permute-start(f32[65,128]{1,0:T(8,128)S(1)} %add_add_fusion.4), channel_id=1, source_target_pairs={{0,68},{1,69},{8,76},{9,77},{16,84},{17,85},{24,92},{25,93},{128,1... | collective-permute-start | bytes 99848 | tf_op jit(solution)/shard_map/ppermute | solution.py:11
  30.8 3.8 %collective-permute-start.15 = (f32[256,128]{1,0:T(8,128)S(1)}, f32[256,128]{1,0:T(8,128)S(1)}, u32[]{:S(2)}, u32[]{:S(2)}) collective-permute-start(f32[256,128]{1,0:T(8,128)S(1)} %add_add_fusion.1), channel_id=1, source_target_pairs={{0,2},{1,3},{4,6},{5,7},{8,10},{9,11},{16,18},{17,19},{20,22},{21,... | collective-permute-start | bytes 393224 | tf_op jit(solution)/shard_map/ppermute | solution.py:108
  32.1 2.5 %collective-permute-start.16 = (f32[256,128]{1,0:T(8,128)S(1)}, f32[256,128]{1,0:T(8,128)S(1)}, u32[]{:S(2)}, u32[]{:S(2)}) collective-permute-start(f32[256,128]{1,0:T(8,128)S(1)} %add_add_fusion.1), channel_id=1, source_target_pairs={{8,12},{9,13},{4,14},{5,15},{24,28},{25,29},{20,30},{21,31},{40,44... | collective-permute-start | bytes 393224 | tf_op jit(solution)/shard_map/ppermute | solution.py:108
  34.6 22.4 %collective-permute-start.17 = (f32[65,128]{1,0:T(8,128)S(1)}, f32[65,128]{1,0:T(8,128)S(1)}, u32[]{:S(2)}, u32[]{:S(2)}) collective-permute-start(f32[65,128]{1,0:T(8,128)S(1)} %add_add_fusion.3), channel_id=1, source_target_pairs={{0,32},{1,33},{4,36},{5,37},{8,40},{9,41},{12,44},{13,45},{16,48},... | collective-permute-start | bytes 99848 | tf_op jit(solution)/shard_map/ppermute | solution.py:11
  35.9 21.1 %collective-permute-start.18 = (f32[65,128]{1,0:T(8,128)S(1)}, f32[65,128]{1,0:T(8,128)S(1)}, u32[]{:S(2)}, u32[]{:S(2)}) collective-permute-start(f32[65,128]{1,0:T(8,128)S(1)} %add_add_fusion.3), channel_id=1, source_target_pairs={{0,2},{1,3},{4,6},{5,7},{8,10},{9,11},{12,14},{13,15},{16,18},{17,... | collective-permute-start | bytes 99848 | tf_op jit(solution)/shard_map/ppermute | solution.py:11
  39.7 17.4 %collective-permute-start.19 = (f32[65,128]{1,0:T(8,128)S(1)}, f32[65,128]{1,0:T(8,128)S(1)}, u32[]{:S(2)}, u32[]{:S(2)}) collective-permute-start(f32[65,128]{1,0:T(8,128)S(1)} %add_add_fusion.3), channel_id=1, source_target_pairs={{0,34},{1,35},{4,38},{5,39},{8,42},{9,43},{12,46},{13,47},{16,50},... | collective-permute-start | bytes 99848 | tf_op jit(solution)/shard_map/ppermute | solution.py:11
  41.0 40.8 %collective-permute-start.20 = (f32[256,128]{1,0:T(8,128)S(1)}, f32[256,128]{1,0:T(8,128)S(1)}, u32[]{:S(2)}, u32[]{:S(2)}) collective-permute-start(f32[256,128]{1,0:T(8,128)S(1)} %add_add_fusion), channel_id=1, source_target_pairs={{0,0},{16,1},{32,2},{48,3},{64,4},{80,5},{96,6},{112,7},{128,8},{1... | collective-permute-start | bytes 393224 | tf_op jit(solution)/shard_map/ppermute | solution.py:11
  49.9 31.9 %collective-permute-start.21 = (f32[256,128]{1,0:T(8,128)S(1)}, f32[256,128]{1,0:T(8,128)S(1)}, u32[]{:S(2)}, u32[]{:S(2)}) collective-permute-start(f32[256,128]{1,0:T(8,128)S(1)} %add_add_fusion), channel_id=1, source_target_pairs={{0,256},{16,257},{32,258},{48,259},{64,260},{80,261},{96,262},{112... | collective-permute-start | bytes 393224 | tf_op jit(solution)/shard_map/ppermute | solution.py:11

commit v18 on v15

--- a/solution.py
+++ b/solution.py
@@ -100,7 +100,7 @@
     ]
     panel_rounds = [
         [[(0, 8), (1, 9)], [(0, 4), (1, 5)]],
-        [[(0, 2), (1, 3), (4, 6), (5, 7), (8, 10), (9, 11)], [(8, 12), (9, 13), (4, 14), (5, 15)]],
+        [[(8, 12), (9, 13), (4, 14), (5, 15)], [(0, 2), (1, 3), (4, 6), (5, 7), (8, 10), (9, 11)]],
     ]
     for pairs_list, offsets in zip(panel_rounds, corner_offsets[:2]):
         sent = panel

time: 84.6 us -> 85.2 us (level)
  no operation moved by 1% of the time
where the time goes in v18:
time: 85.2 us; the launch traced here: 84.6 us
  starting transfers between devices  46.4 us (54%)
  other arithmetic  25.4 us (30%)
  waiting for transfers between devices  7.98 us (9%)
  local copies, waits for them, and re-layouts  2.72 us (3%)
  matrix products  1.55 us (2%)
    ppermute x17, starting transfers between devices, both_axes(): return lax.ppermute(x, ('row', 'col'), pairs)  32.8 us
    another operation x3, other arithmetic, per_device(): factor = jnp.linalg.cholesky(lead_block)  12.4 us
    ppermute x4, starting transfers between devices, per_device(): panel = panel + lax.ppermute(sent, 'col', pairs)  11.7 us
    another operation x2, other arithmetic, lower_inverse(): return jax.scipy.linalg.solve_triangular(factor, eye, lower=True)  10.5 us
    ppermute x17, waiting for transfers between devices, both_axes(): return lax.ppermute(x, ('row', 'col'), pairs)  4.29 us
    ppermute x4, waiting for transfers between devices, per_device(): panel = panel + lax.ppermute(sent, 'col', pairs)  2.44 us
    ppermute x1, starting transfers between devices, per_device(): swapped = lax.ppermute(mine, 'col', [(0, 1), (1, 0)])  1.92 us
  transfers between devices with their start and end apart: 22, of which 3 were waited for; matrix products, arithmetic and copies ran while one was open for 31% of the time, Pallas kernels for 0%

profile of v18, /device:TPU:48, one launch (start us, length us, event | category | flops | bytes accessed | tf_op | source)
XLA Modules:
  0.0 84.6 jit_solution(9790204004948373872)
XLA Ops:
  0.0 0.8 slice.60
  0.8 0.7 collective-permute-start.1
  1.5 0.7 collective-permute-start.2
  2.2 0.9 %slice.61 = f32[256,64]{1,0:T(8,128)S(1)} slice(f32[256,512]{1,0:T(8,128)} %param.1), slice={[0:256], [0:64]} | slice | bytes 131072 | tf_op jit(solution)/shard_map/slice | solution.py:86
  3.1 1.9 %collective-permute-start = (f32[256,64]{1,0:T(8,128)S(1)}, f32[256,64]{1,0:T(8,128)S(1)}, u32[]{:S(2)}, u32[]{:S(2)}) collective-permute-start(f32[256,64]{1,0:T(8,128)S(1)} %slice.61), channel_id=1, source_target_pairs={{0,1},{1,0},{16,17},{17,16},{32,33},{33,32},{48,49},{49,48},{64,65... | collective-permute-start | bytes 196616 | tf_op jit(solution)/shard_map/ppermute | solution.py:87
  5.1 1.2 %collective-permute-done = f32[256,64]{1,0:T(8,128)S(1)} collective-permute-done((f32[256,64]{1,0:T(8,128)S(1)}, f32[256,64]{1,0:T(8,128)S(1)}, u32[]{:S(2)}, u32[]{:S(2)}) %collective-permute-start) | collective-permute-done | bytes 65568 | tf_op jit(solution)/shard_map/ppermute | solution.py:87
  6.3 0.8 select_select_fusion.1
  7.3 0.7 collective-permute-start.3
  8.0 0.7 collective-permute-start.4
  8.6 0.7 collective-permute-start.5
  9.3 0.7 collective-permute-start.6
  10.0 0.7 collective-permute-start.7
  10.7 1.3 %collective-permute-start.8 = (f32[65,128]{1,0:T(8,128)S(1)}, f32[65,128]{1,0:T(8,128)S(1)}, u32[]{:S(2)}, u32[]{:S(2)}) collective-permute-start(f32[65,128]{1,0:T(8,128)S(1)} %fusion.4), channel_id=1, source_target_pairs={{0,384},{1,385},{16,400},{17,401}} | collective-permute-start | bytes 99848 | tf_op jit(solution)/shard_map/ppermute | solution.py:11
  12.0 0.7 collective-permute-start.9
  12.8 8.4 %collective-permute-start.13 = (f32[256,128]{1,0:T(8,128)S(1)}, f32[256,128]{1,0:T(8,128)S(1)}, u32[]{:S(2)}, u32[]{:S(2)}) collective-permute-start(f32[256,128]{1,0:T(8,128)S(1)} %maximum_select_fusion), channel_id=1, source_target_pairs={{0,8},{1,9},{16,24},{17,25},{32,40},{33,41},{48,56},{49,57},{64,72... | collective-permute-start | bytes 393224 | tf_op jit(solution)/shard_map/ppermute | solution.py:108
  21.2 1.3 %collective-permute-start.14 = (f32[256,128]{1,0:T(8,128)S(1)}, f32[256,128]{1,0:T(8,128)S(1)}, u32[]{:S(2)}, u32[]{:S(2)}) collective-permute-start(f32[256,128]{1,0:T(8,128)S(1)} %maximum_select_fusion), channel_id=1, source_target_pairs={{0,4},{1,5},{16,20},{17,21},{32,36},{33,37},{48,52},{49,53},{64,68... | collective-permute-start | bytes 393224 | tf_op jit(solution)/shard_map/ppermute | solution.py:108
  22.6 4.3 %collective-permute-done.8 = f32[65,128]{1,0:T(8,128)S(1)} collective-permute-done((f32[65,128]{1,0:T(8,128)S(1)}, f32[65,128]{1,0:T(8,128)S(1)}, u32[]{:S(2)}, u32[]{:S(2)}) %collective-permute-start.8) | collective-permute-done | bytes 33312 | tf_op jit(solution)/shard_map/ppermute | solution.py:11
  26.8 1.3 %collective-permute-start.10 = (f32[65,128]{1,0:T(8,128)S(1)}, f32[65,128]{1,0:T(8,128)S(1)}, u32[]{:S(2)}, u32[]{:S(2)}) collective-permute-start(f32[65,128]{1,0:T(8,128)S(1)} %add_add_fusion.4), channel_id=1, source_target_pairs={{0,64},{1,65},{8,72},{9,73},{16,80},{17,81},{24,88},{25,89},{128,1... | collective-permute-start | bytes 99848 | tf_op jit(solution)/shard_map/ppermute | solution.py:11
  28.1 1.3 %collective-permute-start.11 = (f32[65,128]{1,0:T(8,128)S(1)}, f32[65,128]{1,0:T(8,128)S(1)}, u32[]{:S(2)}, u32[]{:S(2)}) collective-permute-start(f32[65,128]{1,0:T(8,128)S(1)} %add_add_fusion.4), channel_id=1, source_target_pairs={{0,4},{1,5},{8,12},{9,13},{16,20},{17,21},{24,28},{25,29},{128,132... | collective-permute-start | bytes 99848 | tf_op jit(solution)/shard_map/ppermute | solution.py:11
  29.4 1.3 %collective-permute-start.12 = (f32[65,128]{1,0:T(8,128)S(1)}, f32[65,128]{1,0:T(8,128)S(1)}, u32[]{:S(2)}, u32[]{:S(2)}) collective-permute-start(f32[65,128]{1,0:T(8,128)S(1)} %add_add_fusion.4), channel_id=1, source_target_pairs={{0,68},{1,69},{8,76},{9,77},{16,84},{17,85},{24,92},{25,93},{128,1... | collective-permute-start | bytes 99848 | tf_op jit(solution)/shard_map/ppermute | solution.py:11
  30.8 0.7 collective-permute-start.15
  31.5 1.3 %collective-permute-start.16 = (f32[256,128]{1,0:T(8,128)S(1)}, f32[256,128]{1,0:T(8,128)S(1)}, u32[]{:S(2)}, u32[]{:S(2)}) collective-permute-start(f32[256,128]{1,0:T(8,128)S(1)} %add_add_fusion.1), channel_id=1, source_target_pairs={{0,2},{1,3},{4,6},{5,7},{8,10},{9,11},{16,18},{17,19},{20,22},{21,... | collective-permute-start | bytes 393224 | tf_op jit(solution)/shard_map/ppermute | solution.py:108
  32.8 2.4 %collective-permute-done.16 = f32[256,128]{1,0:T(8,128)S(1)} collective-permute-done((f32[256,128]{1,0:T(8,128)S(1)}, f32[256,128]{1,0:T(8,128)S(1)}, u32[]{:S(2)}, u32[]{:S(2)}) %collective-permute-start.16) | collective-permute-done | bytes 131104 | tf_op jit(solution)/shard_map/ppermute | solution.py:108
  35.3 1.3 %collective-permute-start.17 = (f32[65,128]{1,0:T(8,128)S(1)}, f32[65,128]{1,0:T(8,128)S(1)}, u32[]{:S(2)}, u32[]{:S(2)}) collective-permute-start(f32[65,128]{1,0:T(8,128)S(1)} %add_add_fusion.3), channel_id=1, source_target_pairs={{0,32},{1,33},{4,36},{5,37},{8,40},{9,41},{12,44},{13,45},{16,48},... | collective-permute-start | bytes 99848 | tf_op jit(solution)/shard_map/ppermute | solution.py:11
  36.6 3.7 %collective-permute-start.18 = (f32[65,128]{1,0:T(8,128)S(1)}, f32[65,128]{1,0:T(8,128)S(1)}, u32[]{:S(2)}, u32[]{:S(2)}) collective-permute-start(f32[65,128]{1,0:T(8,128)S(1)} %add_add_fusion.3), channel_id=1, source_target_pairs={{0,2},{1,3},{4,6},{5,7},{8,10},{9,11},{12,14},{13,15},{16,18},{17,... | collective-permute-start | bytes 99848 | tf_op jit(solution)/shard_map/ppermute | solution.py:11
  40.3 1.3 %collective-permute-start.19 = (f32[65,128]{1,0:T(8,128)S(1)}, f32[65,128]{1,0:T(8,128)S(1)}, u32[]{:S(2)}, u32[]{:S(2)}) collective-permute-start(f32[65,128]{1,0:T(8,128)S(1)} %add_add_fusion.3), channel_id=1, source_target_pairs={{0,34},{1,35},{4,38},{5,39},{8,42},{9,43},{12,46},{13,47},{16,50},... | collective-permute-start | bytes 99848 | tf_op jit(solution)/shard_map/ppermute | solution.py:11
  41.7 9.7 %collective-permute-start.20 = (f32[256,128]{1,0:T(8,128)S(1)}, f32[256,128]{1,0:T(8,128)S(1)}, u32[]{:S(2)}, u32[]{:S(2)}) collective-permute-start(f32[256,128]{1,0:T(8,128)S(1)} %add_add_fusion), channel_id=1, source_target_pairs={{0,0},{16,1},{32,2},{48,3},{64,4},{80,5},{96,6},{112,7},{128,8},{1... | collective-permute-start | bytes 393224 | tf_op jit(solution)/shard_map/ppermute | solution.py:11
  51.3 6.3 %collective-permute-start.21 = (f32[256,128]{1,0:T(8,128)S(1)}, f32[256,128]{1,0:T(8,128)S(1)}, u32[]{:S(2)}, u32[]{:S(2)}) collective-permute-start(f32[256,128]{1,0:T(8,128)S(1)} %add_add_fusion), channel_id=1, source_target_pairs={{0,256},{16,257},{32,258},{48,259},{64,260},{80,261},{96,262},{112... | collective-permute-start | bytes 393224 | tf_op jit(solution)/shard_map/ppermute | solution.py:11
  58.3 11.7 %cholesky.20 = f32[128,128]{1,0:T(8,128)S(1)} custom-call(f32[128,128]{1,0:T(8,128)S(1)} %fusion.3), custom_call_target="Cholesky" | custom-call | tf_op jit(solution)/shard_map/jit(cholesky)/cholesky | solution.py:129
  70.7 0.7 select_bitcast_fusion
  71.4 9.8 %custom-call.7 = f32[1,128,128]{1,2,0:T(8,128)S(1)} custom-call(f32[1,128,128]{2,1,0:T(8,128)S(1)} %get-tuple-element.13), custom_call_target="InvertDiagBlocksLowerTriangular" | custom-call | tf_op jit(solution)/shard_map/jit(_solve_triangular)/triangular_solve | solution.py:71
  83.6 1.0 %pad_maximum_fusion = f32[256,512]{1,0:T(8,128)} fusion(f32[256,448]{1,0:T(8,128)S(1)} %slice.82, f32[256,64]{1,0:T(8,128)S(1)} %slice_select_fusion), kind=kLoop, calls=%fused_computation.2 | loop fusion | flops 131072 | bytes 1048576 | tf_op jit(solution)/shard_map/concatenate | solution.py:155
  (59 shorter events, 4.0 us)
Async XLA Ops:
  0.0 7.2 %copy-start = (f32[256,512]{1,0:T(8,128)S(1)}, f32[256,512]{1,0:T(8,128)}, u32[]{:S(2)}) copy-start(f32[256,512]{1,0:T(8,128)} %param.1) | copy-start | bytes 1572868
  0.8 4.2 %collective-permute-start.1 = (f32[64,64]{1,0:T(8,128)S(1)}, f32[64,64]{1,0:T(8,128)S(1)}, u32[]{:S(2)}, u32[]{:S(2)}) collective-permute-start(f32[64,64]{1,0:T(8,128)S(1)} %slice.60), channel_id=1, source_target_pairs={{17,0},{0,16}} | collective-permute-start | bytes 49160 | tf_op jit(solution)/shard_map/ppermute | solution.py:11
  1.5 3.6 %collective-permute-start.2 = (f32[64,64]{1,0:T(8,128)S(1)}, f32[64,64]{1,0:T(8,128)S(1)}, u32[]{:S(2)}, u32[]{:S(2)}) collective-permute-start(f32[64,64]{1,0:T(8,128)S(1)} %slice.60), channel_id=1, source_target_pairs={{17,1},{0,17}} | collective-permute-start | bytes 49160 | tf_op jit(solution)/shard_map/ppermute | solution.py:11
  3.1 3.2 %collective-permute-start = (f32[256,64]{1,0:T(8,128)S(1)}, f32[256,64]{1,0:T(8,128)S(1)}, u32[]{:S(2)}, u32[]{:S(2)}) collective-permute-start(f32[256,64]{1,0:T(8,128)S(1)} %slice.61), channel_id=1, source_target_pairs={{0,1},{1,0},{16,17},{17,16},{32,33},{33,32},{48,49},{49,48},{64,65... | collective-permute-start | bytes 196616 | tf_op jit(solution)/shard_map/ppermute | solution.py:87
  7.3 3.4 %collective-permute-start.3 = (f32[65,128]{1,0:T(8,128)S(1)}, f32[65,128]{1,0:T(8,128)S(1)}, u32[]{:S(2)}, u32[]{:S(2)}) collective-permute-start(f32[65,128]{1,0:T(8,128)S(1)} %fusion.4), channel_id=1, source_target_pairs={{0,8},{1,9},{16,24},{17,25}} | collective-permute-start | bytes 99848 | tf_op jit(solution)/shard_map/ppermute | solution.py:11
  8.0 4.0 %collective-permute-start.4 = (f32[65,128]{1,0:T(8,128)S(1)}, f32[65,128]{1,0:T(8,128)S(1)}, u32[]{:S(2)}, u32[]{:S(2)}) collective-permute-start(f32[65,128]{1,0:T(8,128)S(1)} %fusion.4), channel_id=1, source_target_pairs={{0,128},{1,129},{16,144},{17,145}} | collective-permute-start | bytes 99848 | tf_op jit(solution)/shard_map/ppermute | solution.py:11
  8.6 4.2 %collective-permute-start.5 = (f32[65,128]{1,0:T(8,128)S(1)}, f32[65,128]{1,0:T(8,128)S(1)}, u32[]{:S(2)}, u32[]{:S(2)}) collective-permute-start(f32[65,128]{1,0:T(8,128)S(1)} %fusion.4), channel_id=1, source_target_pairs={{0,136},{1,137},{16,152},{17,153}} | collective-permute-start | bytes 99848 | tf_op jit(solution)/shard_map/ppermute | solution.py:11
  9.3 11.9 %collective-permute-start.6 = (f32[65,128]{1,0:T(8,128)S(1)}, f32[65,128]{1,0:T(8,128)S(1)}, u32[]{:S(2)}, u32[]{:S(2)}) collective-permute-start(f32[65,128]{1,0:T(8,128)S(1)} %fusion.4), channel_id=1, source_target_pairs={{0,256},{1,257},{16,272},{17,273}} | collective-permute-start | bytes 99848 | tf_op jit(solution)/shard_map/ppermute | solution.py:11
  10.0 12.6 %collective-permute-start.7 = (f32[65,128]{1,0:T(8,128)S(1)}, f32[65,128]{1,0:T(8,128)S(1)}, u32[]{:S(2)}, u32[]{:S(2)}) collective-permute-start(f32[65,128]{1,0:T(8,128)S(1)} %fusion.4), channel_id=1, source_target_pairs={{0,264},{1,265},{16,280},{17,281}} | collective-permute-start | bytes 99848 | tf_op jit(solution)/shard_map/ppermute | solution.py:11
  10.7 16.1 %collective-permute-start.8 = (f32[65,128]{1,0:T(8,128)S(1)}, f32[65,128]{1,0:T(8,128)S(1)}, u32[]{:S(2)}, u32[]{:S(2)}) collective-permute-start(f32[65,128]{1,0:T(8,128)S(1)} %fusion.4), channel_id=1, source_target_pairs={{0,384},{1,385},{16,400},{17,401}} | collective-permute-start | bytes 99848 | tf_op jit(solution)/shard_map/ppermute | solution.py:11
  12.0 14.8 %collective-permute-start.9 = (f32[65,128]{1,0:T(8,128)S(1)}, f32[65,128]{1,0:T(8,128)S(1)}, u32[]{:S(2)}, u32[]{:S(2)}) collective-permute-start(f32[65,128]{1,0:T(8,128)S(1)} %fusion.4), channel_id=1, source_target_pairs={{0,392},{1,393},{16,408},{17,409}} | collective-permute-start | bytes 99848 | tf_op jit(solution)/shard_map/ppermute | solution.py:11
  12.8 18.0 %collective-permute-start.13 = (f32[256,128]{1,0:T(8,128)S(1)}, f32[256,128]{1,0:T(8,128)S(1)}, u32[]{:S(2)}, u32[]{:S(2)}) collective-permute-start(f32[256,128]{1,0:T(8,128)S(1)} %maximum_select_fusion), channel_id=1, source_target_pairs={{0,8},{1,9},{16,24},{17,25},{32,40},{33,41},{48,56},{49,57},{64,72... | collective-permute-start | bytes 393224 | tf_op jit(solution)/shard_map/ppermute | solution.py:108
  21.2 9.5 %collective-permute-start.14 = (f32[256,128]{1,0:T(8,128)S(1)}, f32[256,128]{1,0:T(8,128)S(1)}, u32[]{:S(2)}, u32[]{:S(2)}) collective-permute-start(f32[256,128]{1,0:T(8,128)S(1)} %maximum_select_fusion), channel_id=1, source_target_pairs={{0,4},{1,5},{16,20},{17,21},{32,36},{33,37},{48,52},{49,53},{64,68... | collective-permute-start | bytes 393224 | tf_op jit(solution)/shard_map/ppermute | solution.py:108
  26.8 5.9 %collective-permute-start.10 = (f32[65,128]{1,0:T(8,128)S(1)}, f32[65,128]{1,0:T(8,128)S(1)}, u32[]{:S(2)}, u32[]{:S(2)}) collective-permute-start(f32[65,128]{1,0:T(8,128)S(1)} %add_add_fusion.4), channel_id=1, source_target_pairs={{0,64},{1,65},{8,72},{9,73},{16,80},{17,81},{24,88},{25,89},{128,1... | collective-permute-start | bytes 99848 | tf_op jit(solution)/shard_map/ppermute | solution.py:11
  28.1 4.6 %collective-permute-start.11 = (f32[65,128]{1,0:T(8,128)S(1)}, f32[65,128]{1,0:T(8,128)S(1)}, u32[]{:S(2)}, u32[]{:S(2)}) collective-permute-start(f32[65,128]{1,0:T(8,128)S(1)} %add_add_fusion.4), channel_id=1, source_target_pairs={{0,4},{1,5},{8,12},{9,13},{16,20},{17,21},{24,28},{25,29},{128,132... | collective-permute-start | bytes 99848 | tf_op jit(solution)/shard_map/ppermute | solution.py:11
  29.4 3.4 %collective-permute-start.12 = (f32[65,128]{1,0:T(8,128)S(1)}, f32[65,128]{1,0:T(8,128)S(1)}, u32[]{:S(2)}, u32[]{:S(2)}) collective-permute-start(f32[65,128]{1,0:T(8,128)S(1)} %add_add_fusion.4), channel_id=1, source_target_pairs={{0,68},{1,69},{8,76},{9,77},{16,84},{17,85},{24,92},{25,93},{128,1... | collective-permute-start | bytes 99848 | tf_op jit(solution)/shard_map/ppermute | solution.py:11
  30.8 2.0 %collective-permute-start.15 = (f32[256,128]{1,0:T(8,128)S(1)}, f32[256,128]{1,0:T(8,128)S(1)}, u32[]{:S(2)}, u32[]{:S(2)}) collective-permute-start(f32[256,128]{1,0:T(8,128)S(1)} %add_add_fusion.1), channel_id=1, source_target_pairs={{8,12},{9,13},{4,14},{5,15},{24,28},{25,29},{20,30},{21,31},{40,44... | collective-permute-start | bytes 393224 | tf_op jit(solution)/shard_map/ppermute | solution.py:108
  31.5 3.8 %collective-permute-start.16 = (f32[256,128]{1,0:T(8,128)S(1)}, f32[256,128]{1,0:T(8,128)S(1)}, u32[]{:S(2)}, u32[]{:S(2)}) collective-permute-start(f32[256,128]{1,0:T(8,128)S(1)} %add_add_fusion.1), channel_id=1, source_target_pairs={{0,2},{1,3},{4,6},{5,7},{8,10},{9,11},{16,18},{17,19},{20,22},{21,... | collective-permute-start | bytes 393224 | tf_op jit(solution)/shard_map/ppermute | solution.py:108
  35.3 22.4 %collective-permute-start.17 = (f32[65,128]{1,0:T(8,128)S(1)}, f32[65,128]{1,0:T(8,128)S(1)}, u32[]{:S(2)}, u32[]{:S(2)}) collective-permute-start(f32[65,128]{1,0:T(8,128)S(1)} %add_add_fusion.3), channel_id=1, source_target_pairs={{0,32},{1,33},{4,36},{5,37},{8,40},{9,41},{12,44},{13,45},{16,48},... | collective-permute-start | bytes 99848 | tf_op jit(solution)/shard_map/ppermute | solution.py:11
  36.6 21.1 %collective-permute-start.18 = (f32[65,128]{1,0:T(8,128)S(1)}, f32[65,128]{1,0:T(8,128)S(1)}, u32[]{:S(2)}, u32[]{:S(2)}) collective-permute-start(f32[65,128]{1,0:T(8,128)S(1)} %add_add_fusion.3), channel_id=1, source_target_pairs={{0,2},{1,3},{4,6},{5,7},{8,10},{9,11},{12,14},{13,15},{16,18},{17,... | collective-permute-start | bytes 99848 | tf_op jit(solution)/shard_map/ppermute | solution.py:11
  40.3 17.4 %collective-permute-start.19 = (f32[65,128]{1,0:T(8,128)S(1)}, f32[65,128]{1,0:T(8,128)S(1)}, u32[]{:S(2)}, u32[]{:S(2)}) collective-permute-start(f32[65,128]{1,0:T(8,128)S(1)} %add_add_fusion.3), channel_id=1, source_target_pairs={{0,34},{1,35},{4,38},{5,39},{8,42},{9,43},{12,46},{13,47},{16,50},... | collective-permute-start | bytes 99848 | tf_op jit(solution)/shard_map/ppermute | solution.py:11
  41.7 41.0 %collective-permute-start.20 = (f32[256,128]{1,0:T(8,128)S(1)}, f32[256,128]{1,0:T(8,128)S(1)}, u32[]{:S(2)}, u32[]{:S(2)}) collective-permute-start(f32[256,128]{1,0:T(8,128)S(1)} %add_add_fusion), channel_id=1, source_target_pairs={{0,0},{16,1},{32,2},{48,3},{64,4},{80,5},{96,6},{112,7},{128,8},{1... | collective-permute-start | bytes 393224 | tf_op jit(solution)/shard_map/ppermute | solution.py:11
  51.3 31.3 %collective-permute-start.21 = (f32[256,128]{1,0:T(8,128)S(1)}, f32[256,128]{1,0:T(8,128)S(1)}, u32[]{:S(2)}, u32[]{:S(2)}) collective-permute-start(f32[256,128]{1,0:T(8,128)S(1)} %add_add_fusion), channel_id=1, source_target_pairs={{0,256},{16,257},{32,258},{48,259},{64,260},{80,261},{96,262},{112... | collective-permute-start | bytes 393224 | tf_op jit(solution)/shard_map/ppermute | solution.py:11

commit v19 on v15

--- a/solution.py
+++ b/solution.py
@@ -94,7 +94,7 @@
     holders_col = [0, 1]
     holders_k = {(0, 0), (0, 1), (1, 0), (1, 1)}
     corner_offsets = [
-        [(a * 16 + b * 8, c * 8) for a in (0, 1) for b in (0, 1) for c in (0, 1)][1:],
+        [(a * 16 + b * 8, c * 8) for a in (0, 1) for b in (0, 1) for c in (0, 1)][:0:-1],
         [(4, 0), (0, 4), (4, 4)],
         [(2, 0), (0, 2), (2, 2)],
     ]

time: 84.6 us -> 88.9 us (1.051)
  the two profiles are of different devices: /device:TPU:48 before, /device:TPU:57 now
where the time goes in v19:
time: 88.9 us; the launch traced here: 88.2 us
  starting transfers between devices  49.8 us (56%)
  other arithmetic  25.4 us (29%)
  waiting for transfers between devices  8.19 us (9%)
  local copies, waits for them, and re-layouts  2.72 us (3%)
  matrix products  1.55 us (2%)
    ppermute x17, starting transfers between devices, both_axes(): return lax.ppermute(x, ('row', 'col'), pairs)  36.1 us
    another operation x3, other arithmetic, per_device(): factor = jnp.linalg.cholesky(lead_block)  12.4 us
    ppermute x4, starting transfers between devices, per_device(): panel = panel + lax.ppermute(sent, 'col', pairs)  11.1 us
    another operation x2, other arithmetic, lower_inverse(): return jax.scipy.linalg.solve_triangular(factor, eye, lower=True)  10.5 us
    ppermute x17, waiting for transfers between devices, both_axes(): return lax.ppermute(x, ('row', 'col'), pairs)  6.36 us
    ppermute x1, starting transfers between devices, per_device(): swapped = lax.ppermute(mine, 'col', [(0, 1), (1, 0)])  2.58 us
  transfers between devices with their start and end apart: 22, of which 3 were waited for; matrix products, arithmetic and copies ran while one was open for 29% of the time, Pallas kernels for 0%

profile of v19, /device:TPU:57, one launch (start us, length us, event | category | flops | bytes accessed | tf_op | source)
XLA Modules:
  0.0 88.2 jit_solution(14244402903776865367)
XLA Ops:
  0.0 0.8 slice.60
  0.8 0.7 collective-permute-start.1
  1.5 0.7 collective-permute-start.2
  2.2 0.9 %slice.61 = f32[256,64]{1,0:T(8,128)S(1)} slice(f32[256,512]{1,0:T(8,128)} %param.1), slice={[0:256], [0:64]} | slice | bytes 131072 | tf_op jit(solution)/shard_map/slice | solution.py:86
  3.1 2.6 %collective-permute-start = (f32[256,64]{1,0:T(8,128)S(1)}, f32[256,64]{1,0:T(8,128)S(1)}, u32[]{:S(2)}, u32[]{:S(2)}) collective-permute-start(f32[256,64]{1,0:T(8,128)S(1)} %slice.61), channel_id=1, source_target_pairs={{0,1},{1,0},{16,17},{17,16},{32,33},{33,32},{48,49},{49,48},{64,65... | collective-permute-start | bytes 196616 | tf_op jit(solution)/shard_map/ppermute | solution.py:87
  5.7 0.9 %collective-permute-done = f32[256,64]{1,0:T(8,128)S(1)} collective-permute-done((f32[256,64]{1,0:T(8,128)S(1)}, f32[256,64]{1,0:T(8,128)S(1)}, u32[]{:S(2)}, u32[]{:S(2)}) %collective-permute-start) | collective-permute-done | bytes 65568 | tf_op jit(solution)/shard_map/ppermute | solution.py:87
  6.6 0.8 select_select_fusion.1
  7.6 0.7 collective-permute-start.3
  8.3 0.7 collective-permute-start.4
  8.9 0.7 collective-permute-start.5
  9.6 0.7 collective-permute-start.6
  10.3 0.7 collective-permute-start.7
  11.0 0.7 collective-permute-start.8
  11.7 0.7 collective-permute-start.9
  12.5 7.8 %collective-permute-start.13 = (f32[256,128]{1,0:T(8,128)S(1)}, f32[256,128]{1,0:T(8,128)S(1)}, u32[]{:S(2)}, u32[]{:S(2)}) collective-permute-start(f32[256,128]{1,0:T(8,128)S(1)} %maximum_select_fusion), channel_id=1, source_target_pairs={{0,8},{1,9},{16,24},{17,25},{32,40},{33,41},{48,56},{49,57},{64,72... | collective-permute-start | bytes 393224 | tf_op jit(solution)/shard_map/ppermute | solution.py:108
  20.3 1.3 %collective-permute-start.14 = (f32[256,128]{1,0:T(8,128)S(1)}, f32[256,128]{1,0:T(8,128)S(1)}, u32[]{:S(2)}, u32[]{:S(2)}) collective-permute-start(f32[256,128]{1,0:T(8,128)S(1)} %maximum_select_fusion), channel_id=1, source_target_pairs={{0,4},{1,5},{16,20},{17,21},{32,36},{33,37},{48,52},{49,53},{64,68... | collective-permute-start | bytes 393224 | tf_op jit(solution)/shard_map/ppermute | solution.py:108
  21.7 1.3 %collective-permute-start.10 = (f32[65,128]{1,0:T(8,128)S(1)}, f32[65,128]{1,0:T(8,128)S(1)}, u32[]{:S(2)}, u32[]{:S(2)}) collective-permute-start(f32[65,128]{1,0:T(8,128)S(1)} %add_add_fusion.4), channel_id=1, source_target_pairs={{0,64},{1,65},{8,72},{9,73},{16,80},{17,81},{24,88},{25,89},{128,1... | collective-permute-start | bytes 99848 | tf_op jit(solution)/shard_map/ppermute | solution.py:11
  23.0 0.7 collective-permute-start.11
  23.7 0.7 collective-permute-start.12
  24.4 0.9 %collective-permute-done.14 = f32[256,128]{1,0:T(8,128)S(1)} collective-permute-done((f32[256,128]{1,0:T(8,128)S(1)}, f32[256,128]{1,0:T(8,128)S(1)}, u32[]{:S(2)}, u32[]{:S(2)}) %collective-permute-start.14) | collective-permute-done | bytes 131104 | tf_op jit(solution)/shard_map/ppermute | solution.py:108
  25.3 1.3 %collective-permute-start.15 = (f32[256,128]{1,0:T(8,128)S(1)}, f32[256,128]{1,0:T(8,128)S(1)}, u32[]{:S(2)}, u32[]{:S(2)}) collective-permute-start(f32[256,128]{1,0:T(8,128)S(1)} %add_add_fusion.1), channel_id=1, source_target_pairs={{0,2},{1,3},{4,6},{5,7},{8,10},{9,11},{16,18},{17,19},{20,22},{21,... | collective-permute-start | bytes 393224 | tf_op jit(solution)/shard_map/ppermute | solution.py:108
  26.6 0.7 collective-permute-start.16
  27.3 6.3 %collective-permute-done.10 = f32[65,128]{1,0:T(8,128)S(1)} collective-permute-done((f32[65,128]{1,0:T(8,128)S(1)}, f32[65,128]{1,0:T(8,128)S(1)}, u32[]{:S(2)}, u32[]{:S(2)}) %collective-permute-start.10) | collective-permute-done | bytes 33312 | tf_op jit(solution)/shard_map/ppermute | solution.py:11
  33.7 1.3 %collective-permute-start.17 = (f32[65,128]{1,0:T(8,128)S(1)}, f32[65,128]{1,0:T(8,128)S(1)}, u32[]{:S(2)}, u32[]{:S(2)}) collective-permute-start(f32[65,128]{1,0:T(8,128)S(1)} %add_add_fusion.3), channel_id=1, source_target_pairs={{0,32},{1,33},{4,36},{5,37},{8,40},{9,41},{12,44},{13,45},{16,48},... | collective-permute-start | bytes 99848 | tf_op jit(solution)/shard_map/ppermute | solution.py:11
  35.0 1.3 %collective-permute-start.18 = (f32[65,128]{1,0:T(8,128)S(1)}, f32[65,128]{1,0:T(8,128)S(1)}, u32[]{:S(2)}, u32[]{:S(2)}) collective-permute-start(f32[65,128]{1,0:T(8,128)S(1)} %add_add_fusion.3), channel_id=1, source_target_pairs={{0,2},{1,3},{4,6},{5,7},{8,10},{9,11},{12,14},{13,15},{16,18},{17,... | collective-permute-start | bytes 99848 | tf_op jit(solution)/shard_map/ppermute | solution.py:11
  36.3 1.3 %collective-permute-start.19 = (f32[65,128]{1,0:T(8,128)S(1)}, f32[65,128]{1,0:T(8,128)S(1)}, u32[]{:S(2)}, u32[]{:S(2)}) collective-permute-start(f32[65,128]{1,0:T(8,128)S(1)} %add_add_fusion.3), channel_id=1, source_target_pairs={{0,34},{1,35},{4,38},{5,39},{8,42},{9,43},{12,46},{13,47},{16,50},... | collective-permute-start | bytes 99848 | tf_op jit(solution)/shard_map/ppermute | solution.py:11
  37.6 21.8 %collective-permute-start.20 = (f32[256,128]{1,0:T(8,128)S(1)}, f32[256,128]{1,0:T(8,128)S(1)}, u32[]{:S(2)}, u32[]{:S(2)}) collective-permute-start(f32[256,128]{1,0:T(8,128)S(1)} %add_add_fusion), channel_id=1, source_target_pairs={{0,0},{16,1},{32,2},{48,3},{64,4},{80,5},{96,6},{112,7},{128,8},{1... | collective-permute-start | bytes 393224 | tf_op jit(solution)/shard_map/ppermute | solution.py:11
  59.4 1.9 %collective-permute-start.21 = (f32[256,128]{1,0:T(8,128)S(1)}, f32[256,128]{1,0:T(8,128)S(1)}, u32[]{:S(2)}, u32[]{:S(2)}) collective-permute-start(f32[256,128]{1,0:T(8,128)S(1)} %add_add_fusion), channel_id=1, source_target_pairs={{0,256},{16,257},{32,258},{48,259},{64,260},{80,261},{96,262},{112... | collective-permute-start | bytes 393224 | tf_op jit(solution)/shard_map/ppermute | solution.py:11
  61.9 11.7 %cholesky.20 = f32[128,128]{1,0:T(8,128)S(1)} custom-call(f32[128,128]{1,0:T(8,128)S(1)} %fusion.3), custom_call_target="Cholesky" | custom-call | tf_op jit(solution)/shard_map/jit(cholesky)/cholesky | solution.py:129
  74.3 0.7 select_bitcast_fusion
  75.0 9.8 %custom-call.7 = f32[1,128,128]{1,2,0:T(8,128)S(1)} custom-call(f32[1,128,128]{2,1,0:T(8,128)S(1)} %get-tuple-element.13), custom_call_target="InvertDiagBlocksLowerTriangular" | custom-call | tf_op jit(solution)/shard_map/jit(_solve_triangular)/triangular_solve | solution.py:71
  87.2 1.0 %pad_maximum_fusion = f32[256,512]{1,0:T(8,128)} fusion(f32[256,448]{1,0:T(8,128)S(1)} %slice.82, f32[256,64]{1,0:T(8,128)S(1)} %slice_select_fusion), kind=kLoop, calls=%fused_computation.2 | loop fusion | flops 131072 | bytes 1048576 | tf_op jit(solution)/shard_map/concatenate | solution.py:155
  (59 shorter events, 4.0 us)
Async XLA Ops:
  0.0 7.5 %copy-start = (f32[256,512]{1,0:T(8,128)S(1)}, f32[256,512]{1,0:T(8,128)}, u32[]{:S(2)}) copy-start(f32[256,512]{1,0:T(8,128)} %param.1) | copy-start | bytes 1572868
  0.8 4.9 %collective-permute-start.1 = (f32[64,64]{1,0:T(8,128)S(1)}, f32[64,64]{1,0:T(8,128)S(1)}, u32[]{:S(2)}, u32[]{:S(2)}) collective-permute-start(f32[64,64]{1,0:T(8,128)S(1)} %slice.60), channel_id=1, source_target_pairs={{17,0},{0,16}} | collective-permute-start | bytes 49160 | tf_op jit(solution)/shard_map/ppermute | solution.py:11
  1.5 4.2 %collective-permute-start.2 = (f32[64,64]{1,0:T(8,128)S(1)}, f32[64,64]{1,0:T(8,128)S(1)}, u32[]{:S(2)}, u32[]{:S(2)}) collective-permute-start(f32[64,64]{1,0:T(8,128)S(1)} %slice.60), channel_id=1, source_target_pairs={{17,1},{0,17}} | collective-permute-start | bytes 49160 | tf_op jit(solution)/shard_map/ppermute | solution.py:11
  3.1 3.6 %collective-permute-start = (f32[256,64]{1,0:T(8,128)S(1)}, f32[256,64]{1,0:T(8,128)S(1)}, u32[]{:S(2)}, u32[]{:S(2)}) collective-permute-start(f32[256,64]{1,0:T(8,128)S(1)} %slice.61), channel_id=1, source_target_pairs={{0,1},{1,0},{16,17},{17,16},{32,33},{33,32},{48,49},{49,48},{64,65... | collective-permute-start | bytes 196616 | tf_op jit(solution)/shard_map/ppermute | solution.py:87
  7.6 3.4 %collective-permute-start.3 = (f32[65,128]{1,0:T(8,128)S(1)}, f32[65,128]{1,0:T(8,128)S(1)}, u32[]{:S(2)}, u32[]{:S(2)}) collective-permute-start(f32[65,128]{1,0:T(8,128)S(1)} %fusion.4), channel_id=1, source_target_pairs={{0,392},{1,393},{16,408},{17,409}} | collective-permute-start | bytes 99848 | tf_op jit(solution)/shard_map/ppermute | solution.py:11
  8.3 3.4 %collective-permute-start.4 = (f32[65,128]{1,0:T(8,128)S(1)}, f32[65,128]{1,0:T(8,128)S(1)}, u32[]{:S(2)}, u32[]{:S(2)}) collective-permute-start(f32[65,128]{1,0:T(8,128)S(1)} %fusion.4), channel_id=1, source_target_pairs={{0,384},{1,385},{16,400},{17,401}} | collective-permute-start | bytes 99848 | tf_op jit(solution)/shard_map/ppermute | solution.py:11
  8.9 3.5 %collective-permute-start.5 = (f32[65,128]{1,0:T(8,128)S(1)}, f32[65,128]{1,0:T(8,128)S(1)}, u32[]{:S(2)}, u32[]{:S(2)}) collective-permute-start(f32[65,128]{1,0:T(8,128)S(1)} %fusion.4), channel_id=1, source_target_pairs={{0,264},{1,265},{16,280},{17,281}} | collective-permute-start | bytes 99848 | tf_op jit(solution)/shard_map/ppermute | solution.py:11
  9.6 10.7 %collective-permute-start.6 = (f32[65,128]{1,0:T(8,128)S(1)}, f32[65,128]{1,0:T(8,128)S(1)}, u32[]{:S(2)}, u32[]{:S(2)}) collective-permute-start(f32[65,128]{1,0:T(8,128)S(1)} %fusion.4), channel_id=1, source_target_pairs={{0,256},{1,257},{16,272},{17,273}} | collective-permute-start | bytes 99848 | tf_op jit(solution)/shard_map/ppermute | solution.py:11
  10.3 11.4 %collective-permute-start.7 = (f32[65,128]{1,0:T(8,128)S(1)}, f32[65,128]{1,0:T(8,128)S(1)}, u32[]{:S(2)}, u32[]{:S(2)}) collective-permute-start(f32[65,128]{1,0:T(8,128)S(1)} %fusion.4), channel_id=1, source_target_pairs={{0,136},{1,137},{16,152},{17,153}} | collective-permute-start | bytes 99848 | tf_op jit(solution)/shard_map/ppermute | solution.py:11
  11.0 10.7 %collective-permute-start.8 = (f32[65,128]{1,0:T(8,128)S(1)}, f32[65,128]{1,0:T(8,128)S(1)}, u32[]{:S(2)}, u32[]{:S(2)}) collective-permute-start(f32[65,128]{1,0:T(8,128)S(1)} %fusion.4), channel_id=1, source_target_pairs={{0,128},{1,129},{16,144},{17,145}} | collective-permute-start | bytes 99848 | tf_op jit(solution)/shard_map/ppermute | solution.py:11
  11.7 10.0 %collective-permute-start.9 = (f32[65,128]{1,0:T(8,128)S(1)}, f32[65,128]{1,0:T(8,128)S(1)}, u32[]{:S(2)}, u32[]{:S(2)}) collective-permute-start(f32[65,128]{1,0:T(8,128)S(1)} %fusion.4), channel_id=1, source_target_pairs={{0,8},{1,9},{16,24},{17,25}} | collective-permute-start | bytes 99848 | tf_op jit(solution)/shard_map/ppermute | solution.py:11
  12.5 11.9 %collective-permute-start.13 = (f32[256,128]{1,0:T(8,128)S(1)}, f32[256,128]{1,0:T(8,128)S(1)}, u32[]{:S(2)}, u32[]{:S(2)}) collective-permute-start(f32[256,128]{1,0:T(8,128)S(1)} %maximum_select_fusion), channel_id=1, source_target_pairs={{0,8},{1,9},{16,24},{17,25},{32,40},{33,41},{48,56},{49,57},{64,72... | collective-permute-start | bytes 393224 | tf_op jit(solution)/shard_map/ppermute | solution.py:108
  20.3 4.9 %collective-permute-start.14 = (f32[256,128]{1,0:T(8,128)S(1)}, f32[256,128]{1,0:T(8,128)S(1)}, u32[]{:S(2)}, u32[]{:S(2)}) collective-permute-start(f32[256,128]{1,0:T(8,128)S(1)} %maximum_select_fusion), channel_id=1, source_target_pairs={{0,4},{1,5},{16,20},{17,21},{32,36},{33,37},{48,52},{49,53},{64,68... | collective-permute-start | bytes 393224 | tf_op jit(solution)/shard_map/ppermute | solution.py:108
  21.7 11.9 %collective-permute-start.10 = (f32[65,128]{1,0:T(8,128)S(1)}, f32[65,128]{1,0:T(8,128)S(1)}, u32[]{:S(2)}, u32[]{:S(2)}) collective-permute-start(f32[65,128]{1,0:T(8,128)S(1)} %add_add_fusion.4), channel_id=1, source_target_pairs={{0,64},{1,65},{8,72},{9,73},{16,80},{17,81},{24,88},{25,89},{128,1... | collective-permute-start | bytes 99848 | tf_op jit(solution)/shard_map/ppermute | solution.py:11
  23.0 10.6 %collective-permute-start.11 = (f32[65,128]{1,0:T(8,128)S(1)}, f32[65,128]{1,0:T(8,128)S(1)}, u32[]{:S(2)}, u32[]{:S(2)}) collective-permute-start(f32[65,128]{1,0:T(8,128)S(1)} %add_add_fusion.4), channel_id=1, source_target_pairs={{0,4},{1,5},{8,12},{9,13},{16,20},{17,21},{24,28},{25,29},{128,132... | collective-permute-start | bytes 99848 | tf_op jit(solution)/shard_map/ppermute | solution.py:11
  23.7 9.9 %collective-permute-start.12 = (f32[65,128]{1,0:T(8,128)S(1)}, f32[65,128]{1,0:T(8,128)S(1)}, u32[]{:S(2)}, u32[]{:S(2)}) collective-permute-start(f32[65,128]{1,0:T(8,128)S(1)} %add_add_fusion.4), channel_id=1, source_target_pairs={{0,68},{1,69},{8,76},{9,77},{16,84},{17,85},{24,92},{25,93},{128,1... | collective-permute-start | bytes 99848 | tf_op jit(solution)/shard_map/ppermute | solution.py:11
  25.3 8.3 %collective-permute-start.15 = (f32[256,128]{1,0:T(8,128)S(1)}, f32[256,128]{1,0:T(8,128)S(1)}, u32[]{:S(2)}, u32[]{:S(2)}) collective-permute-start(f32[256,128]{1,0:T(8,128)S(1)} %add_add_fusion.1), channel_id=1, source_target_pairs={{0,2},{1,3},{4,6},{5,7},{8,10},{9,11},{16,18},{17,19},{20,22},{21,... | collective-permute-start | bytes 393224 | tf_op jit(solution)/shard_map/ppermute | solution.py:108
  26.6 7.0 %collective-permute-start.16 = (f32[256,128]{1,0:T(8,128)S(1)}, f32[256,128]{1,0:T(8,128)S(1)}, u32[]{:S(2)}, u32[]{:S(2)}) collective-permute-start(f32[256,128]{1,0:T(8,128)S(1)} %add_add_fusion.1), channel_id=1, source_target_pairs={{8,12},{9,13},{4,14},{5,15},{24,28},{25,29},{20,30},{21,31},{40,44... | collective-permute-start | bytes 393224 | tf_op jit(solution)/shard_map/ppermute | solution.py:108
  33.7 27.6 %collective-permute-start.17 = (f32[65,128]{1,0:T(8,128)S(1)}, f32[65,128]{1,0:T(8,128)S(1)}, u32[]{:S(2)}, u32[]{:S(2)}) collective-permute-start(f32[65,128]{1,0:T(8,128)S(1)} %add_add_fusion.3), channel_id=1, source_target_pairs={{0,32},{1,33},{4,36},{5,37},{8,40},{9,41},{12,44},{13,45},{16,48},... | collective-permute-start | bytes 99848 | tf_op jit(solution)/shard_map/ppermute | solution.py:11
  35.0 26.3 %collective-permute-start.18 = (f32[65,128]{1,0:T(8,128)S(1)}, f32[65,128]{1,0:T(8,128)S(1)}, u32[]{:S(2)}, u32[]{:S(2)}) collective-permute-start(f32[65,128]{1,0:T(8,128)S(1)} %add_add_fusion.3), channel_id=1, source_target_pairs={{0,2},{1,3},{4,6},{5,7},{8,10},{9,11},{12,14},{13,15},{16,18},{17,... | collective-permute-start | bytes 99848 | tf_op jit(solution)/shard_map/ppermute | solution.py:11
  36.3 25.1 %collective-permute-start.19 = (f32[65,128]{1,0:T(8,128)S(1)}, f32[65,128]{1,0:T(8,128)S(1)}, u32[]{:S(2)}, u32[]{:S(2)}) collective-permute-start(f32[65,128]{1,0:T(8,128)S(1)} %add_add_fusion.3), channel_id=1, source_target_pairs={{0,34},{1,35},{4,38},{5,39},{8,42},{9,43},{12,46},{13,47},{16,50},... | collective-permute-start | bytes 99848 | tf_op jit(solution)/shard_map/ppermute | solution.py:11
  37.6 48.7 %collective-permute-start.20 = (f32[256,128]{1,0:T(8,128)S(1)}, f32[256,128]{1,0:T(8,128)S(1)}, u32[]{:S(2)}, u32[]{:S(2)}) collective-permute-start(f32[256,128]{1,0:T(8,128)S(1)} %add_add_fusion), channel_id=1, source_target_pairs={{0,0},{16,1},{32,2},{48,3},{64,4},{80,5},{96,6},{112,7},{128,8},{1... | collective-permute-start | bytes 393224 | tf_op jit(solution)/shard_map/ppermute | solution.py:11
  59.4 26.9 %collective-permute-start.21 = (f32[256,128]{1,0:T(8,128)S(1)}, f32[256,128]{1,0:T(8,128)S(1)}, u32[]{:S(2)}, u32[]{:S(2)}) collective-permute-start(f32[256,128]{1,0:T(8,128)S(1)} %add_add_fusion), channel_id=1, source_target_pairs={{0,256},{16,257},{32,258},{48,259},{64,260},{80,261},{96,262},{112... | collective-permute-start | bytes 393224 | tf_op jit(solution)/shard_map/ppermute | solution.py:11
